TPU v7x, 512 devices: a whole 4x8x8 slice. The times are simulated.
512 devices in a mesh: gx: 32 (over x, z), gy: 16 (over y, core).
Axes of the slice: x: 4, y: 8, z: 8, core: 2. Of those that a mesh axis runs over, the one named last changes fastest.
Arguments:
- sources: float32 [1024, 512, 192], P('gx', 'gy'), may hold values from -12 to 12
- permeability: float32 [1024, 512], P('gx', 'gy'), may hold values from 0.2 to 5
- storage: float32 [1024, 512], P('gx', 'gy'), may hold values from 0.05 to 1
- basis: float32 [8, 1024, 512], P(None, 'gx', 'gy'), may hold values from -0.3 to 0.3
- local_inverse: bfloat16 [32, 16, 1024, 1600], P('gx', 'gy'), may hold values from -0.2 to 0.4
- coarse_inverse: float32 [4096, 4096], P(('gx', 'gy')), may hold values from -1.2 to 2.2
Outputs:
- solution: float32 [1024, 512, 192], P('gx', 'gy')
- residual_norms: float32 [3, 192], replicated
- initial_norms: float32 [192], replicated
All inputs are finite; a program needn't handle non-finite values.
Results may differ from a plain program's by a relative error of at most 0.0007.
Values may be sent and summed in bfloat16 or wider, within the bound.
No kernel may reach another device: no remote copies, remote signals or barrier semaphores. Data moves between devices by JAX's collectives and lax.ppermute only.
A program may use at most 64 MiB of HBM per device.

v0:
```python
import jax
import jax.numpy as jnp
from jax import lax
from jax.sharding import PartitionSpec as P

OV = 4
ITERS = 3


lower_bound = 0.15
upper_bound = 1.9
highest = lax.Precision.HIGHEST


def extended(cells, sides, width):
    for axis, dim in sides:
        count = lax.axis_size(axis)
        ends = count - 1
        head = lax.slice_in_dim(cells, 0, width, axis=dim)
        tail = lax.slice_in_dim(cells, cells.shape[dim] - width, cells.shape[dim], axis=dim)
        cells = jnp.concatenate(
            [
                lax.ppermute(tail, axis, [(i, (i + 1) % count) for i in range(ends)]),
                cells,
                lax.ppermute(head, axis, [((i + 1) % count, i) for i in range(ends)]),
            ],
            axis=dim,
        )
    return cells


def neighbour(padded, offset_row, offset_col):
    inner_rows = padded.shape[0] - 2
    inner_cols = padded.shape[1] - 2
    return padded[
        1 + offset_row : 1 + offset_row + inner_rows, 1 + offset_col : 1 + offset_col + inner_cols
    ]


def operate(field_pad, kappa_pad, storage_used):
    centre = neighbour(field_pad, 0, 0)
    kappa = neighbour(kappa_pad, 0, 0)
    total = storage_used[:, :, None] * centre
    for offset_row, offset_col in ((1, 0), (-1, 0), (0, 1), (0, -1)):
        faces = 0.5 * (kappa + neighbour(kappa_pad, offset_row, offset_col))
        total = total + faces[:, :, None] * (centre - neighbour(field_pad, offset_row, offset_col))
    return total


def on_device(sources, permeability, storage, basis, local_inverse, coarse_inverse):
    patch = sources.shape[0]
    fields = sources.shape[2]
    modes = basis.shape[0]
    margin = OV
    extent = patch + 2 * margin
    cells = float(patch * patch * lax.axis_size("gx") * lax.axis_size("gy"))
    flat_basis = basis.reshape(modes, patch * patch)
    inverse_rows = local_inverse[0, 0]
    stacked = jnp.stack([permeability, storage])
    padded = extended(stacked, (("gx", 1), ("gy", 2)), 1)
    kappa_pad = padded[0]
    state = sources

    def rounded_window(current):
        return extended(current.astype(jnp.bfloat16), (("gx", 0), ("gy", 1)), margin)

    def squares_total(current_core):
        return lax.psum(jnp.sum(current_core * current_core, axis=(0, 1)), ("gx", "gy"))

    def precondition(current):
        window = rounded_window(current).reshape(extent * extent, fields)
        local_part = jnp.dot(inverse_rows, window, preferred_element_type=jnp.float32).reshape(
            patch, patch, fields
        )
        flat_core = current.reshape(patch * patch, fields)
        restricted = jnp.dot(flat_basis, flat_core, precision=highest)
        coarse_part = jnp.dot(
            coarse_inverse,
            lax.all_gather(restricted, ("gx", "gy"), axis=0, tiled=True),
            precision=highest,
        )
        squares = squares_total(current)
        prolonged = jnp.dot(flat_basis.T, coarse_part, precision=highest).reshape(
            patch, patch, fields
        )
        return (local_part + prolonged, squares)

    centre = 0.5 * (upper_bound + lower_bound)
    half_width = 0.5 * (upper_bound - lower_bound)
    relative = centre / half_width
    weight_prev = 1.0 / relative
    solution = jnp.zeros_like(sources)
    corrected, initial = precondition(state)
    history = []
    update = corrected / centre
    for index in range(ITERS):
        solution = solution + update
        step_pad = extended(update, (("gx", 0), ("gy", 1)), 1)
        state = state - operate(step_pad, kappa_pad, storage)
        if index + 1 < ITERS:
            corrected, squares = precondition(state)
            history.append(squares)
            weight_next = 1.0 / (2.0 * relative - weight_prev)
            update = weight_next * weight_prev * update + 2.0 * weight_next / half_width * corrected
            weight_prev = weight_next
        else:
            history.append(squares_total(state))
    return (solution, jnp.sqrt(jnp.stack(history) / cells), jnp.sqrt(initial / cells))


def solution(mesh):
    placed = (
        P("gx", "gy", None),
        P("gx", "gy"),
        P("gx", "gy"),
        P(None, "gx", "gy"),
        P("gx", "gy", None, None),
        P(("gx", "gy"), None),
    )
    return jax.shard_map(
        on_device,
        mesh=mesh,
        in_specs=placed,
        out_specs=(P("gx", "gy", None), P(), P()),
        check_vma=False,
    )
```

profile of v0, /device:TPU:1, one launch (start us, length us, event | category | flops | bytes accessed | tf_op | source)
XLA Modules:
  0.0 572.1 jit_solution(11102322538769110874)
XLA Ops:
  7.2 2.8 convolution_bitcast_fusion.2
  11.5 5.4 collective-permute-start.4
  18.1 2.4 multiply_reduce_fusion
  22.0 4.7 collective-permute-start
  30.0 2.0 collective-permute-done.1
  33.1 5.6 collective-permute-start.2
  38.7 2.5 collective-permute-start.3
  41.9 3.1 collective-permute-start.6
  45.0 1.9 collective-permute-start.7
  47.0 2.4 pad_maximum_fusion.24
  49.4 86.9 %all-gather.4.cloned.1.call-done = f32[4096,192]{1,0:T(8,128)} async-done(((f32[8,192]{1,0:T(8,128)}), f32[4096,192]{1,0:T(8,128)}) %all-gather.4.cloned.1.call-update) | async-done | bytes 3145744 | tf_op jit(solution)/shard_map/all_gather | solution.py:79
  136.3 4.3 fusion.90
  143.2 2.5 copy.18
  147.2 2.7 collective-permute-start.9
  152.1 2.5 collective-permute-done.8
  154.7 3.6 collective-permute-start.10
  158.3 2.3 collective-permute-start.11
  161.6 2.5 multiply_reduce_fusion.2
  167.7 3.1 collective-permute-start.12
  172.5 4.0 collective-permute-done.13
  176.5 5.0 collective-permute-start.14
  181.6 2.1 collective-permute-start.15
  183.7 4.0 collective-permute-done.15
  189.1 96.9 %all-gather.6.cloned.1.call-done = f32[4096,192]{1,0:T(8,128)} async-done(((f32[8,192]{1,0:T(8,128)}), f32[4096,192]{1,0:T(8,128)}) %all-gather.6.cloned.1.call-update) | async-done | bytes 3145744 | tf_op jit(solution)/shard_map/all_gather | solution.py:79
  285.9 4.3 fusion.92
  292.9 2.5 copy.20
  297.2 2.7 collective-permute-start.17
  301.2 3.3 collective-permute-done.16
  304.6 3.6 collective-permute-start.18
  308.3 2.3 collective-permute-start.19
  311.6 2.6 fusion.81
  317.3 3.1 collective-permute-start.20
  322.1 3.9 collective-permute-done.21
  327.0 5.1 collective-permute-start.22
  332.1 1.9 collective-permute-start.23
  334.1 4.0 collective-permute-done.23
  338.0 2.4 pad_maximum_fusion.26
  340.4 95.6 %all-gather.8.cloned.1.call-done = f32[4096,192]{1,0:T(8,128)} async-done(((f32[8,192]{1,0:T(8,128)}), f32[4096,192]{1,0:T(8,128)}) %all-gather.8.cloned.1.call-update) | async-done | bytes 3145744 | tf_op jit(solution)/shard_map/all_gather | solution.py:79
  436.0 4.3 fusion.94
  441.1 1.9 fusion.27
  443.0 2.4 copy.22
  445.4 3.3 multiply_add_fusion
  448.8 2.8 collective-permute-start.25
  452.9 3.3 collective-permute-done.24
  456.3 3.6 collective-permute-start.26
  460.0 2.3 collective-permute-start.27
  463.3 2.0 multiply_reduce_fusion.1
  465.3 99.0 %all-reduce = (f32[1,192]{1,0:T(1,128)S(1)}, f32[1,192]{1,0:T(1,128)S(1)}, f32[1,192]{1,0:T(1,128)S(1)}, f32[192]{0:T(256)S(1)}) all-reduce(f32[1,192]{1,0:T(1,128)S(1)} %bitcast.86, f32[1,192]{1,0:T(1,128)S(1)} %bitcast.85, f32[1,192]{1,0:T(1,128)S(1)} %bitcast.87, f32[192]{0:T(256)S(1)} %copy-done.32), channel_id=1, replica_groups=mesh['gx'=32,'gy'=16] {'gx','gy'}, use_global_device_ids=true, to_apply=%region_5.0 | all-reduce | flops 768 | bytes 6144 | tf_op jit(solution)/shard_map/psum | solution.py:68
  (133 shorter events, 40.5 us)
Async XLA Ops:
  7.2 134.2 %copy-start = (bf16[1,1,1024,1600]{2,3,1,0:T(8,128)(2,1)S(1)}, bf16[1,1,1024,1600]{2,3,1,0:T(8,128)(2,1)}, u32[]{:S(2)}) copy-start(bf16[1,1,1024,1600]{2,3,1,0:T(8,128)(2,1)} %param.10) | copy-start | bytes 9830404
  7.2 21.4 %copy-start.12 = (f32[8,32,32]{2,1,0:T(8,128)S(1)}, f32[8,32,32]{2,1,0:T(8,128)}, u32[]{:S(2)}) copy-start(f32[8,32,32]{2,1,0:T(8,128)} %param.9) | copy-start | bytes 98308
  7.2 20.8 %copy-start.14 = (f32[32,32]{1,0:T(8,128)S(1)}, f32[32,32]{1,0:T(8,128)}, u32[]{:S(2)}) copy-start(f32[32,32]{1,0:T(8,128)} %param.8) | copy-start | bytes 12292
  7.2 129.1 %all-gather.4.cloned.1.call-start = ((), (), s32[]{:S(2)}) async-start(), calls=%async_computation | async-start | bytes 4202496 | tf_op jit(solution)/shard_map/all_gather | solution.py:79
  10.1 275.8 %all-gather.6.cloned.1.call-start = ((), (), s32[]{:S(2)}) async-start(), calls=%async_computation.1 | async-start | bytes 4202496 | tf_op jit(solution)/shard_map/all_gather | solution.py:79
  11.5 17.8 %collective-permute-start.4 = (f32[2,1,32]{2,1,0:T(1,128)}, f32[2,1,32]{2,1,0:T(1,128)}, u32[]{:S(2)}, u32[]{:S(2)}) collective-permute-start(f32[2,1,32]{2,1,0:T(1,128)} %get-tuple-element.43), channel_id=1, source_target_pairs={{0,16},{16,32},{32,48},{48,64},{64,80},{80,96},{96,112},{112,128},... | collective-permute-start | bytes 776 | tf_op jit(solution)/shard_map/ppermute | solution.py:23
  16.8 12.5 %collective-permute-start.5 = (f32[2,1,32]{2,1,0:T(1,128)}, f32[2,1,32]{2,1,0:T(1,128)}, u32[]{:S(2)}, u32[]{:S(2)}) collective-permute-start(f32[2,1,32]{2,1,0:T(1,128)} %get-tuple-element.44), channel_id=1, source_target_pairs={{16,0},{32,16},{48,32},{64,48},{80,64},{96,80},{112,96},{128,112},... | collective-permute-start | bytes 776 | tf_op jit(solution)/shard_map/ppermute | solution.py:25
  20.5 115.8 %copy-start.13 = (f32[8,4096]{1,0:T(8,128)S(1)}, f32[8,4096]{1,0:T(8,128)}, u32[]{:S(2)}) copy-start(f32[8,4096]{1,0:T(8,128)} %param.11) | copy-start | bytes 393220
  22.0 8.1 %collective-permute-start = (bf16[4,32,192]{2,1,0:T(8,128)(2,1)}, bf16[4,32,192]{2,1,0:T(8,128)(2,1)}, u32[]{:S(2)}, u32[]{:S(2)}) collective-permute-start(bf16[4,32,192]{2,1,0:T(8,128)(2,1)} %get-tuple-element.39), channel_id=1, source_target_pairs={{0,16},{16,32},{32,48},{48,64},{64,80},{80,96},{96,112},{112,128},... | collective-permute-start | bytes 147464 | tf_op jit(solution)/shard_map/ppermute | solution.py:23
  26.7 5.3 collective-permute-start.1
  33.1 13.8 %collective-permute-start.2 = (bf16[40,4,192]{2,1,0:T(4,128)(2,1)S(1)}, bf16[40,4,192]{2,1,0:T(4,128)(2,1)S(1)}, u32[]{:S(2)}, u32[]{:S(2)}) collective-permute-start(bf16[40,4,192]{2,1,0:T(4,128)(2,1)S(1)} %get-tuple-element.33), channel_id=1, source_target_pairs={{0,1},{1,2},{2,3},{3,4},{4,5},{5,6},{6,7},{7,8},{8,9},{9,10},{10,1... | collective-permute-start | bytes 184328 | tf_op jit(solution)/shard_map/ppermute | solution.py:23
  38.7 8.2 %collective-permute-start.3 = (bf16[40,4,192]{2,1,0:T(4,128)(2,1)S(1)}, bf16[40,4,192]{2,1,0:T(4,128)(2,1)S(1)}, u32[]{:S(2)}, u32[]{:S(2)}) collective-permute-start(bf16[40,4,192]{2,1,0:T(4,128)(2,1)S(1)} %get-tuple-element.34), channel_id=1, source_target_pairs={{1,0},{2,1},{3,2},{4,3},{5,4},{6,5},{7,6},{8,7},{9,8},{10,9},{11,1... | collective-permute-start | bytes 184328 | tf_op jit(solution)/shard_map/ppermute | solution.py:25
  41.9 109.3 %collective-permute-start.6 = (f32[2,34,1]{2,1,0:T(8,128)}, f32[2,34,1]{2,1,0:T(8,128)}, u32[]{:S(2)}, u32[]{:S(2)}) collective-permute-start(f32[2,34,1]{2,1,0:T(8,128)} %get-tuple-element.41), channel_id=1, source_target_pairs={{0,1},{1,2},{2,3},{3,4},{4,5},{5,6},{6,7},{7,8},{8,9},{9,10},{10,1... | collective-permute-start | bytes 824 | tf_op jit(solution)/shard_map/ppermute | solution.py:23
  45.0 106.2 %collective-permute-start.7 = (f32[2,34,1]{2,1,0:T(8,128)}, f32[2,34,1]{2,1,0:T(8,128)}, u32[]{:S(2)}, u32[]{:S(2)}) collective-permute-start(f32[2,34,1]{2,1,0:T(8,128)} %get-tuple-element.42), channel_id=1, source_target_pairs={{1,0},{2,1},{3,2},{4,3},{5,4},{6,5},{7,6},{8,7},{9,8},{10,9},{11,1... | collective-permute-start | bytes 824 | tf_op jit(solution)/shard_map/ppermute | solution.py:25
  145.7 15.9 %copy-start.7 = (f32[32,32,192]{2,1,0:T(8,128)S(1)}, f32[32,32,192]{2,1,0:T(8,128)}, u32[]{:S(2)}) copy-start(f32[32,32,192]{2,1,0:T(8,128)} %param.6) | copy-start | bytes 2359300
  145.7 15.9 %copy-start.31 = (f32[32,32]{1,0:T(8,128)S(1)}, f32[32,32]{1,0:T(8,128)}, u32[]{:S(2)}) copy-start(f32[32,32]{1,0:T(8,128)} %broadcast_multiply_fusion.1) | copy-start | bytes 12292
  147.2 4.9 collective-permute-start.9
  149.9 4.7 collective-permute-start.8
  154.7 6.0 %collective-permute-start.10 = (f32[34,1,192]{2,1,0:T(1,128)S(1)}, f32[34,1,192]{2,1,0:T(1,128)S(1)}, u32[]{:S(2)}, u32[]{:S(2)}) collective-permute-start(f32[34,1,192]{2,1,0:T(1,128)S(1)} %get-tuple-element.19), channel_id=1, source_target_pairs={{1,0},{2,1},{3,2},{4,3},{5,4},{6,5},{7,6},{8,7},{9,8},{10,9},{11,1... | collective-permute-start | bytes 78344 | tf_op jit(solution)/shard_map/ppermute | solution.py:25
  158.3 3.3 collective-permute-start.11
  166.4 269.6 %all-gather.8.cloned.1.call-start = ((), (), s32[]{:S(2)}) async-start(), calls=%async_computation.2 | async-start | bytes 4202496 | tf_op jit(solution)/shard_map/all_gather | solution.py:79
  167.7 4.7 collective-permute-start.12
  170.8 5.6 collective-permute-start.13
  176.5 7.2 %collective-permute-start.14 = (bf16[40,4,192]{2,1,0:T(4,128)(2,1)S(1)}, bf16[40,4,192]{2,1,0:T(4,128)(2,1)S(1)}, u32[]{:S(2)}, u32[]{:S(2)}) collective-permute-start(bf16[40,4,192]{2,1,0:T(4,128)(2,1)S(1)} %get-tuple-element.31), channel_id=1, source_target_pairs={{0,1},{1,2},{2,3},{3,4},{4,5},{5,6},{6,7},{7,8},{8,9},{9,10},{10,1... | collective-permute-start | bytes 184328 | tf_op jit(solution)/shard_map/ppermute | solution.py:23
  181.6 6.2 %collective-permute-start.15 = (bf16[40,4,192]{2,1,0:T(4,128)(2,1)S(1)}, bf16[40,4,192]{2,1,0:T(4,128)(2,1)S(1)}, u32[]{:S(2)}, u32[]{:S(2)}) collective-permute-start(bf16[40,4,192]{2,1,0:T(4,128)(2,1)S(1)} %get-tuple-element.32), channel_id=1, source_target_pairs={{1,0},{2,1},{3,2},{4,3},{5,4},{6,5},{7,6},{8,7},{9,8},{10,9},{11,1... | collective-permute-start | bytes 184328 | tf_op jit(solution)/shard_map/ppermute | solution.py:25
  295.3 16.2 %copy-start.4 = (f32[32,32,192]{2,1,0:T(8,128)S(1)}, f32[32,32,192]{2,1,0:T(8,128)}, u32[]{:S(2)}) copy-start(f32[32,32,192]{2,1,0:T(8,128)} %copy-done.3) | copy-start | bytes 2359300
  295.4 16.2 %copy-start.19 = (f32[32,32]{1,0:T(8,128)S(1)}, f32[32,32]{1,0:T(8,128)}, u32[]{:S(2)}) copy-start(f32[32,32]{1,0:T(8,128)} %copy-done.18) | copy-start | bytes 12292
  295.4 16.2 %copy-start.22 = (f32[32,32]{1,0:T(8,128)S(1)}, f32[32,32]{1,0:T(8,128)}, u32[]{:S(2)}) copy-start(f32[32,32]{1,0:T(8,128)} %copy-done.21) | copy-start | bytes 12292
  295.4 16.2 %copy-start.25 = (f32[32,32]{1,0:T(8,128)S(1)}, f32[32,32]{1,0:T(8,128)}, u32[]{:S(2)}) copy-start(f32[32,32]{1,0:T(8,128)} %copy-done.24) | copy-start | bytes 12292
  295.4 16.2 %copy-start.28 = (f32[32,32]{1,0:T(8,128)S(1)}, f32[32,32]{1,0:T(8,128)}, u32[]{:S(2)}) copy-start(f32[32,32]{1,0:T(8,128)} %copy-done.27) | copy-start | bytes 12292
  297.2 17.0 %copy-start.2 = (f32[32,32,192]{2,1,0:T(8,128)}, f32[32,32,192]{2,1,0:T(8,128)S(1)}, u32[]{:S(2)}) copy-start(f32[32,32,192]{2,1,0:T(8,128)S(1)} %multiply_add_fusion.1) | copy-start | bytes 2359300
  297.2 4.0 collective-permute-start.17
  299.9 4.7 collective-permute-start.16
  304.6 5.9 %collective-permute-start.18 = (f32[34,1,192]{2,1,0:T(1,128)S(1)}, f32[34,1,192]{2,1,0:T(1,128)S(1)}, u32[]{:S(2)}, u32[]{:S(2)}) collective-permute-start(f32[34,1,192]{2,1,0:T(1,128)S(1)} %get-tuple-element.17), channel_id=1, source_target_pairs={{1,0},{2,1},{3,2},{4,3},{5,4},{6,5},{7,6},{8,7},{9,8},{10,9},{11,1... | collective-permute-start | bytes 78344 | tf_op jit(solution)/shard_map/ppermute | solution.py:25
  308.3 3.3 collective-permute-start.19
  317.3 4.8 collective-permute-start.20
  320.4 5.6 collective-permute-start.21
  327.0 7.0 %collective-permute-start.22 = (bf16[40,4,192]{2,1,0:T(4,128)(2,1)S(1)}, bf16[40,4,192]{2,1,0:T(4,128)(2,1)S(1)}, u32[]{:S(2)}, u32[]{:S(2)}) collective-permute-start(bf16[40,4,192]{2,1,0:T(4,128)(2,1)S(1)} %get-tuple-element.29), channel_id=1, source_target_pairs={{0,1},{1,2},{2,3},{3,4},{4,5},{5,6},{6,7},{7,8},{8,9},{9,10},{10,1... | collective-permute-start | bytes 184328 | tf_op jit(solution)/shard_map/ppermute | solution.py:23
  332.1 5.9 %collective-permute-start.23 = (bf16[40,4,192]{2,1,0:T(4,128)(2,1)S(1)}, bf16[40,4,192]{2,1,0:T(4,128)(2,1)S(1)}, u32[]{:S(2)}, u32[]{:S(2)}) collective-permute-start(bf16[40,4,192]{2,1,0:T(4,128)(2,1)S(1)} %get-tuple-element.30), channel_id=1, source_target_pairs={{1,0},{2,1},{3,2},{4,3},{5,4},{6,5},{7,6},{8,7},{9,8},{10,9},{11,1... | collective-permute-start | bytes 184328 | tf_op jit(solution)/shard_map/ppermute | solution.py:25
  340.4 99.9 %copy-start.17 = (f32[8,1024]{1,0:T(8,128)S(1)}, f32[8,1024]{1,0:T(8,128)}, u32[]{:S(2)}) copy-start(f32[8,1024]{1,0:T(8,128)} %reshape.40) | copy-start | bytes 98308
  445.4 17.8 %copy-start.20 = (f32[32,32]{1,0:T(8,128)S(1)}, f32[32,32]{1,0:T(8,128)}, u32[]{:S(2)}) copy-start(f32[32,32]{1,0:T(8,128)} %copy-done.18) | copy-start | bytes 12292
  445.4 17.8 %copy-start.23 = (f32[32,32]{1,0:T(8,128)S(1)}, f32[32,32]{1,0:T(8,128)}, u32[]{:S(2)}) copy-start(f32[32,32]{1,0:T(8,128)} %copy-done.21) | copy-start | bytes 12292
  445.4 17.8 %copy-start.26 = (f32[32,32]{1,0:T(8,128)S(1)}, f32[32,32]{1,0:T(8,128)}, u32[]{:S(2)}) copy-start(f32[32,32]{1,0:T(8,128)} %copy-done.24) | copy-start | bytes 12292
  445.4 17.8 %copy-start.29 = (f32[32,32]{1,0:T(8,128)S(1)}, f32[32,32]{1,0:T(8,128)}, u32[]{:S(2)}) copy-start(f32[32,32]{1,0:T(8,128)} %copy-done.27) | copy-start | bytes 12292
  448.8 4.2 collective-permute-start.25
  451.6 4.7 collective-permute-start.24
  456.3 5.9 %collective-permute-start.26 = (f32[34,1,192]{2,1,0:T(1,128)S(1)}, f32[34,1,192]{2,1,0:T(1,128)S(1)}, u32[]{:S(2)}, u32[]{:S(2)}) collective-permute-start(f32[34,1,192]{2,1,0:T(1,128)S(1)} %get-tuple-element.15), channel_id=1, source_target_pairs={{1,0},{2,1},{3,2},{4,3},{5,4},{6,5},{7,6},{8,7},{9,8},{10,9},{11,1... | collective-permute-start | bytes 78344 | tf_op jit(solution)/shard_map/ppermute | solution.py:25
  460.0 3.3 collective-permute-start.27
  (17 other events, 103.9 us)
Sparse Core Ops, SparseCore 0:
  12.2 124.0 all-gather.3
  166.5 119.3 all-gather.5
  316.6 119.3 all-gather.7
where the time goes:
time: 574 us; the launch traced here: 572 us
  waiting for transfers between devices  310 us (54%)
  blocking collectives  99 us (17%)
  starting transfers between devices  78.5 us (14%)
  other arithmetic  30.5 us (5%)
  matrix products  26.2 us (5%)
  between operations  14.4 us (3%)
  local copies, waits for them, and re-layouts  13.3 us (2%)
    all_gather x3, waiting for transfers between devices, precondition(): lax.all_gather(restricted, ('gx', 'gy'), axis=0, tiled=True)  279 us
    psum x1, blocking collectives, squares_total(): lax.psum(jnp.sum(current_core * current_core, axis=(0, 1)), ('gx', 'gy'))  99 us
    ppermute x14, starting transfers between devices, extended(): lax.ppermute(tail, axis, [(i, (i + 1) % count) for i in range(ends)])  50.1 us
    ppermute x14, starting transfers between devices, extended(): lax.ppermute(head, axis, [((i + 1) % count, i) for i in range(ends)])  28.3 us
    ppermute x14, waiting for transfers between devices, extended(): lax.ppermute(head, axis, [((i + 1) % count, i) for i in range(ends)])  27 us
    dot_general x3, matrix products, precondition(): jnp.dot(coarse_inverse, lax.all_gather(restricted, ('gx', 'gy'), axis=0,...  12.9 us
  transfers between devices with their start and end apart: 31, of which 16 were waited for; matrix products, arithmetic and copies ran while one was open for 5% of the time, Pallas kernels for 0%

commit v1 on v0

--- a/solution.py
+++ b/solution.py
@@ -47,13 +47,21 @@
     return total
 
 
+def total_over_mesh(values):
+    for axis in ("gx", "gy"):
+        values = jnp.sum(lax.all_gather(values, axis, axis=0), axis=0)
+    return values
+
+
 def on_device(sources, permeability, storage, basis, local_inverse, coarse_inverse):
     patch = sources.shape[0]
     fields = sources.shape[2]
     modes = basis.shape[0]
+    rows_x = lax.axis_size("gx")
+    cols_y = lax.axis_size("gy")
     margin = OV
     extent = patch + 2 * margin
-    cells = float(patch * patch * lax.axis_size("gx") * lax.axis_size("gy"))
+    cells = float(patch * patch * rows_x * cols_y)
     flat_basis = basis.reshape(modes, patch * patch)
     inverse_rows = local_inverse[0, 0]
     stacked = jnp.stack([permeability, storage])
@@ -61,11 +69,12 @@
     kappa_pad = padded[0]
     state = sources
 
+    pieces = coarse_inverse.reshape(modes, rows_x, cols_y, modes).transpose(2, 0, 1, 3)
+    pieces = lax.all_to_all(pieces, "gy", 0, 0, tiled=True)
+    coarse_block = pieces.reshape(cols_y * modes, rows_x * modes)
+
     def rounded_window(current):
         return extended(current.astype(jnp.bfloat16), (("gx", 0), ("gy", 1)), margin)
-
-    def squares_total(current_core):
-        return lax.psum(jnp.sum(current_core * current_core, axis=(0, 1)), ("gx", "gy"))
 
     def precondition(current):
         window = rounded_window(current).reshape(extent * extent, fields)
@@ -74,16 +83,24 @@
         )
         flat_core = current.reshape(patch * patch, fields)
         restricted = jnp.dot(flat_basis, flat_core, precision=highest)
-        coarse_part = jnp.dot(
-            coarse_inverse,
-            lax.all_gather(restricted, ("gx", "gy"), axis=0, tiled=True),
-            precision=highest,
+        squares = jnp.sum(flat_core * flat_core, axis=0)
+        carried = jnp.concatenate([restricted, squares[None]], axis=0)
+        gathered = lax.all_gather(carried, "gx", axis=0)
+        column_total = jnp.sum(gathered[:, modes], axis=0)
+        column_coarse = gathered[:, :modes].reshape(rows_x * modes, fields)
+        partial = jnp.dot(coarse_block, column_coarse, precision=highest).reshape(
+            cols_y, modes, fields
         )
-        squares = squares_total(current)
+        partial = jnp.concatenate(
+            [partial, jnp.broadcast_to(column_total, (cols_y, 1, fields))], axis=1
+        )
+        reduced = lax.psum_scatter(partial, "gy", scatter_dimension=0, tiled=True)[0]
+        coarse_part = reduced[:modes]
+        squares_all = reduced[modes]
         prolonged = jnp.dot(flat_basis.T, coarse_part, precision=highest).reshape(
             patch, patch, fields
         )
-        return (local_part + prolonged, squares)
+        return (local_part + prolonged, squares_all)
 
     centre = 0.5 * (upper_bound + lower_bound)
     half_width = 0.5 * (upper_bound - lower_bound)
@@ -104,7 +121,8 @@
             update = weight_next * weight_prev * update + 2.0 * weight_next / half_width * corrected
             weight_prev = weight_next
         else:
-            history.append(squares_total(state))
+            flat_state = state.reshape(patch * patch, fields)
+            history.append(total_over_mesh(jnp.sum(flat_state * flat_state, axis=0)))
     return (solution, jnp.sqrt(jnp.stack(history) / cells), jnp.sqrt(initial / cells))
 
 

time: 574 us -> 716 us (1.25)
  blocking collectives: 99 us -> 309 us
  waiting for transfers between devices: 310 us -> 153 us
  starting transfers between devices: 78.5 us -> 126 us
  local copies, waits for them, and re-layouts: 13.3 us -> 39.3 us
  other arithmetic: 30.5 us -> 44 us
    all_gather x3 -> x0, waiting for transfers between devices: 279 us -> none  [precondition(): lax.all_gather(restricted, ('gx', 'gy'), axis=0, tiled=True)]
    unnamed x0 -> x2, blocking collectives: none -> 184 us
    reduce_scatter x0 -> x3, waiting for transfers between devices: none -> 135 us  [precondition(): lax.psum_scatter(partial, 'gy', scatter_dimension=0, tiled=True)[0]]
    all_gather x0 -> x3, blocking collectives: none -> 125 us  [precondition(): gathered = lax.all_gather(carried, 'gx', axis=0)]
    psum x1 -> x0, blocking collectives: 99 us -> none  [squares_total(): lax.psum(jnp.sum(current_core * current_core, axis=(0, 1)), ('gx', 'gy'))]
    ppermute x14, starting transfers between devices: 50.1 us -> 80.7 us  [extended(): lax.ppermute(tail, axis, [(i, (i + 1) % count) for i in range(ends)])]
    ppermute x14, waiting for transfers between devices: 27 us -> 16.4 us  [extended(): lax.ppermute(head, axis, [((i + 1) % count, i) for i in range(ends)])]
    ppermute x14, starting transfers between devices: 28.3 us -> 37 us  [extended(): lax.ppermute(head, axis, [((i + 1) % count, i) for i in range(ends)])]
  transfers between devices with their start and end apart: 31 -> 32, of which waited for: 16 -> 11; matrix products, arithmetic and copies ran while one was open for 5% -> 9% of each run, Pallas kernels for 0% -> 0%
where the time goes in v1:
time: 716 us; the launch traced here: 709 us
  blocking collectives  309 us (43%)
  waiting for transfers between devices  153 us (21%)
  starting transfers between devices  126 us (18%)
  other arithmetic  44 us (6%)
  local copies, waits for them, and re-layouts  39.3 us (5%)
  matrix products  21.5 us (3%)
  between operations  15.8 us (2%)
    unnamed x2, blocking collectives  184 us
    reduce_scatter x3, waiting for transfers between devices, precondition(): lax.psum_scatter(partial, 'gy', scatter_dimension=0, tiled=True)[0]  135 us
    all_gather x3, blocking collectives, precondition(): gathered = lax.all_gather(carried, 'gx', axis=0)  125 us
    ppermute x14, starting transfers between devices, extended(): lax.ppermute(tail, axis, [(i, (i + 1) % count) for i in range(ends)])  80.7 us
    ppermute x14, starting transfers between devices, extended(): lax.ppermute(head, axis, [((i + 1) % count, i) for i in range(ends)])  37 us
    ppermute x14, waiting for transfers between devices, extended(): lax.ppermute(head, axis, [((i + 1) % count, i) for i in range(ends)])  16.4 us
  transfers between devices with their start and end apart: 32, of which 11 were waited for; matrix products, arithmetic and copies ran while one was open for 9% of the time, Pallas kernels for 0%

profile of v1, /device:TPU:1, one launch (start us, length us, event | category | flops | bytes accessed | tf_op | source)
XLA Modules:
  0.0 709.3 jit_solution(15328770682874855957)
XLA Ops:
  8.7 5.4 collective-permute-start.4
  15.3 2.4 fusion.91
  19.2 4.7 collective-permute-start
  25.1 2.5 reshape.76
  27.7 3.3 copy.39
  33.0 8.5 %all-to-all-start = ((f32[16,1,2048]{2,1,0:T(1,128)}), f32[16,1,2048]{2,1,0:T(1,128)S(1)}, u32[]{:S(2)}, u32[]{:S(2)}) async-start(f32[16,1,2048]{2,1,0:T(1,128)} %reshape.113), calls=%async_computation | async-start | bytes 262144 | tf_op jit(solution)/shard_map/all_to_all | solution.py:73
  42.2 2.0 convolution_bitcast_fusion.5
  44.8 46.0 %all-gather.5 = f32[32,9,192]{2,1,0:T(8,128)S(1)} all-gather(f32[1,9,192]{2,1,0:T(8,128)S(1)} %maximum_bitcast_fusion), channel_id=2, replica_groups=mesh['gx'=32,'gy'=16] {'gx'}, dimensions={0}, use_global_device_ids=true | all-gather | bytes 228096 | tf_op jit(solution)/shard_map/all_gather | solution.py:88
  96.1 14.9 %collective-permute-start.2 = (bf16[40,4,192]{2,1,0:T(4,128)(2,1)}, bf16[40,4,192]{2,1,0:T(4,128)(2,1)}, u32[]{:S(2)}, u32[]{:S(2)}) collective-permute-start(bf16[40,4,192]{2,1,0:T(4,128)(2,1)} %get-tuple-element.27), channel_id=1, source_target_pairs={{0,1},{1,2},{2,3},{3,4},{4,5},{5,6},{6,7},{7,8},{8,9},{9,10},{10,1... | collective-permute-start | bytes 184328 | tf_op jit(solution)/shard_map/ppermute | solution.py:23
  117.0 3.0 copy.40
  120.0 2.8 reshape.77
  122.8 2.1 convolution_bitcast_fusion.2
  130.5 3.6 collective-permute-start.6
  136.1 2.4 pad_maximum_fusion.24
  138.6 45.1 %reduce-scatter.4.cloned.1.call-done = f32[1,9,192]{2,1,0:T(8,128)} async-done(((f32[16,9,192]{2,1,0:T(8,128)}), f32[1,9,192]{2,1,0:T(8,128)}) %reduce-scatter.4.cloned.1.call-update) | async-done | bytes 6928 | tf_op jit(solution)/shard_map/reduce_scatter | solution.py:97
  185.3 2.9 fusion.9
  188.2 2.4 copy.42
  192.1 2.3 collective-permute-start.9
  196.7 2.5 collective-permute-done.8
  199.2 6.5 collective-permute-start.10
  211.6 39.6 %all-gather.6 = f32[32,9,192]{2,1,0:T(8,128)S(1)} all-gather(f32[1,9,192]{2,1,0:T(8,128)S(1)} %maximum_bitcast_fusion.1), channel_id=3, replica_groups=mesh['gx'=32,'gy'=16] {'gx'}, dimensions={0}, use_global_device_ids=true | all-gather | bytes 228096 | tf_op jit(solution)/shard_map/all_gather | solution.py:88
  253.7 4.3 collective-permute-start.12
  264.4 16.9 %collective-permute-start.14 = (bf16[40,4,192]{2,1,0:T(4,128)(2,1)S(1)}, bf16[40,4,192]{2,1,0:T(4,128)(2,1)S(1)}, u32[]{:S(2)}, u32[]{:S(2)}) collective-permute-start(bf16[40,4,192]{2,1,0:T(4,128)(2,1)S(1)} %get-tuple-element.25), channel_id=1, source_target_pairs={{0,1},{1,2},{2,3},{3,4},{4,5},{5,6},{6,7},{7,8},{8,9},{9,10},{10,1... | collective-permute-start | bytes 184328 | tf_op jit(solution)/shard_map/ppermute | solution.py:23
  283.2 3.8 collective-permute-done.15
  287.1 2.4 pad_maximum_fusion.25
  289.5 46.0 %reduce-scatter.6.cloned.1.call-done = f32[1,9,192]{2,1,0:T(8,128)} async-done(((f32[16,9,192]{2,1,0:T(8,128)}), f32[1,9,192]{2,1,0:T(8,128)}) %reduce-scatter.6.cloned.1.call-update) | async-done | bytes 6928 | tf_op jit(solution)/shard_map/reduce_scatter | solution.py:97
  337.1 3.0 fusion.18
  340.1 2.5 copy.45
  344.3 2.2 collective-permute-start.17
  347.8 3.3 collective-permute-done.16
  351.9 6.6 collective-permute-start.18
  364.2 5.0 fusion.84
  370.1 39.4 %all-gather.7 = f32[32,9,192]{2,1,0:T(8,128)S(1)} all-gather(f32[1,9,192]{2,1,0:T(8,128)S(1)} %maximum_bitcast_fusion.2), channel_id=4, replica_groups=mesh['gx'=32,'gy'=16] {'gx'}, dimensions={0}, use_global_device_ids=true | all-gather | bytes 228096 | tf_op jit(solution)/shard_map/all_gather | solution.py:88
  411.5 3.8 collective-permute-start.20
  418.4 2.3 collective-permute-done.21
  421.7 14.3 %collective-permute-start.22 = (bf16[40,4,192]{2,1,0:T(4,128)(2,1)S(1)}, bf16[40,4,192]{2,1,0:T(4,128)(2,1)S(1)}, u32[]{:S(2)}, u32[]{:S(2)}) collective-permute-start(bf16[40,4,192]{2,1,0:T(4,128)(2,1)S(1)} %get-tuple-element.23), channel_id=1, source_target_pairs={{0,1},{1,2},{2,3},{3,4},{4,5},{5,6},{6,7},{7,8},{8,9},{9,10},{10,1... | collective-permute-start | bytes 184328 | tf_op jit(solution)/shard_map/ppermute | solution.py:23
  436.1 2.6 collective-permute-start.23
  441.8 2.4 pad_maximum_fusion.26
  444.2 44.0 %reduce-scatter.8.cloned.1.call-done = f32[1,9,192]{2,1,0:T(8,128)} async-done(((f32[16,9,192]{2,1,0:T(8,128)}), f32[1,9,192]{2,1,0:T(8,128)}) %reduce-scatter.8.cloned.1.call-update) | async-done | bytes 6928 | tf_op jit(solution)/shard_map/reduce_scatter | solution.py:97
  489.8 2.9 fusion.27
  492.7 2.5 copy.48
  495.2 3.3 multiply_add_fusion
  498.5 2.4 collective-permute-start.25
  502.9 2.7 collective-permute-done.24
  505.6 6.6 collective-permute-start.26
  515.3 1.9 fusion.35
  517.6 114.3 %all-reduce = f32[6144]{0:T(1024)S(1)} all-reduce(f32[6144]{0:T(1024)S(1)} %dynamic-update-slice), channel_id=5, replica_groups=mesh['gx'=32,'gy'=16] {'gx'}, use_global_device_ids=true, to_apply=%add | all-reduce | flops 6144 | bytes 49152
  632.2 69.8 %all-reduce.1 = f32[3072]{0:T(1024)S(1)} all-reduce(f32[3072]{0:T(1024)S(1)} %dynamic-update-slice.1), channel_id=6, replica_groups=mesh['gx'=32,'gy'=16] {'gy'}, use_global_device_ids=true, to_apply=%add.1 | all-reduce | flops 3072 | bytes 24576
  (163 shorter events, 77.1 us)
Async XLA Ops:
  7.2 178.1 %copy-start = (bf16[1,1,1024,1600]{2,3,1,0:T(8,128)(2,1)S(1)}, bf16[1,1,1024,1600]{2,3,1,0:T(8,128)(2,1)}, u32[]{:S(2)}) copy-start(bf16[1,1,1024,1600]{2,3,1,0:T(8,128)(2,1)} %param.10) | copy-start | bytes 9830404
  7.2 18.0 %copy-start.26 = (f32[8,4096]{1,0:T(8,128)S(1)}, f32[8,4096]{1,0:T(8,128)}, u32[]{:S(2)}) copy-start(f32[8,4096]{1,0:T(8,128)} %param.11) | copy-start | bytes 393220
  8.7 84.3 %collective-permute-start.4 = (f32[2,1,32]{2,1,0:T(1,128)}, f32[2,1,32]{2,1,0:T(1,128)}, u32[]{:S(2)}, u32[]{:S(2)}) collective-permute-start(f32[2,1,32]{2,1,0:T(1,128)} %get-tuple-element.37), channel_id=1, source_target_pairs={{0,16},{16,32},{32,48},{48,64},{64,80},{80,96},{96,112},{112,128},... | collective-permute-start | bytes 776 | tf_op jit(solution)/shard_map/ppermute | solution.py:23
  14.1 78.9 %collective-permute-start.5 = (f32[2,1,32]{2,1,0:T(1,128)}, f32[2,1,32]{2,1,0:T(1,128)}, u32[]{:S(2)}, u32[]{:S(2)}) collective-permute-start(f32[2,1,32]{2,1,0:T(1,128)} %get-tuple-element.38), channel_id=1, source_target_pairs={{16,0},{32,16},{48,32},{64,48},{80,64},{96,80},{112,96},{128,112},... | collective-permute-start | bytes 776 | tf_op jit(solution)/shard_map/ppermute | solution.py:25
  19.2 75.2 %collective-permute-start = (bf16[4,32,192]{2,1,0:T(8,128)(2,1)}, bf16[4,32,192]{2,1,0:T(8,128)(2,1)}, u32[]{:S(2)}, u32[]{:S(2)}) collective-permute-start(bf16[4,32,192]{2,1,0:T(8,128)(2,1)} %get-tuple-element.33), channel_id=1, source_target_pairs={{0,16},{16,32},{32,48},{48,64},{64,80},{80,96},{96,112},{112,128},... | collective-permute-start | bytes 147464 | tf_op jit(solution)/shard_map/ppermute | solution.py:23
  23.9 70.5 %collective-permute-start.1 = (bf16[4,32,192]{2,1,0:T(8,128)(2,1)}, bf16[4,32,192]{2,1,0:T(8,128)(2,1)}, u32[]{:S(2)}, u32[]{:S(2)}) collective-permute-start(bf16[4,32,192]{2,1,0:T(8,128)(2,1)} %get-tuple-element.34), channel_id=1, source_target_pairs={{16,0},{32,16},{48,32},{64,48},{80,64},{96,80},{112,96},{128,112},... | collective-permute-start | bytes 147464 | tf_op jit(solution)/shard_map/ppermute | solution.py:25
  27.7 14.5 %copy-start.10 = (f32[8,32,32]{2,1,0:T(8,128)S(1)}, f32[8,32,32]{2,1,0:T(8,128)}, u32[]{:S(2)}) copy-start(f32[8,32,32]{2,1,0:T(8,128)} %param.9) | copy-start | bytes 98308
  33.0 80.0 %all-to-all-start = ((f32[16,1,2048]{2,1,0:T(1,128)}), f32[16,1,2048]{2,1,0:T(1,128)S(1)}, u32[]{:S(2)}, u32[]{:S(2)}) async-start(f32[16,1,2048]{2,1,0:T(1,128)} %reshape.113), calls=%async_computation | async-start | bytes 262144 | tf_op jit(solution)/shard_map/all_to_all | solution.py:73
  41.5 142.2 %reduce-scatter.4.cloned.1.call-start = ((), (), s32[]{:S(2)}) async-start(), calls=%async_computation.4 | async-start | bytes 278528 | tf_op jit(solution)/shard_map/reduce_scatter | solution.py:97
  96.1 40.0 %collective-permute-start.2 = (bf16[40,4,192]{2,1,0:T(4,128)(2,1)}, bf16[40,4,192]{2,1,0:T(4,128)(2,1)}, u32[]{:S(2)}, u32[]{:S(2)}) collective-permute-start(bf16[40,4,192]{2,1,0:T(4,128)(2,1)} %get-tuple-element.27), channel_id=1, source_target_pairs={{0,1},{1,2},{2,3},{3,4},{4,5},{5,6},{6,7},{7,8},{8,9},{9,10},{10,1... | collective-permute-start | bytes 184328 | tf_op jit(solution)/shard_map/ppermute | solution.py:23
  111.0 25.1 %collective-permute-start.3 = (bf16[40,4,192]{2,1,0:T(4,128)(2,1)}, bf16[40,4,192]{2,1,0:T(4,128)(2,1)}, u32[]{:S(2)}, u32[]{:S(2)}) collective-permute-start(bf16[40,4,192]{2,1,0:T(4,128)(2,1)} %get-tuple-element.28), channel_id=1, source_target_pairs={{1,0},{2,1},{3,2},{4,3},{5,4},{6,5},{7,6},{8,7},{9,8},{10,9},{11,1... | collective-permute-start | bytes 184328 | tf_op jit(solution)/shard_map/ppermute | solution.py:25
  128.9 206.6 %reduce-scatter.6.cloned.1.call-start = ((), (), s32[]{:S(2)}) async-start(), calls=%async_computation.5 | async-start | bytes 278528 | tf_op jit(solution)/shard_map/reduce_scatter | solution.py:97
  130.5 65.2 %collective-permute-start.6 = (f32[2,34,1]{2,1,0:T(8,128)}, f32[2,34,1]{2,1,0:T(8,128)}, u32[]{:S(2)}, u32[]{:S(2)}) collective-permute-start(f32[2,34,1]{2,1,0:T(8,128)} %get-tuple-element.35), channel_id=1, source_target_pairs={{0,1},{1,2},{2,3},{3,4},{4,5},{5,6},{6,7},{7,8},{8,9},{9,10},{10,1... | collective-permute-start | bytes 824 | tf_op jit(solution)/shard_map/ppermute | solution.py:23
  134.2 61.6 %collective-permute-start.7 = (f32[2,34,1]{2,1,0:T(8,128)}, f32[2,34,1]{2,1,0:T(8,128)}, u32[]{:S(2)}, u32[]{:S(2)}) collective-permute-start(f32[2,34,1]{2,1,0:T(8,128)} %get-tuple-element.36), channel_id=1, source_target_pairs={{1,0},{2,1},{3,2},{4,3},{5,4},{6,5},{7,6},{8,7},{9,8},{10,9},{11,1... | collective-permute-start | bytes 824 | tf_op jit(solution)/shard_map/ppermute | solution.py:25
  190.6 18.2 %copy-start.1 = (f32[1024,192]{1,0:T(8,128)S(1)}, f32[1024,192]{1,0:T(8,128)}, u32[]{:S(2)}) copy-start(f32[1024,192]{1,0:T(8,128)} %copy.42) | copy-start | bytes 2359300
  190.6 18.2 %copy-start.6 = (f32[32,32,192]{2,1,0:T(8,128)S(1)}, f32[32,32,192]{2,1,0:T(8,128)}, u32[]{:S(2)}) copy-start(f32[32,32,192]{2,1,0:T(8,128)} %param.6) | copy-start | bytes 2359300
  190.6 18.2 %copy-start.27 = (f32[32,32]{1,0:T(8,128)S(1)}, f32[32,32]{1,0:T(8,128)}, u32[]{:S(2)}) copy-start(f32[32,32]{1,0:T(8,128)} %broadcast_multiply_fusion.1) | copy-start | bytes 12292
  192.1 4.5 collective-permute-start.9
  194.5 4.7 collective-permute-start.8
  199.2 8.6 %collective-permute-start.10 = (f32[34,1,192]{2,1,0:T(1,128)S(1)}, f32[34,1,192]{2,1,0:T(1,128)S(1)}, u32[]{:S(2)}, u32[]{:S(2)}) collective-permute-start(f32[34,1,192]{2,1,0:T(1,128)S(1)} %get-tuple-element.13), channel_id=1, source_target_pairs={{1,0},{2,1},{3,2},{4,3},{5,4},{6,5},{7,6},{8,7},{9,8},{10,9},{11,1... | collective-permute-start | bytes 78344 | tf_op jit(solution)/shard_map/ppermute | solution.py:25
  205.7 3.1 collective-permute-start.11
  210.7 42.2 %copy-start.5 = (f32[32,32,192]{2,1,0:T(8,128)}, f32[32,32,192]{2,1,0:T(8,128)S(1)}, u32[]{:S(2)}) copy-start(f32[32,32,192]{2,1,0:T(8,128)S(1)} %get-tuple-element.6) | copy-start | bytes 2359300
  210.8 42.2 %copy-start.9 = (bf16[32,32,192]{2,1,0:T(8,128)(2,1)}, bf16[32,32,192]{2,1,0:T(8,128)(2,1)S(1)}, u32[]{:S(2)}) copy-start(bf16[32,32,192]{2,1,0:T(8,128)(2,1)S(1)} %get-tuple-element.5) | copy-start | bytes 1179652
  253.7 9.6 %collective-permute-start.12 = (bf16[4,32,192]{2,1,0:T(8,128)(2,1)}, bf16[4,32,192]{2,1,0:T(8,128)(2,1)}, u32[]{:S(2)}, u32[]{:S(2)}) collective-permute-start(bf16[4,32,192]{2,1,0:T(8,128)(2,1)} %get-tuple-element.31), channel_id=1, source_target_pairs={{0,16},{16,32},{32,48},{48,64},{64,80},{80,96},{96,112},{112,128},... | collective-permute-start | bytes 147464 | tf_op jit(solution)/shard_map/ppermute | solution.py:23
  258.0 5.3 collective-permute-start.13
  263.3 225.0 %reduce-scatter.8.cloned.1.call-start = ((), (), s32[]{:S(2)}) async-start(), calls=%async_computation.6 | async-start | bytes 278528 | tf_op jit(solution)/shard_map/reduce_scatter | solution.py:97
  264.4 18.8 %collective-permute-start.14 = (bf16[40,4,192]{2,1,0:T(4,128)(2,1)S(1)}, bf16[40,4,192]{2,1,0:T(4,128)(2,1)S(1)}, u32[]{:S(2)}, u32[]{:S(2)}) collective-permute-start(bf16[40,4,192]{2,1,0:T(4,128)(2,1)S(1)} %get-tuple-element.25), channel_id=1, source_target_pairs={{0,1},{1,2},{2,3},{3,4},{4,5},{5,6},{6,7},{7,8},{8,9},{9,10},{10,1... | collective-permute-start | bytes 184328 | tf_op jit(solution)/shard_map/ppermute | solution.py:23
  281.3 5.8 collective-permute-start.15
  344.3 3.6 collective-permute-start.17
  346.5 4.7 collective-permute-start.16
  351.9 12.3 %collective-permute-start.18 = (f32[34,1,192]{2,1,0:T(1,128)}, f32[34,1,192]{2,1,0:T(1,128)}, u32[]{:S(2)}, u32[]{:S(2)}) collective-permute-start(f32[34,1,192]{2,1,0:T(1,128)} %get-tuple-element.11), channel_id=1, source_target_pairs={{1,0},{2,1},{3,2},{4,3},{5,4},{6,5},{7,6},{8,7},{9,8},{10,9},{11,1... | collective-permute-start | bytes 78344 | tf_op jit(solution)/shard_map/ppermute | solution.py:25
  358.4 5.8 collective-permute-start.19
  369.2 41.5 %copy-start.3 = (f32[32,32,192]{2,1,0:T(8,128)}, f32[32,32,192]{2,1,0:T(8,128)S(1)}, u32[]{:S(2)}) copy-start(f32[32,32,192]{2,1,0:T(8,128)S(1)} %get-tuple-element.4) | copy-start | bytes 2359300
  369.3 41.5 %copy-start.7 = (bf16[32,32,192]{2,1,0:T(8,128)(2,1)}, bf16[32,32,192]{2,1,0:T(8,128)(2,1)S(1)}, u32[]{:S(2)}) copy-start(bf16[32,32,192]{2,1,0:T(8,128)(2,1)S(1)} %get-tuple-element.3) | copy-start | bytes 1179652
  411.5 6.9 collective-permute-start.20
  415.3 73.0 %copy-start.13 = (f32[8,1024]{1,0:T(8,128)S(1)}, f32[8,1024]{1,0:T(8,128)}, u32[]{:S(2)}) copy-start(f32[8,1024]{1,0:T(8,128)} %reshape.79) | copy-start | bytes 98308
  415.3 5.3 collective-permute-start.21
  421.7 18.2 %collective-permute-start.22 = (bf16[40,4,192]{2,1,0:T(4,128)(2,1)S(1)}, bf16[40,4,192]{2,1,0:T(4,128)(2,1)S(1)}, u32[]{:S(2)}, u32[]{:S(2)}) collective-permute-start(bf16[40,4,192]{2,1,0:T(4,128)(2,1)S(1)} %get-tuple-element.23), channel_id=1, source_target_pairs={{0,1},{1,2},{2,3},{3,4},{4,5},{5,6},{6,7},{7,8},{8,9},{9,10},{10,1... | collective-permute-start | bytes 184328 | tf_op jit(solution)/shard_map/ppermute | solution.py:23
  436.1 5.8 collective-permute-start.23
  495.2 20.1 %copy-start.16 = (f32[32,32]{1,0:T(8,128)S(1)}, f32[32,32]{1,0:T(8,128)}, u32[]{:S(2)}) copy-start(f32[32,32]{1,0:T(8,128)} %copy-done.15) | copy-start | bytes 12292
  495.2 20.1 %copy-start.18 = (f32[32,32]{1,0:T(8,128)S(1)}, f32[32,32]{1,0:T(8,128)}, u32[]{:S(2)}) copy-start(f32[32,32]{1,0:T(8,128)} %copy-done.17) | copy-start | bytes 12292
  495.2 20.1 %copy-start.20 = (f32[32,32]{1,0:T(8,128)S(1)}, f32[32,32]{1,0:T(8,128)}, u32[]{:S(2)}) copy-start(f32[32,32]{1,0:T(8,128)} %copy-done.19) | copy-start | bytes 12292
  495.2 20.1 %copy-start.22 = (f32[32,32]{1,0:T(8,128)S(1)}, f32[32,32]{1,0:T(8,128)}, u32[]{:S(2)}) copy-start(f32[32,32]{1,0:T(8,128)} %copy-done.21) | copy-start | bytes 12292
  498.5 16.8 %copy-start.4 = (f32[32,32,192]{2,1,0:T(8,128)S(1)}, f32[32,32,192]{2,1,0:T(8,128)}, u32[]{:S(2)}) copy-start(f32[32,32,192]{2,1,0:T(8,128)} %copy-done.3) | copy-start | bytes 2359300
  498.5 4.4 collective-permute-start.25
  500.9 4.7 collective-permute-start.24
  505.6 9.2 %collective-permute-start.26 = (f32[34,1,192]{2,1,0:T(1,128)S(1)}, f32[34,1,192]{2,1,0:T(1,128)S(1)}, u32[]{:S(2)}, u32[]{:S(2)}) collective-permute-start(f32[34,1,192]{2,1,0:T(1,128)S(1)} %get-tuple-element.9), channel_id=1, source_target_pairs={{1,0},{2,1},{3,2},{4,3},{5,4},{6,5},{7,6},{8,7},{9,8},{10,9},{11,1... | collective-permute-start | bytes 78344 | tf_op jit(solution)/shard_map/ppermute | solution.py:25
  512.2 3.1 collective-permute-start.27
  (12 other events, 44.8 us)
Sparse Core Ops, SparseCore 0:
  129.1 54.5 reduce-scatter.3
  263.4 72.0 reduce-scatter.5
  418.5 69.7 reduce-scatter.7

commit v2 on v1

--- a/solution.py
+++ b/solution.py
@@ -47,9 +47,56 @@
     return total
 
 
+def exchange(values, axis, distance):
+    count = lax.axis_size(axis)
+    return lax.ppermute(values, axis, [(i, i ^ distance) for i in range(count)])
+
+
+def gather_by_doubling(block, axis):
+    count = lax.axis_size(axis)
+    me = lax.axis_index(axis)
+    held = block
+    distance = 1
+    while distance < count:
+        other = exchange(held, axis, distance)
+        upper = (me // distance) % 2 == 1
+        held = jnp.where(
+            upper, jnp.concatenate([other, held], axis=0), jnp.concatenate([held, other], axis=0)
+        )
+        distance *= 2
+    return held
+
+
+def scatter_by_halving(blocks, extra, axis):
+    count = lax.axis_size(axis)
+    me = lax.axis_index(axis)
+    tail = blocks.shape[1:]
+    distance = 1
+    while distance < count:
+        pairs = blocks.reshape((blocks.shape[0] // 2, 2) + tail)
+        upper = (me // distance) % 2 == 1
+        keep = jnp.where(upper, pairs[:, 1], pairs[:, 0])
+        send = jnp.where(upper, pairs[:, 0], pairs[:, 1])
+        message = jnp.concatenate([send.reshape((-1,) + tail[1:]), extra[None]], axis=0)
+        other = exchange(message, axis, distance)
+        blocks = keep + other[:-1].reshape(keep.shape)
+        extra = extra + other[-1]
+        distance *= 2
+    return blocks[0], extra
+
+
+def total_by_doubling(values, axis):
+    count = lax.axis_size(axis)
+    distance = 1
+    while distance < count:
+        values = values + exchange(values, axis, distance)
+        distance *= 2
+    return values
+
+
 def total_over_mesh(values):
-    for axis in ("gx", "gy"):
-        values = jnp.sum(lax.all_gather(values, axis, axis=0), axis=0)
+    for axis in ("gy", "gx"):
+        values = total_by_doubling(values, axis)
     return values
 
 
@@ -85,18 +132,13 @@
         restricted = jnp.dot(flat_basis, flat_core, precision=highest)
         squares = jnp.sum(flat_core * flat_core, axis=0)
         carried = jnp.concatenate([restricted, squares[None]], axis=0)
-        gathered = lax.all_gather(carried, "gx", axis=0)
+        gathered = gather_by_doubling(carried[None], "gx")
         column_total = jnp.sum(gathered[:, modes], axis=0)
         column_coarse = gathered[:, :modes].reshape(rows_x * modes, fields)
         partial = jnp.dot(coarse_block, column_coarse, precision=highest).reshape(
             cols_y, modes, fields
         )
-        partial = jnp.concatenate(
-            [partial, jnp.broadcast_to(column_total, (cols_y, 1, fields))], axis=1
-        )
-        reduced = lax.psum_scatter(partial, "gy", scatter_dimension=0, tiled=True)[0]
-        coarse_part = reduced[:modes]
-        squares_all = reduced[modes]
+        coarse_part, squares_all = scatter_by_halving(partial, column_total, "gy")
         prolonged = jnp.dot(flat_basis.T, coarse_part, precision=highest).reshape(
             patch, patch, fields
         )

time: 716 us -> 439 us (0.61)
  the two profiles are of different devices: /device:TPU:1 before, /device:TPU:60 now
where the time goes in v2:
time: 439 us; the launch traced here: 435 us
  starting transfers between devices  206 us (47%)
  waiting for transfers between devices  137 us (31%)
  other arithmetic  41.3 us (9%)
  local copies, waits for them, and re-layouts  33.3 us (8%)
  matrix products  14.6 us (3%)
    ppermute x36, waiting for transfers between devices, exchange(): return lax.ppermute(values, axis, [(i, i ^ distance) for i in range(count)])  125 us
    ppermute x36, starting transfers between devices, exchange(): return lax.ppermute(values, axis, [(i, i ^ distance) for i in range(count)])  107 us
    ppermute x14, starting transfers between devices, extended(): lax.ppermute(head, axis, [((i + 1) % count, i) for i in range(ends)])  62 us
    ppermute x14, starting transfers between devices, extended(): lax.ppermute(tail, axis, [(i, (i + 1) % count) for i in range(ends)])  30.1 us
  transfers between devices with their start and end apart: 65, of which 34 were waited for; matrix products, arithmetic and copies ran while one was open for 11% of the time, Pallas kernels for 0%

profile of v2, /device:TPU:60, one launch (start us, length us, event | category | flops | bytes accessed | tf_op | source)
XLA Modules:
  0.0 435.4 jit_solution(5181504760699812108)
XLA Ops:
  4.1 4.3 collective-permute-start.4
  10.1 6.1 %collective-permute-start.5 = (f32[2,9,192]{2,1,0:T(8,128)S(1)}, f32[2,9,192]{2,1,0:T(8,128)}, u32[]{:S(2)}, u32[]{:S(2)}) collective-permute-start(f32[2,9,192]{2,1,0:T(8,128)S(1)} %maximum_select_fusion.12), channel_id=1, source_target_pairs={{0,32},{16,48},{32,0},{48,16},{64,96},{80,112},{96,64},{112,80},{1... | collective-permute-start | bytes 41480 | tf_op jit(solution)/shard_map/ppermute | solution.py:52
  19.1 9.3 %collective-permute-start.6 = (f32[4,9,192]{2,1,0:T(8,128)S(1)}, f32[4,9,192]{2,1,0:T(8,128)}, u32[]{:S(2)}, u32[]{:S(2)}) collective-permute-start(f32[4,9,192]{2,1,0:T(8,128)S(1)} %maximum_select_fusion.9), channel_id=1, source_target_pairs={{0,64},{16,80},{32,96},{48,112},{64,0},{80,16},{96,32},{112,48},{1... | collective-permute-start | bytes 82952 | tf_op jit(solution)/shard_map/ppermute | solution.py:52
  29.0 3.4 collective-permute-start.13
  32.3 4.6 %collective-permute-start.14 = (f32[2,1,32]{2,1,0:T(1,128)}, f32[2,1,32]{2,1,0:T(1,128)}, u32[]{:S(2)}, u32[]{:S(2)}) collective-permute-start(f32[2,1,32]{2,1,0:T(1,128)} %get-tuple-element.54), channel_id=1, source_target_pairs={{16,0},{32,16},{48,32},{64,48},{80,64},{96,80},{112,96},{128,112},... | collective-permute-start | bytes 776 | tf_op jit(solution)/shard_map/ppermute | solution.py:25
  44.5 6.0 %collective-permute-start.1 = (bf16[4,32,192]{2,1,0:T(8,128)(2,1)}, bf16[4,32,192]{2,1,0:T(8,128)(2,1)}, u32[]{:S(2)}, u32[]{:S(2)}) collective-permute-start(bf16[4,32,192]{2,1,0:T(8,128)(2,1)} %get-tuple-element.34), channel_id=1, source_target_pairs={{16,0},{32,16},{48,32},{64,48},{80,64},{96,80},{112,96},{128,112},... | collective-permute-start | bytes 147464 | tf_op jit(solution)/shard_map/ppermute | solution.py:25
  50.5 3.4 reshape.320
  53.9 3.3 copy.69
  59.2 6.9 %all-to-all-start = ((f32[16,1,2048]{2,1,0:T(1,128)}), f32[16,1,2048]{2,1,0:T(1,128)}, u32[]{:S(2)}, u32[]{:S(2)}) async-start(f32[16,1,2048]{2,1,0:T(1,128)} %reshape.339), calls=%async_computation | async-start | bytes 262144 | tf_op jit(solution)/shard_map/all_to_all | solution.py:120
  71.0 8.8 %collective-permute-done.8 = f32[16,9,192]{2,1,0:T(8,128)} collective-permute-done((f32[16,9,192]{2,1,0:T(8,128)}, f32[16,9,192]{2,1,0:T(8,128)}, u32[]{:S(2)}, u32[]{:S(2)}) %collective-permute-start.8) | collective-permute-done | bytes 110624 | tf_op jit(solution)/shard_map/ppermute | solution.py:52
  101.6 3.4 collective-permute-start.10
  107.6 3.6 collective-permute-start.16
  111.8 4.3 collective-permute-start.11
  118.9 3.6 collective-permute-start.3
  126.7 6.1 %collective-permute-done.12 = f32[9,192]{1,0:T(8,128)S(1)} collective-permute-done((f32[9,192]{1,0:T(8,128)S(1)}, f32[9,192]{1,0:T(8,128)S(1)}, u32[]{:S(2)}, u32[]{:S(2)}) %collective-permute-start.12) | collective-permute-done | bytes 6944 | tf_op jit(solution)/shard_map/ppermute | solution.py:52
  141.4 6.0 %collective-permute-start.17 = (f32[1,32,192]{2,1,0:T(8,128)S(1)}, f32[1,32,192]{2,1,0:T(8,128)S(1)}, u32[]{:S(2)}, u32[]{:S(2)}) collective-permute-start(f32[1,32,192]{2,1,0:T(8,128)S(1)} %get-tuple-element.20), channel_id=1, source_target_pairs={{16,0},{32,16},{48,32},{64,48},{80,64},{96,80},{112,96},{128,112},... | collective-permute-start | bytes 73736 | tf_op jit(solution)/shard_map/ppermute | solution.py:25
  161.6 3.7 collective-permute-done.25
  167.3 4.8 %collective-permute-done.26 = f32[2,9,192]{2,1,0:T(8,128)S(1)} collective-permute-done((f32[2,9,192]{2,1,0:T(8,128)S(1)}, f32[2,9,192]{2,1,0:T(8,128)S(1)}, u32[]{:S(2)}, u32[]{:S(2)}) %collective-permute-start.26) | collective-permute-done | bytes 13856 | tf_op jit(solution)/shard_map/ppermute | solution.py:52
  172.0 4.6 %collective-permute-start.27 = (f32[4,9,192]{2,1,0:T(8,128)S(1)}, f32[4,9,192]{2,1,0:T(8,128)S(1)}, u32[]{:S(2)}, u32[]{:S(2)}) collective-permute-start(f32[4,9,192]{2,1,0:T(8,128)S(1)} %maximum_select_fusion.10), channel_id=1, source_target_pairs={{0,64},{16,80},{32,96},{48,112},{64,0},{80,16},{96,32},{112,48},{1... | collective-permute-start | bytes 82952 | tf_op jit(solution)/shard_map/ppermute | solution.py:52
  176.6 5.5 %collective-permute-done.27 = f32[4,9,192]{2,1,0:T(8,128)S(1)} collective-permute-done((f32[4,9,192]{2,1,0:T(8,128)S(1)}, f32[4,9,192]{2,1,0:T(8,128)S(1)}, u32[]{:S(2)}, u32[]{:S(2)}) %collective-permute-start.27) | collective-permute-done | bytes 27680 | tf_op jit(solution)/shard_map/ppermute | solution.py:52
  185.0 5.4 %collective-permute-done.28 = f32[8,9,192]{2,1,0:T(8,128)S(1)} collective-permute-done((f32[8,9,192]{2,1,0:T(8,128)S(1)}, f32[8,9,192]{2,1,0:T(8,128)S(1)}, u32[]{:S(2)}, u32[]{:S(2)}) %collective-permute-start.28) | collective-permute-done | bytes 55328 | tf_op jit(solution)/shard_map/ppermute | solution.py:52
  192.4 7.8 %collective-permute-done.29 = f32[16,9,192]{2,1,0:T(8,128)S(1)} collective-permute-done((f32[16,9,192]{2,1,0:T(8,128)S(1)}, f32[16,9,192]{2,1,0:T(8,128)S(1)}, u32[]{:S(2)}, u32[]{:S(2)}) %collective-permute-start.29) | collective-permute-done | bytes 110624 | tf_op jit(solution)/shard_map/ppermute | solution.py:52
  209.3 3.5 collective-permute-start.31
  215.6 7.0 %collective-permute-start.22 = (bf16[4,32,192]{2,1,0:T(8,128)(2,1)S(1)}, bf16[4,32,192]{2,1,0:T(8,128)(2,1)S(1)}, u32[]{:S(2)}, u32[]{:S(2)}) collective-permute-start(bf16[4,32,192]{2,1,0:T(8,128)(2,1)S(1)} %get-tuple-element.32), channel_id=1, source_target_pairs={{16,0},{32,16},{48,32},{64,48},{80,64},{96,80},{112,96},{128,112},... | collective-permute-start | bytes 147464 | tf_op jit(solution)/shard_map/ppermute | solution.py:25
  222.6 3.7 collective-permute-start.32
  228.4 3.6 collective-permute-start.24
  234.5 7.1 %collective-permute-done.33 = f32[9,192]{1,0:T(8,128)S(1)} collective-permute-done((f32[9,192]{1,0:T(8,128)S(1)}, f32[9,192]{1,0:T(8,128)S(1)}, u32[]{:S(2)}, u32[]{:S(2)}) %collective-permute-start.33) | collective-permute-done | bytes 6944 | tf_op jit(solution)/shard_map/ppermute | solution.py:52
  250.5 6.0 %collective-permute-start.34 = (f32[1,32,192]{2,1,0:T(8,128)S(1)}, f32[1,32,192]{2,1,0:T(8,128)S(1)}, u32[]{:S(2)}, u32[]{:S(2)}) collective-permute-start(f32[1,32,192]{2,1,0:T(8,128)S(1)} %get-tuple-element.18), channel_id=1, source_target_pairs={{16,0},{32,16},{48,32},{64,48},{80,64},{96,80},{112,96},{128,112},... | collective-permute-start | bytes 73736 | tf_op jit(solution)/shard_map/ppermute | solution.py:25
  270.7 3.7 collective-permute-done.42
  276.9 4.3 collective-permute-done.43
  281.2 4.6 %collective-permute-start.44 = (f32[4,9,192]{2,1,0:T(8,128)S(1)}, f32[4,9,192]{2,1,0:T(8,128)S(1)}, u32[]{:S(2)}, u32[]{:S(2)}) collective-permute-start(f32[4,9,192]{2,1,0:T(8,128)S(1)} %maximum_select_fusion.11), channel_id=1, source_target_pairs={{0,64},{16,80},{32,96},{48,112},{64,0},{80,16},{96,32},{112,48},{1... | collective-permute-start | bytes 82952 | tf_op jit(solution)/shard_map/ppermute | solution.py:52
  285.7 5.5 %collective-permute-done.44 = f32[4,9,192]{2,1,0:T(8,128)S(1)} collective-permute-done((f32[4,9,192]{2,1,0:T(8,128)S(1)}, f32[4,9,192]{2,1,0:T(8,128)S(1)}, u32[]{:S(2)}, u32[]{:S(2)}) %collective-permute-start.44) | collective-permute-done | bytes 27680 | tf_op jit(solution)/shard_map/ppermute | solution.py:52
  294.1 5.4 %collective-permute-done.45 = f32[8,9,192]{2,1,0:T(8,128)S(1)} collective-permute-done((f32[8,9,192]{2,1,0:T(8,128)S(1)}, f32[8,9,192]{2,1,0:T(8,128)S(1)}, u32[]{:S(2)}, u32[]{:S(2)}) %collective-permute-start.45) | collective-permute-done | bytes 55328 | tf_op jit(solution)/shard_map/ppermute | solution.py:52
  301.5 7.8 %collective-permute-done.46 = f32[16,9,192]{2,1,0:T(8,128)S(1)} collective-permute-done((f32[16,9,192]{2,1,0:T(8,128)S(1)}, f32[16,9,192]{2,1,0:T(8,128)S(1)}, u32[]{:S(2)}, u32[]{:S(2)}) %collective-permute-start.46) | collective-permute-done | bytes 110624 | tf_op jit(solution)/shard_map/ppermute | solution.py:52
  321.6 6.0 %collective-permute-start.39 = (bf16[4,32,192]{2,1,0:T(8,128)(2,1)S(1)}, bf16[4,32,192]{2,1,0:T(8,128)(2,1)S(1)}, u32[]{:S(2)}, u32[]{:S(2)}) collective-permute-start(bf16[4,32,192]{2,1,0:T(8,128)(2,1)S(1)} %get-tuple-element.30), channel_id=1, source_target_pairs={{16,0},{32,16},{48,32},{64,48},{80,64},{96,80},{112,96},{128,112},... | collective-permute-start | bytes 147464 | tf_op jit(solution)/shard_map/ppermute | solution.py:25
  327.7 6.5 %collective-permute-start.49 = (f32[17,192]{1,0:T(8,128)S(1)}, f32[17,192]{1,0:T(8,128)S(1)}, u32[]{:S(2)}, u32[]{:S(2)}) collective-permute-start(f32[17,192]{1,0:T(8,128)S(1)} %pad_maximum_fusion.54), channel_id=1, source_target_pairs={{0,4},{1,5},{2,6},{3,7},{4,0},{5,1},{6,2},{7,3},{8,12},{9,13},{10,... | collective-permute-start | bytes 39176 | tf_op jit(solution)/shard_map/ppermute | solution.py:52
  336.3 3.6 collective-permute-start.41
  342.6 6.9 %collective-permute-done.50 = f32[9,192]{1,0:T(8,128)S(1)} collective-permute-done((f32[9,192]{1,0:T(8,128)S(1)}, f32[9,192]{1,0:T(8,128)S(1)}, u32[]{:S(2)}, u32[]{:S(2)}) %collective-permute-start.50) | collective-permute-done | bytes 6944 | tf_op jit(solution)/shard_map/ppermute | solution.py:52
  354.7 3.3 multiply_add_fusion
  360.1 6.0 %collective-permute-start.51 = (f32[1,32,192]{2,1,0:T(8,128)S(1)}, f32[1,32,192]{2,1,0:T(8,128)S(1)}, u32[]{:S(2)}, u32[]{:S(2)}) collective-permute-start(f32[1,32,192]{2,1,0:T(8,128)S(1)} %get-tuple-element.16), channel_id=1, source_target_pairs={{16,0},{32,16},{48,32},{64,48},{80,64},{96,80},{112,96},{128,112},... | collective-permute-start | bytes 73736 | tf_op jit(solution)/shard_map/ppermute | solution.py:25
  381.9 3.5 collective-permute-done.56
  388.1 3.7 collective-permute-done.57
  394.8 6.4 %collective-permute-done.58 = f32[192]{0:T(256)S(1)} collective-permute-done((f32[192]{0:T(256)S(1)}, f32[192]{0:T(256)S(1)}, u32[]{:S(2)}, u32[]{:S(2)}) %collective-permute-start.58) | collective-permute-done | bytes 800 | tf_op jit(solution)/shard_map/ppermute | solution.py:52
  403.1 3.5 collective-permute-done.59
  408.6 4.4 %collective-permute-done.60 = f32[192]{0:T(256)S(1)} collective-permute-done((f32[192]{0:T(256)S(1)}, f32[192]{0:T(256)S(1)}, u32[]{:S(2)}, u32[]{:S(2)}) %collective-permute-start.60) | collective-permute-done | bytes 800 | tf_op jit(solution)/shard_map/ppermute | solution.py:52
  413.0 3.4 collective-permute-start.61
  417.1 5.3 %collective-permute-done.61 = f32[192]{0:T(256)S(1)} collective-permute-done((f32[192]{0:T(256)S(1)}, f32[192]{0:T(256)S(1)}, u32[]{:S(2)}, u32[]{:S(2)}) %collective-permute-start.61) | collective-permute-done | bytes 800 | tf_op jit(solution)/shard_map/ppermute | solution.py:52
  429.8 5.0 %collective-permute-done.63 = f32[192]{0:T(256)S(1)} collective-permute-done((f32[192]{0:T(256)S(1)}, f32[192]{0:T(256)S(1)}, u32[]{:S(2)}, u32[]{:S(2)}) %collective-permute-start.63) | collective-permute-done | bytes 800 | tf_op jit(solution)/shard_map/ppermute | solution.py:52
  (307 shorter events, 188.2 us)
Async XLA Ops:
  4.1 6.0 %collective-permute-start.4 = (f32[1,9,192]{2,1,0:T(8,128)S(1)}, f32[1,9,192]{2,1,0:T(8,128)S(1)}, u32[]{:S(2)}, u32[]{:S(2)}) collective-permute-start(f32[1,9,192]{2,1,0:T(8,128)S(1)} %maximum_bitcast_fusion), channel_id=1, source_target_pairs={{0,16},{16,0},{32,48},{48,32},{64,80},{80,64},{96,112},{112,96},{1... | collective-permute-start | bytes 20744 | tf_op jit(solution)/shard_map/ppermute | solution.py:52
  10.1 8.1 %collective-permute-start.5 = (f32[2,9,192]{2,1,0:T(8,128)S(1)}, f32[2,9,192]{2,1,0:T(8,128)}, u32[]{:S(2)}, u32[]{:S(2)}) collective-permute-start(f32[2,9,192]{2,1,0:T(8,128)S(1)} %maximum_select_fusion.12), channel_id=1, source_target_pairs={{0,32},{16,48},{32,0},{48,16},{64,96},{80,112},{96,64},{112,80},{1... | collective-permute-start | bytes 41480 | tf_op jit(solution)/shard_map/ppermute | solution.py:52
  19.1 17.9 %collective-permute-start.6 = (f32[4,9,192]{2,1,0:T(8,128)S(1)}, f32[4,9,192]{2,1,0:T(8,128)}, u32[]{:S(2)}, u32[]{:S(2)}) collective-permute-start(f32[4,9,192]{2,1,0:T(8,128)S(1)} %maximum_select_fusion.9), channel_id=1, source_target_pairs={{0,64},{16,80},{32,96},{48,112},{64,0},{80,16},{96,32},{112,48},{1... | collective-permute-start | bytes 82952 | tf_op jit(solution)/shard_map/ppermute | solution.py:52
  29.0 70.1 %collective-permute-start.13 = (f32[2,1,32]{2,1,0:T(1,128)}, f32[2,1,32]{2,1,0:T(1,128)}, u32[]{:S(2)}, u32[]{:S(2)}) collective-permute-start(f32[2,1,32]{2,1,0:T(1,128)} %get-tuple-element.53), channel_id=1, source_target_pairs={{0,16},{16,32},{32,48},{48,64},{64,80},{80,96},{96,112},{112,128},... | collective-permute-start | bytes 776 | tf_op jit(solution)/shard_map/ppermute | solution.py:23
  32.3 66.8 %collective-permute-start.14 = (f32[2,1,32]{2,1,0:T(1,128)}, f32[2,1,32]{2,1,0:T(1,128)}, u32[]{:S(2)}, u32[]{:S(2)}) collective-permute-start(f32[2,1,32]{2,1,0:T(1,128)} %get-tuple-element.54), channel_id=1, source_target_pairs={{16,0},{32,16},{48,32},{64,48},{80,64},{96,80},{112,96},{128,112},... | collective-permute-start | bytes 776 | tf_op jit(solution)/shard_map/ppermute | solution.py:25
  37.9 28.1 %collective-permute-start.7 = (f32[8,9,192]{2,1,0:T(8,128)S(1)}, f32[8,9,192]{2,1,0:T(8,128)}, u32[]{:S(2)}, u32[]{:S(2)}) collective-permute-start(f32[8,9,192]{2,1,0:T(8,128)S(1)} %maximum_select_fusion.6), channel_id=1, source_target_pairs={{0,128},{16,144},{32,160},{48,176},{64,192},{80,208},{96,224},{112... | collective-permute-start | bytes 165896 | tf_op jit(solution)/shard_map/ppermute | solution.py:52
  42.6 73.5 %collective-permute-start = (bf16[4,32,192]{2,1,0:T(8,128)(2,1)}, bf16[4,32,192]{2,1,0:T(8,128)(2,1)}, u32[]{:S(2)}, u32[]{:S(2)}) collective-permute-start(bf16[4,32,192]{2,1,0:T(8,128)(2,1)} %get-tuple-element.33), channel_id=1, source_target_pairs={{0,16},{16,32},{32,48},{48,64},{64,80},{80,96},{96,112},{112,128},... | collective-permute-start | bytes 147464 | tf_op jit(solution)/shard_map/ppermute | solution.py:23
  44.5 71.6 %collective-permute-start.1 = (bf16[4,32,192]{2,1,0:T(8,128)(2,1)}, bf16[4,32,192]{2,1,0:T(8,128)(2,1)}, u32[]{:S(2)}, u32[]{:S(2)}) collective-permute-start(bf16[4,32,192]{2,1,0:T(8,128)(2,1)} %get-tuple-element.34), channel_id=1, source_target_pairs={{16,0},{32,16},{48,32},{64,48},{80,64},{96,80},{112,96},{128,112},... | collective-permute-start | bytes 147464 | tf_op jit(solution)/shard_map/ppermute | solution.py:25
  59.2 23.3 %all-to-all-start = ((f32[16,1,2048]{2,1,0:T(1,128)}), f32[16,1,2048]{2,1,0:T(1,128)}, u32[]{:S(2)}, u32[]{:S(2)}) async-start(f32[16,1,2048]{2,1,0:T(1,128)} %reshape.339), calls=%async_computation | async-start | bytes 262144 | tf_op jit(solution)/shard_map/all_to_all | solution.py:120
  67.8 12.0 %collective-permute-start.8 = (f32[16,9,192]{2,1,0:T(8,128)}, f32[16,9,192]{2,1,0:T(8,128)}, u32[]{:S(2)}, u32[]{:S(2)}) collective-permute-start(f32[16,9,192]{2,1,0:T(8,128)} %maximum_select_fusion.3), channel_id=1, source_target_pairs={{0,256},{16,272},{32,288},{48,304},{64,320},{80,336},{96,352},{112... | collective-permute-start | bytes 331784 | tf_op jit(solution)/shard_map/ppermute | solution.py:52
  101.6 9.6 %collective-permute-start.10 = (f32[33,192]{1,0:T(8,128)S(1)}, f32[33,192]{1,0:T(8,128)S(1)}, u32[]{:S(2)}, u32[]{:S(2)}) collective-permute-start(f32[33,192]{1,0:T(8,128)S(1)} %pad_maximum_fusion.39), channel_id=1, source_target_pairs={{0,2},{1,3},{2,0},{3,1},{4,6},{5,7},{6,4},{7,5},{8,10},{9,11},{10,... | collective-permute-start | bytes 76040 | tf_op jit(solution)/shard_map/ppermute | solution.py:52
  105.7 41.8 %collective-permute-start.15 = (f32[2,34,1]{2,1,0:T(8,128)}, f32[2,34,1]{2,1,0:T(8,128)}, u32[]{:S(2)}, u32[]{:S(2)}) collective-permute-start(f32[2,34,1]{2,1,0:T(8,128)} %get-tuple-element.51), channel_id=1, source_target_pairs={{0,1},{1,2},{2,3},{3,4},{4,5},{5,6},{6,7},{7,8},{8,9},{9,10},{10,1... | collective-permute-start | bytes 824 | tf_op jit(solution)/shard_map/ppermute | solution.py:23
  107.6 39.8 %collective-permute-start.16 = (f32[2,34,1]{2,1,0:T(8,128)}, f32[2,34,1]{2,1,0:T(8,128)}, u32[]{:S(2)}, u32[]{:S(2)}) collective-permute-start(f32[2,34,1]{2,1,0:T(8,128)} %get-tuple-element.52), channel_id=1, source_target_pairs={{1,0},{2,1},{3,2},{4,3},{5,4},{6,5},{7,6},{8,7},{9,8},{10,9},{11,1... | collective-permute-start | bytes 824 | tf_op jit(solution)/shard_map/ppermute | solution.py:25
  111.8 10.7 %collective-permute-start.11 = (f32[17,192]{1,0:T(8,128)S(1)}, f32[17,192]{1,0:T(8,128)S(1)}, u32[]{:S(2)}, u32[]{:S(2)}) collective-permute-start(f32[17,192]{1,0:T(8,128)S(1)} %pad_maximum_fusion.52), channel_id=1, source_target_pairs={{0,4},{1,5},{2,6},{3,7},{4,0},{5,1},{6,2},{7,3},{8,12},{9,13},{10,... | collective-permute-start | bytes 39176 | tf_op jit(solution)/shard_map/ppermute | solution.py:52
  117.0 8.5 %collective-permute-start.2 = (bf16[40,4,192]{2,1,0:T(4,128)(2,1)S(1)}, bf16[40,4,192]{2,1,0:T(4,128)(2,1)S(1)}, u32[]{:S(2)}, u32[]{:S(2)}) collective-permute-start(bf16[40,4,192]{2,1,0:T(4,128)(2,1)S(1)} %get-tuple-element.27), channel_id=1, source_target_pairs={{0,1},{1,2},{2,3},{3,4},{4,5},{5,6},{6,7},{7,8},{8,9},{9,10},{10,1... | collective-permute-start | bytes 184328 | tf_op jit(solution)/shard_map/ppermute | solution.py:23
  118.9 6.5 %collective-permute-start.3 = (bf16[40,4,192]{2,1,0:T(4,128)(2,1)S(1)}, bf16[40,4,192]{2,1,0:T(4,128)(2,1)S(1)}, u32[]{:S(2)}, u32[]{:S(2)}) collective-permute-start(bf16[40,4,192]{2,1,0:T(4,128)(2,1)S(1)} %get-tuple-element.28), channel_id=1, source_target_pairs={{1,0},{2,1},{3,2},{4,3},{5,4},{6,5},{7,6},{8,7},{9,8},{10,9},{11,1... | collective-permute-start | bytes 184328 | tf_op jit(solution)/shard_map/ppermute | solution.py:25
  123.1 9.7 %collective-permute-start.12 = (f32[9,192]{1,0:T(8,128)S(1)}, f32[9,192]{1,0:T(8,128)S(1)}, u32[]{:S(2)}, u32[]{:S(2)}) collective-permute-start(f32[9,192]{1,0:T(8,128)S(1)} %pad_maximum_fusion.60), channel_id=1, source_target_pairs={{0,8},{1,9},{2,10},{3,11},{4,12},{5,13},{6,14},{7,15},{8,0},{9,1},... | collective-permute-start | bytes 20744 | tf_op jit(solution)/shard_map/ppermute | solution.py:52
  139.5 8.8 %collective-permute-start.18 = (f32[1,32,192]{2,1,0:T(8,128)S(1)}, f32[1,32,192]{2,1,0:T(8,128)S(1)}, u32[]{:S(2)}, u32[]{:S(2)}) collective-permute-start(f32[1,32,192]{2,1,0:T(8,128)S(1)} %get-tuple-element.19), channel_id=1, source_target_pairs={{0,16},{16,32},{32,48},{48,64},{64,80},{80,96},{96,112},{112,128},... | collective-permute-start | bytes 73736 | tf_op jit(solution)/shard_map/ppermute | solution.py:23
  141.4 7.6 %collective-permute-start.17 = (f32[1,32,192]{2,1,0:T(8,128)S(1)}, f32[1,32,192]{2,1,0:T(8,128)S(1)}, u32[]{:S(2)}, u32[]{:S(2)}) collective-permute-start(f32[1,32,192]{2,1,0:T(8,128)S(1)} %get-tuple-element.20), channel_id=1, source_target_pairs={{16,0},{32,16},{48,32},{64,48},{80,64},{96,80},{112,96},{128,112},... | collective-permute-start | bytes 73736 | tf_op jit(solution)/shard_map/ppermute | solution.py:25
  165.3 6.7 %collective-permute-start.26 = (f32[2,9,192]{2,1,0:T(8,128)S(1)}, f32[2,9,192]{2,1,0:T(8,128)S(1)}, u32[]{:S(2)}, u32[]{:S(2)}) collective-permute-start(f32[2,9,192]{2,1,0:T(8,128)S(1)} %maximum_select_fusion.13), channel_id=1, source_target_pairs={{0,32},{16,48},{32,0},{48,16},{64,96},{80,112},{96,64},{112,80},{1... | collective-permute-start | bytes 41480 | tf_op jit(solution)/shard_map/ppermute | solution.py:52
  172.0 10.1 %collective-permute-start.27 = (f32[4,9,192]{2,1,0:T(8,128)S(1)}, f32[4,9,192]{2,1,0:T(8,128)S(1)}, u32[]{:S(2)}, u32[]{:S(2)}) collective-permute-start(f32[4,9,192]{2,1,0:T(8,128)S(1)} %maximum_select_fusion.10), channel_id=1, source_target_pairs={{0,64},{16,80},{32,96},{48,112},{64,0},{80,16},{96,32},{112,48},{1... | collective-permute-start | bytes 82952 | tf_op jit(solution)/shard_map/ppermute | solution.py:52
  182.1 8.3 %collective-permute-start.28 = (f32[8,9,192]{2,1,0:T(8,128)S(1)}, f32[8,9,192]{2,1,0:T(8,128)S(1)}, u32[]{:S(2)}, u32[]{:S(2)}) collective-permute-start(f32[8,9,192]{2,1,0:T(8,128)S(1)} %maximum_select_fusion.7), channel_id=1, source_target_pairs={{0,128},{16,144},{32,160},{48,176},{64,192},{80,208},{96,224},{112... | collective-permute-start | bytes 165896 | tf_op jit(solution)/shard_map/ppermute | solution.py:52
  190.4 9.8 %collective-permute-start.29 = (f32[16,9,192]{2,1,0:T(8,128)S(1)}, f32[16,9,192]{2,1,0:T(8,128)S(1)}, u32[]{:S(2)}, u32[]{:S(2)}) collective-permute-start(f32[16,9,192]{2,1,0:T(8,128)S(1)} %maximum_select_fusion.4), channel_id=1, source_target_pairs={{0,256},{16,272},{32,288},{48,304},{64,320},{80,336},{96,352},{112... | collective-permute-start | bytes 331784 | tf_op jit(solution)/shard_map/ppermute | solution.py:52
  209.3 13.3 %collective-permute-start.31 = (f32[33,192]{1,0:T(8,128)S(1)}, f32[33,192]{1,0:T(8,128)S(1)}, u32[]{:S(2)}, u32[]{:S(2)}) collective-permute-start(f32[33,192]{1,0:T(8,128)S(1)} %pad_maximum_fusion.41), channel_id=1, source_target_pairs={{0,2},{1,3},{2,0},{3,1},{4,6},{5,7},{6,4},{7,5},{8,10},{9,11},{10,... | collective-permute-start | bytes 76040 | tf_op jit(solution)/shard_map/ppermute | solution.py:52
  213.7 12.7 %collective-permute-start.21 = (bf16[4,32,192]{2,1,0:T(8,128)(2,1)S(1)}, bf16[4,32,192]{2,1,0:T(8,128)(2,1)S(1)}, u32[]{:S(2)}, u32[]{:S(2)}) collective-permute-start(bf16[4,32,192]{2,1,0:T(8,128)(2,1)S(1)} %get-tuple-element.31), channel_id=1, source_target_pairs={{0,16},{16,32},{32,48},{48,64},{64,80},{80,96},{96,112},{112,128},... | collective-permute-start | bytes 147464 | tf_op jit(solution)/shard_map/ppermute | solution.py:23
  215.6 10.8 %collective-permute-start.22 = (bf16[4,32,192]{2,1,0:T(8,128)(2,1)S(1)}, bf16[4,32,192]{2,1,0:T(8,128)(2,1)S(1)}, u32[]{:S(2)}, u32[]{:S(2)}) collective-permute-start(bf16[4,32,192]{2,1,0:T(8,128)(2,1)S(1)} %get-tuple-element.32), channel_id=1, source_target_pairs={{16,0},{32,16},{48,32},{64,48},{80,64},{96,80},{112,96},{128,112},... | collective-permute-start | bytes 147464 | tf_op jit(solution)/shard_map/ppermute | solution.py:25
  222.6 9.4 %collective-permute-start.32 = (f32[17,192]{1,0:T(8,128)S(1)}, f32[17,192]{1,0:T(8,128)S(1)}, u32[]{:S(2)}, u32[]{:S(2)}) collective-permute-start(f32[17,192]{1,0:T(8,128)S(1)} %pad_maximum_fusion.53), channel_id=1, source_target_pairs={{0,4},{1,5},{2,6},{3,7},{4,0},{5,1},{6,2},{7,3},{8,12},{9,13},{10,... | collective-permute-start | bytes 39176 | tf_op jit(solution)/shard_map/ppermute | solution.py:52
  226.5 7.6 %collective-permute-start.23 = (bf16[40,4,192]{2,1,0:T(4,128)(2,1)S(1)}, bf16[40,4,192]{2,1,0:T(4,128)(2,1)S(1)}, u32[]{:S(2)}, u32[]{:S(2)}) collective-permute-start(bf16[40,4,192]{2,1,0:T(4,128)(2,1)S(1)} %get-tuple-element.25), channel_id=1, source_target_pairs={{0,1},{1,2},{2,3},{3,4},{4,5},{5,6},{6,7},{7,8},{8,9},{9,10},{10,1... | collective-permute-start | bytes 184328 | tf_op jit(solution)/shard_map/ppermute | solution.py:23
  232.1 9.5 %collective-permute-start.33 = (f32[9,192]{1,0:T(8,128)S(1)}, f32[9,192]{1,0:T(8,128)S(1)}, u32[]{:S(2)}, u32[]{:S(2)}) collective-permute-start(f32[9,192]{1,0:T(8,128)S(1)} %pad_maximum_fusion.61), channel_id=1, source_target_pairs={{0,8},{1,9},{2,10},{3,11},{4,12},{5,13},{6,14},{7,15},{8,0},{9,1},... | collective-permute-start | bytes 20744 | tf_op jit(solution)/shard_map/ppermute | solution.py:52
  248.6 8.0 %collective-permute-start.35 = (f32[1,32,192]{2,1,0:T(8,128)S(1)}, f32[1,32,192]{2,1,0:T(8,128)S(1)}, u32[]{:S(2)}, u32[]{:S(2)}) collective-permute-start(f32[1,32,192]{2,1,0:T(8,128)S(1)} %get-tuple-element.17), channel_id=1, source_target_pairs={{0,16},{16,32},{32,48},{48,64},{64,80},{80,96},{96,112},{112,128},... | collective-permute-start | bytes 73736 | tf_op jit(solution)/shard_map/ppermute | solution.py:23
  250.5 7.6 %collective-permute-start.34 = (f32[1,32,192]{2,1,0:T(8,128)S(1)}, f32[1,32,192]{2,1,0:T(8,128)S(1)}, u32[]{:S(2)}, u32[]{:S(2)}) collective-permute-start(f32[1,32,192]{2,1,0:T(8,128)S(1)} %get-tuple-element.18), channel_id=1, source_target_pairs={{16,0},{32,16},{48,32},{64,48},{80,64},{96,80},{112,96},{128,112},... | collective-permute-start | bytes 73736 | tf_op jit(solution)/shard_map/ppermute | solution.py:25
  274.5 6.7 %collective-permute-start.43 = (f32[2,9,192]{2,1,0:T(8,128)S(1)}, f32[2,9,192]{2,1,0:T(8,128)S(1)}, u32[]{:S(2)}, u32[]{:S(2)}) collective-permute-start(f32[2,9,192]{2,1,0:T(8,128)S(1)} %maximum_select_fusion.14), channel_id=1, source_target_pairs={{0,32},{16,48},{32,0},{48,16},{64,96},{80,112},{96,64},{112,80},{1... | collective-permute-start | bytes 41480 | tf_op jit(solution)/shard_map/ppermute | solution.py:52
  281.2 10.1 %collective-permute-start.44 = (f32[4,9,192]{2,1,0:T(8,128)S(1)}, f32[4,9,192]{2,1,0:T(8,128)S(1)}, u32[]{:S(2)}, u32[]{:S(2)}) collective-permute-start(f32[4,9,192]{2,1,0:T(8,128)S(1)} %maximum_select_fusion.11), channel_id=1, source_target_pairs={{0,64},{16,80},{32,96},{48,112},{64,0},{80,16},{96,32},{112,48},{1... | collective-permute-start | bytes 82952 | tf_op jit(solution)/shard_map/ppermute | solution.py:52
  291.3 8.3 %collective-permute-start.45 = (f32[8,9,192]{2,1,0:T(8,128)S(1)}, f32[8,9,192]{2,1,0:T(8,128)S(1)}, u32[]{:S(2)}, u32[]{:S(2)}) collective-permute-start(f32[8,9,192]{2,1,0:T(8,128)S(1)} %maximum_select_fusion.8), channel_id=1, source_target_pairs={{0,128},{16,144},{32,160},{48,176},{64,192},{80,208},{96,224},{112... | collective-permute-start | bytes 165896 | tf_op jit(solution)/shard_map/ppermute | solution.py:52
  299.6 9.8 %collective-permute-start.46 = (f32[16,9,192]{2,1,0:T(8,128)S(1)}, f32[16,9,192]{2,1,0:T(8,128)S(1)}, u32[]{:S(2)}, u32[]{:S(2)}) collective-permute-start(f32[16,9,192]{2,1,0:T(8,128)S(1)} %maximum_select_fusion.5), channel_id=1, source_target_pairs={{0,256},{16,272},{32,288},{48,304},{64,320},{80,336},{96,352},{112... | collective-permute-start | bytes 331784 | tf_op jit(solution)/shard_map/ppermute | solution.py:52
  316.8 10.8 %collective-permute-start.48 = (f32[33,192]{1,0:T(8,128)S(1)}, f32[33,192]{1,0:T(8,128)S(1)}, u32[]{:S(2)}, u32[]{:S(2)}) collective-permute-start(f32[33,192]{1,0:T(8,128)S(1)} %pad_maximum_fusion.42), channel_id=1, source_target_pairs={{0,2},{1,3},{2,0},{3,1},{4,6},{5,7},{6,4},{7,5},{8,10},{9,11},{10,... | collective-permute-start | bytes 76040 | tf_op jit(solution)/shard_map/ppermute | solution.py:52
  319.6 14.6 %collective-permute-start.38 = (bf16[4,32,192]{2,1,0:T(8,128)(2,1)S(1)}, bf16[4,32,192]{2,1,0:T(8,128)(2,1)S(1)}, u32[]{:S(2)}, u32[]{:S(2)}) collective-permute-start(bf16[4,32,192]{2,1,0:T(8,128)(2,1)S(1)} %get-tuple-element.29), channel_id=1, source_target_pairs={{0,16},{16,32},{32,48},{48,64},{64,80},{80,96},{96,112},{112,128},... | collective-permute-start | bytes 147464 | tf_op jit(solution)/shard_map/ppermute | solution.py:23
  321.6 12.7 %collective-permute-start.39 = (bf16[4,32,192]{2,1,0:T(8,128)(2,1)S(1)}, bf16[4,32,192]{2,1,0:T(8,128)(2,1)S(1)}, u32[]{:S(2)}, u32[]{:S(2)}) collective-permute-start(bf16[4,32,192]{2,1,0:T(8,128)(2,1)S(1)} %get-tuple-element.30), channel_id=1, source_target_pairs={{16,0},{32,16},{48,32},{64,48},{80,64},{96,80},{112,96},{128,112},... | collective-permute-start | bytes 147464 | tf_op jit(solution)/shard_map/ppermute | solution.py:25
  327.7 12.2 %collective-permute-start.49 = (f32[17,192]{1,0:T(8,128)S(1)}, f32[17,192]{1,0:T(8,128)S(1)}, u32[]{:S(2)}, u32[]{:S(2)}) collective-permute-start(f32[17,192]{1,0:T(8,128)S(1)} %pad_maximum_fusion.54), channel_id=1, source_target_pairs={{0,4},{1,5},{2,6},{3,7},{4,0},{5,1},{6,2},{7,3},{8,12},{9,13},{10,... | collective-permute-start | bytes 39176 | tf_op jit(solution)/shard_map/ppermute | solution.py:52
  334.3 7.8 %collective-permute-start.40 = (bf16[40,4,192]{2,1,0:T(4,128)(2,1)S(1)}, bf16[40,4,192]{2,1,0:T(4,128)(2,1)S(1)}, u32[]{:S(2)}, u32[]{:S(2)}) collective-permute-start(bf16[40,4,192]{2,1,0:T(4,128)(2,1)S(1)} %get-tuple-element.23), channel_id=1, source_target_pairs={{0,1},{1,2},{2,3},{3,4},{4,5},{5,6},{6,7},{7,8},{8,9},{9,10},{10,1... | collective-permute-start | bytes 184328 | tf_op jit(solution)/shard_map/ppermute | solution.py:23
  340.0 9.5 %collective-permute-start.50 = (f32[9,192]{1,0:T(8,128)S(1)}, f32[9,192]{1,0:T(8,128)S(1)}, u32[]{:S(2)}, u32[]{:S(2)}) collective-permute-start(f32[9,192]{1,0:T(8,128)S(1)} %pad_maximum_fusion.62), channel_id=1, source_target_pairs={{0,8},{1,9},{2,10},{3,11},{4,12},{5,13},{6,14},{7,15},{8,0},{9,1},... | collective-permute-start | bytes 20744 | tf_op jit(solution)/shard_map/ppermute | solution.py:52
  358.0 8.2 %collective-permute-start.52 = (f32[1,32,192]{2,1,0:T(8,128)S(1)}, f32[1,32,192]{2,1,0:T(8,128)S(1)}, u32[]{:S(2)}, u32[]{:S(2)}) collective-permute-start(f32[1,32,192]{2,1,0:T(8,128)S(1)} %get-tuple-element.15), channel_id=1, source_target_pairs={{0,16},{16,32},{32,48},{48,64},{64,80},{80,96},{96,112},{112,128},... | collective-permute-start | bytes 73736 | tf_op jit(solution)/shard_map/ppermute | solution.py:23
  360.1 7.6 %collective-permute-start.51 = (f32[1,32,192]{2,1,0:T(8,128)S(1)}, f32[1,32,192]{2,1,0:T(8,128)S(1)}, u32[]{:S(2)}, u32[]{:S(2)}) collective-permute-start(f32[1,32,192]{2,1,0:T(8,128)S(1)} %get-tuple-element.16), channel_id=1, source_target_pairs={{16,0},{32,16},{48,32},{64,48},{80,64},{96,80},{112,96},{128,112},... | collective-permute-start | bytes 73736 | tf_op jit(solution)/shard_map/ppermute | solution.py:25
  385.4 6.4 %collective-permute-start.57 = (f32[192]{0:T(256)S(1)}, f32[192]{0:T(256)S(1)}, u32[]{:S(2)}, u32[]{:S(2)}) collective-permute-start(f32[192]{0:T(256)S(1)} %add.361), channel_id=1, source_target_pairs={{0,4},{1,5},{2,6},{3,7},{4,0},{5,1},{6,2},{7,3},{8,12},{9,13},{10,... | collective-permute-start | bytes 2312 | tf_op jit(solution)/shard_map/ppermute | solution.py:52
  391.8 9.4 %collective-permute-start.58 = (f32[192]{0:T(256)S(1)}, f32[192]{0:T(256)S(1)}, u32[]{:S(2)}, u32[]{:S(2)}) collective-permute-start(f32[192]{0:T(256)S(1)} %add.362), channel_id=1, source_target_pairs={{0,8},{1,9},{2,10},{3,11},{4,12},{5,13},{6,14},{7,15},{8,0},{9,1},... | collective-permute-start | bytes 2312 | tf_op jit(solution)/shard_map/ppermute | solution.py:52
  406.6 6.4 %collective-permute-start.60 = (f32[192]{0:T(256)S(1)}, f32[192]{0:T(256)S(1)}, u32[]{:S(2)}, u32[]{:S(2)}) collective-permute-start(f32[192]{0:T(256)S(1)} %add.364), channel_id=1, source_target_pairs={{0,32},{16,48},{32,0},{48,16},{64,96},{80,112},{96,64},{112,80},{1... | collective-permute-start | bytes 2312 | tf_op jit(solution)/shard_map/ppermute | solution.py:52
  413.0 9.4 %collective-permute-start.61 = (f32[192]{0:T(256)S(1)}, f32[192]{0:T(256)S(1)}, u32[]{:S(2)}, u32[]{:S(2)}) collective-permute-start(f32[192]{0:T(256)S(1)} %add.365), channel_id=1, source_target_pairs={{0,64},{16,80},{32,96},{48,112},{64,0},{80,16},{96,32},{112,48},{1... | collective-permute-start | bytes 2312 | tf_op jit(solution)/shard_map/ppermute | solution.py:52
  427.8 7.0 %collective-permute-start.63 = (f32[192]{0:T(256)S(1)}, f32[192]{0:T(256)S(1)}, u32[]{:S(2)}, u32[]{:S(2)}) collective-permute-start(f32[192]{0:T(256)S(1)} %add.367), channel_id=1, source_target_pairs={{0,256},{16,272},{32,288},{48,304},{64,320},{80,336},{96,352},{112... | collective-permute-start | bytes 2312 | tf_op jit(solution)/shard_map/ppermute | solution.py:52
  (60 other events, 1186.5 us)

commit v3 on v1

--- a/solution.py
+++ b/solution.py
@@ -47,9 +47,19 @@
     return total
 
 
+def gathered_by_exchange(block, axis):
+    count = lax.axis_size(axis)
+    copies = jnp.broadcast_to(block[None], (count,) + block.shape)
+    return lax.all_to_all(copies, axis, 0, 0, tiled=True)
+
+
+def summed_by_exchange(blocks, axis):
+    return jnp.sum(lax.all_to_all(blocks, axis, 0, 0, tiled=True), axis=0)
+
+
 def total_over_mesh(values):
-    for axis in ("gx", "gy"):
-        values = jnp.sum(lax.all_gather(values, axis, axis=0), axis=0)
+    for axis in ("gy", "gx"):
+        values = jnp.sum(gathered_by_exchange(values, axis), axis=0)
     return values
 
 
@@ -85,7 +95,7 @@
         restricted = jnp.dot(flat_basis, flat_core, precision=highest)
         squares = jnp.sum(flat_core * flat_core, axis=0)
         carried = jnp.concatenate([restricted, squares[None]], axis=0)
-        gathered = lax.all_gather(carried, "gx", axis=0)
+        gathered = gathered_by_exchange(carried, "gx")
         column_total = jnp.sum(gathered[:, modes], axis=0)
         column_coarse = gathered[:, :modes].reshape(rows_x * modes, fields)
         partial = jnp.dot(coarse_block, column_coarse, precision=highest).reshape(
@@ -94,7 +104,7 @@
         partial = jnp.concatenate(
             [partial, jnp.broadcast_to(column_total, (cols_y, 1, fields))], axis=1
         )
-        reduced = lax.psum_scatter(partial, "gy", scatter_dimension=0, tiled=True)[0]
+        reduced = summed_by_exchange(partial, "gy")
         coarse_part = reduced[:modes]
         squares_all = reduced[modes]
         prolonged = jnp.dot(flat_basis.T, coarse_part, precision=highest).reshape(

time: 716 us -> 361 us (0.50)
  blocking collectives: 309 us -> 18.7 us
  waiting for transfers between devices: 153 us -> 40 us
  starting transfers between devices: 126 us -> 152 us
  local copies, waits for them, and re-layouts: 39.3 us -> 59.9 us
  other arithmetic: 44 us -> 63.5 us
  between operations: 15.8 us -> 1.36 us
    unnamed x2 -> x0, blocking collectives: 184 us -> none
    reduce_scatter x3 -> x0, waiting for transfers between devices: 135 us -> none  [precondition(): lax.psum_scatter(partial, 'gy', scatter_dimension=0, tiled=True)[0]]
    all_gather x3 -> x0, blocking collectives: 125 us -> none  [precondition(): gathered = lax.all_gather(carried, 'gx', axis=0)]
    all_to_all x0 -> x7, starting transfers between devices: none -> 68.1 us  [the longest x4 39 us: gathered_by_exchange(): return lax.all_to_all(copies, axis, 0, 0, tiled=True)]
    ppermute x14, starting transfers between devices: 80.7 us -> 51.2 us  [extended(): lax.ppermute(tail, axis, [(i, (i + 1) % count) for i in range(ends)])]
    all_to_all x0 -> x1, blocking collectives: none -> 18.7 us  [gathered_by_exchange(): return lax.all_to_all(copies, axis, 0, 0, tiled=True)]
    unnamed x64 -> x68, local copies, waits for them, and re-layouts: 8.35 us -> 25.8 us
    all_to_all x0 -> x7, waiting for transfers between devices: none -> 16.6 us  [the longest x4 16.6 us: gathered_by_exchange(): return lax.all_to_all(copies, axis, 0, 0, tiled=True)]
  transfers between devices with their start and end apart: 32 -> 36, of which waited for: 11 -> 12; matrix products, arithmetic and copies ran while one was open for 9% -> 27% of each run, Pallas kernels for 0% -> 0%
where the time goes in v3:
time: 361 us; the launch traced here: 358 us
  starting transfers between devices  152 us (42%)
  other arithmetic  63.5 us (18%)
  local copies, waits for them, and re-layouts  59.9 us (17%)
  waiting for transfers between devices  40 us (11%)
  matrix products  22.8 us (6%)
  blocking collectives  18.7 us (5%)
    ppermute x14, starting transfers between devices, extended(): lax.ppermute(tail, axis, [(i, (i + 1) % count) for i in range(ends)])  51.2 us
    all_to_all x4, starting transfers between devices, gathered_by_exchange(): return lax.all_to_all(copies, axis, 0, 0, tiled=True)  39 us
    all_to_all x3, starting transfers between devices, summed_by_exchange(): return jnp.sum(lax.all_to_all(blocks, axis, 0, 0, tiled=True), axis=0)  29.1 us
    unnamed x68, local copies, waits for them, and re-layouts  25.8 us
    ppermute x14, starting transfers between devices, extended(): lax.ppermute(head, axis, [((i + 1) % count, i) for i in range(ends)])  23.5 us
    all_to_all x1, blocking collectives, gathered_by_exchange(): return lax.all_to_all(copies, axis, 0, 0, tiled=True)  18.7 us
    ppermute x14, waiting for transfers between devices, extended(): lax.ppermute(head, axis, [((i + 1) % count, i) for i in range(ends)])  17.4 us
    all_to_all x4, waiting for transfers between devices, gathered_by_exchange(): return lax.all_to_all(copies, axis, 0, 0, tiled=True)  16.6 us
  transfers between devices with their start and end apart: 36, of which 12 were waited for; matrix products, arithmetic and copies ran while one was open for 27% of the time, Pallas kernels for 0%

profile of v3, /device:TPU:1, one launch (start us, length us, event | category | flops | bytes accessed | tf_op | source)
XLA Modules:
  0.0 357.8 jit_solution(14156003277185950594)
XLA Ops:
  2.2 5.4 %collective-permute-start.4 = (f32[2,1,32]{2,1,0:T(1,128)}, f32[2,1,32]{2,1,0:T(1,128)}, u32[]{:S(2)}, u32[]{:S(2)}) collective-permute-start(f32[2,1,32]{2,1,0:T(1,128)} %get-tuple-element.37), channel_id=1, source_target_pairs={{0,16},{16,32},{32,48},{48,64},{64,80},{80,96},{96,112},{112,128},... | collective-permute-start | bytes 776 | tf_op jit(solution)/shard_map/ppermute | solution.py:23
  12.6 4.7 %collective-permute-start = (bf16[4,32,192]{2,1,0:T(8,128)(2,1)}, bf16[4,32,192]{2,1,0:T(8,128)(2,1)}, u32[]{:S(2)}, u32[]{:S(2)}) collective-permute-start(bf16[4,32,192]{2,1,0:T(8,128)(2,1)} %get-tuple-element.33), channel_id=1, source_target_pairs={{0,16},{16,32},{32,48},{48,64},{64,80},{80,96},{96,112},{112,128},... | collective-permute-start | bytes 147464 | tf_op jit(solution)/shard_map/ppermute | solution.py:23
  18.6 2.5 reshape.84
  21.1 3.3 copy.64
  26.4 8.7 %all-to-all-start.1 = ((f32[16,1,2048]{2,1,0:T(1,128)}), f32[16,1,2048]{2,1,0:T(1,128)S(1)}, u32[]{:S(2)}, u32[]{:S(2)}) async-start(f32[16,1,2048]{2,1,0:T(1,128)} %reshape.99), calls=%async_computation.1 | async-start | bytes 262144 | tf_op jit(solution)/shard_map/all_to_all | solution.py:83
  40.7 3.3 all-to-all-done.1
  44.0 14.5 %all-to-all-start = ((f32[32,1,1728]{2,1,0:T(1,128)}), f32[32,1,1728]{2,1,0:T(1,128)}, u32[]{:S(2)}, u32[]{:S(2)}) async-start(f32[32,1,1728]{2,1,0:T(1,128)} %reshape.97), calls=%async_computation | async-start | bytes 458752 | tf_op jit(solution)/shard_map/all_to_all | solution.py:53
  65.3 2.6 collective-permute-start.3
  71.3 3.0 copy.65
  74.3 2.8 reshape.85
  77.1 2.8 reduce.9
  91.2 6.0 %all-to-all-start.2 = ((f32[16,1,1728]{2,1,0:T(1,128)}), f32[16,1,1728]{2,1,0:T(1,128)}, u32[]{:S(2)}, u32[]{:S(2)}) async-start(f32[16,1,1728]{2,1,0:T(1,128)} %reshape.101), calls=%async_computation.2 | async-start | bytes 229376 | tf_op jit(solution)/shard_map/all_to_all | solution.py:57
  98.7 3.5 collective-permute-start.6
  104.2 2.4 pad_maximum_fusion.24
  106.7 2.5 reduce.11
  114.0 2.9 fusion.9
  120.9 3.4 collective-permute-start.9
  126.4 3.0 collective-permute-done.8
  131.8 4.3 %collective-permute-start.11 = (f32[34,1,192]{2,1,0:T(1,128)S(1)}, f32[34,1,192]{2,1,0:T(1,128)S(1)}, u32[]{:S(2)}, u32[]{:S(2)}) collective-permute-start(f32[34,1,192]{2,1,0:T(1,128)S(1)} %get-tuple-element.14), channel_id=1, source_target_pairs={{0,1},{1,2},{2,3},{3,4},{4,5},{5,6},{6,7},{7,8},{8,9},{9,10},{10,1... | collective-permute-start | bytes 78344 | tf_op jit(solution)/shard_map/ppermute | solution.py:23
  137.0 2.5 fusion.89
  144.1 9.6 %all-to-all-start.3 = ((f32[32,1,1728]{2,1,0:T(1,128)}), f32[32,1,1728]{2,1,0:T(1,128)}, u32[]{:S(2)}, u32[]{:S(2)}) async-start(f32[32,1,1728]{2,1,0:T(1,128)} %reshape.103), calls=%async_computation.3 | async-start | bytes 458752 | tf_op jit(solution)/shard_map/all_to_all | solution.py:53
  155.3 3.7 %collective-permute-start.12 = (bf16[4,32,192]{2,1,0:T(8,128)(2,1)}, bf16[4,32,192]{2,1,0:T(8,128)(2,1)}, u32[]{:S(2)}, u32[]{:S(2)}) collective-permute-start(bf16[4,32,192]{2,1,0:T(8,128)(2,1)} %get-tuple-element.31), channel_id=1, source_target_pairs={{0,16},{16,32},{32,48},{48,64},{64,80},{80,96},{96,112},{112,128},... | collective-permute-start | bytes 147464 | tf_op jit(solution)/shard_map/ppermute | solution.py:23
  160.2 4.5 %all-to-all-done.3 = f32[32,1,1728]{2,1,0:T(1,128)} async-done(((f32[32,1,1728]{2,1,0:T(1,128)}), f32[32,1,1728]{2,1,0:T(1,128)}, u32[]{:S(2)}, u32[]{:S(2)}) %all-to-all-start.3) | async-done | bytes 221216 | tf_op jit(solution)/shard_map/all_to_all | solution.py:53
  164.8 2.8 reduce.12
  178.9 11.4 %all-to-all-start.4 = ((f32[16,1,1728]{2,1,0:T(1,128)}), f32[16,1,1728]{2,1,0:T(1,128)}, u32[]{:S(2)}, u32[]{:S(2)}) async-start(f32[16,1,1728]{2,1,0:T(1,128)} %reshape.105), calls=%async_computation.4 | async-start | bytes 229376 | tf_op jit(solution)/shard_map/all_to_all | solution.py:57
  191.4 3.5 collective-permute-start.14
  196.8 3.8 %collective-permute-done.15 = bf16[40,4,192]{2,1,0:T(4,128)(2,1)S(1)} collective-permute-done((bf16[40,4,192]{2,1,0:T(4,128)(2,1)S(1)}, bf16[40,4,192]{2,1,0:T(4,128)(2,1)S(1)}, u32[]{:S(2)}, u32[]{:S(2)}) %collective-permute-start.15) | collective-permute-done | bytes 61472 | tf_op jit(solution)/shard_map/ppermute | solution.py:25
  203.1 2.5 reduce.13
  210.4 2.9 fusion.18
  221.3 3.3 collective-permute-done.16
  226.7 3.6 %collective-permute-start.19 = (f32[34,1,192]{2,1,0:T(1,128)S(1)}, f32[34,1,192]{2,1,0:T(1,128)S(1)}, u32[]{:S(2)}, u32[]{:S(2)}) collective-permute-start(f32[34,1,192]{2,1,0:T(1,128)S(1)} %get-tuple-element.12), channel_id=1, source_target_pairs={{0,1},{1,2},{2,3},{3,4},{4,5},{5,6},{6,7},{7,8},{8,9},{9,10},{10,1... | collective-permute-start | bytes 78344 | tf_op jit(solution)/shard_map/ppermute | solution.py:23
  231.4 2.5 fusion.87
  238.4 7.6 %all-to-all-start.5 = ((f32[32,1,1728]{2,1,0:T(1,128)}), f32[32,1,1728]{2,1,0:T(1,128)}, u32[]{:S(2)}, u32[]{:S(2)}) async-start(f32[32,1,1728]{2,1,0:T(1,128)} %reshape.107), calls=%async_computation.5 | async-start | bytes 458752 | tf_op jit(solution)/shard_map/all_to_all | solution.py:53
  247.5 3.7 %collective-permute-start.20 = (bf16[4,32,192]{2,1,0:T(8,128)(2,1)}, bf16[4,32,192]{2,1,0:T(8,128)(2,1)}, u32[]{:S(2)}, u32[]{:S(2)}) collective-permute-start(bf16[4,32,192]{2,1,0:T(8,128)(2,1)} %get-tuple-element.29), channel_id=1, source_target_pairs={{0,16},{16,32},{32,48},{48,64},{64,80},{80,96},{96,112},{112,128},... | collective-permute-start | bytes 147464 | tf_op jit(solution)/shard_map/ppermute | solution.py:23
  252.5 4.6 %all-to-all-done.5 = f32[32,1,1728]{2,1,0:T(1,128)} async-done(((f32[32,1,1728]{2,1,0:T(1,128)}), f32[32,1,1728]{2,1,0:T(1,128)}, u32[]{:S(2)}, u32[]{:S(2)}) %all-to-all-start.5) | async-done | bytes 221216 | tf_op jit(solution)/shard_map/all_to_all | solution.py:53
  257.1 2.8 reduce.14
  266.8 11.7 %all-to-all-start.6 = ((f32[16,1,1728]{2,1,0:T(1,128)}), f32[16,1,1728]{2,1,0:T(1,128)S(1)}, u32[]{:S(2)}, u32[]{:S(2)}) async-start(f32[16,1,1728]{2,1,0:T(1,128)} %reshape.109), calls=%async_computation.6 | async-start | bytes 229376 | tf_op jit(solution)/shard_map/all_to_all | solution.py:57
  279.6 3.5 collective-permute-start.22
  285.1 3.8 %collective-permute-done.23 = bf16[40,4,192]{2,1,0:T(4,128)(2,1)S(1)} collective-permute-done((bf16[40,4,192]{2,1,0:T(4,128)(2,1)S(1)}, bf16[40,4,192]{2,1,0:T(4,128)(2,1)S(1)}, u32[]{:S(2)}, u32[]{:S(2)}) %collective-permute-start.23) | collective-permute-done | bytes 61472 | tf_op jit(solution)/shard_map/ppermute | solution.py:25
  296.1 2.9 fusion.27
  299.0 2.5 copy.76
  301.5 3.3 multiply_add_fusion
  304.8 3.5 collective-permute-start.25
  309.7 3.3 collective-permute-done.24
  315.0 3.6 %collective-permute-start.27 = (f32[34,1,192]{2,1,0:T(1,128)S(1)}, f32[34,1,192]{2,1,0:T(1,128)S(1)}, u32[]{:S(2)}, u32[]{:S(2)}) collective-permute-start(f32[34,1,192]{2,1,0:T(1,128)S(1)} %get-tuple-element.10), channel_id=1, source_target_pairs={{0,1},{1,2},{2,3},{3,4},{4,5},{5,6},{6,7},{7,8},{8,9},{9,10},{10,1... | collective-permute-start | bytes 78344 | tf_op jit(solution)/shard_map/ppermute | solution.py:23
  321.7 18.7 %all_to_all.47 = f32[16,1,192]{2,1,0:T(1,128)S(1)} all-to-all(f32[16,1,192]{2,1,0:T(1,128)S(1)} %broadcast_in_dim.31), channel_id=1, replica_groups=mesh['gx'=32,'gy'=16] {'gy'}, dimensions={0} | all-to-all | bytes 24576 | tf_op jit(solution)/shard_map/all_to_all | solution.py:53
  341.0 7.3 %all-to-all-start.8 = ((f32[32,1,192]{2,1,0:T(1,128)}), f32[32,1,192]{2,1,0:T(1,128)S(1)}, u32[]{:S(2)}, u32[]{:S(2)}) async-start(f32[32,1,192]{2,1,0:T(1,128)} %broadcast_in_dim.32), calls=%async_computation.8 | async-start | bytes 65536 | tf_op jit(solution)/shard_map/all_to_all | solution.py:53
  349.6 7.5 %all-to-all-done.8 = f32[32,1,192]{2,1,0:T(1,128)S(1)} async-done(((f32[32,1,192]{2,1,0:T(1,128)}), f32[32,1,192]{2,1,0:T(1,128)S(1)}, u32[]{:S(2)}, u32[]{:S(2)}) %all-to-all-start.8) | async-done | bytes 24608 | tf_op jit(solution)/shard_map/all_to_all | solution.py:53
  (182 shorter events, 127.4 us)
Async XLA Ops:
  0.6 113.4 %copy-start = (bf16[1,1,1024,1600]{2,3,1,0:T(8,128)(2,1)S(1)}, bf16[1,1,1024,1600]{2,3,1,0:T(8,128)(2,1)}, u32[]{:S(2)}) copy-start(bf16[1,1,1024,1600]{2,3,1,0:T(8,128)(2,1)} %param.10) | copy-start | bytes 9830404
  0.6 18.0 %copy-start.25 = (f32[8,4096]{1,0:T(8,128)S(1)}, f32[8,4096]{1,0:T(8,128)}, u32[]{:S(2)}) copy-start(f32[8,4096]{1,0:T(8,128)} %param.11) | copy-start | bytes 393220
  2.2 57.7 %collective-permute-start.4 = (f32[2,1,32]{2,1,0:T(1,128)}, f32[2,1,32]{2,1,0:T(1,128)}, u32[]{:S(2)}, u32[]{:S(2)}) collective-permute-start(f32[2,1,32]{2,1,0:T(1,128)} %get-tuple-element.37), channel_id=1, source_target_pairs={{0,16},{16,32},{32,48},{48,64},{64,80},{80,96},{96,112},{112,128},... | collective-permute-start | bytes 776 | tf_op jit(solution)/shard_map/ppermute | solution.py:23
  7.5 52.3 %collective-permute-start.5 = (f32[2,1,32]{2,1,0:T(1,128)}, f32[2,1,32]{2,1,0:T(1,128)}, u32[]{:S(2)}, u32[]{:S(2)}) collective-permute-start(f32[2,1,32]{2,1,0:T(1,128)} %get-tuple-element.38), channel_id=1, source_target_pairs={{16,0},{32,16},{48,32},{64,48},{80,64},{96,80},{112,96},{128,112},... | collective-permute-start | bytes 776 | tf_op jit(solution)/shard_map/ppermute | solution.py:25
  12.6 48.6 %collective-permute-start = (bf16[4,32,192]{2,1,0:T(8,128)(2,1)}, bf16[4,32,192]{2,1,0:T(8,128)(2,1)}, u32[]{:S(2)}, u32[]{:S(2)}) collective-permute-start(bf16[4,32,192]{2,1,0:T(8,128)(2,1)} %get-tuple-element.33), channel_id=1, source_target_pairs={{0,16},{16,32},{32,48},{48,64},{64,80},{80,96},{96,112},{112,128},... | collective-permute-start | bytes 147464 | tf_op jit(solution)/shard_map/ppermute | solution.py:23
  17.3 43.9 %collective-permute-start.1 = (bf16[4,32,192]{2,1,0:T(8,128)(2,1)}, bf16[4,32,192]{2,1,0:T(8,128)(2,1)}, u32[]{:S(2)}, u32[]{:S(2)}) collective-permute-start(bf16[4,32,192]{2,1,0:T(8,128)(2,1)} %get-tuple-element.34), channel_id=1, source_target_pairs={{16,0},{32,16},{48,32},{64,48},{80,64},{96,80},{112,96},{128,112},... | collective-permute-start | bytes 147464 | tf_op jit(solution)/shard_map/ppermute | solution.py:25
  26.4 32.1 %copy-start.10 = (f32[32,32]{1,0:T(8,128)S(1)}, f32[32,32]{1,0:T(8,128)}, u32[]{:S(2)}) copy-start(f32[32,32]{1,0:T(8,128)} %param.8) | copy-start | bytes 12292
  26.4 17.6 %all-to-all-start.1 = ((f32[16,1,2048]{2,1,0:T(1,128)}), f32[16,1,2048]{2,1,0:T(1,128)S(1)}, u32[]{:S(2)}, u32[]{:S(2)}) async-start(f32[16,1,2048]{2,1,0:T(1,128)} %reshape.99), calls=%async_computation.1 | async-start | bytes 262144 | tf_op jit(solution)/shard_map/all_to_all | solution.py:83
  44.0 23.9 %copy-start.11 = (f32[16,1,2048]{2,1,0:T(1,128)}, f32[16,1,2048]{2,1,0:T(1,128)S(1)}, u32[]{:S(2)}) copy-start(f32[16,1,2048]{2,1,0:T(1,128)S(1)} %all-to-all-done.1) | copy-start | bytes 393220
  44.0 33.1 %all-to-all-start = ((f32[32,1,1728]{2,1,0:T(1,128)}), f32[32,1,1728]{2,1,0:T(1,128)}, u32[]{:S(2)}, u32[]{:S(2)}) async-start(f32[32,1,1728]{2,1,0:T(1,128)} %reshape.97), calls=%async_computation | async-start | bytes 458752 | tf_op jit(solution)/shard_map/all_to_all | solution.py:53
  62.9 41.3 %collective-permute-start.2 = (bf16[40,4,192]{2,1,0:T(4,128)(2,1)}, bf16[40,4,192]{2,1,0:T(4,128)(2,1)}, u32[]{:S(2)}, u32[]{:S(2)}) collective-permute-start(bf16[40,4,192]{2,1,0:T(4,128)(2,1)} %get-tuple-element.27), channel_id=1, source_target_pairs={{0,1},{1,2},{2,3},{3,4},{4,5},{5,6},{6,7},{7,8},{8,9},{9,10},{10,1... | collective-permute-start | bytes 184328 | tf_op jit(solution)/shard_map/ppermute | solution.py:23
  65.3 39.0 %collective-permute-start.3 = (bf16[40,4,192]{2,1,0:T(4,128)(2,1)}, bf16[40,4,192]{2,1,0:T(4,128)(2,1)}, u32[]{:S(2)}, u32[]{:S(2)}) collective-permute-start(bf16[40,4,192]{2,1,0:T(4,128)(2,1)} %get-tuple-element.28), channel_id=1, source_target_pairs={{1,0},{2,1},{3,2},{4,3},{5,4},{6,5},{7,6},{8,7},{9,8},{10,9},{11,1... | collective-permute-start | bytes 184328 | tf_op jit(solution)/shard_map/ppermute | solution.py:25
  91.2 15.5 %all-to-all-start.2 = ((f32[16,1,1728]{2,1,0:T(1,128)}), f32[16,1,1728]{2,1,0:T(1,128)}, u32[]{:S(2)}, u32[]{:S(2)}) async-start(f32[16,1,1728]{2,1,0:T(1,128)} %reshape.101), calls=%async_computation.2 | async-start | bytes 229376 | tf_op jit(solution)/shard_map/all_to_all | solution.py:57
  98.7 26.8 %collective-permute-start.6 = (f32[2,34,1]{2,1,0:T(8,128)}, f32[2,34,1]{2,1,0:T(8,128)}, u32[]{:S(2)}, u32[]{:S(2)}) collective-permute-start(f32[2,34,1]{2,1,0:T(8,128)} %get-tuple-element.35), channel_id=1, source_target_pairs={{0,1},{1,2},{2,3},{3,4},{4,5},{5,6},{6,7},{7,8},{8,9},{9,10},{10,1... | collective-permute-start | bytes 824 | tf_op jit(solution)/shard_map/ppermute | solution.py:23
  102.3 23.3 %collective-permute-start.7 = (f32[2,34,1]{2,1,0:T(8,128)}, f32[2,34,1]{2,1,0:T(8,128)}, u32[]{:S(2)}, u32[]{:S(2)}) collective-permute-start(f32[2,34,1]{2,1,0:T(8,128)} %get-tuple-element.36), channel_id=1, source_target_pairs={{1,0},{2,1},{3,2},{4,3},{5,4},{6,5},{7,6},{8,7},{9,8},{10,9},{11,1... | collective-permute-start | bytes 824 | tf_op jit(solution)/shard_map/ppermute | solution.py:25
  119.4 17.6 %copy-start.7 = (f32[32,32,192]{2,1,0:T(8,128)S(1)}, f32[32,32,192]{2,1,0:T(8,128)}, u32[]{:S(2)}) copy-start(f32[32,32,192]{2,1,0:T(8,128)} %param.6) | copy-start | bytes 2359300
  119.4 17.6 %copy-start.26 = (f32[32,32]{1,0:T(8,128)S(1)}, f32[32,32]{1,0:T(8,128)}, u32[]{:S(2)}) copy-start(f32[32,32]{1,0:T(8,128)} %broadcast_multiply_fusion.1) | copy-start | bytes 12292
  120.9 5.5 %collective-permute-start.9 = (f32[1,32,192]{2,1,0:T(8,128)S(1)}, f32[1,32,192]{2,1,0:T(8,128)S(1)}, u32[]{:S(2)}, u32[]{:S(2)}) collective-permute-start(f32[1,32,192]{2,1,0:T(8,128)S(1)} %get-tuple-element.19), channel_id=1, source_target_pairs={{0,16},{16,32},{32,48},{48,64},{64,80},{80,96},{96,112},{112,128},... | collective-permute-start | bytes 73736 | tf_op jit(solution)/shard_map/ppermute | solution.py:23
  124.3 5.2 %collective-permute-start.8 = (f32[1,32,192]{2,1,0:T(8,128)S(1)}, f32[1,32,192]{2,1,0:T(8,128)S(1)}, u32[]{:S(2)}, u32[]{:S(2)}) collective-permute-start(f32[1,32,192]{2,1,0:T(8,128)S(1)} %get-tuple-element.20), channel_id=1, source_target_pairs={{16,0},{32,16},{48,32},{64,48},{80,64},{96,80},{112,96},{128,112},... | collective-permute-start | bytes 73736 | tf_op jit(solution)/shard_map/ppermute | solution.py:25
  129.5 6.8 %collective-permute-start.10 = (f32[34,1,192]{2,1,0:T(1,128)S(1)}, f32[34,1,192]{2,1,0:T(1,128)S(1)}, u32[]{:S(2)}, u32[]{:S(2)}) collective-permute-start(f32[34,1,192]{2,1,0:T(1,128)S(1)} %get-tuple-element.13), channel_id=1, source_target_pairs={{1,0},{2,1},{3,2},{4,3},{5,4},{6,5},{7,6},{8,7},{9,8},{10,9},{11,1... | collective-permute-start | bytes 78344 | tf_op jit(solution)/shard_map/ppermute | solution.py:25
  131.8 5.2 %collective-permute-start.11 = (f32[34,1,192]{2,1,0:T(1,128)S(1)}, f32[34,1,192]{2,1,0:T(1,128)S(1)}, u32[]{:S(2)}, u32[]{:S(2)}) collective-permute-start(f32[34,1,192]{2,1,0:T(1,128)S(1)} %get-tuple-element.14), channel_id=1, source_target_pairs={{0,1},{1,2},{2,3},{3,4},{4,5},{5,6},{6,7},{7,8},{8,9},{9,10},{10,1... | collective-permute-start | bytes 78344 | tf_op jit(solution)/shard_map/ppermute | solution.py:23
  144.1 20.6 %all-to-all-start.3 = ((f32[32,1,1728]{2,1,0:T(1,128)}), f32[32,1,1728]{2,1,0:T(1,128)}, u32[]{:S(2)}, u32[]{:S(2)}) async-start(f32[32,1,1728]{2,1,0:T(1,128)} %reshape.103), calls=%async_computation.3 | async-start | bytes 458752 | tf_op jit(solution)/shard_map/all_to_all | solution.py:53
  155.3 35.0 %collective-permute-start.12 = (bf16[4,32,192]{2,1,0:T(8,128)(2,1)}, bf16[4,32,192]{2,1,0:T(8,128)(2,1)}, u32[]{:S(2)}, u32[]{:S(2)}) collective-permute-start(bf16[4,32,192]{2,1,0:T(8,128)(2,1)} %get-tuple-element.31), channel_id=1, source_target_pairs={{0,16},{16,32},{32,48},{48,64},{64,80},{80,96},{96,112},{112,128},... | collective-permute-start | bytes 147464 | tf_op jit(solution)/shard_map/ppermute | solution.py:23
  159.0 31.3 %collective-permute-start.13 = (bf16[4,32,192]{2,1,0:T(8,128)(2,1)}, bf16[4,32,192]{2,1,0:T(8,128)(2,1)}, u32[]{:S(2)}, u32[]{:S(2)}) collective-permute-start(bf16[4,32,192]{2,1,0:T(8,128)(2,1)} %get-tuple-element.32), channel_id=1, source_target_pairs={{16,0},{32,16},{48,32},{64,48},{80,64},{96,80},{112,96},{128,112},... | collective-permute-start | bytes 147464 | tf_op jit(solution)/shard_map/ppermute | solution.py:25
  178.9 24.2 %all-to-all-start.4 = ((f32[16,1,1728]{2,1,0:T(1,128)}), f32[16,1,1728]{2,1,0:T(1,128)}, u32[]{:S(2)}, u32[]{:S(2)}) async-start(f32[16,1,1728]{2,1,0:T(1,128)} %reshape.105), calls=%async_computation.4 | async-start | bytes 229376 | tf_op jit(solution)/shard_map/all_to_all | solution.py:57
  191.4 5.5 %collective-permute-start.14 = (bf16[40,4,192]{2,1,0:T(4,128)(2,1)S(1)}, bf16[40,4,192]{2,1,0:T(4,128)(2,1)S(1)}, u32[]{:S(2)}, u32[]{:S(2)}) collective-permute-start(bf16[40,4,192]{2,1,0:T(4,128)(2,1)S(1)} %get-tuple-element.25), channel_id=1, source_target_pairs={{0,1},{1,2},{2,3},{3,4},{4,5},{5,6},{6,7},{7,8},{8,9},{9,10},{10,1... | collective-permute-start | bytes 184328 | tf_op jit(solution)/shard_map/ppermute | solution.py:23
  194.9 5.8 %collective-permute-start.15 = (bf16[40,4,192]{2,1,0:T(4,128)(2,1)S(1)}, bf16[40,4,192]{2,1,0:T(4,128)(2,1)S(1)}, u32[]{:S(2)}, u32[]{:S(2)}) collective-permute-start(bf16[40,4,192]{2,1,0:T(4,128)(2,1)S(1)} %get-tuple-element.26), channel_id=1, source_target_pairs={{1,0},{2,1},{3,2},{4,3},{5,4},{6,5},{7,6},{8,7},{9,8},{10,9},{11,1... | collective-permute-start | bytes 184328 | tf_op jit(solution)/shard_map/ppermute | solution.py:25
  217.6 3.7 %collective-permute-start.17 = (f32[1,32,192]{2,1,0:T(8,128)S(1)}, f32[1,32,192]{2,1,0:T(8,128)S(1)}, u32[]{:S(2)}, u32[]{:S(2)}) collective-permute-start(f32[1,32,192]{2,1,0:T(8,128)S(1)} %get-tuple-element.17), channel_id=1, source_target_pairs={{0,16},{16,32},{32,48},{48,64},{64,80},{80,96},{96,112},{112,128},... | collective-permute-start | bytes 73736 | tf_op jit(solution)/shard_map/ppermute | solution.py:23
  220.0 4.7 %collective-permute-start.16 = (f32[1,32,192]{2,1,0:T(8,128)S(1)}, f32[1,32,192]{2,1,0:T(8,128)S(1)}, u32[]{:S(2)}, u32[]{:S(2)}) collective-permute-start(f32[1,32,192]{2,1,0:T(8,128)S(1)} %get-tuple-element.18), channel_id=1, source_target_pairs={{16,0},{32,16},{48,32},{64,48},{80,64},{96,80},{112,96},{128,112},... | collective-permute-start | bytes 73736 | tf_op jit(solution)/shard_map/ppermute | solution.py:25
  224.7 5.6 %collective-permute-start.18 = (f32[34,1,192]{2,1,0:T(1,128)S(1)}, f32[34,1,192]{2,1,0:T(1,128)S(1)}, u32[]{:S(2)}, u32[]{:S(2)}) collective-permute-start(f32[34,1,192]{2,1,0:T(1,128)S(1)} %get-tuple-element.11), channel_id=1, source_target_pairs={{1,0},{2,1},{3,2},{4,3},{5,4},{6,5},{7,6},{8,7},{9,8},{10,9},{11,1... | collective-permute-start | bytes 78344 | tf_op jit(solution)/shard_map/ppermute | solution.py:25
  226.7 4.7 %collective-permute-start.19 = (f32[34,1,192]{2,1,0:T(1,128)S(1)}, f32[34,1,192]{2,1,0:T(1,128)S(1)}, u32[]{:S(2)}, u32[]{:S(2)}) collective-permute-start(f32[34,1,192]{2,1,0:T(1,128)S(1)} %get-tuple-element.12), channel_id=1, source_target_pairs={{0,1},{1,2},{2,3},{3,4},{4,5},{5,6},{6,7},{7,8},{8,9},{9,10},{10,1... | collective-permute-start | bytes 78344 | tf_op jit(solution)/shard_map/ppermute | solution.py:23
  238.4 18.6 %all-to-all-start.5 = ((f32[32,1,1728]{2,1,0:T(1,128)}), f32[32,1,1728]{2,1,0:T(1,128)}, u32[]{:S(2)}, u32[]{:S(2)}) async-start(f32[32,1,1728]{2,1,0:T(1,128)} %reshape.107), calls=%async_computation.5 | async-start | bytes 458752 | tf_op jit(solution)/shard_map/all_to_all | solution.py:53
  247.5 31.0 %collective-permute-start.20 = (bf16[4,32,192]{2,1,0:T(8,128)(2,1)}, bf16[4,32,192]{2,1,0:T(8,128)(2,1)}, u32[]{:S(2)}, u32[]{:S(2)}) collective-permute-start(bf16[4,32,192]{2,1,0:T(8,128)(2,1)} %get-tuple-element.29), channel_id=1, source_target_pairs={{0,16},{16,32},{32,48},{48,64},{64,80},{80,96},{96,112},{112,128},... | collective-permute-start | bytes 147464 | tf_op jit(solution)/shard_map/ppermute | solution.py:23
  251.2 27.3 %collective-permute-start.21 = (bf16[4,32,192]{2,1,0:T(8,128)(2,1)}, bf16[4,32,192]{2,1,0:T(8,128)(2,1)}, u32[]{:S(2)}, u32[]{:S(2)}) collective-permute-start(bf16[4,32,192]{2,1,0:T(8,128)(2,1)} %get-tuple-element.30), channel_id=1, source_target_pairs={{16,0},{32,16},{48,32},{64,48},{80,64},{96,80},{112,96},{128,112},... | collective-permute-start | bytes 147464 | tf_op jit(solution)/shard_map/ppermute | solution.py:25
  266.8 24.6 %all-to-all-start.6 = ((f32[16,1,1728]{2,1,0:T(1,128)}), f32[16,1,1728]{2,1,0:T(1,128)S(1)}, u32[]{:S(2)}, u32[]{:S(2)}) async-start(f32[16,1,1728]{2,1,0:T(1,128)} %reshape.109), calls=%async_computation.6 | async-start | bytes 229376 | tf_op jit(solution)/shard_map/all_to_all | solution.py:57
  279.6 5.5 %collective-permute-start.22 = (bf16[40,4,192]{2,1,0:T(4,128)(2,1)S(1)}, bf16[40,4,192]{2,1,0:T(4,128)(2,1)S(1)}, u32[]{:S(2)}, u32[]{:S(2)}) collective-permute-start(bf16[40,4,192]{2,1,0:T(4,128)(2,1)S(1)} %get-tuple-element.23), channel_id=1, source_target_pairs={{0,1},{1,2},{2,3},{3,4},{4,5},{5,6},{6,7},{7,8},{8,9},{9,10},{10,1... | collective-permute-start | bytes 184328 | tf_op jit(solution)/shard_map/ppermute | solution.py:23
  283.2 5.8 %collective-permute-start.23 = (bf16[40,4,192]{2,1,0:T(4,128)(2,1)S(1)}, bf16[40,4,192]{2,1,0:T(4,128)(2,1)S(1)}, u32[]{:S(2)}, u32[]{:S(2)}) collective-permute-start(bf16[40,4,192]{2,1,0:T(4,128)(2,1)S(1)} %get-tuple-element.24), channel_id=1, source_target_pairs={{1,0},{2,1},{3,2},{4,3},{5,4},{6,5},{7,6},{8,7},{9,8},{10,9},{11,1... | collective-permute-start | bytes 184328 | tf_op jit(solution)/shard_map/ppermute | solution.py:25
  301.5 18.2 %copy-start.14 = (f32[32,32]{1,0:T(8,128)S(1)}, f32[32,32]{1,0:T(8,128)}, u32[]{:S(2)}) copy-start(f32[32,32]{1,0:T(8,128)} %copy-done.12) | copy-start | bytes 12292
  301.5 18.2 %copy-start.17 = (f32[32,32]{1,0:T(8,128)S(1)}, f32[32,32]{1,0:T(8,128)}, u32[]{:S(2)}) copy-start(f32[32,32]{1,0:T(8,128)} %copy-done.15) | copy-start | bytes 12292
  301.5 18.2 %copy-start.20 = (f32[32,32]{1,0:T(8,128)S(1)}, f32[32,32]{1,0:T(8,128)}, u32[]{:S(2)}) copy-start(f32[32,32]{1,0:T(8,128)} %copy-done.18) | copy-start | bytes 12292
  301.5 18.2 %copy-start.23 = (f32[32,32]{1,0:T(8,128)S(1)}, f32[32,32]{1,0:T(8,128)}, u32[]{:S(2)}) copy-start(f32[32,32]{1,0:T(8,128)} %copy-done.21) | copy-start | bytes 12292
  304.8 4.9 %collective-permute-start.25 = (f32[1,32,192]{2,1,0:T(8,128)S(1)}, f32[1,32,192]{2,1,0:T(8,128)S(1)}, u32[]{:S(2)}, u32[]{:S(2)}) collective-permute-start(f32[1,32,192]{2,1,0:T(8,128)S(1)} %get-tuple-element.15), channel_id=1, source_target_pairs={{0,16},{16,32},{32,48},{48,64},{64,80},{80,96},{96,112},{112,128},... | collective-permute-start | bytes 73736 | tf_op jit(solution)/shard_map/ppermute | solution.py:23
  308.4 48.8 %slice-start = ((f32[9,192]{1,0:T(8,128)}), f32[1,192]{1,0:T(1,128)S(1)}, s32[]{:S(2)}) async-start(f32[9,192]{1,0:T(8,128)} %reduce_sum.113), calls=%async_computation.9 | async-start | bytes 2048 | tf_op jit(solution)/shard_map/slice | solution.py:109
  308.4 48.8 %slice-start.1 = ((f32[9,192]{1,0:T(8,128)}), f32[1,192]{1,0:T(1,128)S(1)}, s32[]{:S(2)}) async-start(f32[9,192]{1,0:T(8,128)} %reduce_sum.116), calls=%async_computation.10 | async-start | bytes 2048 | tf_op jit(solution)/shard_map/slice | solution.py:109
  308.4 4.7 %collective-permute-start.24 = (f32[1,32,192]{2,1,0:T(8,128)S(1)}, f32[1,32,192]{2,1,0:T(8,128)S(1)}, u32[]{:S(2)}, u32[]{:S(2)}) collective-permute-start(f32[1,32,192]{2,1,0:T(8,128)S(1)} %get-tuple-element.16), channel_id=1, source_target_pairs={{16,0},{32,16},{48,32},{64,48},{80,64},{96,80},{112,96},{128,112},... | collective-permute-start | bytes 73736 | tf_op jit(solution)/shard_map/ppermute | solution.py:25
  313.1 5.6 %collective-permute-start.26 = (f32[34,1,192]{2,1,0:T(1,128)S(1)}, f32[34,1,192]{2,1,0:T(1,128)S(1)}, u32[]{:S(2)}, u32[]{:S(2)}) collective-permute-start(f32[34,1,192]{2,1,0:T(1,128)S(1)} %get-tuple-element.9), channel_id=1, source_target_pairs={{1,0},{2,1},{3,2},{4,3},{5,4},{6,5},{7,6},{8,7},{9,8},{10,9},{11,1... | collective-permute-start | bytes 78344 | tf_op jit(solution)/shard_map/ppermute | solution.py:25
  315.0 4.7 %collective-permute-start.27 = (f32[34,1,192]{2,1,0:T(1,128)S(1)}, f32[34,1,192]{2,1,0:T(1,128)S(1)}, u32[]{:S(2)}, u32[]{:S(2)}) collective-permute-start(f32[34,1,192]{2,1,0:T(1,128)S(1)} %get-tuple-element.10), channel_id=1, source_target_pairs={{0,1},{1,2},{2,3},{3,4},{4,5},{5,6},{6,7},{7,8},{8,9},{9,10},{10,1... | collective-permute-start | bytes 78344 | tf_op jit(solution)/shard_map/ppermute | solution.py:23
  341.0 16.1 %all-to-all-start.8 = ((f32[32,1,192]{2,1,0:T(1,128)}), f32[32,1,192]{2,1,0:T(1,128)S(1)}, u32[]{:S(2)}, u32[]{:S(2)}) async-start(f32[32,1,192]{2,1,0:T(1,128)} %broadcast_in_dim.32), calls=%async_computation.8 | async-start | bytes 65536 | tf_op jit(solution)/shard_map/all_to_all | solution.py:53
  (17 other events, 162.8 us)

commit v4 on v3

--- a/solution.py
+++ b/solution.py
@@ -29,6 +29,24 @@
     return cells
 
 
+def with_edges(cells):
+    rows_x = lax.axis_size("gx")
+    cols_y = lax.axis_size("gy")
+    down = [(i, i + 1) for i in range(rows_x - 1)]
+    up = [(i + 1, i) for i in range(rows_x - 1)]
+    right = [(i, i + 1) for i in range(cols_y - 1)]
+    left = [(i + 1, i) for i in range(cols_y - 1)]
+    north = lax.ppermute(cells[-1:], "gx", down)
+    south = lax.ppermute(cells[:1], "gx", up)
+    west = lax.ppermute(cells[:, -1:], "gy", right)
+    east = lax.ppermute(cells[:, :1], "gy", left)
+    rows = jnp.concatenate([north, cells, south], axis=0)
+    corner = [(1, 1), (0, 0)] + [(0, 0)] * (cells.ndim - 2)
+    return jnp.concatenate(
+        [jnp.pad(west, corner), rows, jnp.pad(east, corner)], axis=1
+    )
+
+
 def neighbour(padded, offset_row, offset_col):
     inner_rows = padded.shape[0] - 2
     inner_cols = padded.shape[1] - 2
@@ -58,9 +76,7 @@
 
 
 def total_over_mesh(values):
-    for axis in ("gy", "gx"):
-        values = jnp.sum(gathered_by_exchange(values, axis), axis=0)
-    return values
+    return jnp.sum(gathered_by_exchange(values, ("gx", "gy")), axis=0)
 
 
 def on_device(sources, permeability, storage, basis, local_inverse, coarse_inverse):
@@ -74,9 +90,7 @@
     cells = float(patch * patch * rows_x * cols_y)
     flat_basis = basis.reshape(modes, patch * patch)
     inverse_rows = local_inverse[0, 0]
-    stacked = jnp.stack([permeability, storage])
-    padded = extended(stacked, (("gx", 1), ("gy", 2)), 1)
-    kappa_pad = padded[0]
+    kappa_pad = with_edges(permeability)
     state = sources
 
     pieces = coarse_inverse.reshape(modes, rows_x, cols_y, modes).transpose(2, 0, 1, 3)
@@ -122,7 +136,7 @@
     update = corrected / centre
     for index in range(ITERS):
         solution = solution + update
-        step_pad = extended(update, (("gx", 0), ("gy", 1)), 1)
+        step_pad = with_edges(update)
         state = state - operate(step_pad, kappa_pad, storage)
         if index + 1 < ITERS:
             corrected, squares = precondition(state)

time: 361 us -> 355 us (0.983)
  blocking collectives: 18.7 us -> 0 us
  starting transfers between devices: 152 us -> 160 us
  waiting for transfers between devices: 40 us -> 46.7 us
    ppermute x0 -> x16, starting transfers between devices: none -> 42 us  [the longest x4 14.5 us: with_edges(): west = lax.ppermute(cells[:, -1:], 'gy', right)]
    ppermute x14 -> x6, starting transfers between devices: 51.2 us -> 21.1 us  [extended(): lax.ppermute(tail, axis, [(i, (i + 1) % count) for i in range(ends)])]
    all_to_all x1 -> x0, blocking collectives: 18.7 us -> none  [gathered_by_exchange(): return lax.all_to_all(copies, axis, 0, 0, tiled=True)]
    ppermute x14 -> x6, starting transfers between devices: 23.5 us -> 9.61 us  [extended(): lax.ppermute(head, axis, [((i + 1) % count, i) for i in range(ends)])]
    all_to_all x4, starting transfers between devices: 39 us -> 51.1 us  [gathered_by_exchange(): return lax.all_to_all(copies, axis, 0, 0, tiled=True)]
    ppermute x0 -> x16, waiting for transfers between devices: none -> 9.28 us  [the longest x4 9.25 us: with_edges(): south = lax.ppermute(cells[:1], 'gx', up)]
    ppermute x14 -> x6, waiting for transfers between devices: 17.4 us -> 8.45 us  [extended(): lax.ppermute(head, axis, [((i + 1) % count, i) for i in range(ends)])]
    all_to_all x4, waiting for transfers between devices: 16.6 us -> 24.8 us  [gathered_by_exchange(): return lax.all_to_all(copies, axis, 0, 0, tiled=True)]
  transfers between devices with their start and end apart: 36 -> 36, of which waited for: 12 -> 11; matrix products, arithmetic and copies ran while one was open for 27% -> 27% of each run, Pallas kernels for 0% -> 0%
where the time goes in v4:
time: 355 us; the launch traced here: 352 us
  starting transfers between devices  160 us (45%)
  local copies, waits for them, and re-layouts  61.6 us (17%)
  other arithmetic  60.4 us (17%)
  waiting for transfers between devices  46.7 us (13%)
  matrix products  21.6 us (6%)
    all_to_all x4, starting transfers between devices, gathered_by_exchange(): return lax.all_to_all(copies, axis, 0, 0, tiled=True)  51.1 us
    all_to_all x3, starting transfers between devices, summed_by_exchange(): return jnp.sum(lax.all_to_all(blocks, axis, 0, 0, tiled=True), axis=0)  28 us
    unnamed x72, local copies, waits for them, and re-layouts  25.1 us
    all_to_all x4, waiting for transfers between devices, gathered_by_exchange(): return lax.all_to_all(copies, axis, 0, 0, tiled=True)  24.8 us
    ppermute x6, starting transfers between devices, extended(): lax.ppermute(tail, axis, [(i, (i + 1) % count) for i in range(ends)])  21.1 us
    ppermute x4, starting transfers between devices, with_edges(): west = lax.ppermute(cells[:, -1:], 'gy', right)  14.5 us
    ppermute x4, starting transfers between devices, with_edges(): north = lax.ppermute(cells[-1:], 'gx', down)  13.9 us
    ppermute x6, starting transfers between devices, extended(): lax.ppermute(head, axis, [((i + 1) % count, i) for i in range(ends)])  9.61 us
  transfers between devices with their start and end apart: 36, of which 11 were waited for; matrix products, arithmetic and copies ran while one was open for 27% of the time, Pallas kernels for 0%

profile of v4, /device:TPU:1, one launch (start us, length us, event | category | flops | bytes accessed | tf_op | source)
XLA Modules:
  0.0 351.6 jit_solution(16209095621401921157)
XLA Ops:
  2.1 5.4 %collective-permute-start.6 = (f32[1,32]{1,0:T(1,128)}, f32[1,32]{1,0:T(1,128)}, u32[]{:S(2)}, u32[]{:S(2)}) collective-permute-start(f32[1,32]{1,0:T(1,128)} %get-tuple-element.41), channel_id=1, source_target_pairs={{0,16},{16,32},{32,48},{48,64},{64,80},{80,96},{96,112},{112,128},... | collective-permute-start | bytes 392 | tf_op jit(solution)/shard_map/ppermute | solution.py:39
  8.8 3.4 reshape.78
  12.2 3.3 copy.64
  17.5 8.1 %all-to-all-start.1 = ((f32[16,1,2048]{2,1,0:T(1,128)}), f32[16,1,2048]{2,1,0:T(1,128)S(1)}, u32[]{:S(2)}, u32[]{:S(2)}) async-start(f32[16,1,2048]{2,1,0:T(1,128)} %reshape.93), calls=%async_computation.1 | async-start | bytes 262144 | tf_op jit(solution)/shard_map/all_to_all | solution.py:97
  25.6 2.6 fusion.108
  31.8 2.6 all-to-all-done.1
  34.4 13.9 %all-to-all-start = ((f32[32,1,1728]{2,1,0:T(1,128)}), f32[32,1,1728]{2,1,0:T(1,128)}, u32[]{:S(2)}, u32[]{:S(2)}) async-start(f32[32,1,1728]{2,1,0:T(1,128)} %reshape.91), calls=%async_computation | async-start | bytes 458752 | tf_op jit(solution)/shard_map/all_to_all | solution.py:71
  49.2 3.1 collective-permute-start
  54.3 2.6 collective-permute-start.8
  59.5 3.6 %collective-permute-start.2 = (bf16[40,4,192]{2,1,0:T(4,128)(2,1)}, bf16[40,4,192]{2,1,0:T(4,128)(2,1)}, u32[]{:S(2)}, u32[]{:S(2)}) collective-permute-start(bf16[40,4,192]{2,1,0:T(4,128)(2,1)} %get-tuple-element.27), channel_id=1, source_target_pairs={{0,1},{1,2},{2,3},{3,4},{4,5},{5,6},{6,7},{7,8},{8,9},{9,10},{10,1... | collective-permute-start | bytes 184328 | tf_op jit(solution)/shard_map/ppermute | solution.py:23
  68.4 3.0 copy.65
  71.4 2.8 reshape.79
  74.2 2.8 reduce.8
  88.3 7.4 %all-to-all-start.2 = ((f32[16,1,1728]{2,1,0:T(1,128)}), f32[16,1,1728]{2,1,0:T(1,128)}, u32[]{:S(2)}, u32[]{:S(2)}) async-start(f32[16,1,1728]{2,1,0:T(1,128)} %reshape.95), calls=%async_computation.2 | async-start | bytes 229376 | tf_op jit(solution)/shard_map/all_to_all | solution.py:75
  97.1 3.5 %collective-permute-start.10 = (f32[32,1]{1,0:T(8,128)}, f32[32,1]{1,0:T(8,128)}, u32[]{:S(2)}, u32[]{:S(2)}) collective-permute-start(f32[32,1]{1,0:T(8,128)} %get-tuple-element.40), channel_id=1, source_target_pairs={{0,1},{1,2},{2,3},{3,4},{4,5},{5,6},{6,7},{7,8},{8,9},{9,10},{10,1... | collective-permute-start | bytes 392 | tf_op jit(solution)/shard_map/ppermute | solution.py:41
  100.6 2.4 pad_maximum_fusion.18
  104.7 2.5 reduce.10
  111.4 3.0 fusion.9
  120.3 3.6 %collective-permute-start.11 = (f32[32,1,192]{2,1,0:T(1,128)S(1)}, f32[32,1,192]{2,1,0:T(1,128)S(1)}, u32[]{:S(2)}, u32[]{:S(2)}) collective-permute-start(f32[32,1,192]{2,1,0:T(1,128)S(1)} %get-tuple-element.18), channel_id=1, source_target_pairs={{0,1},{1,2},{2,3},{3,4},{4,5},{5,6},{6,7},{7,8},{8,9},{9,10},{10,1... | collective-permute-start | bytes 73736 | tf_op jit(solution)/shard_map/ppermute | solution.py:41
  124.0 3.1 collective-permute-start.7
  129.5 2.6 collective-permute-done.5
  139.1 10.0 %all-to-all-start.3 = ((f32[32,1,1728]{2,1,0:T(1,128)}), f32[32,1,1728]{2,1,0:T(1,128)}, u32[]{:S(2)}, u32[]{:S(2)}) async-start(f32[32,1,1728]{2,1,0:T(1,128)} %reshape.97), calls=%async_computation.3 | async-start | bytes 458752 | tf_op jit(solution)/shard_map/all_to_all | solution.py:71
  150.7 3.7 %collective-permute-start.12 = (bf16[4,32,192]{2,1,0:T(8,128)(2,1)}, bf16[4,32,192]{2,1,0:T(8,128)(2,1)}, u32[]{:S(2)}, u32[]{:S(2)}) collective-permute-start(bf16[4,32,192]{2,1,0:T(8,128)(2,1)} %get-tuple-element.31), channel_id=1, source_target_pairs={{0,16},{16,32},{32,48},{48,64},{64,80},{80,96},{96,112},{112,128},... | collective-permute-start | bytes 147464 | tf_op jit(solution)/shard_map/ppermute | solution.py:23
  155.6 3.0 all-to-all-done.3
  158.6 2.8 reduce.11
  172.7 9.3 %all-to-all-start.4 = ((f32[16,1,1728]{2,1,0:T(1,128)}), f32[16,1,1728]{2,1,0:T(1,128)}, u32[]{:S(2)}, u32[]{:S(2)}) async-start(f32[16,1,1728]{2,1,0:T(1,128)} %reshape.99), calls=%async_computation.4 | async-start | bytes 229376 | tf_op jit(solution)/shard_map/all_to_all | solution.py:75
  183.2 3.5 %collective-permute-start.14 = (bf16[40,4,192]{2,1,0:T(4,128)(2,1)S(1)}, bf16[40,4,192]{2,1,0:T(4,128)(2,1)S(1)}, u32[]{:S(2)}, u32[]{:S(2)}) collective-permute-start(bf16[40,4,192]{2,1,0:T(4,128)(2,1)S(1)} %get-tuple-element.25), channel_id=1, source_target_pairs={{0,1},{1,2},{2,3},{3,4},{4,5},{5,6},{6,7},{7,8},{8,9},{9,10},{10,1... | collective-permute-start | bytes 184328 | tf_op jit(solution)/shard_map/ppermute | solution.py:23
  188.6 3.8 %collective-permute-done.15 = bf16[40,4,192]{2,1,0:T(4,128)(2,1)S(1)} collective-permute-done((bf16[40,4,192]{2,1,0:T(4,128)(2,1)S(1)}, bf16[40,4,192]{2,1,0:T(4,128)(2,1)S(1)}, u32[]{:S(2)}, u32[]{:S(2)}) %collective-permute-start.15) | collective-permute-done | bytes 61472 | tf_op jit(solution)/shard_map/ppermute | solution.py:25
  194.8 2.5 reduce.12
  202.2 2.9 fusion.18
  205.1 2.4 copy.72
  211.4 3.6 %collective-permute-start.19 = (f32[32,1,192]{2,1,0:T(1,128)S(1)}, f32[32,1,192]{2,1,0:T(1,128)S(1)}, u32[]{:S(2)}, u32[]{:S(2)}) collective-permute-start(f32[32,1,192]{2,1,0:T(1,128)S(1)} %get-tuple-element.14), channel_id=1, source_target_pairs={{0,1},{1,2},{2,3},{3,4},{4,5},{5,6},{6,7},{7,8},{8,9},{9,10},{10,1... | collective-permute-start | bytes 73736 | tf_op jit(solution)/shard_map/ppermute | solution.py:41
  218.7 3.3 collective-permute-done.16
  229.0 7.7 %all-to-all-start.5 = ((f32[32,1,1728]{2,1,0:T(1,128)}), f32[32,1,1728]{2,1,0:T(1,128)}, u32[]{:S(2)}, u32[]{:S(2)}) async-start(f32[32,1,1728]{2,1,0:T(1,128)} %reshape.101), calls=%async_computation.5 | async-start | bytes 458752 | tf_op jit(solution)/shard_map/all_to_all | solution.py:71
  238.2 3.7 %collective-permute-start.20 = (bf16[4,32,192]{2,1,0:T(8,128)(2,1)}, bf16[4,32,192]{2,1,0:T(8,128)(2,1)}, u32[]{:S(2)}, u32[]{:S(2)}) collective-permute-start(bf16[4,32,192]{2,1,0:T(8,128)(2,1)} %get-tuple-element.29), channel_id=1, source_target_pairs={{0,16},{16,32},{32,48},{48,64},{64,80},{80,96},{96,112},{112,128},... | collective-permute-start | bytes 147464 | tf_op jit(solution)/shard_map/ppermute | solution.py:23
  243.2 3.0 all-to-all-done.5
  246.2 2.8 reduce.13
  255.9 11.3 %all-to-all-start.6 = ((f32[16,1,1728]{2,1,0:T(1,128)}), f32[16,1,1728]{2,1,0:T(1,128)S(1)}, u32[]{:S(2)}, u32[]{:S(2)}) async-start(f32[16,1,1728]{2,1,0:T(1,128)} %reshape.103), calls=%async_computation.6 | async-start | bytes 229376 | tf_op jit(solution)/shard_map/all_to_all | solution.py:75
  268.3 3.5 %collective-permute-start.22 = (bf16[40,4,192]{2,1,0:T(4,128)(2,1)S(1)}, bf16[40,4,192]{2,1,0:T(4,128)(2,1)S(1)}, u32[]{:S(2)}, u32[]{:S(2)}) collective-permute-start(bf16[40,4,192]{2,1,0:T(4,128)(2,1)S(1)} %get-tuple-element.23), channel_id=1, source_target_pairs={{0,1},{1,2},{2,3},{3,4},{4,5},{5,6},{6,7},{7,8},{8,9},{9,10},{10,1... | collective-permute-start | bytes 184328 | tf_op jit(solution)/shard_map/ppermute | solution.py:23
  273.8 3.8 %collective-permute-done.23 = bf16[40,4,192]{2,1,0:T(4,128)(2,1)S(1)} collective-permute-done((bf16[40,4,192]{2,1,0:T(4,128)(2,1)S(1)}, bf16[40,4,192]{2,1,0:T(4,128)(2,1)S(1)}, u32[]{:S(2)}, u32[]{:S(2)}) %collective-permute-start.23) | collective-permute-done | bytes 61472 | tf_op jit(solution)/shard_map/ppermute | solution.py:25
  284.8 2.9 fusion.27
  287.7 2.5 copy.76
  290.2 3.3 multiply_add_fusion
  295.5 3.6 %collective-permute-start.27 = (f32[32,1,192]{2,1,0:T(1,128)S(1)}, f32[32,1,192]{2,1,0:T(1,128)S(1)}, u32[]{:S(2)}, u32[]{:S(2)}) collective-permute-start(f32[32,1,192]{2,1,0:T(1,128)S(1)} %get-tuple-element.10), channel_id=1, source_target_pairs={{0,1},{1,2},{2,3},{3,4},{4,5},{5,6},{6,7},{7,8},{8,9},{9,10},{10,1... | collective-permute-start | bytes 73736 | tf_op jit(solution)/shard_map/ppermute | solution.py:41
  299.2 3.1 collective-permute-start.25
  303.6 3.3 collective-permute-done.24
  309.8 19.5 %all-to-all-start.7 = ((f32[512,1,192]{2,1,0:T(1,128)}), f32[512,1,192]{2,1,0:T(1,128)}, u32[]{:S(2)}, u32[]{:S(2)}) async-start(f32[512,1,192]{2,1,0:T(1,128)} %broadcast_in_dim.29), calls=%async_computation.7 | async-start | bytes 1048576 | tf_op jit(solution)/shard_map/all_to_all | solution.py:71
  330.6 18.7 %all-to-all-done.7 = f32[512,1,192]{2,1,0:T(1,128)} async-done(((f32[512,1,192]{2,1,0:T(1,128)}), f32[512,1,192]{2,1,0:T(1,128)}, u32[]{:S(2)}, u32[]{:S(2)}) %all-to-all-start.7) | async-done | bytes 393248 | tf_op jit(solution)/shard_map/all_to_all | solution.py:71
  (181 shorter events, 120.9 us)
Async XLA Ops:
  0.6 110.8 %copy-start = (bf16[1,1,1024,1600]{2,3,1,0:T(8,128)(2,1)S(1)}, bf16[1,1,1024,1600]{2,3,1,0:T(8,128)(2,1)}, u32[]{:S(2)}) copy-start(bf16[1,1,1024,1600]{2,3,1,0:T(8,128)(2,1)} %param.10) | copy-start | bytes 9830404
  2.1 118.2 %collective-permute-start.6 = (f32[1,32]{1,0:T(1,128)}, f32[1,32]{1,0:T(1,128)}, u32[]{:S(2)}, u32[]{:S(2)}) collective-permute-start(f32[1,32]{1,0:T(1,128)} %get-tuple-element.41), channel_id=1, source_target_pairs={{0,16},{16,32},{32,48},{48,64},{64,80},{80,96},{96,112},{112,128},... | collective-permute-start | bytes 392 | tf_op jit(solution)/shard_map/ppermute | solution.py:39
  7.5 116.5 %collective-permute-start.4 = (f32[1,32]{1,0:T(1,128)}, f32[1,32]{1,0:T(1,128)}, u32[]{:S(2)}, u32[]{:S(2)}) collective-permute-start(f32[1,32]{1,0:T(1,128)} %get-tuple-element.42), channel_id=1, source_target_pairs={{16,0},{32,16},{48,32},{64,48},{80,64},{96,80},{112,96},{128,112},... | collective-permute-start | bytes 392 | tf_op jit(solution)/shard_map/ppermute | solution.py:40
  17.5 17.0 %all-to-all-start.1 = ((f32[16,1,2048]{2,1,0:T(1,128)}), f32[16,1,2048]{2,1,0:T(1,128)S(1)}, u32[]{:S(2)}, u32[]{:S(2)}) async-start(f32[16,1,2048]{2,1,0:T(1,128)} %reshape.93), calls=%async_computation.1 | async-start | bytes 262144 | tf_op jit(solution)/shard_map/all_to_all | solution.py:97
  28.1 25.5 %copy-start.22 = (f32[32,32]{1,0:T(8,128)S(1)}, f32[32,32]{1,0:T(8,128)}, u32[]{:S(2)}) copy-start(f32[32,32]{1,0:T(8,128)} %param.7) | copy-start | bytes 12292
  34.4 30.6 %copy-start.10 = (f32[16,1,2048]{2,1,0:T(1,128)}, f32[16,1,2048]{2,1,0:T(1,128)S(1)}, u32[]{:S(2)}) copy-start(f32[16,1,2048]{2,1,0:T(1,128)S(1)} %all-to-all-done.1) | copy-start | bytes 393220
  34.4 39.8 %all-to-all-start = ((f32[32,1,1728]{2,1,0:T(1,128)}), f32[32,1,1728]{2,1,0:T(1,128)}, u32[]{:S(2)}, u32[]{:S(2)}) async-start(f32[32,1,1728]{2,1,0:T(1,128)} %reshape.91), calls=%async_computation | async-start | bytes 458752 | tf_op jit(solution)/shard_map/all_to_all | solution.py:71
  49.2 7.7 %collective-permute-start = (bf16[4,32,192]{2,1,0:T(8,128)(2,1)S(1)}, bf16[4,32,192]{2,1,0:T(8,128)(2,1)S(1)}, u32[]{:S(2)}, u32[]{:S(2)}) collective-permute-start(bf16[4,32,192]{2,1,0:T(8,128)(2,1)S(1)} %get-tuple-element.33), channel_id=1, source_target_pairs={{0,16},{16,32},{32,48},{48,64},{64,80},{80,96},{96,112},{112,128},... | collective-permute-start | bytes 147464 | tf_op jit(solution)/shard_map/ppermute | solution.py:23
  52.3 5.4 %collective-permute-start.1 = (bf16[4,32,192]{2,1,0:T(8,128)(2,1)S(1)}, bf16[4,32,192]{2,1,0:T(8,128)(2,1)S(1)}, u32[]{:S(2)}, u32[]{:S(2)}) collective-permute-start(bf16[4,32,192]{2,1,0:T(8,128)(2,1)S(1)} %get-tuple-element.34), channel_id=1, source_target_pairs={{16,0},{32,16},{48,32},{64,48},{80,64},{96,80},{112,96},{128,112},... | collective-permute-start | bytes 147464 | tf_op jit(solution)/shard_map/ppermute | solution.py:25
  54.3 72.8 %collective-permute-start.8 = (f32[32,1]{1,0:T(8,128)}, f32[32,1]{1,0:T(8,128)}, u32[]{:S(2)}, u32[]{:S(2)}) collective-permute-start(f32[32,1]{1,0:T(8,128)} %get-tuple-element.39), channel_id=1, source_target_pairs={{1,0},{2,1},{3,2},{4,3},{5,4},{6,5},{7,6},{8,7},{9,8},{10,9},{11,1... | collective-permute-start | bytes 392 | tf_op jit(solution)/shard_map/ppermute | solution.py:42
  59.5 37.6 %collective-permute-start.2 = (bf16[40,4,192]{2,1,0:T(4,128)(2,1)}, bf16[40,4,192]{2,1,0:T(4,128)(2,1)}, u32[]{:S(2)}, u32[]{:S(2)}) collective-permute-start(bf16[40,4,192]{2,1,0:T(4,128)(2,1)} %get-tuple-element.27), channel_id=1, source_target_pairs={{0,1},{1,2},{2,3},{3,4},{4,5},{5,6},{6,7},{7,8},{8,9},{9,10},{10,1... | collective-permute-start | bytes 184328 | tf_op jit(solution)/shard_map/ppermute | solution.py:23
  63.1 37.6 %collective-permute-start.3 = (bf16[40,4,192]{2,1,0:T(4,128)(2,1)}, bf16[40,4,192]{2,1,0:T(4,128)(2,1)}, u32[]{:S(2)}, u32[]{:S(2)}) collective-permute-start(bf16[40,4,192]{2,1,0:T(4,128)(2,1)} %get-tuple-element.28), channel_id=1, source_target_pairs={{1,0},{2,1},{3,2},{4,3},{5,4},{6,5},{7,6},{8,7},{9,8},{10,9},{11,1... | collective-permute-start | bytes 184328 | tf_op jit(solution)/shard_map/ppermute | solution.py:25
  74.2 21.6 %copy-start.24 = (f32[32,32]{1,0:T(8,128)S(1)}, f32[32,32]{1,0:T(8,128)}, u32[]{:S(2)}) copy-start(f32[32,32]{1,0:T(8,128)} %param.8) | copy-start | bytes 12292
  88.3 16.3 %all-to-all-start.2 = ((f32[16,1,1728]{2,1,0:T(1,128)}), f32[16,1,1728]{2,1,0:T(1,128)}, u32[]{:S(2)}, u32[]{:S(2)}) async-start(f32[16,1,1728]{2,1,0:T(1,128)} %reshape.95), calls=%async_computation.2 | async-start | bytes 229376 | tf_op jit(solution)/shard_map/all_to_all | solution.py:75
  97.1 31.5 %collective-permute-start.10 = (f32[32,1]{1,0:T(8,128)}, f32[32,1]{1,0:T(8,128)}, u32[]{:S(2)}, u32[]{:S(2)}) collective-permute-start(f32[32,1]{1,0:T(8,128)} %get-tuple-element.40), channel_id=1, source_target_pairs={{0,1},{1,2},{2,3},{3,4},{4,5},{5,6},{6,7},{7,8},{8,9},{9,10},{10,1... | collective-permute-start | bytes 392 | tf_op jit(solution)/shard_map/ppermute | solution.py:41
  116.8 15.3 %copy-start.27 = (f32[32,32]{1,0:T(8,128)S(1)}, f32[32,32]{1,0:T(8,128)}, u32[]{:S(2)}) copy-start(f32[32,32]{1,0:T(8,128)} %broadcast_multiply_fusion.1) | copy-start | bytes 12292
  118.4 11.1 %collective-permute-start.9 = (f32[32,1,192]{2,1,0:T(1,128)S(1)}, f32[32,1,192]{2,1,0:T(1,128)S(1)}, u32[]{:S(2)}, u32[]{:S(2)}) collective-permute-start(f32[32,1,192]{2,1,0:T(1,128)S(1)} %get-tuple-element.17), channel_id=1, source_target_pairs={{1,0},{2,1},{3,2},{4,3},{5,4},{6,5},{7,6},{8,7},{9,8},{10,9},{11,1... | collective-permute-start | bytes 73736 | tf_op jit(solution)/shard_map/ppermute | solution.py:42
  120.3 9.2 %collective-permute-start.11 = (f32[32,1,192]{2,1,0:T(1,128)S(1)}, f32[32,1,192]{2,1,0:T(1,128)S(1)}, u32[]{:S(2)}, u32[]{:S(2)}) collective-permute-start(f32[32,1,192]{2,1,0:T(1,128)S(1)} %get-tuple-element.18), channel_id=1, source_target_pairs={{0,1},{1,2},{2,3},{3,4},{4,5},{5,6},{6,7},{7,8},{8,9},{9,10},{10,1... | collective-permute-start | bytes 73736 | tf_op jit(solution)/shard_map/ppermute | solution.py:41
  124.0 5.6 %collective-permute-start.7 = (f32[1,32,192]{2,1,0:T(8,128)S(1)}, f32[1,32,192]{2,1,0:T(8,128)S(1)}, u32[]{:S(2)}, u32[]{:S(2)}) collective-permute-start(f32[1,32,192]{2,1,0:T(8,128)S(1)} %get-tuple-element.19), channel_id=1, source_target_pairs={{0,16},{16,32},{32,48},{48,64},{64,80},{80,96},{96,112},{112,128},... | collective-permute-start | bytes 73736 | tf_op jit(solution)/shard_map/ppermute | solution.py:39
  127.1 5.0 %collective-permute-start.5 = (f32[1,32,192]{2,1,0:T(8,128)S(1)}, f32[1,32,192]{2,1,0:T(8,128)S(1)}, u32[]{:S(2)}, u32[]{:S(2)}) collective-permute-start(f32[1,32,192]{2,1,0:T(8,128)S(1)} %get-tuple-element.20), channel_id=1, source_target_pairs={{16,0},{32,16},{48,32},{64,48},{80,64},{96,80},{112,96},{128,112},... | collective-permute-start | bytes 73736 | tf_op jit(solution)/shard_map/ppermute | solution.py:40
  139.1 19.5 %all-to-all-start.3 = ((f32[32,1,1728]{2,1,0:T(1,128)}), f32[32,1,1728]{2,1,0:T(1,128)}, u32[]{:S(2)}, u32[]{:S(2)}) async-start(f32[32,1,1728]{2,1,0:T(1,128)} %reshape.97), calls=%async_computation.3 | async-start | bytes 458752 | tf_op jit(solution)/shard_map/all_to_all | solution.py:71
  150.7 31.4 %collective-permute-start.12 = (bf16[4,32,192]{2,1,0:T(8,128)(2,1)}, bf16[4,32,192]{2,1,0:T(8,128)(2,1)}, u32[]{:S(2)}, u32[]{:S(2)}) collective-permute-start(bf16[4,32,192]{2,1,0:T(8,128)(2,1)} %get-tuple-element.31), channel_id=1, source_target_pairs={{0,16},{16,32},{32,48},{48,64},{64,80},{80,96},{96,112},{112,128},... | collective-permute-start | bytes 147464 | tf_op jit(solution)/shard_map/ppermute | solution.py:23
  154.3 27.7 %collective-permute-start.13 = (bf16[4,32,192]{2,1,0:T(8,128)(2,1)}, bf16[4,32,192]{2,1,0:T(8,128)(2,1)}, u32[]{:S(2)}, u32[]{:S(2)}) collective-permute-start(bf16[4,32,192]{2,1,0:T(8,128)(2,1)} %get-tuple-element.32), channel_id=1, source_target_pairs={{16,0},{32,16},{48,32},{64,48},{80,64},{96,80},{112,96},{128,112},... | collective-permute-start | bytes 147464 | tf_op jit(solution)/shard_map/ppermute | solution.py:25
  172.7 22.1 %all-to-all-start.4 = ((f32[16,1,1728]{2,1,0:T(1,128)}), f32[16,1,1728]{2,1,0:T(1,128)}, u32[]{:S(2)}, u32[]{:S(2)}) async-start(f32[16,1,1728]{2,1,0:T(1,128)} %reshape.99), calls=%async_computation.4 | async-start | bytes 229376 | tf_op jit(solution)/shard_map/all_to_all | solution.py:75
  183.2 5.5 %collective-permute-start.14 = (bf16[40,4,192]{2,1,0:T(4,128)(2,1)S(1)}, bf16[40,4,192]{2,1,0:T(4,128)(2,1)S(1)}, u32[]{:S(2)}, u32[]{:S(2)}) collective-permute-start(bf16[40,4,192]{2,1,0:T(4,128)(2,1)S(1)} %get-tuple-element.25), channel_id=1, source_target_pairs={{0,1},{1,2},{2,3},{3,4},{4,5},{5,6},{6,7},{7,8},{8,9},{9,10},{10,1... | collective-permute-start | bytes 184328 | tf_op jit(solution)/shard_map/ppermute | solution.py:23
  186.7 5.8 %collective-permute-start.15 = (bf16[40,4,192]{2,1,0:T(4,128)(2,1)S(1)}, bf16[40,4,192]{2,1,0:T(4,128)(2,1)S(1)}, u32[]{:S(2)}, u32[]{:S(2)}) collective-permute-start(bf16[40,4,192]{2,1,0:T(4,128)(2,1)S(1)} %get-tuple-element.26), channel_id=1, source_target_pairs={{1,0},{2,1},{3,2},{4,3},{5,4},{6,5},{7,6},{8,7},{9,8},{10,9},{11,1... | collective-permute-start | bytes 184328 | tf_op jit(solution)/shard_map/ppermute | solution.py:25
  209.5 9.2 %collective-permute-start.18 = (f32[32,1,192]{2,1,0:T(1,128)S(1)}, f32[32,1,192]{2,1,0:T(1,128)S(1)}, u32[]{:S(2)}, u32[]{:S(2)}) collective-permute-start(f32[32,1,192]{2,1,0:T(1,128)S(1)} %get-tuple-element.13), channel_id=1, source_target_pairs={{1,0},{2,1},{3,2},{4,3},{5,4},{6,5},{7,6},{8,7},{9,8},{10,9},{11,1... | collective-permute-start | bytes 73736 | tf_op jit(solution)/shard_map/ppermute | solution.py:42
  211.4 7.3 %collective-permute-start.19 = (f32[32,1,192]{2,1,0:T(1,128)S(1)}, f32[32,1,192]{2,1,0:T(1,128)S(1)}, u32[]{:S(2)}, u32[]{:S(2)}) collective-permute-start(f32[32,1,192]{2,1,0:T(1,128)S(1)} %get-tuple-element.14), channel_id=1, source_target_pairs={{0,1},{1,2},{2,3},{3,4},{4,5},{5,6},{6,7},{7,8},{8,9},{9,10},{10,1... | collective-permute-start | bytes 73736 | tf_op jit(solution)/shard_map/ppermute | solution.py:41
  215.0 3.6 %collective-permute-start.17 = (f32[1,32,192]{2,1,0:T(8,128)S(1)}, f32[1,32,192]{2,1,0:T(8,128)S(1)}, u32[]{:S(2)}, u32[]{:S(2)}) collective-permute-start(f32[1,32,192]{2,1,0:T(8,128)S(1)} %get-tuple-element.15), channel_id=1, source_target_pairs={{0,16},{16,32},{32,48},{48,64},{64,80},{80,96},{96,112},{112,128},... | collective-permute-start | bytes 73736 | tf_op jit(solution)/shard_map/ppermute | solution.py:39
  217.3 4.7 %collective-permute-start.16 = (f32[1,32,192]{2,1,0:T(8,128)S(1)}, f32[1,32,192]{2,1,0:T(8,128)S(1)}, u32[]{:S(2)}, u32[]{:S(2)}) collective-permute-start(f32[1,32,192]{2,1,0:T(8,128)S(1)} %get-tuple-element.16), channel_id=1, source_target_pairs={{16,0},{32,16},{48,32},{64,48},{80,64},{96,80},{112,96},{128,112},... | collective-permute-start | bytes 73736 | tf_op jit(solution)/shard_map/ppermute | solution.py:40
  229.0 17.2 %all-to-all-start.5 = ((f32[32,1,1728]{2,1,0:T(1,128)}), f32[32,1,1728]{2,1,0:T(1,128)}, u32[]{:S(2)}, u32[]{:S(2)}) async-start(f32[32,1,1728]{2,1,0:T(1,128)} %reshape.101), calls=%async_computation.5 | async-start | bytes 458752 | tf_op jit(solution)/shard_map/all_to_all | solution.py:71
  238.2 29.0 %collective-permute-start.20 = (bf16[4,32,192]{2,1,0:T(8,128)(2,1)}, bf16[4,32,192]{2,1,0:T(8,128)(2,1)}, u32[]{:S(2)}, u32[]{:S(2)}) collective-permute-start(bf16[4,32,192]{2,1,0:T(8,128)(2,1)} %get-tuple-element.29), channel_id=1, source_target_pairs={{0,16},{16,32},{32,48},{48,64},{64,80},{80,96},{96,112},{112,128},... | collective-permute-start | bytes 147464 | tf_op jit(solution)/shard_map/ppermute | solution.py:23
  241.9 25.3 %collective-permute-start.21 = (bf16[4,32,192]{2,1,0:T(8,128)(2,1)}, bf16[4,32,192]{2,1,0:T(8,128)(2,1)}, u32[]{:S(2)}, u32[]{:S(2)}) collective-permute-start(bf16[4,32,192]{2,1,0:T(8,128)(2,1)} %get-tuple-element.30), channel_id=1, source_target_pairs={{16,0},{32,16},{48,32},{64,48},{80,64},{96,80},{112,96},{128,112},... | collective-permute-start | bytes 147464 | tf_op jit(solution)/shard_map/ppermute | solution.py:25
  255.9 24.1 %all-to-all-start.6 = ((f32[16,1,1728]{2,1,0:T(1,128)}), f32[16,1,1728]{2,1,0:T(1,128)S(1)}, u32[]{:S(2)}, u32[]{:S(2)}) async-start(f32[16,1,1728]{2,1,0:T(1,128)} %reshape.103), calls=%async_computation.6 | async-start | bytes 229376 | tf_op jit(solution)/shard_map/all_to_all | solution.py:75
  268.3 5.5 %collective-permute-start.22 = (bf16[40,4,192]{2,1,0:T(4,128)(2,1)S(1)}, bf16[40,4,192]{2,1,0:T(4,128)(2,1)S(1)}, u32[]{:S(2)}, u32[]{:S(2)}) collective-permute-start(bf16[40,4,192]{2,1,0:T(4,128)(2,1)S(1)} %get-tuple-element.23), channel_id=1, source_target_pairs={{0,1},{1,2},{2,3},{3,4},{4,5},{5,6},{6,7},{7,8},{8,9},{9,10},{10,1... | collective-permute-start | bytes 184328 | tf_op jit(solution)/shard_map/ppermute | solution.py:23
  271.8 5.8 %collective-permute-start.23 = (bf16[40,4,192]{2,1,0:T(4,128)(2,1)S(1)}, bf16[40,4,192]{2,1,0:T(4,128)(2,1)S(1)}, u32[]{:S(2)}, u32[]{:S(2)}) collective-permute-start(bf16[40,4,192]{2,1,0:T(4,128)(2,1)S(1)} %get-tuple-element.24), channel_id=1, source_target_pairs={{1,0},{2,1},{3,2},{4,3},{5,4},{6,5},{7,6},{8,7},{9,8},{10,9},{11,1... | collective-permute-start | bytes 184328 | tf_op jit(solution)/shard_map/ppermute | solution.py:25
  290.2 16.8 %copy-start.5 = (f32[32,32,192]{2,1,0:T(8,128)S(1)}, f32[32,32,192]{2,1,0:T(8,128)}, u32[]{:S(2)}) copy-start(f32[32,32,192]{2,1,0:T(8,128)} %copy-done.4) | copy-start | bytes 2359300
  290.2 16.8 %copy-start.13 = (f32[32,32]{1,0:T(8,128)S(1)}, f32[32,32]{1,0:T(8,128)}, u32[]{:S(2)}) copy-start(f32[32,32]{1,0:T(8,128)} %copy-done.11) | copy-start | bytes 12292
  290.2 16.8 %copy-start.16 = (f32[32,32]{1,0:T(8,128)S(1)}, f32[32,32]{1,0:T(8,128)}, u32[]{:S(2)}) copy-start(f32[32,32]{1,0:T(8,128)} %copy-done.14) | copy-start | bytes 12292
  290.2 16.8 %copy-start.19 = (f32[32,32]{1,0:T(8,128)S(1)}, f32[32,32]{1,0:T(8,128)}, u32[]{:S(2)}) copy-start(f32[32,32]{1,0:T(8,128)} %copy-done.17) | copy-start | bytes 12292
  290.2 16.8 %copy-start.26 = (f32[32,32]{1,0:T(8,128)S(1)}, f32[32,32]{1,0:T(8,128)}, u32[]{:S(2)}) copy-start(f32[32,32]{1,0:T(8,128)} %param.8) | copy-start | bytes 12292
  293.6 10.0 %collective-permute-start.26 = (f32[32,1,192]{2,1,0:T(1,128)S(1)}, f32[32,1,192]{2,1,0:T(1,128)S(1)}, u32[]{:S(2)}, u32[]{:S(2)}) collective-permute-start(f32[32,1,192]{2,1,0:T(1,128)S(1)} %get-tuple-element.9), channel_id=1, source_target_pairs={{1,0},{2,1},{3,2},{4,3},{5,4},{6,5},{7,6},{8,7},{9,8},{10,9},{11,1... | collective-permute-start | bytes 73736 | tf_op jit(solution)/shard_map/ppermute | solution.py:42
  295.5 8.1 %collective-permute-start.27 = (f32[32,1,192]{2,1,0:T(1,128)S(1)}, f32[32,1,192]{2,1,0:T(1,128)S(1)}, u32[]{:S(2)}, u32[]{:S(2)}) collective-permute-start(f32[32,1,192]{2,1,0:T(1,128)S(1)} %get-tuple-element.10), channel_id=1, source_target_pairs={{0,1},{1,2},{2,3},{3,4},{4,5},{5,6},{6,7},{7,8},{8,9},{9,10},{10,1... | collective-permute-start | bytes 73736 | tf_op jit(solution)/shard_map/ppermute | solution.py:41
  299.2 4.5 %collective-permute-start.25 = (f32[1,32,192]{2,1,0:T(8,128)S(1)}, f32[1,32,192]{2,1,0:T(8,128)S(1)}, u32[]{:S(2)}, u32[]{:S(2)}) collective-permute-start(f32[1,32,192]{2,1,0:T(8,128)S(1)} %get-tuple-element.11), channel_id=1, source_target_pairs={{0,16},{16,32},{32,48},{48,64},{64,80},{80,96},{96,112},{112,128},... | collective-permute-start | bytes 73736 | tf_op jit(solution)/shard_map/ppermute | solution.py:39
  302.3 48.7 %slice-start = ((f32[9,192]{1,0:T(8,128)}), f32[1,192]{1,0:T(1,128)S(1)}, s32[]{:S(2)}) async-start(f32[9,192]{1,0:T(8,128)} %reduce_sum.104), calls=%async_computation.8 | async-start | bytes 2048 | tf_op jit(solution)/shard_map/slice | solution.py:123
  302.3 48.7 %slice-start.1 = ((f32[9,192]{1,0:T(8,128)}), f32[1,192]{1,0:T(1,128)S(1)}, s32[]{:S(2)}) async-start(f32[9,192]{1,0:T(8,128)} %reduce_sum.107), calls=%async_computation.9 | async-start | bytes 2048 | tf_op jit(solution)/shard_map/slice | solution.py:123
  302.3 4.7 %collective-permute-start.24 = (f32[1,32,192]{2,1,0:T(8,128)S(1)}, f32[1,32,192]{2,1,0:T(8,128)S(1)}, u32[]{:S(2)}, u32[]{:S(2)}) collective-permute-start(f32[1,32,192]{2,1,0:T(8,128)S(1)} %get-tuple-element.12), channel_id=1, source_target_pairs={{16,0},{32,16},{48,32},{64,48},{80,64},{96,80},{112,96},{128,112},... | collective-permute-start | bytes 73736 | tf_op jit(solution)/shard_map/ppermute | solution.py:40
  309.8 39.5 %all-to-all-start.7 = ((f32[512,1,192]{2,1,0:T(1,128)}), f32[512,1,192]{2,1,0:T(1,128)}, u32[]{:S(2)}, u32[]{:S(2)}) async-start(f32[512,1,192]{2,1,0:T(1,128)} %broadcast_in_dim.29), calls=%async_computation.7 | async-start | bytes 1048576 | tf_op jit(solution)/shard_map/all_to_all | solution.py:71
  (19 other events, 169.1 us)

commit v5 on v4

--- a/solution.py
+++ b/solution.py
@@ -67,12 +67,16 @@
 
 def gathered_by_exchange(block, axis):
     count = lax.axis_size(axis)
-    copies = jnp.broadcast_to(block[None], (count,) + block.shape)
-    return lax.all_to_all(copies, axis, 0, 0, tiled=True)
+    flat = block.reshape(-1)
+    copies = jnp.broadcast_to(flat[None], (count, flat.shape[0]))
+    return lax.all_to_all(copies, axis, 0, 0, tiled=True).reshape((count,) + block.shape)
 
 
 def summed_by_exchange(blocks, axis):
-    return jnp.sum(lax.all_to_all(blocks, axis, 0, 0, tiled=True), axis=0)
+    count = blocks.shape[0]
+    flat = blocks.reshape(count, -1)
+    received = lax.all_to_all(flat, axis, 0, 0, tiled=True)
+    return jnp.sum(received, axis=0).reshape(blocks.shape[1:])
 
 
 def total_over_mesh(values):
@@ -102,9 +106,8 @@
 
     def precondition(current):
         window = rounded_window(current).reshape(extent * extent, fields)
-        local_part = jnp.dot(inverse_rows, window, preferred_element_type=jnp.float32).reshape(
-            patch, patch, fields
-        )
+        local_part = jnp.dot(inverse_rows, window, preferred_element_type=jnp.float32)
+        local_part = lax.optimization_barrier(local_part).reshape(patch, patch, fields)
         flat_core = current.reshape(patch * patch, fields)
         restricted = jnp.dot(flat_basis, flat_core, precision=highest)
         squares = jnp.sum(flat_core * flat_core, axis=0)

time: 355 us -> 353 us (level)
  waiting for transfers between devices: 46.7 us -> 65.6 us
  starting transfers between devices: 160 us -> 146 us
  local copies, waits for them, and re-layouts: 61.6 us -> 54.8 us
    unnamed x72 -> x58, local copies, waits for them, and re-layouts: 25.1 us -> 4.41 us
    all_to_all x7, starting transfers between devices: 79.1 us -> 62.8 us  [the longest x4 49.4 us: gathered_by_exchange(): lax.all_to_all(copies, axis, 0, 0, tiled=True)]
    all_to_all x7, waiting for transfers between devices: 26.3 us -> 35.8 us  [the longest x4 18.1 us: gathered_by_exchange(): lax.all_to_all(copies, axis, 0, 0, tiled=True)]
    all_to_all x6 -> x3, other arithmetic: 14.9 us -> 6.56 us  [gathered_by_exchange(): lax.all_to_all(copies, axis, 0, 0, tiled=True)]
    ppermute x6, waiting for transfers between devices: 8.45 us -> 15.7 us  [extended(): lax.ppermute(head, axis, [((i + 1) % count, i) for i in range(ends)])]
    reshape x0 -> x3, local copies, waits for them, and re-layouts: none -> 5.63 us  [gathered_by_exchange(): lax.all_to_all(copies, axis, 0, 0, tiled=True)]
    convert_element_type x3 -> x2, other arithmetic: 7.33 us -> 1.74 us  [rounded_window(): current.astype(jnp.bfloat16)]
    reduce_sum x2 -> x3, other arithmetic: 0.32 us -> 5.89 us  [precondition(): squares = jnp.sum(flat_core * flat_core, axis=0)]
  transfers between devices with their start and end apart: 36 -> 36, of which waited for: 11 -> 14; matrix products, arithmetic and copies ran while one was open for 27% -> 21% of each run, Pallas kernels for 0% -> 0%
where the time goes in v5:
time: 353 us; the launch traced here: 349 us
  starting transfers between devices  146 us (41%)
  waiting for transfers between devices  65.6 us (19%)
  other arithmetic  59 us (17%)
  local copies, waits for them, and re-layouts  54.8 us (16%)
  matrix products  22 us (6%)
    all_to_all x4, starting transfers between devices, gathered_by_exchange(): lax.all_to_all(copies, axis, 0, 0, tiled=True)  49.4 us
    ppermute x6, starting transfers between devices, extended(): lax.ppermute(tail, axis, [(i, (i + 1) % count) for i in range(ends)])  22.9 us
    all_to_all x4, waiting for transfers between devices, gathered_by_exchange(): lax.all_to_all(copies, axis, 0, 0, tiled=True)  18.1 us
    all_to_all x3, waiting for transfers between devices, summed_by_exchange(): received = lax.all_to_all(flat, axis, 0, 0, tiled=True)  17.8 us
    ppermute x6, waiting for transfers between devices, extended(): lax.ppermute(head, axis, [((i + 1) % count, i) for i in range(ends)])  15.7 us
    ppermute x4, starting transfers between devices, with_edges(): north = lax.ppermute(cells[-1:], 'gx', down)  14.9 us
    ppermute x4, starting transfers between devices, with_edges(): west = lax.ppermute(cells[:, -1:], 'gy', right)  13.9 us
    all_to_all x3, starting transfers between devices, summed_by_exchange(): received = lax.all_to_all(flat, axis, 0, 0, tiled=True)  13.3 us
  transfers between devices with their start and end apart: 36, of which 14 were waited for; matrix products, arithmetic and copies ran while one was open for 21% of the time, Pallas kernels for 0%

profile of v5, /device:TPU:1, one launch (start us, length us, event | category | flops | bytes accessed | tf_op | source)
XLA Modules:
  0.0 349.1 jit_solution(2685932430472196967)
XLA Ops:
  2.1 5.3 %collective-permute-start.6 = (f32[1,32]{1,0:T(1,128)}, f32[1,32]{1,0:T(1,128)}, u32[]{:S(2)}, u32[]{:S(2)}) collective-permute-start(f32[1,32]{1,0:T(1,128)} %get-tuple-element.41), channel_id=1, source_target_pairs={{0,16},{16,32},{32,48},{48,64},{64,80},{80,96},{96,112},{112,128},... | collective-permute-start | bytes 392 | tf_op jit(solution)/shard_map/ppermute | solution.py:39
  10.2 5.2 %collective-permute-start.8 = (f32[32,1]{1,0:T(8,128)}, f32[32,1]{1,0:T(8,128)}, u32[]{:S(2)}, u32[]{:S(2)}) collective-permute-start(f32[32,1]{1,0:T(8,128)} %get-tuple-element.39), channel_id=1, source_target_pairs={{1,0},{2,1},{3,2},{4,3},{5,4},{6,5},{7,6},{8,7},{9,8},{10,9},{11,1... | collective-permute-start | bytes 392 | tf_op jit(solution)/shard_map/ppermute | solution.py:42
  15.4 2.4 multiply_reduce_fusion.2
  19.3 4.9 %collective-permute-start = (bf16[4,32,192]{2,1,0:T(8,128)(2,1)}, bf16[4,32,192]{2,1,0:T(8,128)(2,1)}, u32[]{:S(2)}, u32[]{:S(2)}) collective-permute-start(bf16[4,32,192]{2,1,0:T(8,128)(2,1)} %get-tuple-element.33), channel_id=1, source_target_pairs={{0,16},{16,32},{32,48},{48,64},{64,80},{80,96},{96,112},{112,128},... | collective-permute-start | bytes 147464 | tf_op jit(solution)/shard_map/ppermute | solution.py:23
  25.4 2.5 reshape.161
  28.0 3.3 copy.56
  33.2 5.2 %all-to-all-start.1 = ((f32[16,1,2048]{2,1,0:T(1,128)}), f32[16,1,2048]{2,1,0:T(1,128)S(1)}, u32[]{:S(2)}, u32[]{:S(2)}) async-start(f32[16,1,2048]{2,1,0:T(1,128)} %reshape.179), calls=%async_computation.1 | async-start | bytes 262144 | tf_op jit(solution)/shard_map/all_to_all | solution.py:101
  43.1 4.2 %all-to-all-done.1 = f32[16,1,2048]{2,1,0:T(1,128)S(1)} async-done(((f32[16,1,2048]{2,1,0:T(1,128)}), f32[16,1,2048]{2,1,0:T(1,128)S(1)}, u32[]{:S(2)}, u32[]{:S(2)}) %all-to-all-start.1) | async-done | bytes 131104 | tf_op jit(solution)/shard_map/all_to_all | solution.py:101
  48.8 14.5 %all-to-all-start = ((f32[32,1,1728]{2,1,0:T(1,128)}), f32[32,1,1728]{2,1,0:T(1,128)}, u32[]{:S(2)}, u32[]{:S(2)}) async-start(f32[32,1,1728]{2,1,0:T(1,128)} %broadcast_in_dim.28), calls=%async_computation | async-start | bytes 458752 | tf_op jit(solution)/shard_map/all_to_all | solution.py:72
  67.5 2.6 collective-permute-start.3
  71.4 2.9 collective-permute-start.10
  74.4 2.4 pad_maximum_fusion.18
  80.2 3.0 copy.57
  83.2 2.8 reshape.162
  98.2 4.4 %all-to-all-start.2 = ((f32[16,1,1728]{2,1,0:T(1,128)}), f32[16,1,1728]{2,1,0:T(1,128)}, u32[]{:S(2)}, u32[]{:S(2)}) async-start(f32[16,1,1728]{2,1,0:T(1,128)} %all_to_all.48), calls=%async_computation.2 | async-start | bytes 229376 | tf_op jit(solution)/shard_map/all_to_all | solution.py:78
  102.7 2.9 fusion.6
  105.6 5.9 %all-to-all-done.2 = f32[16,1,1728]{2,1,0:T(1,128)} async-done(((f32[16,1,1728]{2,1,0:T(1,128)}), f32[16,1,1728]{2,1,0:T(1,128)}, u32[]{:S(2)}, u32[]{:S(2)}) %all-to-all-start.2) | async-done | bytes 110624 | tf_op jit(solution)/shard_map/all_to_all | solution.py:78
  116.3 2.5 copy.60
  122.3 3.6 %collective-permute-start.11 = (f32[32,1,192]{2,1,0:T(1,128)S(1)}, f32[32,1,192]{2,1,0:T(1,128)S(1)}, u32[]{:S(2)}, u32[]{:S(2)}) collective-permute-start(f32[32,1,192]{2,1,0:T(1,128)S(1)} %get-tuple-element.18), channel_id=1, source_target_pairs={{0,1},{1,2},{2,3},{3,4},{4,5},{5,6},{6,7},{7,8},{8,9},{9,10},{10,1... | collective-permute-start | bytes 73736 | tf_op jit(solution)/shard_map/ppermute | solution.py:41
  126.0 3.3 collective-permute-start.7
  141.2 9.6 %all-to-all-start.3 = ((f32[32,1,1728]{2,1,0:T(1,128)}), f32[32,1,1728]{2,1,0:T(1,128)}, u32[]{:S(2)}, u32[]{:S(2)}) async-start(f32[32,1,1728]{2,1,0:T(1,128)} %broadcast_in_dim.32), calls=%async_computation.3 | async-start | bytes 458752 | tf_op jit(solution)/shard_map/all_to_all | solution.py:72
  151.7 3.1 collective-permute-start.12
  156.1 4.0 %collective-permute-done.13 = bf16[4,32,192]{2,1,0:T(8,128)(2,1)S(1)} collective-permute-done((bf16[4,32,192]{2,1,0:T(8,128)(2,1)S(1)}, bf16[4,32,192]{2,1,0:T(8,128)(2,1)S(1)}, u32[]{:S(2)}, u32[]{:S(2)}) %collective-permute-start.13) | collective-permute-done | bytes 49184 | tf_op jit(solution)/shard_map/ppermute | solution.py:25
  161.2 4.9 %collective-permute-start.14 = (bf16[40,4,192]{2,1,0:T(4,128)(2,1)S(1)}, bf16[40,4,192]{2,1,0:T(4,128)(2,1)S(1)}, u32[]{:S(2)}, u32[]{:S(2)}) collective-permute-start(bf16[40,4,192]{2,1,0:T(4,128)(2,1)S(1)} %get-tuple-element.25), channel_id=1, source_target_pairs={{0,1},{1,2},{2,3},{3,4},{4,5},{5,6},{6,7},{7,8},{8,9},{9,10},{10,1... | collective-permute-start | bytes 184328 | tf_op jit(solution)/shard_map/ppermute | solution.py:23
  168.1 3.8 %collective-permute-done.15 = bf16[40,4,192]{2,1,0:T(4,128)(2,1)S(1)} collective-permute-done((bf16[40,4,192]{2,1,0:T(4,128)(2,1)S(1)}, bf16[40,4,192]{2,1,0:T(4,128)(2,1)S(1)}, u32[]{:S(2)}, u32[]{:S(2)}) %collective-permute-start.15) | collective-permute-done | bytes 61472 | tf_op jit(solution)/shard_map/ppermute | solution.py:25
  171.9 2.4 pad_maximum_fusion.19
  187.8 4.5 %all-to-all-start.4 = ((f32[16,1,1728]{2,1,0:T(1,128)}), f32[16,1,1728]{2,1,0:T(1,128)}, u32[]{:S(2)}, u32[]{:S(2)}) async-start(f32[16,1,1728]{2,1,0:T(1,128)} %all_to_all.49), calls=%async_computation.4 | async-start | bytes 229376 | tf_op jit(solution)/shard_map/all_to_all | solution.py:78
  192.3 2.9 fusion.9
  195.2 6.0 %all-to-all-done.4 = f32[16,1,1728]{2,1,0:T(1,128)} async-done(((f32[16,1,1728]{2,1,0:T(1,128)}), f32[16,1,1728]{2,1,0:T(1,128)}, u32[]{:S(2)}, u32[]{:S(2)}) %all-to-all-start.4) | async-done | bytes 110624 | tf_op jit(solution)/shard_map/all_to_all | solution.py:78
  207.8 2.4 copy.64
  214.1 3.6 %collective-permute-start.19 = (f32[32,1,192]{2,1,0:T(1,128)S(1)}, f32[32,1,192]{2,1,0:T(1,128)S(1)}, u32[]{:S(2)}, u32[]{:S(2)}) collective-permute-start(f32[32,1,192]{2,1,0:T(1,128)S(1)} %get-tuple-element.14), channel_id=1, source_target_pairs={{0,1},{1,2},{2,3},{3,4},{4,5},{5,6},{6,7},{7,8},{8,9},{9,10},{10,1... | collective-permute-start | bytes 73736 | tf_op jit(solution)/shard_map/ppermute | solution.py:41
  217.8 3.1 collective-permute-start.17
  222.2 3.7 %collective-permute-done.16 = f32[1,32,192]{2,1,0:T(8,128)S(1)} collective-permute-done((f32[1,32,192]{2,1,0:T(8,128)S(1)}, f32[1,32,192]{2,1,0:T(8,128)S(1)}, u32[]{:S(2)}, u32[]{:S(2)}) %collective-permute-start.16) | collective-permute-done | bytes 24608 | tf_op jit(solution)/shard_map/ppermute | solution.py:40
  230.5 9.3 %all-to-all-start.5 = ((f32[32,1,1728]{2,1,0:T(1,128)}), f32[32,1,1728]{2,1,0:T(1,128)}, u32[]{:S(2)}, u32[]{:S(2)}) async-start(f32[32,1,1728]{2,1,0:T(1,128)} %broadcast_in_dim.70), calls=%async_computation.5 | async-start | bytes 458752 | tf_op jit(solution)/shard_map/all_to_all | solution.py:72
  240.6 3.1 collective-permute-start.20
  245.1 4.0 %collective-permute-done.21 = bf16[4,32,192]{2,1,0:T(8,128)(2,1)S(1)} collective-permute-done((bf16[4,32,192]{2,1,0:T(8,128)(2,1)S(1)}, bf16[4,32,192]{2,1,0:T(8,128)(2,1)S(1)}, u32[]{:S(2)}, u32[]{:S(2)}) %collective-permute-start.21) | collective-permute-done | bytes 49184 | tf_op jit(solution)/shard_map/ppermute | solution.py:25
  250.2 4.7 %collective-permute-start.22 = (bf16[40,4,192]{2,1,0:T(4,128)(2,1)S(1)}, bf16[40,4,192]{2,1,0:T(4,128)(2,1)S(1)}, u32[]{:S(2)}, u32[]{:S(2)}) collective-permute-start(bf16[40,4,192]{2,1,0:T(4,128)(2,1)S(1)} %get-tuple-element.23), channel_id=1, source_target_pairs={{0,1},{1,2},{2,3},{3,4},{4,5},{5,6},{6,7},{7,8},{8,9},{9,10},{10,1... | collective-permute-start | bytes 184328 | tf_op jit(solution)/shard_map/ppermute | solution.py:23
  256.8 3.8 %collective-permute-done.23 = bf16[40,4,192]{2,1,0:T(4,128)(2,1)S(1)} collective-permute-done((bf16[40,4,192]{2,1,0:T(4,128)(2,1)S(1)}, bf16[40,4,192]{2,1,0:T(4,128)(2,1)S(1)}, u32[]{:S(2)}, u32[]{:S(2)}) %collective-permute-start.23) | collective-permute-done | bytes 61472 | tf_op jit(solution)/shard_map/ppermute | solution.py:25
  272.0 4.5 %all-to-all-start.6 = ((f32[16,1,1728]{2,1,0:T(1,128)}), f32[16,1,1728]{2,1,0:T(1,128)S(1)}, u32[]{:S(2)}, u32[]{:S(2)}) async-start(f32[16,1,1728]{2,1,0:T(1,128)} %all_to_all.50), calls=%async_computation.6 | async-start | bytes 229376 | tf_op jit(solution)/shard_map/all_to_all | solution.py:78
  276.5 2.9 fusion.12
  279.4 5.8 %all-to-all-done.6 = f32[16,1,1728]{2,1,0:T(1,128)S(1)} async-done(((f32[16,1,1728]{2,1,0:T(1,128)}), f32[16,1,1728]{2,1,0:T(1,128)S(1)}, u32[]{:S(2)}, u32[]{:S(2)}) %all-to-all-start.6) | async-done | bytes 110624 | tf_op jit(solution)/shard_map/all_to_all | solution.py:78
  288.4 2.4 copy.68
  290.9 3.3 multiply_add_fusion
  296.2 3.6 %collective-permute-start.27 = (f32[32,1,192]{2,1,0:T(1,128)S(1)}, f32[32,1,192]{2,1,0:T(1,128)S(1)}, u32[]{:S(2)}, u32[]{:S(2)}) collective-permute-start(f32[32,1,192]{2,1,0:T(1,128)S(1)} %get-tuple-element.10), channel_id=1, source_target_pairs={{0,1},{1,2},{2,3},{3,4},{4,5},{5,6},{6,7},{7,8},{8,9},{9,10},{10,1... | collective-permute-start | bytes 73736 | tf_op jit(solution)/shard_map/ppermute | solution.py:41
  299.9 3.1 collective-permute-start.25
  304.3 3.7 %collective-permute-done.24 = f32[1,32,192]{2,1,0:T(8,128)S(1)} collective-permute-done((f32[1,32,192]{2,1,0:T(8,128)S(1)}, f32[1,32,192]{2,1,0:T(8,128)S(1)}, u32[]{:S(2)}, u32[]{:S(2)}) %collective-permute-start.24) | collective-permute-done | bytes 24608 | tf_op jit(solution)/shard_map/ppermute | solution.py:40
  310.9 16.0 %all-to-all-start.7 = ((f32[512,1,192]{2,1,0:T(1,128)}), f32[512,1,192]{2,1,0:T(1,128)}, u32[]{:S(2)}, u32[]{:S(2)}) async-start(f32[512,1,192]{2,1,0:T(1,128)} %broadcast_in_dim.72), calls=%async_computation.7 | async-start | bytes 1048576 | tf_op jit(solution)/shard_map/all_to_all | solution.py:72
  328.8 18.1 %all-to-all-done.7 = f32[512,1,192]{2,1,0:T(1,128)} async-done(((f32[512,1,192]{2,1,0:T(1,128)}), f32[512,1,192]{2,1,0:T(1,128)}, u32[]{:S(2)}, u32[]{:S(2)}) %all-to-all-start.7) | async-done | bytes 393248 | tf_op jit(solution)/shard_map/all_to_all | solution.py:72
  (177 shorter events, 121.0 us)
Async XLA Ops:
  0.6 102.0 %copy-start = (bf16[1,1,1024,1600]{2,3,1,0:T(8,128)(2,1)S(1)}, bf16[1,1,1024,1600]{2,3,1,0:T(8,128)(2,1)}, u32[]{:S(2)}) copy-start(bf16[1,1,1024,1600]{2,3,1,0:T(8,128)(2,1)} %param.10) | copy-start | bytes 9830404
  0.6 24.8 %copy-start.25 = (f32[8,4096]{1,0:T(8,128)S(1)}, f32[8,4096]{1,0:T(8,128)}, u32[]{:S(2)}) copy-start(f32[8,4096]{1,0:T(8,128)} %param.11) | copy-start | bytes 393220
  2.1 120.2 %collective-permute-start.6 = (f32[1,32]{1,0:T(1,128)}, f32[1,32]{1,0:T(1,128)}, u32[]{:S(2)}, u32[]{:S(2)}) collective-permute-start(f32[1,32]{1,0:T(1,128)} %get-tuple-element.41), channel_id=1, source_target_pairs={{0,16},{16,32},{32,48},{48,64},{64,80},{80,96},{96,112},{112,128},... | collective-permute-start | bytes 392 | tf_op jit(solution)/shard_map/ppermute | solution.py:39
  7.5 118.5 %collective-permute-start.4 = (f32[1,32]{1,0:T(1,128)}, f32[1,32]{1,0:T(1,128)}, u32[]{:S(2)}, u32[]{:S(2)}) collective-permute-start(f32[1,32]{1,0:T(1,128)} %get-tuple-element.42), channel_id=1, source_target_pairs={{16,0},{32,16},{48,32},{64,48},{80,64},{96,80},{112,96},{128,112},... | collective-permute-start | bytes 392 | tf_op jit(solution)/shard_map/ppermute | solution.py:40
  10.2 119.1 %collective-permute-start.8 = (f32[32,1]{1,0:T(8,128)}, f32[32,1]{1,0:T(8,128)}, u32[]{:S(2)}, u32[]{:S(2)}) collective-permute-start(f32[32,1]{1,0:T(8,128)} %get-tuple-element.39), channel_id=1, source_target_pairs={{1,0},{2,1},{3,2},{4,3},{5,4},{6,5},{7,6},{8,7},{9,8},{10,9},{11,1... | collective-permute-start | bytes 392 | tf_op jit(solution)/shard_map/ppermute | solution.py:42
  19.3 44.1 %collective-permute-start = (bf16[4,32,192]{2,1,0:T(8,128)(2,1)}, bf16[4,32,192]{2,1,0:T(8,128)(2,1)}, u32[]{:S(2)}, u32[]{:S(2)}) collective-permute-start(bf16[4,32,192]{2,1,0:T(8,128)(2,1)} %get-tuple-element.33), channel_id=1, source_target_pairs={{0,16},{16,32},{32,48},{48,64},{64,80},{80,96},{96,112},{112,128},... | collective-permute-start | bytes 147464 | tf_op jit(solution)/shard_map/ppermute | solution.py:23
  24.1 39.2 %collective-permute-start.1 = (bf16[4,32,192]{2,1,0:T(8,128)(2,1)}, bf16[4,32,192]{2,1,0:T(8,128)(2,1)}, u32[]{:S(2)}, u32[]{:S(2)}) collective-permute-start(bf16[4,32,192]{2,1,0:T(8,128)(2,1)} %get-tuple-element.34), channel_id=1, source_target_pairs={{16,0},{32,16},{48,32},{64,48},{80,64},{96,80},{112,96},{128,112},... | collective-permute-start | bytes 147464 | tf_op jit(solution)/shard_map/ppermute | solution.py:25
  33.2 36.8 %copy-start.22 = (f32[32,32]{1,0:T(8,128)S(1)}, f32[32,32]{1,0:T(8,128)}, u32[]{:S(2)}) copy-start(f32[32,32]{1,0:T(8,128)} %param.8) | copy-start | bytes 12292
  33.2 14.1 %all-to-all-start.1 = ((f32[16,1,2048]{2,1,0:T(1,128)}), f32[16,1,2048]{2,1,0:T(1,128)S(1)}, u32[]{:S(2)}, u32[]{:S(2)}) async-start(f32[16,1,2048]{2,1,0:T(1,128)} %reshape.179), calls=%async_computation.1 | async-start | bytes 262144 | tf_op jit(solution)/shard_map/all_to_all | solution.py:101
  47.3 29.5 %copy-start.11 = (f32[16,1,2048]{2,1,0:T(1,128)}, f32[16,1,2048]{2,1,0:T(1,128)S(1)}, u32[]{:S(2)}) copy-start(f32[16,1,2048]{2,1,0:T(1,128)S(1)} %all-to-all-done.1) | copy-start | bytes 393220
  48.8 37.2 %all-to-all-start = ((f32[32,1,1728]{2,1,0:T(1,128)}), f32[32,1,1728]{2,1,0:T(1,128)}, u32[]{:S(2)}, u32[]{:S(2)}) async-start(f32[32,1,1728]{2,1,0:T(1,128)} %broadcast_in_dim.28), calls=%async_computation | async-start | bytes 458752 | tf_op jit(solution)/shard_map/all_to_all | solution.py:72
  65.1 6.3 %collective-permute-start.2 = (bf16[40,4,192]{2,1,0:T(4,128)(2,1)}, bf16[40,4,192]{2,1,0:T(4,128)(2,1)}, u32[]{:S(2)}, u32[]{:S(2)}) collective-permute-start(bf16[40,4,192]{2,1,0:T(4,128)(2,1)} %get-tuple-element.27), channel_id=1, source_target_pairs={{0,1},{1,2},{2,3},{3,4},{4,5},{5,6},{6,7},{7,8},{8,9},{9,10},{10,1... | collective-permute-start | bytes 184328 | tf_op jit(solution)/shard_map/ppermute | solution.py:23
  67.5 6.9 %collective-permute-start.3 = (bf16[40,4,192]{2,1,0:T(4,128)(2,1)}, bf16[40,4,192]{2,1,0:T(4,128)(2,1)}, u32[]{:S(2)}, u32[]{:S(2)}) collective-permute-start(bf16[40,4,192]{2,1,0:T(4,128)(2,1)} %get-tuple-element.28), channel_id=1, source_target_pairs={{1,0},{2,1},{3,2},{4,3},{5,4},{6,5},{7,6},{8,7},{9,8},{10,9},{11,1... | collective-permute-start | bytes 184328 | tf_op jit(solution)/shard_map/ppermute | solution.py:25
  71.4 59.4 %collective-permute-start.10 = (f32[32,1]{1,0:T(8,128)}, f32[32,1]{1,0:T(8,128)}, u32[]{:S(2)}, u32[]{:S(2)}) collective-permute-start(f32[32,1]{1,0:T(8,128)} %get-tuple-element.40), channel_id=1, source_target_pairs={{0,1},{1,2},{2,3},{3,4},{4,5},{5,6},{6,7},{7,8},{8,9},{9,10},{10,1... | collective-permute-start | bytes 392 | tf_op jit(solution)/shard_map/ppermute | solution.py:41
  98.2 13.3 %all-to-all-start.2 = ((f32[16,1,1728]{2,1,0:T(1,128)}), f32[16,1,1728]{2,1,0:T(1,128)}, u32[]{:S(2)}, u32[]{:S(2)}) async-start(f32[16,1,1728]{2,1,0:T(1,128)} %all_to_all.48), calls=%async_computation.2 | async-start | bytes 229376 | tf_op jit(solution)/shard_map/all_to_all | solution.py:78
  120.4 11.3 %collective-permute-start.9 = (f32[32,1,192]{2,1,0:T(1,128)S(1)}, f32[32,1,192]{2,1,0:T(1,128)S(1)}, u32[]{:S(2)}, u32[]{:S(2)}) collective-permute-start(f32[32,1,192]{2,1,0:T(1,128)S(1)} %get-tuple-element.17), channel_id=1, source_target_pairs={{1,0},{2,1},{3,2},{4,3},{5,4},{6,5},{7,6},{8,7},{9,8},{10,9},{11,1... | collective-permute-start | bytes 73736 | tf_op jit(solution)/shard_map/ppermute | solution.py:42
  122.3 9.4 %collective-permute-start.11 = (f32[32,1,192]{2,1,0:T(1,128)S(1)}, f32[32,1,192]{2,1,0:T(1,128)S(1)}, u32[]{:S(2)}, u32[]{:S(2)}) collective-permute-start(f32[32,1,192]{2,1,0:T(1,128)S(1)} %get-tuple-element.18), channel_id=1, source_target_pairs={{0,1},{1,2},{2,3},{3,4},{4,5},{5,6},{6,7},{7,8},{8,9},{9,10},{10,1... | collective-permute-start | bytes 73736 | tf_op jit(solution)/shard_map/ppermute | solution.py:41
  126.0 5.8 %collective-permute-start.7 = (f32[1,32,192]{2,1,0:T(8,128)S(1)}, f32[1,32,192]{2,1,0:T(8,128)S(1)}, u32[]{:S(2)}, u32[]{:S(2)}) collective-permute-start(f32[1,32,192]{2,1,0:T(8,128)S(1)} %get-tuple-element.19), channel_id=1, source_target_pairs={{0,16},{16,32},{32,48},{48,64},{64,80},{80,96},{96,112},{112,128},... | collective-permute-start | bytes 73736 | tf_op jit(solution)/shard_map/ppermute | solution.py:39
  129.3 4.7 %collective-permute-start.5 = (f32[1,32,192]{2,1,0:T(8,128)S(1)}, f32[1,32,192]{2,1,0:T(8,128)S(1)}, u32[]{:S(2)}, u32[]{:S(2)}) collective-permute-start(f32[1,32,192]{2,1,0:T(8,128)S(1)} %get-tuple-element.20), channel_id=1, source_target_pairs={{16,0},{32,16},{48,32},{64,48},{80,64},{96,80},{112,96},{128,112},... | collective-permute-start | bytes 73736 | tf_op jit(solution)/shard_map/ppermute | solution.py:40
  141.2 33.1 %all-to-all-start.3 = ((f32[32,1,1728]{2,1,0:T(1,128)}), f32[32,1,1728]{2,1,0:T(1,128)}, u32[]{:S(2)}, u32[]{:S(2)}) async-start(f32[32,1,1728]{2,1,0:T(1,128)} %broadcast_in_dim.32), calls=%async_computation.3 | async-start | bytes 458752 | tf_op jit(solution)/shard_map/all_to_all | solution.py:72
  151.7 4.5 %collective-permute-start.12 = (bf16[4,32,192]{2,1,0:T(8,128)(2,1)S(1)}, bf16[4,32,192]{2,1,0:T(8,128)(2,1)S(1)}, u32[]{:S(2)}, u32[]{:S(2)}) collective-permute-start(bf16[4,32,192]{2,1,0:T(8,128)(2,1)S(1)} %get-tuple-element.31), channel_id=1, source_target_pairs={{0,16},{16,32},{32,48},{48,64},{64,80},{80,96},{96,112},{112,128},... | collective-permute-start | bytes 147464 | tf_op jit(solution)/shard_map/ppermute | solution.py:23
  154.7 5.4 %collective-permute-start.13 = (bf16[4,32,192]{2,1,0:T(8,128)(2,1)S(1)}, bf16[4,32,192]{2,1,0:T(8,128)(2,1)S(1)}, u32[]{:S(2)}, u32[]{:S(2)}) collective-permute-start(bf16[4,32,192]{2,1,0:T(8,128)(2,1)S(1)} %get-tuple-element.32), channel_id=1, source_target_pairs={{16,0},{32,16},{48,32},{64,48},{80,64},{96,80},{112,96},{128,112},... | collective-permute-start | bytes 147464 | tf_op jit(solution)/shard_map/ppermute | solution.py:25
  161.2 6.9 %collective-permute-start.14 = (bf16[40,4,192]{2,1,0:T(4,128)(2,1)S(1)}, bf16[40,4,192]{2,1,0:T(4,128)(2,1)S(1)}, u32[]{:S(2)}, u32[]{:S(2)}) collective-permute-start(bf16[40,4,192]{2,1,0:T(4,128)(2,1)S(1)} %get-tuple-element.25), channel_id=1, source_target_pairs={{0,1},{1,2},{2,3},{3,4},{4,5},{5,6},{6,7},{7,8},{8,9},{9,10},{10,1... | collective-permute-start | bytes 184328 | tf_op jit(solution)/shard_map/ppermute | solution.py:23
  166.2 5.8 %collective-permute-start.15 = (bf16[40,4,192]{2,1,0:T(4,128)(2,1)S(1)}, bf16[40,4,192]{2,1,0:T(4,128)(2,1)S(1)}, u32[]{:S(2)}, u32[]{:S(2)}) collective-permute-start(bf16[40,4,192]{2,1,0:T(4,128)(2,1)S(1)} %get-tuple-element.26), channel_id=1, source_target_pairs={{1,0},{2,1},{3,2},{4,3},{5,4},{6,5},{7,6},{8,7},{9,8},{10,9},{11,1... | collective-permute-start | bytes 184328 | tf_op jit(solution)/shard_map/ppermute | solution.py:25
  187.8 13.4 %all-to-all-start.4 = ((f32[16,1,1728]{2,1,0:T(1,128)}), f32[16,1,1728]{2,1,0:T(1,128)}, u32[]{:S(2)}, u32[]{:S(2)}) async-start(f32[16,1,1728]{2,1,0:T(1,128)} %all_to_all.49), calls=%async_computation.4 | async-start | bytes 229376 | tf_op jit(solution)/shard_map/all_to_all | solution.py:78
  210.3 15.6 %copy-start.16 = (f32[32,32]{1,0:T(8,128)S(1)}, f32[32,32]{1,0:T(8,128)}, u32[]{:S(2)}) copy-start(f32[32,32]{1,0:T(8,128)} %copy-done.15) | copy-start | bytes 12292
  210.3 15.6 %copy-start.19 = (f32[32,32]{1,0:T(8,128)S(1)}, f32[32,32]{1,0:T(8,128)}, u32[]{:S(2)}) copy-start(f32[32,32]{1,0:T(8,128)} %copy-done.18) | copy-start | bytes 12292
  210.3 15.6 %copy-start.23 = (f32[32,32]{1,0:T(8,128)S(1)}, f32[32,32]{1,0:T(8,128)}, u32[]{:S(2)}) copy-start(f32[32,32]{1,0:T(8,128)} %param.8) | copy-start | bytes 12292
  212.2 10.0 %collective-permute-start.18 = (f32[32,1,192]{2,1,0:T(1,128)S(1)}, f32[32,1,192]{2,1,0:T(1,128)S(1)}, u32[]{:S(2)}, u32[]{:S(2)}) collective-permute-start(f32[32,1,192]{2,1,0:T(1,128)S(1)} %get-tuple-element.13), channel_id=1, source_target_pairs={{1,0},{2,1},{3,2},{4,3},{5,4},{6,5},{7,6},{8,7},{9,8},{10,9},{11,1... | collective-permute-start | bytes 73736 | tf_op jit(solution)/shard_map/ppermute | solution.py:42
  214.1 8.1 %collective-permute-start.19 = (f32[32,1,192]{2,1,0:T(1,128)S(1)}, f32[32,1,192]{2,1,0:T(1,128)S(1)}, u32[]{:S(2)}, u32[]{:S(2)}) collective-permute-start(f32[32,1,192]{2,1,0:T(1,128)S(1)} %get-tuple-element.14), channel_id=1, source_target_pairs={{0,1},{1,2},{2,3},{3,4},{4,5},{5,6},{6,7},{7,8},{8,9},{9,10},{10,1... | collective-permute-start | bytes 73736 | tf_op jit(solution)/shard_map/ppermute | solution.py:41
  217.8 4.4 %collective-permute-start.17 = (f32[1,32,192]{2,1,0:T(8,128)S(1)}, f32[1,32,192]{2,1,0:T(8,128)S(1)}, u32[]{:S(2)}, u32[]{:S(2)}) collective-permute-start(f32[1,32,192]{2,1,0:T(8,128)S(1)} %get-tuple-element.15), channel_id=1, source_target_pairs={{0,16},{16,32},{32,48},{48,64},{64,80},{80,96},{96,112},{112,128},... | collective-permute-start | bytes 73736 | tf_op jit(solution)/shard_map/ppermute | solution.py:39
  220.9 5.0 %collective-permute-start.16 = (f32[1,32,192]{2,1,0:T(8,128)S(1)}, f32[1,32,192]{2,1,0:T(8,128)S(1)}, u32[]{:S(2)}, u32[]{:S(2)}) collective-permute-start(f32[1,32,192]{2,1,0:T(8,128)S(1)} %get-tuple-element.16), channel_id=1, source_target_pairs={{16,0},{32,16},{48,32},{64,48},{80,64},{96,80},{112,96},{128,112},... | collective-permute-start | bytes 73736 | tf_op jit(solution)/shard_map/ppermute | solution.py:40
  230.5 32.5 %all-to-all-start.5 = ((f32[32,1,1728]{2,1,0:T(1,128)}), f32[32,1,1728]{2,1,0:T(1,128)}, u32[]{:S(2)}, u32[]{:S(2)}) async-start(f32[32,1,1728]{2,1,0:T(1,128)} %broadcast_in_dim.70), calls=%async_computation.5 | async-start | bytes 458752 | tf_op jit(solution)/shard_map/all_to_all | solution.py:72
  240.6 4.4 %collective-permute-start.20 = (bf16[4,32,192]{2,1,0:T(8,128)(2,1)S(1)}, bf16[4,32,192]{2,1,0:T(8,128)(2,1)S(1)}, u32[]{:S(2)}, u32[]{:S(2)}) collective-permute-start(bf16[4,32,192]{2,1,0:T(8,128)(2,1)S(1)} %get-tuple-element.29), channel_id=1, source_target_pairs={{0,16},{16,32},{32,48},{48,64},{64,80},{80,96},{96,112},{112,128},... | collective-permute-start | bytes 147464 | tf_op jit(solution)/shard_map/ppermute | solution.py:23
  243.7 5.4 %collective-permute-start.21 = (bf16[4,32,192]{2,1,0:T(8,128)(2,1)S(1)}, bf16[4,32,192]{2,1,0:T(8,128)(2,1)S(1)}, u32[]{:S(2)}, u32[]{:S(2)}) collective-permute-start(bf16[4,32,192]{2,1,0:T(8,128)(2,1)S(1)} %get-tuple-element.30), channel_id=1, source_target_pairs={{16,0},{32,16},{48,32},{64,48},{80,64},{96,80},{112,96},{128,112},... | collective-permute-start | bytes 147464 | tf_op jit(solution)/shard_map/ppermute | solution.py:25
  250.2 6.6 %collective-permute-start.22 = (bf16[40,4,192]{2,1,0:T(4,128)(2,1)S(1)}, bf16[40,4,192]{2,1,0:T(4,128)(2,1)S(1)}, u32[]{:S(2)}, u32[]{:S(2)}) collective-permute-start(bf16[40,4,192]{2,1,0:T(4,128)(2,1)S(1)} %get-tuple-element.23), channel_id=1, source_target_pairs={{0,1},{1,2},{2,3},{3,4},{4,5},{5,6},{6,7},{7,8},{8,9},{9,10},{10,1... | collective-permute-start | bytes 184328 | tf_op jit(solution)/shard_map/ppermute | solution.py:23
  254.8 5.8 %collective-permute-start.23 = (bf16[40,4,192]{2,1,0:T(4,128)(2,1)S(1)}, bf16[40,4,192]{2,1,0:T(4,128)(2,1)S(1)}, u32[]{:S(2)}, u32[]{:S(2)}) collective-permute-start(bf16[40,4,192]{2,1,0:T(4,128)(2,1)S(1)} %get-tuple-element.24), channel_id=1, source_target_pairs={{1,0},{2,1},{3,2},{4,3},{5,4},{6,5},{7,6},{8,7},{9,8},{10,9},{11,1... | collective-permute-start | bytes 184328 | tf_op jit(solution)/shard_map/ppermute | solution.py:25
  272.0 13.3 %all-to-all-start.6 = ((f32[16,1,1728]{2,1,0:T(1,128)}), f32[16,1,1728]{2,1,0:T(1,128)S(1)}, u32[]{:S(2)}, u32[]{:S(2)}) async-start(f32[16,1,1728]{2,1,0:T(1,128)} %all_to_all.50), calls=%async_computation.6 | async-start | bytes 229376 | tf_op jit(solution)/shard_map/all_to_all | solution.py:78
  290.8 17.2 %copy-start.5 = (f32[32,32,192]{2,1,0:T(8,128)S(1)}, f32[32,32,192]{2,1,0:T(8,128)}, u32[]{:S(2)}) copy-start(f32[32,32,192]{2,1,0:T(8,128)} %copy-done.4) | copy-start | bytes 2359300
  290.8 17.2 %copy-start.14 = (f32[32,32]{1,0:T(8,128)S(1)}, f32[32,32]{1,0:T(8,128)}, u32[]{:S(2)}) copy-start(f32[32,32]{1,0:T(8,128)} %copy-done.12) | copy-start | bytes 12292
  290.8 17.2 %copy-start.17 = (f32[32,32]{1,0:T(8,128)S(1)}, f32[32,32]{1,0:T(8,128)}, u32[]{:S(2)}) copy-start(f32[32,32]{1,0:T(8,128)} %copy-done.15) | copy-start | bytes 12292
  290.8 17.2 %copy-start.20 = (f32[32,32]{1,0:T(8,128)S(1)}, f32[32,32]{1,0:T(8,128)}, u32[]{:S(2)}) copy-start(f32[32,32]{1,0:T(8,128)} %copy-done.18) | copy-start | bytes 12292
  290.9 17.2 %copy-start.24 = (f32[32,32]{1,0:T(8,128)S(1)}, f32[32,32]{1,0:T(8,128)}, u32[]{:S(2)}) copy-start(f32[32,32]{1,0:T(8,128)} %param.8) | copy-start | bytes 12292
  294.3 10.0 %collective-permute-start.26 = (f32[32,1,192]{2,1,0:T(1,128)S(1)}, f32[32,1,192]{2,1,0:T(1,128)S(1)}, u32[]{:S(2)}, u32[]{:S(2)}) collective-permute-start(f32[32,1,192]{2,1,0:T(1,128)S(1)} %get-tuple-element.9), channel_id=1, source_target_pairs={{1,0},{2,1},{3,2},{4,3},{5,4},{6,5},{7,6},{8,7},{9,8},{10,9},{11,1... | collective-permute-start | bytes 73736 | tf_op jit(solution)/shard_map/ppermute | solution.py:42
  296.2 8.1 %collective-permute-start.27 = (f32[32,1,192]{2,1,0:T(1,128)S(1)}, f32[32,1,192]{2,1,0:T(1,128)S(1)}, u32[]{:S(2)}, u32[]{:S(2)}) collective-permute-start(f32[32,1,192]{2,1,0:T(1,128)S(1)} %get-tuple-element.10), channel_id=1, source_target_pairs={{0,1},{1,2},{2,3},{3,4},{4,5},{5,6},{6,7},{7,8},{8,9},{9,10},{10,1... | collective-permute-start | bytes 73736 | tf_op jit(solution)/shard_map/ppermute | solution.py:41
  299.9 4.4 %collective-permute-start.25 = (f32[1,32,192]{2,1,0:T(8,128)S(1)}, f32[1,32,192]{2,1,0:T(8,128)S(1)}, u32[]{:S(2)}, u32[]{:S(2)}) collective-permute-start(f32[1,32,192]{2,1,0:T(8,128)S(1)} %get-tuple-element.11), channel_id=1, source_target_pairs={{0,16},{16,32},{32,48},{48,64},{64,80},{80,96},{96,112},{112,128},... | collective-permute-start | bytes 73736 | tf_op jit(solution)/shard_map/ppermute | solution.py:39
  303.0 5.1 %collective-permute-start.24 = (f32[1,32,192]{2,1,0:T(8,128)S(1)}, f32[1,32,192]{2,1,0:T(8,128)S(1)}, u32[]{:S(2)}, u32[]{:S(2)}) collective-permute-start(f32[1,32,192]{2,1,0:T(8,128)S(1)} %get-tuple-element.12), channel_id=1, source_target_pairs={{16,0},{32,16},{48,32},{64,48},{80,64},{96,80},{112,96},{128,112},... | collective-permute-start | bytes 73736 | tf_op jit(solution)/shard_map/ppermute | solution.py:40
  310.9 36.0 %all-to-all-start.7 = ((f32[512,1,192]{2,1,0:T(1,128)}), f32[512,1,192]{2,1,0:T(1,128)}, u32[]{:S(2)}, u32[]{:S(2)}) async-start(f32[512,1,192]{2,1,0:T(1,128)} %broadcast_in_dim.72), calls=%async_computation.7 | async-start | bytes 1048576 | tf_op jit(solution)/shard_map/all_to_all | solution.py:72
  (16 other events, 145.2 us)

commit v6 on v5

--- a/solution.py
+++ b/solution.py
@@ -97,9 +97,9 @@
     kappa_pad = with_edges(permeability)
     state = sources
 
-    pieces = coarse_inverse.reshape(modes, rows_x, cols_y, modes).transpose(2, 0, 1, 3)
-    pieces = lax.all_to_all(pieces, "gy", 0, 0, tiled=True)
-    coarse_block = pieces.reshape(cols_y * modes, rows_x * modes)
+    pieces = coarse_inverse.reshape(modes, rows_x, cols_y * modes).transpose(1, 0, 2)
+    pieces = lax.all_to_all(pieces, "gx", 0, 0, tiled=True)
+    coarse_block = pieces.reshape(rows_x * modes, cols_y * modes)
 
     def rounded_window(current):
         return extended(current.astype(jnp.bfloat16), (("gx", 0), ("gy", 1)), margin)
@@ -112,16 +112,16 @@
         restricted = jnp.dot(flat_basis, flat_core, precision=highest)
         squares = jnp.sum(flat_core * flat_core, axis=0)
         carried = jnp.concatenate([restricted, squares[None]], axis=0)
-        gathered = gathered_by_exchange(carried, "gx")
-        column_total = jnp.sum(gathered[:, modes], axis=0)
-        column_coarse = gathered[:, :modes].reshape(rows_x * modes, fields)
-        partial = jnp.dot(coarse_block, column_coarse, precision=highest).reshape(
-            cols_y, modes, fields
+        gathered = gathered_by_exchange(carried, "gy")
+        row_total = jnp.sum(gathered[:, modes], axis=0)
+        row_coarse = gathered[:, :modes].reshape(cols_y * modes, fields)
+        partial = jnp.dot(coarse_block, row_coarse, precision=highest).reshape(
+            rows_x, modes, fields
         )
         partial = jnp.concatenate(
-            [partial, jnp.broadcast_to(column_total, (cols_y, 1, fields))], axis=1
+            [partial, jnp.broadcast_to(row_total, (rows_x, 1, fields))], axis=1
         )
-        reduced = summed_by_exchange(partial, "gy")
+        reduced = summed_by_exchange(partial, "gx")
         coarse_part = reduced[:modes]
         squares_all = reduced[modes]
         prolonged = jnp.dot(flat_basis.T, coarse_part, precision=highest).reshape(

time: 353 us -> 332 us (0.941)
  local copies, waits for them, and re-layouts: 54.8 us -> 41.9 us
  starting transfers between devices: 146 us -> 158 us
  waiting for transfers between devices: 65.6 us -> 54.7 us
  matrix products: 22 us -> 17.5 us
  other arithmetic: 59 us -> 54.5 us
    all_to_all x3, starting transfers between devices: 13.3 us -> 26.7 us  [summed_by_exchange(): received = lax.all_to_all(flat, axis, 0, 0, tiled=True)]
    all_to_all x4, starting transfers between devices: 49.4 us -> 37.8 us  [gathered_by_exchange(): lax.all_to_all(copies, axis, 0, 0, tiled=True)]
    all_to_all x1, starting transfers between devices: 5.18 us -> 13.8 us  [on_device(): pieces = lax.all_to_all(pieces, 'gx', 0, 0, tiled=True)]
    ppermute x6, waiting for transfers between devices: 15.7 us -> 8.08 us  [extended(): lax.ppermute(head, axis, [((i + 1) % count, i) for i in range(ends)])]
    reshape x2 -> x0, local copies, waits for them, and re-layouts: 5.3 us -> none  [the longest x1 2.79 us: on_device(): coarse_block = pieces.reshape(cols_y * modes, rows_x * modes)]
    all_to_all x1, waiting for transfers between devices: 4.19 us -> 0.01 us  [on_device(): pieces = lax.all_to_all(pieces, 'gx', 0, 0, tiled=True)]
    ppermute x4, starting transfers between devices: 13.9 us -> 18 us  [with_edges(): west = lax.ppermute(cells[:, -1:], 'gy', right)]
    all_to_all x2 -> x0, local copies, waits for them, and re-layouts: 3.53 us -> none  [on_device(): pieces = lax.all_to_all(pieces, 'gy', 0, 0, tiled=True)]
  transfers between devices with their start and end apart: 36 -> 36, of which waited for: 14 -> 10; matrix products, arithmetic and copies ran while one was open for 21% -> 21% of each run, Pallas kernels for 0% -> 0%
where the time goes in v6:
time: 332 us; the launch traced here: 328 us
  starting transfers between devices  158 us (48%)
  waiting for transfers between devices  54.7 us (16%)
  other arithmetic  54.5 us (16%)
  local copies, waits for them, and re-layouts  41.9 us (13%)
  matrix products  17.5 us (5%)
    all_to_all x4, starting transfers between devices, gathered_by_exchange(): lax.all_to_all(copies, axis, 0, 0, tiled=True)  37.8 us
    all_to_all x3, starting transfers between devices, summed_by_exchange(): received = lax.all_to_all(flat, axis, 0, 0, tiled=True)  26.7 us
    ppermute x6, starting transfers between devices, extended(): lax.ppermute(tail, axis, [(i, (i + 1) % count) for i in range(ends)])  21.3 us
    all_to_all x3, waiting for transfers between devices, summed_by_exchange(): received = lax.all_to_all(flat, axis, 0, 0, tiled=True)  19 us
    all_to_all x4, waiting for transfers between devices, gathered_by_exchange(): lax.all_to_all(copies, axis, 0, 0, tiled=True)  18.5 us
    ppermute x4, starting transfers between devices, with_edges(): west = lax.ppermute(cells[:, -1:], 'gy', right)  18 us
    ppermute x4, starting transfers between devices, with_edges(): north = lax.ppermute(cells[-1:], 'gx', down)  15 us
    all_to_all x1, starting transfers between devices, on_device(): pieces = lax.all_to_all(pieces, 'gx', 0, 0, tiled=True)  13.8 us
  transfers between devices with their start and end apart: 36, of which 10 were waited for; matrix products, arithmetic and copies ran while one was open for 21% of the time, Pallas kernels for 0%

profile of v6, /device:TPU:1, one launch (start us, length us, event | category | flops | bytes accessed | tf_op | source)
XLA Modules:
  0.0 328.5 jit_solution(13652060757608253566)
XLA Ops:
  2.0 5.4 %collective-permute-start.6 = (f32[1,32]{1,0:T(1,128)}, f32[1,32]{1,0:T(1,128)}, u32[]{:S(2)}, u32[]{:S(2)}) collective-permute-start(f32[1,32]{1,0:T(1,128)} %get-tuple-element.41), channel_id=1, source_target_pairs={{0,16},{16,32},{32,48},{48,64},{64,80},{80,96},{96,112},{112,128},... | collective-permute-start | bytes 392 | tf_op jit(solution)/shard_map/ppermute | solution.py:39
  10.2 5.3 %collective-permute-start.8 = (f32[32,1]{1,0:T(8,128)}, f32[32,1]{1,0:T(8,128)}, u32[]{:S(2)}, u32[]{:S(2)}) collective-permute-start(f32[32,1]{1,0:T(8,128)} %get-tuple-element.39), channel_id=1, source_target_pairs={{1,0},{2,1},{3,2},{4,3},{5,4},{6,5},{7,6},{8,7},{9,8},{10,9},{11,1... | collective-permute-start | bytes 392 | tf_op jit(solution)/shard_map/ppermute | solution.py:42
  15.5 2.5 multiply_reduce_fusion.2
  19.6 4.9 %all-to-all-start = ((f32[16,1,1728]{2,1,0:T(1,128)}), f32[16,1,1728]{2,1,0:T(1,128)S(1)}, u32[]{:S(2)}, u32[]{:S(2)}) async-start(f32[16,1,1728]{2,1,0:T(1,128)} %broadcast_in_dim.28), calls=%async_computation | async-start | bytes 229376 | tf_op jit(solution)/shard_map/all_to_all | solution.py:72
  26.0 4.9 %collective-permute-start = (bf16[4,32,192]{2,1,0:T(8,128)(2,1)}, bf16[4,32,192]{2,1,0:T(8,128)(2,1)}, u32[]{:S(2)}, u32[]{:S(2)}) collective-permute-start(bf16[4,32,192]{2,1,0:T(8,128)(2,1)} %get-tuple-element.33), channel_id=1, source_target_pairs={{0,16},{16,32},{32,48},{48,64},{64,80},{80,96},{96,112},{112,128},... | collective-permute-start | bytes 147464 | tf_op jit(solution)/shard_map/ppermute | solution.py:23
  33.9 13.8 %all-to-all-start.1 = ((f32[32,8,128]{2,1,0:T(8,128)}), f32[32,8,128]{2,1,0:T(8,128)S(1)}, u32[]{:S(2)}, u32[]{:S(2)}) async-start(f32[32,8,128]{2,1,0:T(8,128)} %bitcast.102), calls=%async_computation.1 | async-start | bytes 262144 | tf_op jit(solution)/shard_map/all_to_all | solution.py:101
  50.8 3.6 %collective-permute-start.2 = (bf16[40,4,192]{2,1,0:T(4,128)(2,1)}, bf16[40,4,192]{2,1,0:T(4,128)(2,1)}, u32[]{:S(2)}, u32[]{:S(2)}) collective-permute-start(bf16[40,4,192]{2,1,0:T(4,128)(2,1)} %get-tuple-element.27), channel_id=1, source_target_pairs={{0,1},{1,2},{2,3},{3,4},{4,5},{5,6},{6,7},{7,8},{8,9},{9,10},{10,1... | collective-permute-start | bytes 184328 | tf_op jit(solution)/shard_map/ppermute | solution.py:23
  54.4 1.9 collective-permute-start.3
  60.8 2.0 convolution_bitcast_fusion.5
  66.4 2.0 all_to_all.48
  68.5 9.6 %all-to-all-start.2 = ((f32[32,1,1728]{2,1,0:T(1,128)}), f32[32,1,1728]{2,1,0:T(1,128)}, u32[]{:S(2)}, u32[]{:S(2)}) async-start(f32[32,1,1728]{2,1,0:T(1,128)} %all_to_all.48), calls=%async_computation.2 | async-start | bytes 458752 | tf_op jit(solution)/shard_map/all_to_all | solution.py:78
  78.1 3.9 %collective-permute-start.10 = (f32[32,1]{1,0:T(8,128)}, f32[32,1]{1,0:T(8,128)}, u32[]{:S(2)}, u32[]{:S(2)}) collective-permute-start(f32[32,1]{1,0:T(8,128)} %get-tuple-element.40), channel_id=1, source_target_pairs={{0,1},{1,2},{2,3},{3,4},{4,5},{5,6},{6,7},{7,8},{8,9},{9,10},{10,1... | collective-permute-start | bytes 392 | tf_op jit(solution)/shard_map/ppermute | solution.py:41
  85.4 3.9 %all-to-all-done.2 = f32[32,1,1728]{2,1,0:T(1,128)} async-done(((f32[32,1,1728]{2,1,0:T(1,128)}), f32[32,1,1728]{2,1,0:T(1,128)}, u32[]{:S(2)}, u32[]{:S(2)}) %all-to-all-start.2) | async-done | bytes 221216 | tf_op jit(solution)/shard_map/all_to_all | solution.py:78
  92.1 2.1 add.98
  94.2 2.5 copy.53
  100.2 4.5 %collective-permute-start.11 = (f32[32,1,192]{2,1,0:T(1,128)S(1)}, f32[32,1,192]{2,1,0:T(1,128)S(1)}, u32[]{:S(2)}, u32[]{:S(2)}) collective-permute-start(f32[32,1,192]{2,1,0:T(1,128)S(1)} %get-tuple-element.18), channel_id=1, source_target_pairs={{0,1},{1,2},{2,3},{3,4},{4,5},{5,6},{6,7},{7,8},{8,9},{9,10},{10,1... | collective-permute-start | bytes 73736 | tf_op jit(solution)/shard_map/ppermute | solution.py:41
  104.8 3.2 collective-permute-start.7
  110.2 2.4 collective-permute-done.5
  119.7 7.9 %all-to-all-start.3 = ((f32[16,1,1728]{2,1,0:T(1,128)}), f32[16,1,1728]{2,1,0:T(1,128)}, u32[]{:S(2)}, u32[]{:S(2)}) async-start(f32[16,1,1728]{2,1,0:T(1,128)} %broadcast_in_dim.32), calls=%async_computation.3 | async-start | bytes 229376 | tf_op jit(solution)/shard_map/all_to_all | solution.py:72
  131.6 4.1 %collective-permute-done.13 = bf16[4,32,192]{2,1,0:T(8,128)(2,1)S(1)} collective-permute-done((bf16[4,32,192]{2,1,0:T(8,128)(2,1)S(1)}, bf16[4,32,192]{2,1,0:T(8,128)(2,1)S(1)}, u32[]{:S(2)}, u32[]{:S(2)}) %collective-permute-start.13) | collective-permute-done | bytes 49184 | tf_op jit(solution)/shard_map/ppermute | solution.py:25
  137.4 4.6 %collective-permute-start.14 = (bf16[40,4,192]{2,1,0:T(4,128)(2,1)}, bf16[40,4,192]{2,1,0:T(4,128)(2,1)}, u32[]{:S(2)}, u32[]{:S(2)}) collective-permute-start(bf16[40,4,192]{2,1,0:T(4,128)(2,1)} %get-tuple-element.25), channel_id=1, source_target_pairs={{0,1},{1,2},{2,3},{3,4},{4,5},{5,6},{6,7},{7,8},{8,9},{9,10},{10,1... | collective-permute-start | bytes 184328 | tf_op jit(solution)/shard_map/ppermute | solution.py:23
  142.0 1.9 collective-permute-start.15
  148.9 2.0 convolution_bitcast_fusion.4
  155.2 2.0 all_to_all.49
  157.2 8.7 %all-to-all-start.4 = ((f32[32,1,1728]{2,1,0:T(1,128)}), f32[32,1,1728]{2,1,0:T(1,128)}, u32[]{:S(2)}, u32[]{:S(2)}) async-start(f32[32,1,1728]{2,1,0:T(1,128)} %all_to_all.49), calls=%async_computation.4 | async-start | bytes 458752 | tf_op jit(solution)/shard_map/all_to_all | solution.py:78
  169.3 7.4 %all-to-all-done.4 = f32[32,1,1728]{2,1,0:T(1,128)} async-done(((f32[32,1,1728]{2,1,0:T(1,128)}), f32[32,1,1728]{2,1,0:T(1,128)}, u32[]{:S(2)}, u32[]{:S(2)}) %all-to-all-start.4) | async-done | bytes 221216 | tf_op jit(solution)/shard_map/all_to_all | solution.py:78
  181.4 2.1 add_multiply_fusion.1
  183.6 2.5 copy.57
  187.9 1.9 collective-permute-start.18
  189.9 4.8 %collective-permute-start.19 = (f32[32,1,192]{2,1,0:T(1,128)S(1)}, f32[32,1,192]{2,1,0:T(1,128)S(1)}, u32[]{:S(2)}, u32[]{:S(2)}) collective-permute-start(f32[32,1,192]{2,1,0:T(1,128)S(1)} %get-tuple-element.14), channel_id=1, source_target_pairs={{0,1},{1,2},{2,3},{3,4},{4,5},{5,6},{6,7},{7,8},{8,9},{9,10},{10,1... | collective-permute-start | bytes 73736 | tf_op jit(solution)/shard_map/ppermute | solution.py:41
  194.6 3.2 collective-permute-start.17
  199.2 3.3 %collective-permute-done.16 = f32[1,32,192]{2,1,0:T(8,128)S(1)} collective-permute-done((f32[1,32,192]{2,1,0:T(8,128)S(1)}, f32[1,32,192]{2,1,0:T(8,128)S(1)}, u32[]{:S(2)}, u32[]{:S(2)}) %collective-permute-start.16) | collective-permute-done | bytes 24608 | tf_op jit(solution)/shard_map/ppermute | solution.py:40
  206.9 7.9 %all-to-all-start.5 = ((f32[16,1,1728]{2,1,0:T(1,128)}), f32[16,1,1728]{2,1,0:T(1,128)S(1)}, u32[]{:S(2)}, u32[]{:S(2)}) async-start(f32[16,1,1728]{2,1,0:T(1,128)} %broadcast_in_dim.70), calls=%async_computation.5 | async-start | bytes 229376 | tf_op jit(solution)/shard_map/all_to_all | solution.py:72
  218.8 4.0 %collective-permute-done.21 = bf16[4,32,192]{2,1,0:T(8,128)(2,1)S(1)} collective-permute-done((bf16[4,32,192]{2,1,0:T(8,128)(2,1)S(1)}, bf16[4,32,192]{2,1,0:T(8,128)(2,1)S(1)}, u32[]{:S(2)}, u32[]{:S(2)}) %collective-permute-start.21) | collective-permute-done | bytes 49184 | tf_op jit(solution)/shard_map/ppermute | solution.py:25
  224.6 4.7 %collective-permute-start.22 = (bf16[40,4,192]{2,1,0:T(4,128)(2,1)}, bf16[40,4,192]{2,1,0:T(4,128)(2,1)}, u32[]{:S(2)}, u32[]{:S(2)}) collective-permute-start(bf16[40,4,192]{2,1,0:T(4,128)(2,1)} %get-tuple-element.23), channel_id=1, source_target_pairs={{0,1},{1,2},{2,3},{3,4},{4,5},{5,6},{6,7},{7,8},{8,9},{9,10},{10,1... | collective-permute-start | bytes 184328 | tf_op jit(solution)/shard_map/ppermute | solution.py:23
  229.3 1.9 collective-permute-start.23
  235.3 2.0 convolution_bitcast_fusion.3
  239.9 2.0 all_to_all.50
  242.0 8.4 %all-to-all-start.6 = ((f32[32,1,1728]{2,1,0:T(1,128)}), f32[32,1,1728]{2,1,0:T(1,128)S(1)}, u32[]{:S(2)}, u32[]{:S(2)}) async-start(f32[32,1,1728]{2,1,0:T(1,128)} %all_to_all.50), calls=%async_computation.6 | async-start | bytes 458752 | tf_op jit(solution)/shard_map/all_to_all | solution.py:78
  253.8 7.6 %all-to-all-done.6 = f32[32,1,1728]{2,1,0:T(1,128)S(1)} async-done(((f32[32,1,1728]{2,1,0:T(1,128)}), f32[32,1,1728]{2,1,0:T(1,128)S(1)}, u32[]{:S(2)}, u32[]{:S(2)}) %all-to-all-start.6) | async-done | bytes 221216 | tf_op jit(solution)/shard_map/all_to_all | solution.py:78
  263.7 2.2 add_multiply_fusion
  265.9 2.4 copy.61
  268.4 3.3 %multiply_add_fusion = (f32[32,32,192]{2,1,0:T(8,128)S(1)}, f32[32,32,192]{2,1,0:T(8,128)}) fusion(f32[32,32,192]{2,1,0:T(8,128)} %bitcast.94, f32[32,32,192]{2,1,0:T(8,128)} %copy-done.6, f32[1024,192]{1,0:T(8,128)} %copy.53), kind=kLoop, calls=%fused_computation.92 | loop fusion | flops 983040 | bytes 3932160 | tf_op jit(solution)/shard_map/add | solution.py:148
  273.7 4.8 %collective-permute-start.27 = (f32[32,1,192]{2,1,0:T(1,128)S(1)}, f32[32,1,192]{2,1,0:T(1,128)S(1)}, u32[]{:S(2)}, u32[]{:S(2)}) collective-permute-start(f32[32,1,192]{2,1,0:T(1,128)S(1)} %get-tuple-element.10), channel_id=1, source_target_pairs={{0,1},{1,2},{2,3},{3,4},{4,5},{5,6},{6,7},{7,8},{8,9},{9,10},{10,1... | collective-permute-start | bytes 73736 | tf_op jit(solution)/shard_map/ppermute | solution.py:41
  278.5 3.2 collective-permute-start.25
  283.0 3.3 %collective-permute-done.24 = f32[1,32,192]{2,1,0:T(8,128)S(1)} collective-permute-done((f32[1,32,192]{2,1,0:T(8,128)S(1)}, f32[1,32,192]{2,1,0:T(8,128)S(1)}, u32[]{:S(2)}, u32[]{:S(2)}) %collective-permute-start.24) | collective-permute-done | bytes 24608 | tf_op jit(solution)/shard_map/ppermute | solution.py:40
  289.2 17.1 %all-to-all-start.7 = ((f32[512,1,192]{2,1,0:T(1,128)}), f32[512,1,192]{2,1,0:T(1,128)}, u32[]{:S(2)}, u32[]{:S(2)}) async-start(f32[512,1,192]{2,1,0:T(1,128)} %broadcast_in_dim.72), calls=%async_computation.7 | async-start | bytes 1048576 | tf_op jit(solution)/shard_map/all_to_all | solution.py:72
  308.9 17.4 %all-to-all-done.7 = f32[512,1,192]{2,1,0:T(1,128)} async-done(((f32[512,1,192]{2,1,0:T(1,128)}), f32[512,1,192]{2,1,0:T(1,128)}, u32[]{:S(2)}, u32[]{:S(2)}) %all-to-all-start.7) | async-done | bytes 393248 | tf_op jit(solution)/shard_map/all_to_all | solution.py:72
  (175 shorter events, 99.7 us)
Async XLA Ops:
  0.6 83.0 %copy-start = (bf16[1,1,1024,1600]{2,3,1,0:T(8,128)(2,1)S(1)}, bf16[1,1,1024,1600]{2,3,1,0:T(8,128)(2,1)}, u32[]{:S(2)}) copy-start(bf16[1,1,1024,1600]{2,3,1,0:T(8,128)(2,1)} %param.10) | copy-start | bytes 9830404
  0.6 17.4 %copy-start.7 = (f32[32,32,192]{2,1,0:T(8,128)S(1)}, f32[32,32,192]{2,1,0:T(8,128)}, u32[]{:S(2)}) copy-start(f32[32,32,192]{2,1,0:T(8,128)} %param.6) | copy-start | bytes 2359300
  0.7 17.4 %copy-start.9 = (f32[8,32,32]{2,1,0:T(8,128)S(1)}, f32[8,32,32]{2,1,0:T(8,128)}, u32[]{:S(2)}) copy-start(f32[8,32,32]{2,1,0:T(8,128)} %param.9) | copy-start | bytes 98308
  2.0 98.1 %collective-permute-start.6 = (f32[1,32]{1,0:T(1,128)}, f32[1,32]{1,0:T(1,128)}, u32[]{:S(2)}, u32[]{:S(2)}) collective-permute-start(f32[1,32]{1,0:T(1,128)} %get-tuple-element.41), channel_id=1, source_target_pairs={{0,16},{16,32},{32,48},{48,64},{64,80},{80,96},{96,112},{112,128},... | collective-permute-start | bytes 392 | tf_op jit(solution)/shard_map/ppermute | solution.py:39
  7.4 97.3 %collective-permute-start.4 = (f32[1,32]{1,0:T(1,128)}, f32[1,32]{1,0:T(1,128)}, u32[]{:S(2)}, u32[]{:S(2)}) collective-permute-start(f32[1,32]{1,0:T(1,128)} %get-tuple-element.42), channel_id=1, source_target_pairs={{16,0},{32,16},{48,32},{64,48},{80,64},{96,80},{112,96},{128,112},... | collective-permute-start | bytes 392 | tf_op jit(solution)/shard_map/ppermute | solution.py:40
  10.2 37.5 %copy-start.26 = (f32[32,32]{1,0:T(8,128)S(1)}, f32[32,32]{1,0:T(8,128)}, u32[]{:S(2)}) copy-start(f32[32,32]{1,0:T(8,128)} %param.8) | copy-start | bytes 12292
  10.2 97.8 %collective-permute-start.8 = (f32[32,1]{1,0:T(8,128)}, f32[32,1]{1,0:T(8,128)}, u32[]{:S(2)}, u32[]{:S(2)}) collective-permute-start(f32[32,1]{1,0:T(8,128)} %get-tuple-element.39), channel_id=1, source_target_pairs={{1,0},{2,1},{3,2},{4,3},{5,4},{6,5},{7,6},{8,7},{9,8},{10,9},{11,1... | collective-permute-start | bytes 392 | tf_op jit(solution)/shard_map/ppermute | solution.py:42
  19.6 13.7 %all-to-all-start = ((f32[16,1,1728]{2,1,0:T(1,128)}), f32[16,1,1728]{2,1,0:T(1,128)S(1)}, u32[]{:S(2)}, u32[]{:S(2)}) async-start(f32[16,1,1728]{2,1,0:T(1,128)} %broadcast_in_dim.28), calls=%async_computation | async-start | bytes 229376 | tf_op jit(solution)/shard_map/all_to_all | solution.py:72
  26.0 23.0 %collective-permute-start = (bf16[4,32,192]{2,1,0:T(8,128)(2,1)}, bf16[4,32,192]{2,1,0:T(8,128)(2,1)}, u32[]{:S(2)}, u32[]{:S(2)}) collective-permute-start(bf16[4,32,192]{2,1,0:T(8,128)(2,1)} %get-tuple-element.33), channel_id=1, source_target_pairs={{0,16},{16,32},{32,48},{48,64},{64,80},{80,96},{96,112},{112,128},... | collective-permute-start | bytes 147464 | tf_op jit(solution)/shard_map/ppermute | solution.py:23
  30.9 18.1 %collective-permute-start.1 = (bf16[4,32,192]{2,1,0:T(8,128)(2,1)}, bf16[4,32,192]{2,1,0:T(8,128)(2,1)}, u32[]{:S(2)}, u32[]{:S(2)}) collective-permute-start(bf16[4,32,192]{2,1,0:T(8,128)(2,1)} %get-tuple-element.34), channel_id=1, source_target_pairs={{16,0},{32,16},{48,32},{64,48},{80,64},{96,80},{112,96},{128,112},... | collective-permute-start | bytes 147464 | tf_op jit(solution)/shard_map/ppermute | solution.py:25
  33.9 26.9 %all-to-all-start.1 = ((f32[32,8,128]{2,1,0:T(8,128)}), f32[32,8,128]{2,1,0:T(8,128)S(1)}, u32[]{:S(2)}, u32[]{:S(2)}) async-start(f32[32,8,128]{2,1,0:T(8,128)} %bitcast.102), calls=%async_computation.1 | async-start | bytes 262144 | tf_op jit(solution)/shard_map/all_to_all | solution.py:101
  50.8 27.3 %collective-permute-start.2 = (bf16[40,4,192]{2,1,0:T(4,128)(2,1)}, bf16[40,4,192]{2,1,0:T(4,128)(2,1)}, u32[]{:S(2)}, u32[]{:S(2)}) collective-permute-start(bf16[40,4,192]{2,1,0:T(4,128)(2,1)} %get-tuple-element.27), channel_id=1, source_target_pairs={{0,1},{1,2},{2,3},{3,4},{4,5},{5,6},{6,7},{7,8},{8,9},{9,10},{10,1... | collective-permute-start | bytes 184328 | tf_op jit(solution)/shard_map/ppermute | solution.py:23
  54.4 27.6 %collective-permute-start.3 = (bf16[40,4,192]{2,1,0:T(4,128)(2,1)}, bf16[40,4,192]{2,1,0:T(4,128)(2,1)}, u32[]{:S(2)}, u32[]{:S(2)}) collective-permute-start(bf16[40,4,192]{2,1,0:T(4,128)(2,1)} %get-tuple-element.28), channel_id=1, source_target_pairs={{1,0},{2,1},{3,2},{4,3},{5,4},{6,5},{7,6},{8,7},{9,8},{10,9},{11,1... | collective-permute-start | bytes 184328 | tf_op jit(solution)/shard_map/ppermute | solution.py:25
  68.5 20.9 %all-to-all-start.2 = ((f32[32,1,1728]{2,1,0:T(1,128)}), f32[32,1,1728]{2,1,0:T(1,128)}, u32[]{:S(2)}, u32[]{:S(2)}) async-start(f32[32,1,1728]{2,1,0:T(1,128)} %all_to_all.48), calls=%async_computation.2 | async-start | bytes 458752 | tf_op jit(solution)/shard_map/all_to_all | solution.py:78
  78.1 31.2 %collective-permute-start.10 = (f32[32,1]{1,0:T(8,128)}, f32[32,1]{1,0:T(8,128)}, u32[]{:S(2)}, u32[]{:S(2)}) collective-permute-start(f32[32,1]{1,0:T(8,128)} %get-tuple-element.40), channel_id=1, source_target_pairs={{0,1},{1,2},{2,3},{3,4},{4,5},{5,6},{6,7},{7,8},{8,9},{9,10},{10,1... | collective-permute-start | bytes 392 | tf_op jit(solution)/shard_map/ppermute | solution.py:41
  98.3 11.9 %collective-permute-start.9 = (f32[32,1,192]{2,1,0:T(1,128)S(1)}, f32[32,1,192]{2,1,0:T(1,128)S(1)}, u32[]{:S(2)}, u32[]{:S(2)}) collective-permute-start(f32[32,1,192]{2,1,0:T(1,128)S(1)} %get-tuple-element.17), channel_id=1, source_target_pairs={{1,0},{2,1},{3,2},{4,3},{5,4},{6,5},{7,6},{8,7},{9,8},{10,9},{11,1... | collective-permute-start | bytes 73736 | tf_op jit(solution)/shard_map/ppermute | solution.py:42
  100.2 10.0 %collective-permute-start.11 = (f32[32,1,192]{2,1,0:T(1,128)S(1)}, f32[32,1,192]{2,1,0:T(1,128)S(1)}, u32[]{:S(2)}, u32[]{:S(2)}) collective-permute-start(f32[32,1,192]{2,1,0:T(1,128)S(1)} %get-tuple-element.18), channel_id=1, source_target_pairs={{0,1},{1,2},{2,3},{3,4},{4,5},{5,6},{6,7},{7,8},{8,9},{9,10},{10,1... | collective-permute-start | bytes 73736 | tf_op jit(solution)/shard_map/ppermute | solution.py:41
  104.8 5.5 %collective-permute-start.7 = (f32[1,32,192]{2,1,0:T(8,128)S(1)}, f32[1,32,192]{2,1,0:T(8,128)S(1)}, u32[]{:S(2)}, u32[]{:S(2)}) collective-permute-start(f32[1,32,192]{2,1,0:T(8,128)S(1)} %get-tuple-element.19), channel_id=1, source_target_pairs={{0,16},{16,32},{32,48},{48,64},{64,80},{80,96},{96,112},{112,128},... | collective-permute-start | bytes 73736 | tf_op jit(solution)/shard_map/ppermute | solution.py:39
  108.0 4.7 %collective-permute-start.5 = (f32[1,32,192]{2,1,0:T(8,128)S(1)}, f32[1,32,192]{2,1,0:T(8,128)S(1)}, u32[]{:S(2)}, u32[]{:S(2)}) collective-permute-start(f32[1,32,192]{2,1,0:T(8,128)S(1)} %get-tuple-element.20), channel_id=1, source_target_pairs={{16,0},{32,16},{48,32},{64,48},{80,64},{96,80},{112,96},{128,112},... | collective-permute-start | bytes 73736 | tf_op jit(solution)/shard_map/ppermute | solution.py:40
  119.7 24.2 %all-to-all-start.3 = ((f32[16,1,1728]{2,1,0:T(1,128)}), f32[16,1,1728]{2,1,0:T(1,128)}, u32[]{:S(2)}, u32[]{:S(2)}) async-start(f32[16,1,1728]{2,1,0:T(1,128)} %broadcast_in_dim.32), calls=%async_computation.3 | async-start | bytes 229376 | tf_op jit(solution)/shard_map/all_to_all | solution.py:72
  128.5 3.1 collective-permute-start.12
  130.3 5.4 %collective-permute-start.13 = (bf16[4,32,192]{2,1,0:T(8,128)(2,1)S(1)}, bf16[4,32,192]{2,1,0:T(8,128)(2,1)S(1)}, u32[]{:S(2)}, u32[]{:S(2)}) collective-permute-start(bf16[4,32,192]{2,1,0:T(8,128)(2,1)S(1)} %get-tuple-element.32), channel_id=1, source_target_pairs={{16,0},{32,16},{48,32},{64,48},{80,64},{96,80},{112,96},{128,112},... | collective-permute-start | bytes 147464 | tf_op jit(solution)/shard_map/ppermute | solution.py:25
  137.4 28.5 %collective-permute-start.14 = (bf16[40,4,192]{2,1,0:T(4,128)(2,1)}, bf16[40,4,192]{2,1,0:T(4,128)(2,1)}, u32[]{:S(2)}, u32[]{:S(2)}) collective-permute-start(bf16[40,4,192]{2,1,0:T(4,128)(2,1)} %get-tuple-element.25), channel_id=1, source_target_pairs={{0,1},{1,2},{2,3},{3,4},{4,5},{5,6},{6,7},{7,8},{8,9},{9,10},{10,1... | collective-permute-start | bytes 184328 | tf_op jit(solution)/shard_map/ppermute | solution.py:23
  142.0 24.0 %collective-permute-start.15 = (bf16[40,4,192]{2,1,0:T(4,128)(2,1)}, bf16[40,4,192]{2,1,0:T(4,128)(2,1)}, u32[]{:S(2)}, u32[]{:S(2)}) collective-permute-start(bf16[40,4,192]{2,1,0:T(4,128)(2,1)} %get-tuple-element.26), channel_id=1, source_target_pairs={{1,0},{2,1},{3,2},{4,3},{5,4},{6,5},{7,6},{8,7},{9,8},{10,9},{11,1... | collective-permute-start | bytes 184328 | tf_op jit(solution)/shard_map/ppermute | solution.py:25
  157.2 19.5 %all-to-all-start.4 = ((f32[32,1,1728]{2,1,0:T(1,128)}), f32[32,1,1728]{2,1,0:T(1,128)}, u32[]{:S(2)}, u32[]{:S(2)}) async-start(f32[32,1,1728]{2,1,0:T(1,128)} %all_to_all.49), calls=%async_computation.4 | async-start | bytes 458752 | tf_op jit(solution)/shard_map/all_to_all | solution.py:78
  186.0 16.5 %copy-start.16 = (f32[32,32]{1,0:T(8,128)S(1)}, f32[32,32]{1,0:T(8,128)}, u32[]{:S(2)}) copy-start(f32[32,32]{1,0:T(8,128)} %copy-done.15) | copy-start | bytes 12292
  186.0 16.5 %copy-start.19 = (f32[32,32]{1,0:T(8,128)S(1)}, f32[32,32]{1,0:T(8,128)}, u32[]{:S(2)}) copy-start(f32[32,32]{1,0:T(8,128)} %copy-done.18) | copy-start | bytes 12292
  186.0 16.5 %copy-start.27 = (f32[32,32]{1,0:T(8,128)S(1)}, f32[32,32]{1,0:T(8,128)}, u32[]{:S(2)}) copy-start(f32[32,32]{1,0:T(8,128)} %param.8) | copy-start | bytes 12292
  187.9 11.2 %collective-permute-start.18 = (f32[32,1,192]{2,1,0:T(1,128)S(1)}, f32[32,1,192]{2,1,0:T(1,128)S(1)}, u32[]{:S(2)}, u32[]{:S(2)}) collective-permute-start(f32[32,1,192]{2,1,0:T(1,128)S(1)} %get-tuple-element.13), channel_id=1, source_target_pairs={{1,0},{2,1},{3,2},{4,3},{5,4},{6,5},{7,6},{8,7},{9,8},{10,9},{11,1... | collective-permute-start | bytes 73736 | tf_op jit(solution)/shard_map/ppermute | solution.py:42
  189.9 9.3 %collective-permute-start.19 = (f32[32,1,192]{2,1,0:T(1,128)S(1)}, f32[32,1,192]{2,1,0:T(1,128)S(1)}, u32[]{:S(2)}, u32[]{:S(2)}) collective-permute-start(f32[32,1,192]{2,1,0:T(1,128)S(1)} %get-tuple-element.14), channel_id=1, source_target_pairs={{0,1},{1,2},{2,3},{3,4},{4,5},{5,6},{6,7},{7,8},{8,9},{9,10},{10,1... | collective-permute-start | bytes 73736 | tf_op jit(solution)/shard_map/ppermute | solution.py:41
  194.6 4.5 %collective-permute-start.17 = (f32[1,32,192]{2,1,0:T(8,128)S(1)}, f32[1,32,192]{2,1,0:T(8,128)S(1)}, u32[]{:S(2)}, u32[]{:S(2)}) collective-permute-start(f32[1,32,192]{2,1,0:T(8,128)S(1)} %get-tuple-element.15), channel_id=1, source_target_pairs={{0,16},{16,32},{32,48},{48,64},{64,80},{80,96},{96,112},{112,128},... | collective-permute-start | bytes 73736 | tf_op jit(solution)/shard_map/ppermute | solution.py:39
  197.8 4.7 %collective-permute-start.16 = (f32[1,32,192]{2,1,0:T(8,128)S(1)}, f32[1,32,192]{2,1,0:T(8,128)S(1)}, u32[]{:S(2)}, u32[]{:S(2)}) collective-permute-start(f32[1,32,192]{2,1,0:T(8,128)S(1)} %get-tuple-element.16), channel_id=1, source_target_pairs={{16,0},{32,16},{48,32},{64,48},{80,64},{96,80},{112,96},{128,112},... | collective-permute-start | bytes 73736 | tf_op jit(solution)/shard_map/ppermute | solution.py:40
  206.9 24.3 %all-to-all-start.5 = ((f32[16,1,1728]{2,1,0:T(1,128)}), f32[16,1,1728]{2,1,0:T(1,128)S(1)}, u32[]{:S(2)}, u32[]{:S(2)}) async-start(f32[16,1,1728]{2,1,0:T(1,128)} %broadcast_in_dim.70), calls=%async_computation.5 | async-start | bytes 229376 | tf_op jit(solution)/shard_map/all_to_all | solution.py:72
  215.8 3.1 collective-permute-start.20
  217.5 5.3 %collective-permute-start.21 = (bf16[4,32,192]{2,1,0:T(8,128)(2,1)S(1)}, bf16[4,32,192]{2,1,0:T(8,128)(2,1)S(1)}, u32[]{:S(2)}, u32[]{:S(2)}) collective-permute-start(bf16[4,32,192]{2,1,0:T(8,128)(2,1)S(1)} %get-tuple-element.30), channel_id=1, source_target_pairs={{16,0},{32,16},{48,32},{64,48},{80,64},{96,80},{112,96},{128,112},... | collective-permute-start | bytes 147464 | tf_op jit(solution)/shard_map/ppermute | solution.py:25
  224.6 25.8 %collective-permute-start.22 = (bf16[40,4,192]{2,1,0:T(4,128)(2,1)}, bf16[40,4,192]{2,1,0:T(4,128)(2,1)}, u32[]{:S(2)}, u32[]{:S(2)}) collective-permute-start(bf16[40,4,192]{2,1,0:T(4,128)(2,1)} %get-tuple-element.23), channel_id=1, source_target_pairs={{0,1},{1,2},{2,3},{3,4},{4,5},{5,6},{6,7},{7,8},{8,9},{9,10},{10,1... | collective-permute-start | bytes 184328 | tf_op jit(solution)/shard_map/ppermute | solution.py:23
  229.3 21.1 %collective-permute-start.23 = (bf16[40,4,192]{2,1,0:T(4,128)(2,1)}, bf16[40,4,192]{2,1,0:T(4,128)(2,1)}, u32[]{:S(2)}, u32[]{:S(2)}) collective-permute-start(bf16[40,4,192]{2,1,0:T(4,128)(2,1)} %get-tuple-element.24), channel_id=1, source_target_pairs={{1,0},{2,1},{3,2},{4,3},{5,4},{6,5},{7,6},{8,7},{9,8},{10,9},{11,1... | collective-permute-start | bytes 184328 | tf_op jit(solution)/shard_map/ppermute | solution.py:25
  242.0 19.4 %all-to-all-start.6 = ((f32[32,1,1728]{2,1,0:T(1,128)}), f32[32,1,1728]{2,1,0:T(1,128)S(1)}, u32[]{:S(2)}, u32[]{:S(2)}) async-start(f32[32,1,1728]{2,1,0:T(1,128)} %all_to_all.50), calls=%async_computation.6 | async-start | bytes 458752 | tf_op jit(solution)/shard_map/all_to_all | solution.py:78
  268.3 18.0 %copy-start.5 = (f32[32,32,192]{2,1,0:T(8,128)S(1)}, f32[32,32,192]{2,1,0:T(8,128)}, u32[]{:S(2)}) copy-start(f32[32,32,192]{2,1,0:T(8,128)} %copy-done.4) | copy-start | bytes 2359300
  268.3 18.0 %copy-start.14 = (f32[32,32]{1,0:T(8,128)S(1)}, f32[32,32]{1,0:T(8,128)}, u32[]{:S(2)}) copy-start(f32[32,32]{1,0:T(8,128)} %copy-done.12) | copy-start | bytes 12292
  268.3 18.0 %copy-start.17 = (f32[32,32]{1,0:T(8,128)S(1)}, f32[32,32]{1,0:T(8,128)}, u32[]{:S(2)}) copy-start(f32[32,32]{1,0:T(8,128)} %copy-done.15) | copy-start | bytes 12292
  268.3 18.0 %copy-start.20 = (f32[32,32]{1,0:T(8,128)S(1)}, f32[32,32]{1,0:T(8,128)}, u32[]{:S(2)}) copy-start(f32[32,32]{1,0:T(8,128)} %copy-done.18) | copy-start | bytes 12292
  268.4 18.0 %copy-start.28 = (f32[32,32]{1,0:T(8,128)S(1)}, f32[32,32]{1,0:T(8,128)}, u32[]{:S(2)}) copy-start(f32[32,32]{1,0:T(8,128)} %param.8) | copy-start | bytes 12292
  271.8 11.2 %collective-permute-start.26 = (f32[32,1,192]{2,1,0:T(1,128)S(1)}, f32[32,1,192]{2,1,0:T(1,128)S(1)}, u32[]{:S(2)}, u32[]{:S(2)}) collective-permute-start(f32[32,1,192]{2,1,0:T(1,128)S(1)} %get-tuple-element.9), channel_id=1, source_target_pairs={{1,0},{2,1},{3,2},{4,3},{5,4},{6,5},{7,6},{8,7},{9,8},{10,9},{11,1... | collective-permute-start | bytes 73736 | tf_op jit(solution)/shard_map/ppermute | solution.py:42
  273.7 9.3 %collective-permute-start.27 = (f32[32,1,192]{2,1,0:T(1,128)S(1)}, f32[32,1,192]{2,1,0:T(1,128)S(1)}, u32[]{:S(2)}, u32[]{:S(2)}) collective-permute-start(f32[32,1,192]{2,1,0:T(1,128)S(1)} %get-tuple-element.10), channel_id=1, source_target_pairs={{0,1},{1,2},{2,3},{3,4},{4,5},{5,6},{6,7},{7,8},{8,9},{9,10},{10,1... | collective-permute-start | bytes 73736 | tf_op jit(solution)/shard_map/ppermute | solution.py:41
  278.5 4.5 %collective-permute-start.25 = (f32[1,32,192]{2,1,0:T(8,128)S(1)}, f32[1,32,192]{2,1,0:T(8,128)S(1)}, u32[]{:S(2)}, u32[]{:S(2)}) collective-permute-start(f32[1,32,192]{2,1,0:T(8,128)S(1)} %get-tuple-element.11), channel_id=1, source_target_pairs={{0,16},{16,32},{32,48},{48,64},{64,80},{80,96},{96,112},{112,128},... | collective-permute-start | bytes 73736 | tf_op jit(solution)/shard_map/ppermute | solution.py:39
  281.7 4.7 %collective-permute-start.24 = (f32[1,32,192]{2,1,0:T(8,128)S(1)}, f32[1,32,192]{2,1,0:T(8,128)S(1)}, u32[]{:S(2)}, u32[]{:S(2)}) collective-permute-start(f32[1,32,192]{2,1,0:T(8,128)S(1)} %get-tuple-element.12), channel_id=1, source_target_pairs={{16,0},{32,16},{48,32},{64,48},{80,64},{96,80},{112,96},{128,112},... | collective-permute-start | bytes 73736 | tf_op jit(solution)/shard_map/ppermute | solution.py:40
  289.2 37.1 %all-to-all-start.7 = ((f32[512,1,192]{2,1,0:T(1,128)}), f32[512,1,192]{2,1,0:T(1,128)}, u32[]{:S(2)}, u32[]{:S(2)}) async-start(f32[512,1,192]{2,1,0:T(1,128)} %broadcast_in_dim.72), calls=%async_computation.7 | async-start | bytes 1048576 | tf_op jit(solution)/shard_map/all_to_all | solution.py:72
  (19 other events, 165.0 us)

commit v7 on v6

--- a/solution.py
+++ b/solution.py
@@ -118,16 +118,11 @@
         partial = jnp.dot(coarse_block, row_coarse, precision=highest).reshape(
             rows_x, modes, fields
         )
-        partial = jnp.concatenate(
-            [partial, jnp.broadcast_to(row_total, (rows_x, 1, fields))], axis=1
-        )
-        reduced = summed_by_exchange(partial, "gx")
-        coarse_part = reduced[:modes]
-        squares_all = reduced[modes]
+        coarse_part = summed_by_exchange(partial, "gx")
         prolonged = jnp.dot(flat_basis.T, coarse_part, precision=highest).reshape(
             patch, patch, fields
         )
-        return (local_part + prolonged, squares_all)
+        return (local_part + prolonged, row_total)
 
     centre = 0.5 * (upper_bound + lower_bound)
     half_width = 0.5 * (upper_bound - lower_bound)
@@ -149,8 +144,11 @@
             weight_prev = weight_next
         else:
             flat_state = state.reshape(patch * patch, fields)
-            history.append(total_over_mesh(jnp.sum(flat_state * flat_state, axis=0)))
-    return (solution, jnp.sqrt(jnp.stack(history) / cells), jnp.sqrt(initial / cells))
+            last = jnp.sum(flat_state * flat_state, axis=0)
+            history.append(jnp.sum(gathered_by_exchange(last, "gy"), axis=0))
+    rows = jnp.stack([initial] + history)
+    totals = jnp.sum(gathered_by_exchange(rows, "gx"), axis=0)
+    return (solution, jnp.sqrt(totals[1:] / cells), jnp.sqrt(totals[0] / cells))
 
 
 def solution(mesh):

time: 332 us -> 311 us (0.937)
  blocking collectives: 0 us -> 15.5 us
  waiting for transfers between devices: 54.7 us -> 40 us
  other arithmetic: 54.5 us -> 46 us
  starting transfers between devices: 158 us -> 150 us
  local copies, waits for them, and re-layouts: 41.9 us -> 37.3 us
    all_to_all x0 -> x1, blocking collectives: none -> 15.5 us  [gathered_by_exchange(): lax.all_to_all(copies, axis, 0, 0, tiled=True)]
    all_to_all x4, waiting for transfers between devices: 18.5 us -> 7.49 us  [gathered_by_exchange(): lax.all_to_all(copies, axis, 0, 0, tiled=True)]
    all_to_all x4, starting transfers between devices: 37.8 us -> 29.6 us  [gathered_by_exchange(): lax.all_to_all(copies, axis, 0, 0, tiled=True)]
    concatenate x3 -> x0, other arithmetic: 4.45 us -> none  [precondition(): jnp.concatenate([partial, jnp.broadcast_to(row_total, (rows_x, 1, fields)...]
    slice x5 -> x0, local copies, waits for them, and re-layouts: 3.56 us -> none  [the longest x3 2.2 us: precondition(): coarse_part = reduced[:modes]]
  transfers between devices with their start and end apart: 36 -> 36, of which waited for: 10 -> 10; matrix products, arithmetic and copies ran while one was open for 21% -> 19% of each run, Pallas kernels for 0% -> 0%
where the time goes in v7:
time: 311 us; the launch traced here: 308 us
  starting transfers between devices  150 us (48%)
  other arithmetic  46 us (15%)
  waiting for transfers between devices  40 us (13%)
  local copies, waits for them, and re-layouts  37.3 us (12%)
  matrix products  17.5 us (6%)
  blocking collectives  15.5 us (5%)
    all_to_all x4, starting transfers between devices, gathered_by_exchange(): lax.all_to_all(copies, axis, 0, 0, tiled=True)  29.6 us
    all_to_all x3, starting transfers between devices, summed_by_exchange(): received = lax.all_to_all(flat, axis, 0, 0, tiled=True)  26.6 us
    ppermute x6, starting transfers between devices, extended(): lax.ppermute(tail, axis, [(i, (i + 1) % count) for i in range(ends)])  21.8 us
    all_to_all x3, waiting for transfers between devices, summed_by_exchange(): received = lax.all_to_all(flat, axis, 0, 0, tiled=True)  17.7 us
    ppermute x4, starting transfers between devices, with_edges(): west = lax.ppermute(cells[:, -1:], 'gy', right)  17.6 us
    all_to_all x1, blocking collectives, gathered_by_exchange(): lax.all_to_all(copies, axis, 0, 0, tiled=True)  15.5 us
    ppermute x4, starting transfers between devices, with_edges(): north = lax.ppermute(cells[-1:], 'gx', down)  14.6 us
    all_to_all x1, starting transfers between devices, on_device(): pieces = lax.all_to_all(pieces, 'gx', 0, 0, tiled=True)  13.8 us
  transfers between devices with their start and end apart: 36, of which 10 were waited for; matrix products, arithmetic and copies ran while one was open for 19% of the time, Pallas kernels for 0%

profile of v7, /device:TPU:1, one launch (start us, length us, event | category | flops | bytes accessed | tf_op | source)
XLA Modules:
  0.0 307.7 jit_solution(3049988114377289323)
XLA Ops:
  2.0 5.3 %collective-permute-start.6 = (f32[1,32]{1,0:T(1,128)}, f32[1,32]{1,0:T(1,128)}, u32[]{:S(2)}, u32[]{:S(2)}) collective-permute-start(f32[1,32]{1,0:T(1,128)} %get-tuple-element.41), channel_id=1, source_target_pairs={{0,16},{16,32},{32,48},{48,64},{64,80},{80,96},{96,112},{112,128},... | collective-permute-start | bytes 392 | tf_op jit(solution)/shard_map/ppermute | solution.py:39
  10.1 5.3 %collective-permute-start.8 = (f32[32,1]{1,0:T(8,128)}, f32[32,1]{1,0:T(8,128)}, u32[]{:S(2)}, u32[]{:S(2)}) collective-permute-start(f32[32,1]{1,0:T(8,128)} %get-tuple-element.39), channel_id=1, source_target_pairs={{1,0},{2,1},{3,2},{4,3},{5,4},{6,5},{7,6},{8,7},{9,8},{10,9},{11,1... | collective-permute-start | bytes 392 | tf_op jit(solution)/shard_map/ppermute | solution.py:42
  15.5 2.5 multiply_reduce_fusion.2
  19.6 4.9 %all-to-all-start = ((f32[16,1,1728]{2,1,0:T(1,128)}), f32[16,1,1728]{2,1,0:T(1,128)S(1)}, u32[]{:S(2)}, u32[]{:S(2)}) async-start(f32[16,1,1728]{2,1,0:T(1,128)} %broadcast_in_dim.26), calls=%async_computation | async-start | bytes 229376 | tf_op jit(solution)/shard_map/all_to_all | solution.py:72
  26.0 4.9 %collective-permute-start = (bf16[4,32,192]{2,1,0:T(8,128)(2,1)}, bf16[4,32,192]{2,1,0:T(8,128)(2,1)}, u32[]{:S(2)}, u32[]{:S(2)}) collective-permute-start(bf16[4,32,192]{2,1,0:T(8,128)(2,1)} %get-tuple-element.33), channel_id=1, source_target_pairs={{0,16},{16,32},{32,48},{48,64},{64,80},{80,96},{96,112},{112,128},... | collective-permute-start | bytes 147464 | tf_op jit(solution)/shard_map/ppermute | solution.py:23
  33.9 13.8 %all-to-all-start.1 = ((f32[32,8,128]{2,1,0:T(8,128)}), f32[32,8,128]{2,1,0:T(8,128)S(1)}, u32[]{:S(2)}, u32[]{:S(2)}) async-start(f32[32,8,128]{2,1,0:T(8,128)} %bitcast.94), calls=%async_computation.1 | async-start | bytes 262144 | tf_op jit(solution)/shard_map/all_to_all | solution.py:101
  50.8 3.6 %collective-permute-start.2 = (bf16[40,4,192]{2,1,0:T(4,128)(2,1)}, bf16[40,4,192]{2,1,0:T(4,128)(2,1)}, u32[]{:S(2)}, u32[]{:S(2)}) collective-permute-start(bf16[40,4,192]{2,1,0:T(4,128)(2,1)} %get-tuple-element.27), channel_id=1, source_target_pairs={{0,1},{1,2},{2,3},{3,4},{4,5},{5,6},{6,7},{7,8},{8,9},{9,10},{10,1... | collective-permute-start | bytes 184328 | tf_op jit(solution)/shard_map/ppermute | solution.py:23
  54.5 1.9 collective-permute-start.3
  59.9 2.0 convolution_bitcast_fusion.5
  65.6 9.6 %all-to-all-start.2 = ((f32[32,1,1536]{2,1,0:T(1,128)}), f32[32,1,1536]{2,1,0:T(1,128)}, u32[]{:S(2)}, u32[]{:S(2)}) async-start(f32[32,1,1536]{2,1,0:T(1,128)} %all_to_all.53), calls=%async_computation.2 | async-start | bytes 393216 | tf_op jit(solution)/shard_map/all_to_all | solution.py:78
  75.2 3.9 %collective-permute-start.10 = (f32[32,1]{1,0:T(8,128)}, f32[32,1]{1,0:T(8,128)}, u32[]{:S(2)}, u32[]{:S(2)}) collective-permute-start(f32[32,1]{1,0:T(8,128)} %get-tuple-element.40), channel_id=1, source_target_pairs={{0,1},{1,2},{2,3},{3,4},{4,5},{5,6},{6,7},{7,8},{8,9},{9,10},{10,1... | collective-permute-start | bytes 392 | tf_op jit(solution)/shard_map/ppermute | solution.py:41
  82.5 3.8 %all-to-all-done.2 = f32[32,1,1536]{2,1,0:T(1,128)} async-done(((f32[32,1,1536]{2,1,0:T(1,128)}), f32[32,1,1536]{2,1,0:T(1,128)}, u32[]{:S(2)}, u32[]{:S(2)}) %all-to-all-start.2) | async-done | bytes 196640 | tf_op jit(solution)/shard_map/all_to_all | solution.py:78
  89.0 2.1 add.98
  91.1 2.5 copy.53
  95.1 1.9 collective-permute-start.9
  97.1 4.2 %collective-permute-start.11 = (f32[32,1,192]{2,1,0:T(1,128)S(1)}, f32[32,1,192]{2,1,0:T(1,128)S(1)}, u32[]{:S(2)}, u32[]{:S(2)}) collective-permute-start(f32[32,1,192]{2,1,0:T(1,128)S(1)} %get-tuple-element.18), channel_id=1, source_target_pairs={{0,1},{1,2},{2,3},{3,4},{4,5},{5,6},{6,7},{7,8},{8,9},{9,10},{10,1... | collective-permute-start | bytes 73736 | tf_op jit(solution)/shard_map/ppermute | solution.py:41
  101.2 3.1 %collective-permute-start.7 = (f32[1,32,192]{2,1,0:T(8,128)S(1)}, f32[1,32,192]{2,1,0:T(8,128)S(1)}, u32[]{:S(2)}, u32[]{:S(2)}) collective-permute-start(f32[1,32,192]{2,1,0:T(8,128)S(1)} %get-tuple-element.19), channel_id=1, source_target_pairs={{0,16},{16,32},{32,48},{48,64},{64,80},{80,96},{96,112},{112,128},... | collective-permute-start | bytes 73736 | tf_op jit(solution)/shard_map/ppermute | solution.py:39
  106.6 2.4 collective-permute-done.5
  116.1 8.2 %all-to-all-start.3 = ((f32[16,1,1728]{2,1,0:T(1,128)}), f32[16,1,1728]{2,1,0:T(1,128)}, u32[]{:S(2)}, u32[]{:S(2)}) async-start(f32[16,1,1728]{2,1,0:T(1,128)} %broadcast_in_dim.29), calls=%async_computation.3 | async-start | bytes 229376 | tf_op jit(solution)/shard_map/all_to_all | solution.py:72
  125.2 2.0 collective-permute-start.12
  128.6 4.1 %collective-permute-done.13 = bf16[4,32,192]{2,1,0:T(8,128)(2,1)S(1)} collective-permute-done((bf16[4,32,192]{2,1,0:T(8,128)(2,1)S(1)}, bf16[4,32,192]{2,1,0:T(8,128)(2,1)S(1)}, u32[]{:S(2)}, u32[]{:S(2)}) %collective-permute-start.13) | collective-permute-done | bytes 49184 | tf_op jit(solution)/shard_map/ppermute | solution.py:25
  134.4 4.6 %collective-permute-start.14 = (bf16[40,4,192]{2,1,0:T(4,128)(2,1)}, bf16[40,4,192]{2,1,0:T(4,128)(2,1)}, u32[]{:S(2)}, u32[]{:S(2)}) collective-permute-start(bf16[40,4,192]{2,1,0:T(4,128)(2,1)} %get-tuple-element.25), channel_id=1, source_target_pairs={{0,1},{1,2},{2,3},{3,4},{4,5},{5,6},{6,7},{7,8},{8,9},{9,10},{10,1... | collective-permute-start | bytes 184328 | tf_op jit(solution)/shard_map/ppermute | solution.py:23
  139.0 1.9 collective-permute-start.15
  144.4 2.0 convolution_bitcast_fusion.4
  150.0 8.6 %all-to-all-start.4 = ((f32[32,1,1536]{2,1,0:T(1,128)}), f32[32,1,1536]{2,1,0:T(1,128)}, u32[]{:S(2)}, u32[]{:S(2)}) async-start(f32[32,1,1536]{2,1,0:T(1,128)} %all_to_all.54), calls=%async_computation.4 | async-start | bytes 393216 | tf_op jit(solution)/shard_map/all_to_all | solution.py:78
  162.0 6.9 %all-to-all-done.4 = f32[32,1,1536]{2,1,0:T(1,128)} async-done(((f32[32,1,1536]{2,1,0:T(1,128)}), f32[32,1,1536]{2,1,0:T(1,128)}, u32[]{:S(2)}, u32[]{:S(2)}) %all-to-all-start.4) | async-done | bytes 196640 | tf_op jit(solution)/shard_map/all_to_all | solution.py:78
  173.5 2.1 add_multiply_fusion.1
  175.7 2.5 copy.57
  182.0 4.8 %collective-permute-start.19 = (f32[32,1,192]{2,1,0:T(1,128)S(1)}, f32[32,1,192]{2,1,0:T(1,128)S(1)}, u32[]{:S(2)}, u32[]{:S(2)}) collective-permute-start(f32[32,1,192]{2,1,0:T(1,128)S(1)} %get-tuple-element.14), channel_id=1, source_target_pairs={{0,1},{1,2},{2,3},{3,4},{4,5},{5,6},{6,7},{7,8},{8,9},{9,10},{10,1... | collective-permute-start | bytes 73736 | tf_op jit(solution)/shard_map/ppermute | solution.py:41
  186.7 3.1 %collective-permute-start.17 = (f32[1,32,192]{2,1,0:T(8,128)S(1)}, f32[1,32,192]{2,1,0:T(8,128)S(1)}, u32[]{:S(2)}, u32[]{:S(2)}) collective-permute-start(f32[1,32,192]{2,1,0:T(8,128)S(1)} %get-tuple-element.15), channel_id=1, source_target_pairs={{0,16},{16,32},{32,48},{48,64},{64,80},{80,96},{96,112},{112,128},... | collective-permute-start | bytes 73736 | tf_op jit(solution)/shard_map/ppermute | solution.py:39
  191.2 3.3 %collective-permute-done.16 = f32[1,32,192]{2,1,0:T(8,128)S(1)} collective-permute-done((f32[1,32,192]{2,1,0:T(8,128)S(1)}, f32[1,32,192]{2,1,0:T(8,128)S(1)}, u32[]{:S(2)}, u32[]{:S(2)}) %collective-permute-start.16) | collective-permute-done | bytes 24608 | tf_op jit(solution)/shard_map/ppermute | solution.py:40
  199.0 8.2 %all-to-all-start.5 = ((f32[16,1,1728]{2,1,0:T(1,128)}), f32[16,1,1728]{2,1,0:T(1,128)S(1)}, u32[]{:S(2)}, u32[]{:S(2)}) async-start(f32[16,1,1728]{2,1,0:T(1,128)} %broadcast_in_dim.32), calls=%async_computation.5 | async-start | bytes 229376 | tf_op jit(solution)/shard_map/all_to_all | solution.py:72
  208.1 2.0 collective-permute-start.20
  212.9 2.5 collective-permute-done.21
  217.1 4.7 %collective-permute-start.22 = (bf16[40,4,192]{2,1,0:T(4,128)(2,1)}, bf16[40,4,192]{2,1,0:T(4,128)(2,1)}, u32[]{:S(2)}, u32[]{:S(2)}) collective-permute-start(bf16[40,4,192]{2,1,0:T(4,128)(2,1)} %get-tuple-element.23), channel_id=1, source_target_pairs={{0,1},{1,2},{2,3},{3,4},{4,5},{5,6},{6,7},{7,8},{8,9},{9,10},{10,1... | collective-permute-start | bytes 184328 | tf_op jit(solution)/shard_map/ppermute | solution.py:23
  221.8 1.9 collective-permute-start.23
  226.4 2.0 convolution_bitcast_fusion.3
  230.4 8.4 %all-to-all-start.6 = ((f32[32,1,1536]{2,1,0:T(1,128)}), f32[32,1,1536]{2,1,0:T(1,128)S(1)}, u32[]{:S(2)}, u32[]{:S(2)}) async-start(f32[32,1,1536]{2,1,0:T(1,128)} %all_to_all.55), calls=%async_computation.6 | async-start | bytes 393216 | tf_op jit(solution)/shard_map/all_to_all | solution.py:78
  242.1 7.1 %all-to-all-done.6 = f32[32,1,1536]{2,1,0:T(1,128)S(1)} async-done(((f32[32,1,1536]{2,1,0:T(1,128)}), f32[32,1,1536]{2,1,0:T(1,128)S(1)}, u32[]{:S(2)}, u32[]{:S(2)}) %all-to-all-start.6) | async-done | bytes 196640 | tf_op jit(solution)/shard_map/all_to_all | solution.py:78
  250.2 2.1 add_multiply_fusion
  252.4 2.4 copy.61
  254.9 3.3 %multiply_add_fusion = (f32[32,32,192]{2,1,0:T(8,128)S(1)}, f32[32,32,192]{2,1,0:T(8,128)}) fusion(f32[32,32,192]{2,1,0:T(8,128)} %bitcast.89, f32[32,32,192]{2,1,0:T(8,128)} %copy-done.6, f32[1024,192]{1,0:T(8,128)} %copy.53), kind=kLoop, calls=%fused_computation.92 | loop fusion | flops 983040 | bytes 3932160 | tf_op jit(solution)/shard_map/add | solution.py:143
  260.2 4.8 %collective-permute-start.27 = (f32[32,1,192]{2,1,0:T(1,128)S(1)}, f32[32,1,192]{2,1,0:T(1,128)S(1)}, u32[]{:S(2)}, u32[]{:S(2)}) collective-permute-start(f32[32,1,192]{2,1,0:T(1,128)S(1)} %get-tuple-element.10), channel_id=1, source_target_pairs={{0,1},{1,2},{2,3},{3,4},{4,5},{5,6},{6,7},{7,8},{8,9},{9,10},{10,1... | collective-permute-start | bytes 73736 | tf_op jit(solution)/shard_map/ppermute | solution.py:41
  265.0 3.1 %collective-permute-start.25 = (f32[1,32,192]{2,1,0:T(8,128)S(1)}, f32[1,32,192]{2,1,0:T(8,128)S(1)}, u32[]{:S(2)}, u32[]{:S(2)}) collective-permute-start(f32[1,32,192]{2,1,0:T(8,128)S(1)} %get-tuple-element.11), channel_id=1, source_target_pairs={{0,16},{16,32},{32,48},{48,64},{64,80},{80,96},{96,112},{112,128},... | collective-permute-start | bytes 73736 | tf_op jit(solution)/shard_map/ppermute | solution.py:39
  270.3 2.4 collective-permute-done.24
  275.1 8.2 %all-to-all-start.7 = ((f32[16,1,192]{2,1,0:T(1,128)}), f32[16,1,192]{2,1,0:T(1,128)S(1)}, u32[]{:S(2)}, u32[]{:S(2)}) async-start(f32[16,1,192]{2,1,0:T(1,128)} %broadcast_in_dim.33), calls=%async_computation.7 | async-start | bytes 32768 | tf_op jit(solution)/shard_map/all_to_all | solution.py:72
  284.3 6.4 %all-to-all-done.7 = f32[16,1,192]{2,1,0:T(1,128)S(1)} async-done(((f32[16,1,192]{2,1,0:T(1,128)}), f32[16,1,192]{2,1,0:T(1,128)S(1)}, u32[]{:S(2)}, u32[]{:S(2)}) %all-to-all-start.7) | async-done | bytes 12320 | tf_op jit(solution)/shard_map/all_to_all | solution.py:72
  290.8 15.5 %all_to_all.65 = f32[32,1,768]{2,1,0:T(1,128)S(1)} all-to-all(f32[32,1,768]{2,1,0:T(1,128)S(1)} %broadcast_in_dim.69), channel_id=1, replica_groups=mesh['gx'=32,'gy'=16] {'gx'}, dimensions={0} | all-to-all | bytes 196608 | tf_op jit(solution)/shard_map/all_to_all | solution.py:72
  (173 shorter events, 89.2 us)
Async XLA Ops:
  0.6 80.1 %copy-start = (bf16[1,1,1024,1600]{2,3,1,0:T(8,128)(2,1)S(1)}, bf16[1,1,1024,1600]{2,3,1,0:T(8,128)(2,1)}, u32[]{:S(2)}) copy-start(bf16[1,1,1024,1600]{2,3,1,0:T(8,128)(2,1)} %param.10) | copy-start | bytes 9830404
  0.6 17.4 %copy-start.7 = (f32[32,32,192]{2,1,0:T(8,128)S(1)}, f32[32,32,192]{2,1,0:T(8,128)}, u32[]{:S(2)}) copy-start(f32[32,32,192]{2,1,0:T(8,128)} %param.6) | copy-start | bytes 2359300
  0.7 17.4 %copy-start.9 = (f32[8,32,32]{2,1,0:T(8,128)S(1)}, f32[8,32,32]{2,1,0:T(8,128)}, u32[]{:S(2)}) copy-start(f32[8,32,32]{2,1,0:T(8,128)} %param.9) | copy-start | bytes 98308
  2.0 95.0 %collective-permute-start.6 = (f32[1,32]{1,0:T(1,128)}, f32[1,32]{1,0:T(1,128)}, u32[]{:S(2)}, u32[]{:S(2)}) collective-permute-start(f32[1,32]{1,0:T(1,128)} %get-tuple-element.41), channel_id=1, source_target_pairs={{0,16},{16,32},{32,48},{48,64},{64,80},{80,96},{96,112},{112,128},... | collective-permute-start | bytes 392 | tf_op jit(solution)/shard_map/ppermute | solution.py:39
  7.4 93.8 %collective-permute-start.4 = (f32[1,32]{1,0:T(1,128)}, f32[1,32]{1,0:T(1,128)}, u32[]{:S(2)}, u32[]{:S(2)}) collective-permute-start(f32[1,32]{1,0:T(1,128)} %get-tuple-element.42), channel_id=1, source_target_pairs={{16,0},{32,16},{48,32},{64,48},{80,64},{96,80},{112,96},{128,112},... | collective-permute-start | bytes 392 | tf_op jit(solution)/shard_map/ppermute | solution.py:40
  10.1 37.6 %copy-start.26 = (f32[32,32]{1,0:T(8,128)S(1)}, f32[32,32]{1,0:T(8,128)}, u32[]{:S(2)}) copy-start(f32[32,32]{1,0:T(8,128)} %param.8) | copy-start | bytes 12292
  10.1 94.2 %collective-permute-start.8 = (f32[32,1]{1,0:T(8,128)}, f32[32,1]{1,0:T(8,128)}, u32[]{:S(2)}, u32[]{:S(2)}) collective-permute-start(f32[32,1]{1,0:T(8,128)} %get-tuple-element.39), channel_id=1, source_target_pairs={{1,0},{2,1},{3,2},{4,3},{5,4},{6,5},{7,6},{8,7},{9,8},{10,9},{11,1... | collective-permute-start | bytes 392 | tf_op jit(solution)/shard_map/ppermute | solution.py:42
  19.6 13.7 %all-to-all-start = ((f32[16,1,1728]{2,1,0:T(1,128)}), f32[16,1,1728]{2,1,0:T(1,128)S(1)}, u32[]{:S(2)}, u32[]{:S(2)}) async-start(f32[16,1,1728]{2,1,0:T(1,128)} %broadcast_in_dim.26), calls=%async_computation | async-start | bytes 229376 | tf_op jit(solution)/shard_map/all_to_all | solution.py:72
  26.0 23.1 %collective-permute-start = (bf16[4,32,192]{2,1,0:T(8,128)(2,1)}, bf16[4,32,192]{2,1,0:T(8,128)(2,1)}, u32[]{:S(2)}, u32[]{:S(2)}) collective-permute-start(bf16[4,32,192]{2,1,0:T(8,128)(2,1)} %get-tuple-element.33), channel_id=1, source_target_pairs={{0,16},{16,32},{32,48},{48,64},{64,80},{80,96},{96,112},{112,128},... | collective-permute-start | bytes 147464 | tf_op jit(solution)/shard_map/ppermute | solution.py:23
  30.9 18.2 %collective-permute-start.1 = (bf16[4,32,192]{2,1,0:T(8,128)(2,1)}, bf16[4,32,192]{2,1,0:T(8,128)(2,1)}, u32[]{:S(2)}, u32[]{:S(2)}) collective-permute-start(bf16[4,32,192]{2,1,0:T(8,128)(2,1)} %get-tuple-element.34), channel_id=1, source_target_pairs={{16,0},{32,16},{48,32},{64,48},{80,64},{96,80},{112,96},{128,112},... | collective-permute-start | bytes 147464 | tf_op jit(solution)/shard_map/ppermute | solution.py:25
  33.9 26.0 %all-to-all-start.1 = ((f32[32,8,128]{2,1,0:T(8,128)}), f32[32,8,128]{2,1,0:T(8,128)S(1)}, u32[]{:S(2)}, u32[]{:S(2)}) async-start(f32[32,8,128]{2,1,0:T(8,128)} %bitcast.94), calls=%async_computation.1 | async-start | bytes 262144 | tf_op jit(solution)/shard_map/all_to_all | solution.py:101
  50.8 24.4 %collective-permute-start.2 = (bf16[40,4,192]{2,1,0:T(4,128)(2,1)}, bf16[40,4,192]{2,1,0:T(4,128)(2,1)}, u32[]{:S(2)}, u32[]{:S(2)}) collective-permute-start(bf16[40,4,192]{2,1,0:T(4,128)(2,1)} %get-tuple-element.27), channel_id=1, source_target_pairs={{0,1},{1,2},{2,3},{3,4},{4,5},{5,6},{6,7},{7,8},{8,9},{9,10},{10,1... | collective-permute-start | bytes 184328 | tf_op jit(solution)/shard_map/ppermute | solution.py:23
  54.5 24.7 %collective-permute-start.3 = (bf16[40,4,192]{2,1,0:T(4,128)(2,1)}, bf16[40,4,192]{2,1,0:T(4,128)(2,1)}, u32[]{:S(2)}, u32[]{:S(2)}) collective-permute-start(bf16[40,4,192]{2,1,0:T(4,128)(2,1)} %get-tuple-element.28), channel_id=1, source_target_pairs={{1,0},{2,1},{3,2},{4,3},{5,4},{6,5},{7,6},{8,7},{9,8},{10,9},{11,1... | collective-permute-start | bytes 184328 | tf_op jit(solution)/shard_map/ppermute | solution.py:25
  65.6 20.7 %all-to-all-start.2 = ((f32[32,1,1536]{2,1,0:T(1,128)}), f32[32,1,1536]{2,1,0:T(1,128)}, u32[]{:S(2)}, u32[]{:S(2)}) async-start(f32[32,1,1536]{2,1,0:T(1,128)} %all_to_all.53), calls=%async_computation.2 | async-start | bytes 393216 | tf_op jit(solution)/shard_map/all_to_all | solution.py:78
  75.2 30.5 %collective-permute-start.10 = (f32[32,1]{1,0:T(8,128)}, f32[32,1]{1,0:T(8,128)}, u32[]{:S(2)}, u32[]{:S(2)}) collective-permute-start(f32[32,1]{1,0:T(8,128)} %get-tuple-element.40), channel_id=1, source_target_pairs={{0,1},{1,2},{2,3},{3,4},{4,5},{5,6},{6,7},{7,8},{8,9},{9,10},{10,1... | collective-permute-start | bytes 392 | tf_op jit(solution)/shard_map/ppermute | solution.py:41
  95.1 11.4 %collective-permute-start.9 = (f32[32,1,192]{2,1,0:T(1,128)S(1)}, f32[32,1,192]{2,1,0:T(1,128)S(1)}, u32[]{:S(2)}, u32[]{:S(2)}) collective-permute-start(f32[32,1,192]{2,1,0:T(1,128)S(1)} %get-tuple-element.17), channel_id=1, source_target_pairs={{1,0},{2,1},{3,2},{4,3},{5,4},{6,5},{7,6},{8,7},{9,8},{10,9},{11,1... | collective-permute-start | bytes 73736 | tf_op jit(solution)/shard_map/ppermute | solution.py:42
  97.1 9.5 %collective-permute-start.11 = (f32[32,1,192]{2,1,0:T(1,128)S(1)}, f32[32,1,192]{2,1,0:T(1,128)S(1)}, u32[]{:S(2)}, u32[]{:S(2)}) collective-permute-start(f32[32,1,192]{2,1,0:T(1,128)S(1)} %get-tuple-element.18), channel_id=1, source_target_pairs={{0,1},{1,2},{2,3},{3,4},{4,5},{5,6},{6,7},{7,8},{8,9},{9,10},{10,1... | collective-permute-start | bytes 73736 | tf_op jit(solution)/shard_map/ppermute | solution.py:41
  101.2 5.3 %collective-permute-start.7 = (f32[1,32,192]{2,1,0:T(8,128)S(1)}, f32[1,32,192]{2,1,0:T(8,128)S(1)}, u32[]{:S(2)}, u32[]{:S(2)}) collective-permute-start(f32[1,32,192]{2,1,0:T(8,128)S(1)} %get-tuple-element.19), channel_id=1, source_target_pairs={{0,16},{16,32},{32,48},{48,64},{64,80},{80,96},{96,112},{112,128},... | collective-permute-start | bytes 73736 | tf_op jit(solution)/shard_map/ppermute | solution.py:39
  104.3 4.7 %collective-permute-start.5 = (f32[1,32,192]{2,1,0:T(8,128)S(1)}, f32[1,32,192]{2,1,0:T(8,128)S(1)}, u32[]{:S(2)}, u32[]{:S(2)}) collective-permute-start(f32[1,32,192]{2,1,0:T(8,128)S(1)} %get-tuple-element.20), channel_id=1, source_target_pairs={{16,0},{32,16},{48,32},{64,48},{80,64},{96,80},{112,96},{128,112},... | collective-permute-start | bytes 73736 | tf_op jit(solution)/shard_map/ppermute | solution.py:40
  116.1 24.8 %all-to-all-start.3 = ((f32[16,1,1728]{2,1,0:T(1,128)}), f32[16,1,1728]{2,1,0:T(1,128)}, u32[]{:S(2)}, u32[]{:S(2)}) async-start(f32[16,1,1728]{2,1,0:T(1,128)} %broadcast_in_dim.29), calls=%async_computation.3 | async-start | bytes 229376 | tf_op jit(solution)/shard_map/all_to_all | solution.py:72
  125.2 3.3 %collective-permute-start.12 = (bf16[4,32,192]{2,1,0:T(8,128)(2,1)S(1)}, bf16[4,32,192]{2,1,0:T(8,128)(2,1)S(1)}, u32[]{:S(2)}, u32[]{:S(2)}) collective-permute-start(bf16[4,32,192]{2,1,0:T(8,128)(2,1)S(1)} %get-tuple-element.31), channel_id=1, source_target_pairs={{0,16},{16,32},{32,48},{48,64},{64,80},{80,96},{96,112},{112,128},... | collective-permute-start | bytes 147464 | tf_op jit(solution)/shard_map/ppermute | solution.py:23
  127.2 5.4 %collective-permute-start.13 = (bf16[4,32,192]{2,1,0:T(8,128)(2,1)S(1)}, bf16[4,32,192]{2,1,0:T(8,128)(2,1)S(1)}, u32[]{:S(2)}, u32[]{:S(2)}) collective-permute-start(bf16[4,32,192]{2,1,0:T(8,128)(2,1)S(1)} %get-tuple-element.32), channel_id=1, source_target_pairs={{16,0},{32,16},{48,32},{64,48},{80,64},{96,80},{112,96},{128,112},... | collective-permute-start | bytes 147464 | tf_op jit(solution)/shard_map/ppermute | solution.py:25
  134.4 24.3 %collective-permute-start.14 = (bf16[40,4,192]{2,1,0:T(4,128)(2,1)}, bf16[40,4,192]{2,1,0:T(4,128)(2,1)}, u32[]{:S(2)}, u32[]{:S(2)}) collective-permute-start(bf16[40,4,192]{2,1,0:T(4,128)(2,1)} %get-tuple-element.25), channel_id=1, source_target_pairs={{0,1},{1,2},{2,3},{3,4},{4,5},{5,6},{6,7},{7,8},{8,9},{9,10},{10,1... | collective-permute-start | bytes 184328 | tf_op jit(solution)/shard_map/ppermute | solution.py:23
  139.0 19.7 %collective-permute-start.15 = (bf16[40,4,192]{2,1,0:T(4,128)(2,1)}, bf16[40,4,192]{2,1,0:T(4,128)(2,1)}, u32[]{:S(2)}, u32[]{:S(2)}) collective-permute-start(bf16[40,4,192]{2,1,0:T(4,128)(2,1)} %get-tuple-element.26), channel_id=1, source_target_pairs={{1,0},{2,1},{3,2},{4,3},{5,4},{6,5},{7,6},{8,7},{9,8},{10,9},{11,1... | collective-permute-start | bytes 184328 | tf_op jit(solution)/shard_map/ppermute | solution.py:25
  150.0 18.9 %all-to-all-start.4 = ((f32[32,1,1536]{2,1,0:T(1,128)}), f32[32,1,1536]{2,1,0:T(1,128)}, u32[]{:S(2)}, u32[]{:S(2)}) async-start(f32[32,1,1536]{2,1,0:T(1,128)} %all_to_all.54), calls=%async_computation.4 | async-start | bytes 393216 | tf_op jit(solution)/shard_map/all_to_all | solution.py:78
  178.1 16.4 %copy-start.19 = (f32[32,32]{1,0:T(8,128)S(1)}, f32[32,32]{1,0:T(8,128)}, u32[]{:S(2)}) copy-start(f32[32,32]{1,0:T(8,128)} %copy-done.18) | copy-start | bytes 12292
  178.1 16.4 %copy-start.27 = (f32[32,32]{1,0:T(8,128)S(1)}, f32[32,32]{1,0:T(8,128)}, u32[]{:S(2)}) copy-start(f32[32,32]{1,0:T(8,128)} %param.8) | copy-start | bytes 12292
  180.0 11.1 %collective-permute-start.18 = (f32[32,1,192]{2,1,0:T(1,128)S(1)}, f32[32,1,192]{2,1,0:T(1,128)S(1)}, u32[]{:S(2)}, u32[]{:S(2)}) collective-permute-start(f32[32,1,192]{2,1,0:T(1,128)S(1)} %get-tuple-element.13), channel_id=1, source_target_pairs={{1,0},{2,1},{3,2},{4,3},{5,4},{6,5},{7,6},{8,7},{9,8},{10,9},{11,1... | collective-permute-start | bytes 73736 | tf_op jit(solution)/shard_map/ppermute | solution.py:42
  182.0 9.2 %collective-permute-start.19 = (f32[32,1,192]{2,1,0:T(1,128)S(1)}, f32[32,1,192]{2,1,0:T(1,128)S(1)}, u32[]{:S(2)}, u32[]{:S(2)}) collective-permute-start(f32[32,1,192]{2,1,0:T(1,128)S(1)} %get-tuple-element.14), channel_id=1, source_target_pairs={{0,1},{1,2},{2,3},{3,4},{4,5},{5,6},{6,7},{7,8},{8,9},{9,10},{10,1... | collective-permute-start | bytes 73736 | tf_op jit(solution)/shard_map/ppermute | solution.py:41
  186.7 4.4 %collective-permute-start.17 = (f32[1,32,192]{2,1,0:T(8,128)S(1)}, f32[1,32,192]{2,1,0:T(8,128)S(1)}, u32[]{:S(2)}, u32[]{:S(2)}) collective-permute-start(f32[1,32,192]{2,1,0:T(8,128)S(1)} %get-tuple-element.15), channel_id=1, source_target_pairs={{0,16},{16,32},{32,48},{48,64},{64,80},{80,96},{96,112},{112,128},... | collective-permute-start | bytes 73736 | tf_op jit(solution)/shard_map/ppermute | solution.py:39
  189.9 4.7 %collective-permute-start.16 = (f32[1,32,192]{2,1,0:T(8,128)S(1)}, f32[1,32,192]{2,1,0:T(8,128)S(1)}, u32[]{:S(2)}, u32[]{:S(2)}) collective-permute-start(f32[1,32,192]{2,1,0:T(8,128)S(1)} %get-tuple-element.16), channel_id=1, source_target_pairs={{16,0},{32,16},{48,32},{64,48},{80,64},{96,80},{112,96},{128,112},... | collective-permute-start | bytes 73736 | tf_op jit(solution)/shard_map/ppermute | solution.py:40
  199.0 24.8 %all-to-all-start.5 = ((f32[16,1,1728]{2,1,0:T(1,128)}), f32[16,1,1728]{2,1,0:T(1,128)S(1)}, u32[]{:S(2)}, u32[]{:S(2)}) async-start(f32[16,1,1728]{2,1,0:T(1,128)} %broadcast_in_dim.32), calls=%async_computation.5 | async-start | bytes 229376 | tf_op jit(solution)/shard_map/all_to_all | solution.py:72
  208.1 4.8 %collective-permute-start.20 = (bf16[4,32,192]{2,1,0:T(8,128)(2,1)S(1)}, bf16[4,32,192]{2,1,0:T(8,128)(2,1)S(1)}, u32[]{:S(2)}, u32[]{:S(2)}) collective-permute-start(bf16[4,32,192]{2,1,0:T(8,128)(2,1)S(1)} %get-tuple-element.29), channel_id=1, source_target_pairs={{0,16},{16,32},{32,48},{48,64},{64,80},{80,96},{96,112},{112,128},... | collective-permute-start | bytes 147464 | tf_op jit(solution)/shard_map/ppermute | solution.py:23
  210.1 5.3 %collective-permute-start.21 = (bf16[4,32,192]{2,1,0:T(8,128)(2,1)S(1)}, bf16[4,32,192]{2,1,0:T(8,128)(2,1)S(1)}, u32[]{:S(2)}, u32[]{:S(2)}) collective-permute-start(bf16[4,32,192]{2,1,0:T(8,128)(2,1)S(1)} %get-tuple-element.30), channel_id=1, source_target_pairs={{16,0},{32,16},{48,32},{64,48},{80,64},{96,80},{112,96},{128,112},... | collective-permute-start | bytes 147464 | tf_op jit(solution)/shard_map/ppermute | solution.py:25
  217.1 21.6 %collective-permute-start.22 = (bf16[40,4,192]{2,1,0:T(4,128)(2,1)}, bf16[40,4,192]{2,1,0:T(4,128)(2,1)}, u32[]{:S(2)}, u32[]{:S(2)}) collective-permute-start(bf16[40,4,192]{2,1,0:T(4,128)(2,1)} %get-tuple-element.23), channel_id=1, source_target_pairs={{0,1},{1,2},{2,3},{3,4},{4,5},{5,6},{6,7},{7,8},{8,9},{9,10},{10,1... | collective-permute-start | bytes 184328 | tf_op jit(solution)/shard_map/ppermute | solution.py:23
  221.8 16.9 %collective-permute-start.23 = (bf16[40,4,192]{2,1,0:T(4,128)(2,1)}, bf16[40,4,192]{2,1,0:T(4,128)(2,1)}, u32[]{:S(2)}, u32[]{:S(2)}) collective-permute-start(bf16[40,4,192]{2,1,0:T(4,128)(2,1)} %get-tuple-element.24), channel_id=1, source_target_pairs={{1,0},{2,1},{3,2},{4,3},{5,4},{6,5},{7,6},{8,7},{9,8},{10,9},{11,1... | collective-permute-start | bytes 184328 | tf_op jit(solution)/shard_map/ppermute | solution.py:25
  230.4 18.8 %all-to-all-start.6 = ((f32[32,1,1536]{2,1,0:T(1,128)}), f32[32,1,1536]{2,1,0:T(1,128)S(1)}, u32[]{:S(2)}, u32[]{:S(2)}) async-start(f32[32,1,1536]{2,1,0:T(1,128)} %all_to_all.55), calls=%async_computation.6 | async-start | bytes 393216 | tf_op jit(solution)/shard_map/all_to_all | solution.py:78
  254.8 17.9 %copy-start.5 = (f32[32,32,192]{2,1,0:T(8,128)S(1)}, f32[32,32,192]{2,1,0:T(8,128)}, u32[]{:S(2)}) copy-start(f32[32,32,192]{2,1,0:T(8,128)} %copy-done.4) | copy-start | bytes 2359300
  254.8 17.9 %copy-start.14 = (f32[32,32]{1,0:T(8,128)S(1)}, f32[32,32]{1,0:T(8,128)}, u32[]{:S(2)}) copy-start(f32[32,32]{1,0:T(8,128)} %copy-done.12) | copy-start | bytes 12292
  254.8 17.9 %copy-start.17 = (f32[32,32]{1,0:T(8,128)S(1)}, f32[32,32]{1,0:T(8,128)}, u32[]{:S(2)}) copy-start(f32[32,32]{1,0:T(8,128)} %copy-done.15) | copy-start | bytes 12292
  254.8 17.9 %copy-start.20 = (f32[32,32]{1,0:T(8,128)S(1)}, f32[32,32]{1,0:T(8,128)}, u32[]{:S(2)}) copy-start(f32[32,32]{1,0:T(8,128)} %copy-done.18) | copy-start | bytes 12292
  254.8 17.9 %copy-start.28 = (f32[32,32]{1,0:T(8,128)S(1)}, f32[32,32]{1,0:T(8,128)}, u32[]{:S(2)}) copy-start(f32[32,32]{1,0:T(8,128)} %param.8) | copy-start | bytes 12292
  258.2 32.5 %copy-start.30 = (f32[192]{0:T(256)S(1)}, f32[192]{0:T(256)}, u32[]{:S(2)}) copy-start(f32[192]{0:T(256)} %slice_reduce_fusion.2) | copy-start | bytes 2308
  258.3 12.0 %collective-permute-start.26 = (f32[32,1,192]{2,1,0:T(1,128)S(1)}, f32[32,1,192]{2,1,0:T(1,128)S(1)}, u32[]{:S(2)}, u32[]{:S(2)}) collective-permute-start(f32[32,1,192]{2,1,0:T(1,128)S(1)} %get-tuple-element.9), channel_id=1, source_target_pairs={{1,0},{2,1},{3,2},{4,3},{5,4},{6,5},{7,6},{8,7},{9,8},{10,9},{11,1... | collective-permute-start | bytes 73736 | tf_op jit(solution)/shard_map/ppermute | solution.py:42
  260.2 10.1 %collective-permute-start.27 = (f32[32,1,192]{2,1,0:T(1,128)S(1)}, f32[32,1,192]{2,1,0:T(1,128)S(1)}, u32[]{:S(2)}, u32[]{:S(2)}) collective-permute-start(f32[32,1,192]{2,1,0:T(1,128)S(1)} %get-tuple-element.10), channel_id=1, source_target_pairs={{0,1},{1,2},{2,3},{3,4},{4,5},{5,6},{6,7},{7,8},{8,9},{9,10},{10,1... | collective-permute-start | bytes 73736 | tf_op jit(solution)/shard_map/ppermute | solution.py:41
  265.0 5.4 %collective-permute-start.25 = (f32[1,32,192]{2,1,0:T(8,128)S(1)}, f32[1,32,192]{2,1,0:T(8,128)S(1)}, u32[]{:S(2)}, u32[]{:S(2)}) collective-permute-start(f32[1,32,192]{2,1,0:T(8,128)S(1)} %get-tuple-element.11), channel_id=1, source_target_pairs={{0,16},{16,32},{32,48},{48,64},{64,80},{80,96},{96,112},{112,128},... | collective-permute-start | bytes 73736 | tf_op jit(solution)/shard_map/ppermute | solution.py:39
  268.1 4.7 %collective-permute-start.24 = (f32[1,32,192]{2,1,0:T(8,128)S(1)}, f32[1,32,192]{2,1,0:T(8,128)S(1)}, u32[]{:S(2)}, u32[]{:S(2)}) collective-permute-start(f32[1,32,192]{2,1,0:T(8,128)S(1)} %get-tuple-element.12), channel_id=1, source_target_pairs={{16,0},{32,16},{48,32},{64,48},{80,64},{96,80},{112,96},{128,112},... | collective-permute-start | bytes 73736 | tf_op jit(solution)/shard_map/ppermute | solution.py:40
  275.1 15.6 %all-to-all-start.7 = ((f32[16,1,192]{2,1,0:T(1,128)}), f32[16,1,192]{2,1,0:T(1,128)S(1)}, u32[]{:S(2)}, u32[]{:S(2)}) async-start(f32[16,1,192]{2,1,0:T(1,128)} %broadcast_in_dim.33), calls=%async_computation.7 | async-start | bytes 32768 | tf_op jit(solution)/shard_map/all_to_all | solution.py:72
  (19 other events, 169.7 us)

commit v8 on v7

--- a/solution.py
+++ b/solution.py
@@ -119,9 +119,9 @@
             rows_x, modes, fields
         )
         coarse_part = summed_by_exchange(partial, "gx")
-        prolonged = jnp.dot(flat_basis.T, coarse_part, precision=highest).reshape(
-            patch, patch, fields
-        )
+        prolonged = basis[0][:, :, None] * coarse_part[0]
+        for mode in range(1, modes):
+            prolonged = prolonged + basis[mode][:, :, None] * coarse_part[mode]
         return (local_part + prolonged, row_total)
 
     centre = 0.5 * (upper_bound + lower_bound)

time: 311 us -> 306 us (0.984)
  waiting for transfers between devices: 40 us -> 28.3 us
  starting transfers between devices: 150 us -> 158 us
  matrix products: 17.5 us -> 13.7 us
    all_to_all x3, waiting for transfers between devices: 17.7 us -> 8.95 us  [summed_by_exchange(): received = lax.all_to_all(flat, axis, 0, 0, tiled=True)]
    optimization_barrier x0 -> x3, local copies, waits for them, and re-layouts: none -> 7.43 us  [precondition(): lax.optimization_barrier(local_part).reshape(patch, patch, fields)]
    mul x2 -> x0, other arithmetic: 4.29 us -> none  [on_device(): 2.0 * weight_next / half_width * corrected]
    mul x2 -> x1, local copies, waits for them, and re-layouts: 4.9 us -> 0.66 us  [precondition(): prolonged = basis[0][:, :, None] * coarse_part[0]]
    dot_general x3 -> x0, matrix products: 3.98 us -> none  [precondition(): jnp.dot(flat_basis.T, coarse_part, precision=highest)]
    ppermute x6, starting transfers between devices: 21.8 us -> 25.5 us  [extended(): lax.ppermute(tail, axis, [(i, (i + 1) % count) for i in range(ends)])]
    add x1, other arithmetic: 2.13 us -> 5.66 us  [on_device(): solution = solution + update]
    ppermute x4, waiting for transfers between devices: 8.15 us -> 4.81 us  [with_edges(): south = lax.ppermute(cells[:1], 'gx', up)]
  transfers between devices with their start and end apart: 36 -> 36, of which waited for: 10 -> 10; matrix products, arithmetic and copies ran while one was open for 19% -> 21% of each run, Pallas kernels for 0% -> 0%
where the time goes in v8:
time: 306 us; the launch traced here: 303 us
  starting transfers between devices  158 us (52%)
  other arithmetic  47.3 us (15%)
  local copies, waits for them, and re-layouts  39 us (13%)
  waiting for transfers between devices  28.3 us (9%)
  blocking collectives  15.5 us (5%)
  matrix products  13.7 us (4%)
    all_to_all x4, starting transfers between devices, gathered_by_exchange(): lax.all_to_all(copies, axis, 0, 0, tiled=True)  31.2 us
    all_to_all x3, starting transfers between devices, summed_by_exchange(): received = lax.all_to_all(flat, axis, 0, 0, tiled=True)  27.8 us
    ppermute x6, starting transfers between devices, extended(): lax.ppermute(tail, axis, [(i, (i + 1) % count) for i in range(ends)])  25.5 us
    ppermute x4, starting transfers between devices, with_edges(): west = lax.ppermute(cells[:, -1:], 'gy', right)  19.2 us
    all_to_all x1, blocking collectives, gathered_by_exchange(): lax.all_to_all(copies, axis, 0, 0, tiled=True)  15.5 us
    ppermute x4, starting transfers between devices, with_edges(): north = lax.ppermute(cells[-1:], 'gx', down)  14.6 us
    all_to_all x1, starting transfers between devices, on_device(): pieces = lax.all_to_all(pieces, 'gx', 0, 0, tiled=True)  13.8 us
    ppermute x4, starting transfers between devices, with_edges(): east = lax.ppermute(cells[:, :1], 'gy', left)  11 us
  transfers between devices with their start and end apart: 36, of which 10 were waited for; matrix products, arithmetic and copies ran while one was open for 21% of the time, Pallas kernels for 0%

profile of v8, /device:TPU:1, one launch (start us, length us, event | category | flops | bytes accessed | tf_op | source)
XLA Modules:
  0.0 303.4 jit_solution(12137336057272146048)
XLA Ops:
  2.1 5.3 %collective-permute-start.6 = (f32[1,32]{1,0:T(1,128)}, f32[1,32]{1,0:T(1,128)}, u32[]{:S(2)}, u32[]{:S(2)}) collective-permute-start(f32[1,32]{1,0:T(1,128)} %get-tuple-element.49), channel_id=1, source_target_pairs={{0,16},{16,32},{32,48},{48,64},{64,80},{80,96},{96,112},{112,128},... | collective-permute-start | bytes 392 | tf_op jit(solution)/shard_map/ppermute | solution.py:39
  10.2 5.2 %collective-permute-start.8 = (f32[32,1]{1,0:T(8,128)}, f32[32,1]{1,0:T(8,128)}, u32[]{:S(2)}, u32[]{:S(2)}) collective-permute-start(f32[32,1]{1,0:T(8,128)} %get-tuple-element.47), channel_id=1, source_target_pairs={{1,0},{2,1},{3,2},{4,3},{5,4},{6,5},{7,6},{8,7},{9,8},{10,9},{11,1... | collective-permute-start | bytes 392 | tf_op jit(solution)/shard_map/ppermute | solution.py:42
  15.4 2.5 multiply_reduce_fusion.2
  19.5 4.9 %all-to-all-start = ((f32[16,1,1728]{2,1,0:T(1,128)}), f32[16,1,1728]{2,1,0:T(1,128)S(1)}, u32[]{:S(2)}, u32[]{:S(2)}) async-start(f32[16,1,1728]{2,1,0:T(1,128)} %broadcast_in_dim.26), calls=%async_computation | async-start | bytes 229376 | tf_op jit(solution)/shard_map/all_to_all | solution.py:72
  25.9 4.9 %collective-permute-start = (bf16[4,32,192]{2,1,0:T(8,128)(2,1)}, bf16[4,32,192]{2,1,0:T(8,128)(2,1)}, u32[]{:S(2)}, u32[]{:S(2)}) collective-permute-start(bf16[4,32,192]{2,1,0:T(8,128)(2,1)} %get-tuple-element.33), channel_id=1, source_target_pairs={{0,16},{16,32},{32,48},{48,64},{64,80},{80,96},{96,112},{112,128},... | collective-permute-start | bytes 147464 | tf_op jit(solution)/shard_map/ppermute | solution.py:23
  33.9 13.8 %all-to-all-start.1 = ((f32[32,8,128]{2,1,0:T(8,128)}), f32[32,8,128]{2,1,0:T(8,128)S(1)}, u32[]{:S(2)}, u32[]{:S(2)}) async-start(f32[32,8,128]{2,1,0:T(8,128)} %bitcast.101), calls=%async_computation.1 | async-start | bytes 262144 | tf_op jit(solution)/shard_map/all_to_all | solution.py:101
  50.8 4.3 %collective-permute-start.2 = (bf16[40,4,192]{2,1,0:T(4,128)(2,1)}, bf16[40,4,192]{2,1,0:T(4,128)(2,1)}, u32[]{:S(2)}, u32[]{:S(2)}) collective-permute-start(bf16[40,4,192]{2,1,0:T(4,128)(2,1)} %get-tuple-element.27), channel_id=1, source_target_pairs={{0,1},{1,2},{2,3},{3,4},{4,5},{5,6},{6,7},{7,8},{8,9},{9,10},{10,1... | collective-permute-start | bytes 184328 | tf_op jit(solution)/shard_map/ppermute | solution.py:23
  55.0 1.9 collective-permute-start.3
  60.5 2.0 convolution_bitcast_fusion.2
  66.1 9.6 %all-to-all-start.2 = ((f32[32,1,1536]{2,1,0:T(1,128)}), f32[32,1,1536]{2,1,0:T(1,128)}, u32[]{:S(2)}, u32[]{:S(2)}) async-start(f32[32,1,1536]{2,1,0:T(1,128)} %all_to_all.53), calls=%async_computation.2 | async-start | bytes 393216 | tf_op jit(solution)/shard_map/all_to_all | solution.py:78
  75.8 3.9 %collective-permute-start.10 = (f32[32,1]{1,0:T(8,128)}, f32[32,1]{1,0:T(8,128)}, u32[]{:S(2)}, u32[]{:S(2)}) collective-permute-start(f32[32,1]{1,0:T(8,128)} %get-tuple-element.48), channel_id=1, source_target_pairs={{0,1},{1,2},{2,3},{3,4},{4,5},{5,6},{6,7},{7,8},{8,9},{9,10},{10,1... | collective-permute-start | bytes 392 | tf_op jit(solution)/shard_map/ppermute | solution.py:41
  83.1 2.4 copy.48
  88.6 2.4 broadcast_multiply_fusion
  91.1 1.9 collective-permute-start.9
  93.1 5.1 %collective-permute-start.11 = (f32[32,1,192]{2,1,0:T(1,128)S(1)}, f32[32,1,192]{2,1,0:T(1,128)S(1)}, u32[]{:S(2)}, u32[]{:S(2)}) collective-permute-start(f32[32,1,192]{2,1,0:T(1,128)S(1)} %get-tuple-element.18), channel_id=1, source_target_pairs={{0,1},{1,2},{2,3},{3,4},{4,5},{5,6},{6,7},{7,8},{8,9},{9,10},{10,1... | collective-permute-start | bytes 73736 | tf_op jit(solution)/shard_map/ppermute | solution.py:41
  98.2 3.1 %collective-permute-start.7 = (f32[1,32,192]{2,1,0:T(8,128)S(1)}, f32[1,32,192]{2,1,0:T(8,128)S(1)}, u32[]{:S(2)}, u32[]{:S(2)}) collective-permute-start(f32[1,32,192]{2,1,0:T(8,128)S(1)} %get-tuple-element.19), channel_id=1, source_target_pairs={{0,16},{16,32},{32,48},{48,64},{64,80},{80,96},{96,112},{112,128},... | collective-permute-start | bytes 73736 | tf_op jit(solution)/shard_map/ppermute | solution.py:39
  103.5 2.4 collective-permute-done.5
  106.0 2.6 multiply_reduce_fusion.1
  114.0 8.2 %all-to-all-start.3 = ((f32[16,1,1728]{2,1,0:T(1,128)}), f32[16,1,1728]{2,1,0:T(1,128)}, u32[]{:S(2)}, u32[]{:S(2)}) async-start(f32[16,1,1728]{2,1,0:T(1,128)} %broadcast_in_dim.29), calls=%async_computation.3 | async-start | bytes 229376 | tf_op jit(solution)/shard_map/all_to_all | solution.py:72
  123.1 2.8 collective-permute-start.12
  127.2 4.5 %collective-permute-done.13 = bf16[4,32,192]{2,1,0:T(8,128)(2,1)S(1)} collective-permute-done((bf16[4,32,192]{2,1,0:T(8,128)(2,1)S(1)}, bf16[4,32,192]{2,1,0:T(8,128)(2,1)S(1)}, u32[]{:S(2)}, u32[]{:S(2)}) %collective-permute-start.13) | collective-permute-done | bytes 49184 | tf_op jit(solution)/shard_map/ppermute | solution.py:25
  133.4 4.3 %collective-permute-start.14 = (bf16[40,4,192]{2,1,0:T(4,128)(2,1)}, bf16[40,4,192]{2,1,0:T(4,128)(2,1)}, u32[]{:S(2)}, u32[]{:S(2)}) collective-permute-start(bf16[40,4,192]{2,1,0:T(4,128)(2,1)} %get-tuple-element.25), channel_id=1, source_target_pairs={{0,1},{1,2},{2,3},{3,4},{4,5},{5,6},{6,7},{7,8},{8,9},{9,10},{10,1... | collective-permute-start | bytes 184328 | tf_op jit(solution)/shard_map/ppermute | solution.py:23
  137.7 1.9 collective-permute-start.15
  143.2 2.0 convolution_bitcast_fusion.1
  148.9 9.4 %all-to-all-start.4 = ((f32[32,1,1536]{2,1,0:T(1,128)}), f32[32,1,1536]{2,1,0:T(1,128)}, u32[]{:S(2)}, u32[]{:S(2)}) async-start(f32[32,1,1536]{2,1,0:T(1,128)} %all_to_all.54), calls=%async_computation.4 | async-start | bytes 393216 | tf_op jit(solution)/shard_map/all_to_all | solution.py:78
  161.8 2.5 copy.52
  164.2 4.4 %all-to-all-done.4 = f32[32,1,1536]{2,1,0:T(1,128)} async-done(((f32[32,1,1536]{2,1,0:T(1,128)}), f32[32,1,1536]{2,1,0:T(1,128)}, u32[]{:S(2)}, u32[]{:S(2)}) %all-to-all-start.4) | async-done | bytes 196640 | tf_op jit(solution)/shard_map/all_to_all | solution.py:78
  171.4 3.5 %multiply_add_fusion.1 = f32[32,32,192]{2,1,0:T(8,128)S(1)} fusion(f32[32,32,192]{2,1,0:T(8,128)} %bitcast.95, f32[192]{0:T(256)S(1)} %get-tuple-element.60, f32[192]{0:T(256)S(1)} %get-tuple-element.61, f32[192]{0:T(256)S(1)} %get-tuple-element.62, f32[192]{0:T(256)S(1)} %get-tuple-element.63, f32[192]{0:T(256)S(1)} %get-tuple-element.64, ...), kind=kLoop, calls=%fused_computation.91 | loop fusion | flops 6881280 | bytes 2404352 | tf_op jit(solution)/shard_map/add | solution.py:143
  175.0 3.0 %collective-permute-start.17 = (f32[1,32,192]{2,1,0:T(8,128)S(1)}, f32[1,32,192]{2,1,0:T(8,128)S(1)}, u32[]{:S(2)}, u32[]{:S(2)}) collective-permute-start(f32[1,32,192]{2,1,0:T(8,128)S(1)} %get-tuple-element.15), channel_id=1, source_target_pairs={{0,16},{16,32},{32,48},{48,64},{64,80},{80,96},{96,112},{112,128},... | collective-permute-start | bytes 73736 | tf_op jit(solution)/shard_map/ppermute | solution.py:39
  179.4 1.9 collective-permute-start.18
  181.3 5.1 %collective-permute-start.19 = (f32[32,1,192]{2,1,0:T(1,128)S(1)}, f32[32,1,192]{2,1,0:T(1,128)S(1)}, u32[]{:S(2)}, u32[]{:S(2)}) collective-permute-start(f32[32,1,192]{2,1,0:T(1,128)S(1)} %get-tuple-element.14), channel_id=1, source_target_pairs={{0,1},{1,2},{2,3},{3,4},{4,5},{5,6},{6,7},{7,8},{8,9},{9,10},{10,1... | collective-permute-start | bytes 73736 | tf_op jit(solution)/shard_map/ppermute | solution.py:41
  191.8 9.8 %all-to-all-start.5 = ((f32[16,1,1728]{2,1,0:T(1,128)}), f32[16,1,1728]{2,1,0:T(1,128)S(1)}, u32[]{:S(2)}, u32[]{:S(2)}) async-start(f32[16,1,1728]{2,1,0:T(1,128)} %broadcast_in_dim.32), calls=%async_computation.5 | async-start | bytes 229376 | tf_op jit(solution)/shard_map/all_to_all | solution.py:72
  202.5 4.3 %collective-permute-start.20 = (bf16[4,32,192]{2,1,0:T(8,128)(2,1)S(1)}, bf16[4,32,192]{2,1,0:T(8,128)(2,1)S(1)}, u32[]{:S(2)}, u32[]{:S(2)}) collective-permute-start(bf16[4,32,192]{2,1,0:T(8,128)(2,1)S(1)} %get-tuple-element.29), channel_id=1, source_target_pairs={{0,16},{16,32},{32,48},{48,64},{64,80},{80,96},{96,112},{112,128},... | collective-permute-start | bytes 147464 | tf_op jit(solution)/shard_map/ppermute | solution.py:23
  209.6 2.2 collective-permute-done.21
  213.6 5.0 %collective-permute-start.22 = (bf16[40,4,192]{2,1,0:T(4,128)(2,1)}, bf16[40,4,192]{2,1,0:T(4,128)(2,1)}, u32[]{:S(2)}, u32[]{:S(2)}) collective-permute-start(bf16[40,4,192]{2,1,0:T(4,128)(2,1)} %get-tuple-element.23), channel_id=1, source_target_pairs={{0,1},{1,2},{2,3},{3,4},{4,5},{5,6},{6,7},{7,8},{8,9},{9,10},{10,1... | collective-permute-start | bytes 184328 | tf_op jit(solution)/shard_map/ppermute | solution.py:23
  218.6 1.9 collective-permute-start.23
  223.1 2.0 convolution_bitcast_fusion
  227.1 8.7 %all-to-all-start.6 = ((f32[32,1,1536]{2,1,0:T(1,128)}), f32[32,1,1536]{2,1,0:T(1,128)S(1)}, u32[]{:S(2)}, u32[]{:S(2)}) async-start(f32[32,1,1536]{2,1,0:T(1,128)} %all_to_all.55), calls=%async_computation.6 | async-start | bytes 393216 | tf_op jit(solution)/shard_map/all_to_all | solution.py:78
  239.3 2.5 copy.56
  241.8 4.2 %all-to-all-done.6 = f32[32,1,1536]{2,1,0:T(1,128)S(1)} async-done(((f32[32,1,1536]{2,1,0:T(1,128)}), f32[32,1,1536]{2,1,0:T(1,128)S(1)}, u32[]{:S(2)}, u32[]{:S(2)}) %all-to-all-start.6) | async-done | bytes 196640 | tf_op jit(solution)/shard_map/all_to_all | solution.py:78
  247.8 5.7 %add_add_fusion = (f32[32,32,192]{2,1,0:T(8,128)}, f32[32,32,192]{2,1,0:T(8,128)S(1)}) fusion(f32[32,32,192]{2,1,0:T(8,128)} %bitcast.94, f32[192]{0:T(256)} %copy-done.42, f32[32,32]{1,0:T(8,128)} %get-tuple-element.42, f32[192]{0:T(256)} %copy-done.43, f32[32,32]{1,0:T(8,128)} %get-tuple-element.41, f32[192]{0:T(256)} %copy-done.44, ...), kind=kLoop, calls=%fused_computation.90 | loop fusion | flops 11403264 | bytes 4769792 | tf_op jit(solution)/shard_map/add | solution.py:136
  253.5 1.9 collective-permute-start.26
  255.5 5.1 %collective-permute-start.27 = (f32[32,1,192]{2,1,0:T(1,128)S(1)}, f32[32,1,192]{2,1,0:T(1,128)S(1)}, u32[]{:S(2)}, u32[]{:S(2)}) collective-permute-start(f32[32,1,192]{2,1,0:T(1,128)S(1)} %get-tuple-element.10), channel_id=1, source_target_pairs={{0,1},{1,2},{2,3},{3,4},{4,5},{5,6},{6,7},{7,8},{8,9},{9,10},{10,1... | collective-permute-start | bytes 73736 | tf_op jit(solution)/shard_map/ppermute | solution.py:41
  260.6 3.1 %collective-permute-start.25 = (f32[1,32,192]{2,1,0:T(8,128)S(1)}, f32[1,32,192]{2,1,0:T(8,128)S(1)}, u32[]{:S(2)}, u32[]{:S(2)}) collective-permute-start(f32[1,32,192]{2,1,0:T(8,128)S(1)} %get-tuple-element.11), channel_id=1, source_target_pairs={{0,16},{16,32},{32,48},{48,64},{64,80},{80,96},{96,112},{112,128},... | collective-permute-start | bytes 73736 | tf_op jit(solution)/shard_map/ppermute | solution.py:39
  265.9 2.4 collective-permute-done.24
  270.7 8.2 %all-to-all-start.7 = ((f32[16,1,192]{2,1,0:T(1,128)}), f32[16,1,192]{2,1,0:T(1,128)S(1)}, u32[]{:S(2)}, u32[]{:S(2)}) async-start(f32[16,1,192]{2,1,0:T(1,128)} %broadcast_in_dim.33), calls=%async_computation.7 | async-start | bytes 32768 | tf_op jit(solution)/shard_map/all_to_all | solution.py:72
  279.9 6.4 %all-to-all-done.7 = f32[16,1,192]{2,1,0:T(1,128)S(1)} async-done(((f32[16,1,192]{2,1,0:T(1,128)}), f32[16,1,192]{2,1,0:T(1,128)S(1)}, u32[]{:S(2)}, u32[]{:S(2)}) %all-to-all-start.7) | async-done | bytes 12320 | tf_op jit(solution)/shard_map/all_to_all | solution.py:72
  286.5 15.5 %all_to_all.65 = f32[32,1,768]{2,1,0:T(1,128)S(1)} all-to-all(f32[32,1,768]{2,1,0:T(1,128)S(1)} %broadcast_in_dim.69), channel_id=1, replica_groups=mesh['gx'=32,'gy'=16] {'gx'}, dimensions={0} | all-to-all | bytes 196608 | tf_op jit(solution)/shard_map/all_to_all | solution.py:72
  (221 shorter events, 80.7 us)
Async XLA Ops:
  0.6 80.6 %copy-start = (bf16[1,1,1024,1600]{2,3,1,0:T(8,128)(2,1)S(1)}, bf16[1,1,1024,1600]{2,3,1,0:T(8,128)(2,1)}, u32[]{:S(2)}) copy-start(bf16[1,1,1024,1600]{2,3,1,0:T(8,128)(2,1)} %param.10) | copy-start | bytes 9830404
  2.1 91.0 %collective-permute-start.6 = (f32[1,32]{1,0:T(1,128)}, f32[1,32]{1,0:T(1,128)}, u32[]{:S(2)}, u32[]{:S(2)}) collective-permute-start(f32[1,32]{1,0:T(1,128)} %get-tuple-element.49), channel_id=1, source_target_pairs={{0,16},{16,32},{32,48},{48,64},{64,80},{80,96},{96,112},{112,128},... | collective-permute-start | bytes 392 | tf_op jit(solution)/shard_map/ppermute | solution.py:39
  7.5 90.7 %collective-permute-start.4 = (f32[1,32]{1,0:T(1,128)}, f32[1,32]{1,0:T(1,128)}, u32[]{:S(2)}, u32[]{:S(2)}) collective-permute-start(f32[1,32]{1,0:T(1,128)} %get-tuple-element.50), channel_id=1, source_target_pairs={{16,0},{32,16},{48,32},{64,48},{80,64},{96,80},{112,96},{128,112},... | collective-permute-start | bytes 392 | tf_op jit(solution)/shard_map/ppermute | solution.py:40
  10.2 91.1 %collective-permute-start.8 = (f32[32,1]{1,0:T(8,128)}, f32[32,1]{1,0:T(8,128)}, u32[]{:S(2)}, u32[]{:S(2)}) collective-permute-start(f32[32,1]{1,0:T(8,128)} %get-tuple-element.47), channel_id=1, source_target_pairs={{1,0},{2,1},{3,2},{4,3},{5,4},{6,5},{7,6},{8,7},{9,8},{10,9},{11,1... | collective-permute-start | bytes 392 | tf_op jit(solution)/shard_map/ppermute | solution.py:42
  19.5 13.7 %all-to-all-start = ((f32[16,1,1728]{2,1,0:T(1,128)}), f32[16,1,1728]{2,1,0:T(1,128)S(1)}, u32[]{:S(2)}, u32[]{:S(2)}) async-start(f32[16,1,1728]{2,1,0:T(1,128)} %broadcast_in_dim.26), calls=%async_computation | async-start | bytes 229376 | tf_op jit(solution)/shard_map/all_to_all | solution.py:72
  25.9 23.1 %collective-permute-start = (bf16[4,32,192]{2,1,0:T(8,128)(2,1)}, bf16[4,32,192]{2,1,0:T(8,128)(2,1)}, u32[]{:S(2)}, u32[]{:S(2)}) collective-permute-start(bf16[4,32,192]{2,1,0:T(8,128)(2,1)} %get-tuple-element.33), channel_id=1, source_target_pairs={{0,16},{16,32},{32,48},{48,64},{64,80},{80,96},{96,112},{112,128},... | collective-permute-start | bytes 147464 | tf_op jit(solution)/shard_map/ppermute | solution.py:23
  30.8 18.2 %collective-permute-start.1 = (bf16[4,32,192]{2,1,0:T(8,128)(2,1)}, bf16[4,32,192]{2,1,0:T(8,128)(2,1)}, u32[]{:S(2)}, u32[]{:S(2)}) collective-permute-start(bf16[4,32,192]{2,1,0:T(8,128)(2,1)} %get-tuple-element.34), channel_id=1, source_target_pairs={{16,0},{32,16},{48,32},{64,48},{80,64},{96,80},{112,96},{128,112},... | collective-permute-start | bytes 147464 | tf_op jit(solution)/shard_map/ppermute | solution.py:25
  33.9 26.6 %all-to-all-start.1 = ((f32[32,8,128]{2,1,0:T(8,128)}), f32[32,8,128]{2,1,0:T(8,128)S(1)}, u32[]{:S(2)}, u32[]{:S(2)}) async-start(f32[32,8,128]{2,1,0:T(8,128)} %bitcast.101), calls=%async_computation.1 | async-start | bytes 262144 | tf_op jit(solution)/shard_map/all_to_all | solution.py:101
  50.8 25.0 %collective-permute-start.2 = (bf16[40,4,192]{2,1,0:T(4,128)(2,1)}, bf16[40,4,192]{2,1,0:T(4,128)(2,1)}, u32[]{:S(2)}, u32[]{:S(2)}) collective-permute-start(bf16[40,4,192]{2,1,0:T(4,128)(2,1)} %get-tuple-element.27), channel_id=1, source_target_pairs={{0,1},{1,2},{2,3},{3,4},{4,5},{5,6},{6,7},{7,8},{8,9},{9,10},{10,1... | collective-permute-start | bytes 184328 | tf_op jit(solution)/shard_map/ppermute | solution.py:23
  55.0 24.7 %collective-permute-start.3 = (bf16[40,4,192]{2,1,0:T(4,128)(2,1)}, bf16[40,4,192]{2,1,0:T(4,128)(2,1)}, u32[]{:S(2)}, u32[]{:S(2)}) collective-permute-start(bf16[40,4,192]{2,1,0:T(4,128)(2,1)} %get-tuple-element.28), channel_id=1, source_target_pairs={{1,0},{2,1},{3,2},{4,3},{5,4},{6,5},{7,6},{8,7},{9,8},{10,9},{11,1... | collective-permute-start | bytes 184328 | tf_op jit(solution)/shard_map/ppermute | solution.py:25
  66.1 19.8 %all-to-all-start.2 = ((f32[32,1,1536]{2,1,0:T(1,128)}), f32[32,1,1536]{2,1,0:T(1,128)}, u32[]{:S(2)}, u32[]{:S(2)}) async-start(f32[32,1,1536]{2,1,0:T(1,128)} %all_to_all.53), calls=%async_computation.2 | async-start | bytes 393216 | tf_op jit(solution)/shard_map/all_to_all | solution.py:78
  75.8 26.8 %collective-permute-start.10 = (f32[32,1]{1,0:T(8,128)}, f32[32,1]{1,0:T(8,128)}, u32[]{:S(2)}, u32[]{:S(2)}) collective-permute-start(f32[32,1]{1,0:T(8,128)} %get-tuple-element.48), channel_id=1, source_target_pairs={{0,1},{1,2},{2,3},{3,4},{4,5},{5,6},{6,7},{7,8},{8,9},{9,10},{10,1... | collective-permute-start | bytes 392 | tf_op jit(solution)/shard_map/ppermute | solution.py:41
  88.6 20.0 %copy-start.42 = (f32[192]{0:T(256)}, f32[192]{0:T(256)S(1)}, u32[]{:S(2)}) copy-start(f32[192]{0:T(256)S(1)} %get-tuple-element.68) | copy-start | bytes 2308
  88.6 20.0 %copy-start.43 = (f32[192]{0:T(256)}, f32[192]{0:T(256)S(1)}, u32[]{:S(2)}) copy-start(f32[192]{0:T(256)S(1)} %get-tuple-element.69) | copy-start | bytes 2308
  88.6 20.0 %copy-start.44 = (f32[192]{0:T(256)}, f32[192]{0:T(256)S(1)}, u32[]{:S(2)}) copy-start(f32[192]{0:T(256)S(1)} %get-tuple-element.70) | copy-start | bytes 2308
  88.6 20.0 %copy-start.45 = (f32[192]{0:T(256)}, f32[192]{0:T(256)S(1)}, u32[]{:S(2)}) copy-start(f32[192]{0:T(256)S(1)} %get-tuple-element.71) | copy-start | bytes 2308
  91.1 12.4 %collective-permute-start.9 = (f32[32,1,192]{2,1,0:T(1,128)S(1)}, f32[32,1,192]{2,1,0:T(1,128)S(1)}, u32[]{:S(2)}, u32[]{:S(2)}) collective-permute-start(f32[32,1,192]{2,1,0:T(1,128)S(1)} %get-tuple-element.17), channel_id=1, source_target_pairs={{1,0},{2,1},{3,2},{4,3},{5,4},{6,5},{7,6},{8,7},{9,8},{10,9},{11,1... | collective-permute-start | bytes 73736 | tf_op jit(solution)/shard_map/ppermute | solution.py:42
  93.1 10.4 %collective-permute-start.11 = (f32[32,1,192]{2,1,0:T(1,128)S(1)}, f32[32,1,192]{2,1,0:T(1,128)S(1)}, u32[]{:S(2)}, u32[]{:S(2)}) collective-permute-start(f32[32,1,192]{2,1,0:T(1,128)S(1)} %get-tuple-element.18), channel_id=1, source_target_pairs={{0,1},{1,2},{2,3},{3,4},{4,5},{5,6},{6,7},{7,8},{8,9},{9,10},{10,1... | collective-permute-start | bytes 73736 | tf_op jit(solution)/shard_map/ppermute | solution.py:41
  98.2 5.3 %collective-permute-start.7 = (f32[1,32,192]{2,1,0:T(8,128)S(1)}, f32[1,32,192]{2,1,0:T(8,128)S(1)}, u32[]{:S(2)}, u32[]{:S(2)}) collective-permute-start(f32[1,32,192]{2,1,0:T(8,128)S(1)} %get-tuple-element.19), channel_id=1, source_target_pairs={{0,16},{16,32},{32,48},{48,64},{64,80},{80,96},{96,112},{112,128},... | collective-permute-start | bytes 73736 | tf_op jit(solution)/shard_map/ppermute | solution.py:39
  101.3 4.7 %collective-permute-start.5 = (f32[1,32,192]{2,1,0:T(8,128)S(1)}, f32[1,32,192]{2,1,0:T(8,128)S(1)}, u32[]{:S(2)}, u32[]{:S(2)}) collective-permute-start(f32[1,32,192]{2,1,0:T(8,128)S(1)} %get-tuple-element.20), channel_id=1, source_target_pairs={{16,0},{32,16},{48,32},{64,48},{80,64},{96,80},{112,96},{128,112},... | collective-permute-start | bytes 73736 | tf_op jit(solution)/shard_map/ppermute | solution.py:40
  114.0 25.7 %all-to-all-start.3 = ((f32[16,1,1728]{2,1,0:T(1,128)}), f32[16,1,1728]{2,1,0:T(1,128)}, u32[]{:S(2)}, u32[]{:S(2)}) async-start(f32[16,1,1728]{2,1,0:T(1,128)} %broadcast_in_dim.29), calls=%async_computation.3 | async-start | bytes 229376 | tf_op jit(solution)/shard_map/all_to_all | solution.py:72
  123.1 4.1 %collective-permute-start.12 = (bf16[4,32,192]{2,1,0:T(8,128)(2,1)S(1)}, bf16[4,32,192]{2,1,0:T(8,128)(2,1)S(1)}, u32[]{:S(2)}, u32[]{:S(2)}) collective-permute-start(bf16[4,32,192]{2,1,0:T(8,128)(2,1)S(1)} %get-tuple-element.31), channel_id=1, source_target_pairs={{0,16},{16,32},{32,48},{48,64},{64,80},{80,96},{96,112},{112,128},... | collective-permute-start | bytes 147464 | tf_op jit(solution)/shard_map/ppermute | solution.py:23
  125.9 5.8 %collective-permute-start.13 = (bf16[4,32,192]{2,1,0:T(8,128)(2,1)S(1)}, bf16[4,32,192]{2,1,0:T(8,128)(2,1)S(1)}, u32[]{:S(2)}, u32[]{:S(2)}) collective-permute-start(bf16[4,32,192]{2,1,0:T(8,128)(2,1)S(1)} %get-tuple-element.32), channel_id=1, source_target_pairs={{16,0},{32,16},{48,32},{64,48},{80,64},{96,80},{112,96},{128,112},... | collective-permute-start | bytes 147464 | tf_op jit(solution)/shard_map/ppermute | solution.py:25
  133.4 24.9 %collective-permute-start.14 = (bf16[40,4,192]{2,1,0:T(4,128)(2,1)}, bf16[40,4,192]{2,1,0:T(4,128)(2,1)}, u32[]{:S(2)}, u32[]{:S(2)}) collective-permute-start(bf16[40,4,192]{2,1,0:T(4,128)(2,1)} %get-tuple-element.25), channel_id=1, source_target_pairs={{0,1},{1,2},{2,3},{3,4},{4,5},{5,6},{6,7},{7,8},{8,9},{9,10},{10,1... | collective-permute-start | bytes 184328 | tf_op jit(solution)/shard_map/ppermute | solution.py:23
  137.7 20.6 %collective-permute-start.15 = (bf16[40,4,192]{2,1,0:T(4,128)(2,1)}, bf16[40,4,192]{2,1,0:T(4,128)(2,1)}, u32[]{:S(2)}, u32[]{:S(2)}) collective-permute-start(bf16[40,4,192]{2,1,0:T(4,128)(2,1)} %get-tuple-element.26), channel_id=1, source_target_pairs={{1,0},{2,1},{3,2},{4,3},{5,4},{6,5},{7,6},{8,7},{9,8},{10,9},{11,1... | collective-permute-start | bytes 184328 | tf_op jit(solution)/shard_map/ppermute | solution.py:25
  148.9 19.7 %all-to-all-start.4 = ((f32[32,1,1536]{2,1,0:T(1,128)}), f32[32,1,1536]{2,1,0:T(1,128)}, u32[]{:S(2)}, u32[]{:S(2)}) async-start(f32[32,1,1536]{2,1,0:T(1,128)} %all_to_all.54), calls=%async_computation.4 | async-start | bytes 393216 | tf_op jit(solution)/shard_map/all_to_all | solution.py:78
  175.0 11.4 %collective-permute-start.17 = (f32[1,32,192]{2,1,0:T(8,128)S(1)}, f32[1,32,192]{2,1,0:T(8,128)S(1)}, u32[]{:S(2)}, u32[]{:S(2)}) collective-permute-start(f32[1,32,192]{2,1,0:T(8,128)S(1)} %get-tuple-element.15), channel_id=1, source_target_pairs={{0,16},{16,32},{32,48},{48,64},{64,80},{80,96},{96,112},{112,128},... | collective-permute-start | bytes 73736 | tf_op jit(solution)/shard_map/ppermute | solution.py:39
  178.1 8.4 %collective-permute-start.16 = (f32[1,32,192]{2,1,0:T(8,128)S(1)}, f32[1,32,192]{2,1,0:T(8,128)S(1)}, u32[]{:S(2)}, u32[]{:S(2)}) collective-permute-start(f32[1,32,192]{2,1,0:T(8,128)S(1)} %get-tuple-element.16), channel_id=1, source_target_pairs={{16,0},{32,16},{48,32},{64,48},{80,64},{96,80},{112,96},{128,112},... | collective-permute-start | bytes 73736 | tf_op jit(solution)/shard_map/ppermute | solution.py:40
  179.4 7.1 %collective-permute-start.18 = (f32[32,1,192]{2,1,0:T(1,128)S(1)}, f32[32,1,192]{2,1,0:T(1,128)S(1)}, u32[]{:S(2)}, u32[]{:S(2)}) collective-permute-start(f32[32,1,192]{2,1,0:T(1,128)S(1)} %get-tuple-element.13), channel_id=1, source_target_pairs={{1,0},{2,1},{3,2},{4,3},{5,4},{6,5},{7,6},{8,7},{9,8},{10,9},{11,1... | collective-permute-start | bytes 73736 | tf_op jit(solution)/shard_map/ppermute | solution.py:42
  181.3 6.1 %collective-permute-start.19 = (f32[32,1,192]{2,1,0:T(1,128)S(1)}, f32[32,1,192]{2,1,0:T(1,128)S(1)}, u32[]{:S(2)}, u32[]{:S(2)}) collective-permute-start(f32[32,1,192]{2,1,0:T(1,128)S(1)} %get-tuple-element.14), channel_id=1, source_target_pairs={{0,1},{1,2},{2,3},{3,4},{4,5},{5,6},{6,7},{7,8},{8,9},{9,10},{10,1... | collective-permute-start | bytes 73736 | tf_op jit(solution)/shard_map/ppermute | solution.py:41
  191.8 28.7 %all-to-all-start.5 = ((f32[16,1,1728]{2,1,0:T(1,128)}), f32[16,1,1728]{2,1,0:T(1,128)S(1)}, u32[]{:S(2)}, u32[]{:S(2)}) async-start(f32[16,1,1728]{2,1,0:T(1,128)} %broadcast_in_dim.32), calls=%async_computation.5 | async-start | bytes 229376 | tf_op jit(solution)/shard_map/all_to_all | solution.py:72
  202.5 7.1 %collective-permute-start.20 = (bf16[4,32,192]{2,1,0:T(8,128)(2,1)S(1)}, bf16[4,32,192]{2,1,0:T(8,128)(2,1)S(1)}, u32[]{:S(2)}, u32[]{:S(2)}) collective-permute-start(bf16[4,32,192]{2,1,0:T(8,128)(2,1)S(1)} %get-tuple-element.29), channel_id=1, source_target_pairs={{0,16},{16,32},{32,48},{48,64},{64,80},{80,96},{96,112},{112,128},... | collective-permute-start | bytes 147464 | tf_op jit(solution)/shard_map/ppermute | solution.py:23
  206.8 5.0 %collective-permute-start.21 = (bf16[4,32,192]{2,1,0:T(8,128)(2,1)S(1)}, bf16[4,32,192]{2,1,0:T(8,128)(2,1)S(1)}, u32[]{:S(2)}, u32[]{:S(2)}) collective-permute-start(bf16[4,32,192]{2,1,0:T(8,128)(2,1)S(1)} %get-tuple-element.30), channel_id=1, source_target_pairs={{16,0},{32,16},{48,32},{64,48},{80,64},{96,80},{112,96},{128,112},... | collective-permute-start | bytes 147464 | tf_op jit(solution)/shard_map/ppermute | solution.py:25
  213.6 22.3 %collective-permute-start.22 = (bf16[40,4,192]{2,1,0:T(4,128)(2,1)}, bf16[40,4,192]{2,1,0:T(4,128)(2,1)}, u32[]{:S(2)}, u32[]{:S(2)}) collective-permute-start(bf16[40,4,192]{2,1,0:T(4,128)(2,1)} %get-tuple-element.23), channel_id=1, source_target_pairs={{0,1},{1,2},{2,3},{3,4},{4,5},{5,6},{6,7},{7,8},{8,9},{9,10},{10,1... | collective-permute-start | bytes 184328 | tf_op jit(solution)/shard_map/ppermute | solution.py:23
  218.6 17.3 %collective-permute-start.23 = (bf16[40,4,192]{2,1,0:T(4,128)(2,1)}, bf16[40,4,192]{2,1,0:T(4,128)(2,1)}, u32[]{:S(2)}, u32[]{:S(2)}) collective-permute-start(bf16[40,4,192]{2,1,0:T(4,128)(2,1)} %get-tuple-element.24), channel_id=1, source_target_pairs={{1,0},{2,1},{3,2},{4,3},{5,4},{6,5},{7,6},{8,7},{9,8},{10,9},{11,1... | collective-permute-start | bytes 184328 | tf_op jit(solution)/shard_map/ppermute | solution.py:25
  227.1 18.9 %all-to-all-start.6 = ((f32[32,1,1536]{2,1,0:T(1,128)}), f32[32,1,1536]{2,1,0:T(1,128)S(1)}, u32[]{:S(2)}, u32[]{:S(2)}) async-start(f32[32,1,1536]{2,1,0:T(1,128)} %all_to_all.55), calls=%async_computation.6 | async-start | bytes 393216 | tf_op jit(solution)/shard_map/all_to_all | solution.py:78
  247.7 20.6 %copy-start.5 = (f32[32,32,192]{2,1,0:T(8,128)S(1)}, f32[32,32,192]{2,1,0:T(8,128)}, u32[]{:S(2)}) copy-start(f32[32,32,192]{2,1,0:T(8,128)} %copy-done.4) | copy-start | bytes 2359300
  247.7 20.6 %copy-start.23 = (f32[32,32]{1,0:T(8,128)S(1)}, f32[32,32]{1,0:T(8,128)}, u32[]{:S(2)}) copy-start(f32[32,32]{1,0:T(8,128)} %copy-done.21) | copy-start | bytes 12292
  247.8 20.6 %copy-start.26 = (f32[32,32]{1,0:T(8,128)S(1)}, f32[32,32]{1,0:T(8,128)}, u32[]{:S(2)}) copy-start(f32[32,32]{1,0:T(8,128)} %copy-done.24) | copy-start | bytes 12292
  247.8 20.6 %copy-start.29 = (f32[32,32]{1,0:T(8,128)S(1)}, f32[32,32]{1,0:T(8,128)}, u32[]{:S(2)}) copy-start(f32[32,32]{1,0:T(8,128)} %copy-done.27) | copy-start | bytes 12292
  247.8 20.6 %copy-start.32 = (f32[32,32]{1,0:T(8,128)S(1)}, f32[32,32]{1,0:T(8,128)}, u32[]{:S(2)}) copy-start(f32[32,32]{1,0:T(8,128)} %copy-done.30) | copy-start | bytes 12292
  247.8 20.6 %copy-start.39 = (f32[32,32]{1,0:T(8,128)S(1)}, f32[32,32]{1,0:T(8,128)}, u32[]{:S(2)}) copy-start(f32[32,32]{1,0:T(8,128)} %param.8) | copy-start | bytes 12292
  253.5 32.9 %copy-start.57 = (f32[192]{0:T(256)S(1)}, f32[192]{0:T(256)}, u32[]{:S(2)}) copy-start(f32[192]{0:T(256)} %slice_reduce_fusion.2) | copy-start | bytes 2308
  253.5 12.4 %collective-permute-start.26 = (f32[32,1,192]{2,1,0:T(1,128)S(1)}, f32[32,1,192]{2,1,0:T(1,128)S(1)}, u32[]{:S(2)}, u32[]{:S(2)}) collective-permute-start(f32[32,1,192]{2,1,0:T(1,128)S(1)} %get-tuple-element.9), channel_id=1, source_target_pairs={{1,0},{2,1},{3,2},{4,3},{5,4},{6,5},{7,6},{8,7},{9,8},{10,9},{11,1... | collective-permute-start | bytes 73736 | tf_op jit(solution)/shard_map/ppermute | solution.py:42
  255.5 10.4 %collective-permute-start.27 = (f32[32,1,192]{2,1,0:T(1,128)S(1)}, f32[32,1,192]{2,1,0:T(1,128)S(1)}, u32[]{:S(2)}, u32[]{:S(2)}) collective-permute-start(f32[32,1,192]{2,1,0:T(1,128)S(1)} %get-tuple-element.10), channel_id=1, source_target_pairs={{0,1},{1,2},{2,3},{3,4},{4,5},{5,6},{6,7},{7,8},{8,9},{9,10},{10,1... | collective-permute-start | bytes 73736 | tf_op jit(solution)/shard_map/ppermute | solution.py:41
  260.6 5.4 %collective-permute-start.25 = (f32[1,32,192]{2,1,0:T(8,128)S(1)}, f32[1,32,192]{2,1,0:T(8,128)S(1)}, u32[]{:S(2)}, u32[]{:S(2)}) collective-permute-start(f32[1,32,192]{2,1,0:T(8,128)S(1)} %get-tuple-element.11), channel_id=1, source_target_pairs={{0,16},{16,32},{32,48},{48,64},{64,80},{80,96},{96,112},{112,128},... | collective-permute-start | bytes 73736 | tf_op jit(solution)/shard_map/ppermute | solution.py:39
  263.7 4.7 %collective-permute-start.24 = (f32[1,32,192]{2,1,0:T(8,128)S(1)}, f32[1,32,192]{2,1,0:T(8,128)S(1)}, u32[]{:S(2)}, u32[]{:S(2)}) collective-permute-start(f32[1,32,192]{2,1,0:T(8,128)S(1)} %get-tuple-element.12), channel_id=1, source_target_pairs={{16,0},{32,16},{48,32},{64,48},{80,64},{96,80},{112,96},{128,112},... | collective-permute-start | bytes 73736 | tf_op jit(solution)/shard_map/ppermute | solution.py:40
  270.7 15.6 %all-to-all-start.7 = ((f32[16,1,192]{2,1,0:T(1,128)}), f32[16,1,192]{2,1,0:T(1,128)S(1)}, u32[]{:S(2)}, u32[]{:S(2)}) async-start(f32[16,1,192]{2,1,0:T(1,128)} %broadcast_in_dim.33), calls=%async_computation.7 | async-start | bytes 32768 | tf_op jit(solution)/shard_map/all_to_all | solution.py:72
  (46 other events, 518.5 us)

commit v9 on v8

--- a/solution.py
+++ b/solution.py
@@ -99,6 +99,7 @@
 
     pieces = coarse_inverse.reshape(modes, rows_x, cols_y * modes).transpose(1, 0, 2)
     pieces = lax.all_to_all(pieces, "gx", 0, 0, tiled=True)
+    pieces, state = lax.optimization_barrier((pieces, state))
     coarse_block = pieces.reshape(rows_x * modes, cols_y * modes)
 
     def rounded_window(current):

time: 306 us -> 303 us (level)
  local copies, waits for them, and re-layouts: 39 us -> 34.7 us
    dot_general x3 -> x0, local copies, waits for them, and re-layouts: 4.6 us -> none  [precondition(): jnp.dot(coarse_block, row_coarse, precision=highest)]
  transfers between devices with their start and end apart: 36 -> 36, of which waited for: 10 -> 10; matrix products, arithmetic and copies ran while one was open for 21% -> 19% of each run, Pallas kernels for 0% -> 0%
where the time goes in v9:
time: 303 us; the launch traced here: 300 us
  starting transfers between devices  158 us (52%)
  other arithmetic  45.5 us (15%)
  local copies, waits for them, and re-layouts  34.7 us (11%)
  waiting for transfers between devices  30.2 us (10%)
  blocking collectives  15.5 us (5%)
  matrix products  14.7 us (5%)
    all_to_all x4, starting transfers between devices, gathered_by_exchange(): lax.all_to_all(copies, axis, 0, 0, tiled=True)  33.5 us
    all_to_all x3, starting transfers between devices, summed_by_exchange(): received = lax.all_to_all(flat, axis, 0, 0, tiled=True)  28.5 us
    ppermute x6, starting transfers between devices, extended(): lax.ppermute(tail, axis, [(i, (i + 1) % count) for i in range(ends)])  25.6 us
    ppermute x4, starting transfers between devices, with_edges(): west = lax.ppermute(cells[:, -1:], 'gy', right)  19.2 us
    all_to_all x1, blocking collectives, gathered_by_exchange(): lax.all_to_all(copies, axis, 0, 0, tiled=True)  15.5 us
    all_to_all x1, starting transfers between devices, on_device(): pieces = lax.all_to_all(pieces, 'gx', 0, 0, tiled=True)  14 us
    ppermute x4, starting transfers between devices, with_edges(): north = lax.ppermute(cells[-1:], 'gx', down)  12.9 us
    ppermute x6, starting transfers between devices, extended(): lax.ppermute(head, axis, [((i + 1) % count, i) for i in range(ends)])  9.64 us
  transfers between devices with their start and end apart: 36, of which 10 were waited for; matrix products, arithmetic and copies ran while one was open for 19% of the time, Pallas kernels for 0%

profile of v9, /device:TPU:1, one launch (start us, length us, event | category | flops | bytes accessed | tf_op | source)
XLA Modules:
  0.0 300.2 jit_solution(2025242368090284127)
XLA Ops:
  0.6 14.0 %all-to-all-start = ((f32[32,8,128]{2,1,0:T(8,128)}), f32[32,8,128]{2,1,0:T(8,128)S(1)}, u32[]{:S(2)}, u32[]{:S(2)}) async-start(f32[32,8,128]{2,1,0:T(8,128)} %bitcast.97), calls=%async_computation | async-start | bytes 262144 | tf_op jit(solution)/shard_map/all_to_all | solution.py:101
  15.9 3.6 %collective-permute-start.6 = (f32[1,32]{1,0:T(1,128)}, f32[1,32]{1,0:T(1,128)}, u32[]{:S(2)}, u32[]{:S(2)}) collective-permute-start(f32[1,32]{1,0:T(1,128)} %get-tuple-element.53), channel_id=1, source_target_pairs={{0,16},{16,32},{32,48},{48,64},{64,80},{80,96},{96,112},{112,128},... | collective-permute-start | bytes 392 | tf_op jit(solution)/shard_map/ppermute | solution.py:39
  22.3 3.4 %collective-permute-start.8 = (f32[32,1]{1,0:T(8,128)}, f32[32,1]{1,0:T(8,128)}, u32[]{:S(2)}, u32[]{:S(2)}) collective-permute-start(f32[32,1]{1,0:T(8,128)} %get-tuple-element.51), channel_id=1, source_target_pairs={{1,0},{2,1},{3,2},{4,3},{5,4},{6,5},{7,6},{8,7},{9,8},{10,9},{11,1... | collective-permute-start | bytes 392 | tf_op jit(solution)/shard_map/ppermute | solution.py:42
  27.2 2.0 convolution_bitcast_fusion.2
  30.9 7.2 %all-to-all-start.1 = ((f32[16,1,1728]{2,1,0:T(1,128)}), f32[16,1,1728]{2,1,0:T(1,128)S(1)}, u32[]{:S(2)}, u32[]{:S(2)}) async-start(f32[16,1,1728]{2,1,0:T(1,128)} %broadcast_in_dim.26), calls=%async_computation.1 | async-start | bytes 229376 | tf_op jit(solution)/shard_map/all_to_all | solution.py:72
  39.0 4.3 %collective-permute-start = (bf16[4,32,192]{2,1,0:T(8,128)(2,1)S(1)}, bf16[4,32,192]{2,1,0:T(8,128)(2,1)S(1)}, u32[]{:S(2)}, u32[]{:S(2)}) collective-permute-start(bf16[4,32,192]{2,1,0:T(8,128)(2,1)S(1)} %get-tuple-element.37), channel_id=1, source_target_pairs={{0,16},{16,32},{32,48},{48,64},{64,80},{80,96},{96,112},{112,128},... | collective-permute-start | bytes 147464 | tf_op jit(solution)/shard_map/ppermute | solution.py:23
  45.9 2.4 collective-permute-done.1
  50.0 5.0 %collective-permute-start.2 = (bf16[40,4,192]{2,1,0:T(4,128)(2,1)}, bf16[40,4,192]{2,1,0:T(4,128)(2,1)}, u32[]{:S(2)}, u32[]{:S(2)}) collective-permute-start(bf16[40,4,192]{2,1,0:T(4,128)(2,1)} %get-tuple-element.31), channel_id=1, source_target_pairs={{0,1},{1,2},{2,3},{3,4},{4,5},{5,6},{6,7},{7,8},{8,9},{9,10},{10,1... | collective-permute-start | bytes 184328 | tf_op jit(solution)/shard_map/ppermute | solution.py:23
  55.0 1.9 collective-permute-start.3
  59.6 2.0 fusion.64
  63.4 10.3 %all-to-all-start.2 = ((f32[32,1,1536]{2,1,0:T(1,128)}), f32[32,1,1536]{2,1,0:T(1,128)}, u32[]{:S(2)}, u32[]{:S(2)}) async-start(f32[32,1,1536]{2,1,0:T(1,128)} %all_to_all.53), calls=%async_computation.2 | async-start | bytes 393216 | tf_op jit(solution)/shard_map/all_to_all | solution.py:78
  73.8 3.9 %collective-permute-start.10 = (f32[32,1]{1,0:T(8,128)}, f32[32,1]{1,0:T(8,128)}, u32[]{:S(2)}, u32[]{:S(2)}) collective-permute-start(f32[32,1]{1,0:T(8,128)} %get-tuple-element.52), channel_id=1, source_target_pairs={{0,1},{1,2},{2,3},{3,4},{4,5},{5,6},{6,7},{7,8},{8,9},{9,10},{10,1... | collective-permute-start | bytes 392 | tf_op jit(solution)/shard_map/ppermute | solution.py:41
  81.1 2.5 copy.48
  86.7 2.3 broadcast_multiply_fusion
  89.1 1.9 collective-permute-start.9
  91.0 5.1 %collective-permute-start.11 = (f32[32,1,192]{2,1,0:T(1,128)S(1)}, f32[32,1,192]{2,1,0:T(1,128)S(1)}, u32[]{:S(2)}, u32[]{:S(2)}) collective-permute-start(f32[32,1,192]{2,1,0:T(1,128)S(1)} %get-tuple-element.22), channel_id=1, source_target_pairs={{0,1},{1,2},{2,3},{3,4},{4,5},{5,6},{6,7},{7,8},{8,9},{9,10},{10,1... | collective-permute-start | bytes 73736 | tf_op jit(solution)/shard_map/ppermute | solution.py:41
  96.1 3.1 %collective-permute-start.7 = (f32[1,32,192]{2,1,0:T(8,128)S(1)}, f32[1,32,192]{2,1,0:T(8,128)S(1)}, u32[]{:S(2)}, u32[]{:S(2)}) collective-permute-start(f32[1,32,192]{2,1,0:T(8,128)S(1)} %get-tuple-element.23), channel_id=1, source_target_pairs={{0,16},{16,32},{32,48},{48,64},{64,80},{80,96},{96,112},{112,128},... | collective-permute-start | bytes 73736 | tf_op jit(solution)/shard_map/ppermute | solution.py:39
  101.5 2.4 collective-permute-done.5
  103.9 3.4 %multiply_reduce_fusion.1 = (f32[192]{0:T(256)S(1)}, f32[32,32,192]{2,1,0:T(8,128)S(1)}) fusion(f32[32,32,192]{2,1,0:T(8,128)S(1)} %copy-done.7, f32[32,32,192]{2,1,0:T(8,128)S(1)} %broadcast_multiply_fusion, f32[1,32,192]{2,1,0:T(8,128)S(1)} %collective-permute-done.5, f32[1,32,192]{2,1,0:T(8,128)S(1)} %collective-permute-done.7, ...), kind=kLoop, calls=%fused_computation.89 | loop fusion | flops 9043776 | bytes 3304192 | tf_op jit(solution)/shard_map/reduce_sum | solution.py:114
  112.7 8.2 %all-to-all-start.3 = ((f32[16,1,1728]{2,1,0:T(1,128)}), f32[16,1,1728]{2,1,0:T(1,128)}, u32[]{:S(2)}, u32[]{:S(2)}) async-start(f32[16,1,1728]{2,1,0:T(1,128)} %broadcast_in_dim.29), calls=%async_computation.3 | async-start | bytes 229376 | tf_op jit(solution)/shard_map/all_to_all | solution.py:72
  121.8 2.9 collective-permute-start.12
  126.1 4.5 %collective-permute-done.13 = bf16[4,32,192]{2,1,0:T(8,128)(2,1)S(1)} collective-permute-done((bf16[4,32,192]{2,1,0:T(8,128)(2,1)S(1)}, bf16[4,32,192]{2,1,0:T(8,128)(2,1)S(1)}, u32[]{:S(2)}, u32[]{:S(2)}) %collective-permute-start.13) | collective-permute-done | bytes 49184 | tf_op jit(solution)/shard_map/ppermute | solution.py:25
  132.3 4.3 %collective-permute-start.14 = (bf16[40,4,192]{2,1,0:T(4,128)(2,1)}, bf16[40,4,192]{2,1,0:T(4,128)(2,1)}, u32[]{:S(2)}, u32[]{:S(2)}) collective-permute-start(bf16[40,4,192]{2,1,0:T(4,128)(2,1)} %get-tuple-element.29), channel_id=1, source_target_pairs={{0,1},{1,2},{2,3},{3,4},{4,5},{5,6},{6,7},{7,8},{8,9},{9,10},{10,1... | collective-permute-start | bytes 184328 | tf_op jit(solution)/shard_map/ppermute | solution.py:23
  136.6 1.9 collective-permute-start.15
  142.0 2.0 fusion.63
  145.8 9.4 %all-to-all-start.4 = ((f32[32,1,1536]{2,1,0:T(1,128)}), f32[32,1,1536]{2,1,0:T(1,128)}, u32[]{:S(2)}, u32[]{:S(2)}) async-start(f32[32,1,1536]{2,1,0:T(1,128)} %all_to_all.54), calls=%async_computation.4 | async-start | bytes 393216 | tf_op jit(solution)/shard_map/all_to_all | solution.py:78
  158.6 2.5 copy.52
  161.1 4.4 %all-to-all-done.4 = f32[32,1,1536]{2,1,0:T(1,128)} async-done(((f32[32,1,1536]{2,1,0:T(1,128)}), f32[32,1,1536]{2,1,0:T(1,128)}, u32[]{:S(2)}, u32[]{:S(2)}) %all-to-all-start.4) | async-done | bytes 196640 | tf_op jit(solution)/shard_map/all_to_all | solution.py:78
  168.3 3.5 %multiply_add_fusion.1 = f32[32,32,192]{2,1,0:T(8,128)S(1)} fusion(f32[32,32,192]{2,1,0:T(8,128)} %bitcast.91, f32[192]{0:T(256)S(1)} %get-tuple-element.64, f32[192]{0:T(256)S(1)} %get-tuple-element.65, f32[192]{0:T(256)S(1)} %get-tuple-element.66, f32[192]{0:T(256)S(1)} %get-tuple-element.67, f32[192]{0:T(256)S(1)} %get-tuple-element.68, ...), kind=kLoop, calls=%fused_computation.88 | loop fusion | flops 6881280 | bytes 2404352 | tf_op jit(solution)/shard_map/add | solution.py:144
  171.9 3.0 %collective-permute-start.17 = (f32[1,32,192]{2,1,0:T(8,128)S(1)}, f32[1,32,192]{2,1,0:T(8,128)S(1)}, u32[]{:S(2)}, u32[]{:S(2)}) collective-permute-start(f32[1,32,192]{2,1,0:T(8,128)S(1)} %get-tuple-element.19), channel_id=1, source_target_pairs={{0,16},{16,32},{32,48},{48,64},{64,80},{80,96},{96,112},{112,128},... | collective-permute-start | bytes 73736 | tf_op jit(solution)/shard_map/ppermute | solution.py:39
  176.3 1.9 collective-permute-start.18
  178.2 5.1 %collective-permute-start.19 = (f32[32,1,192]{2,1,0:T(1,128)S(1)}, f32[32,1,192]{2,1,0:T(1,128)S(1)}, u32[]{:S(2)}, u32[]{:S(2)}) collective-permute-start(f32[32,1,192]{2,1,0:T(1,128)S(1)} %get-tuple-element.18), channel_id=1, source_target_pairs={{0,1},{1,2},{2,3},{3,4},{4,5},{5,6},{6,7},{7,8},{8,9},{9,10},{10,1... | collective-permute-start | bytes 73736 | tf_op jit(solution)/shard_map/ppermute | solution.py:41
  188.8 9.8 %all-to-all-start.5 = ((f32[16,1,1728]{2,1,0:T(1,128)}), f32[16,1,1728]{2,1,0:T(1,128)S(1)}, u32[]{:S(2)}, u32[]{:S(2)}) async-start(f32[16,1,1728]{2,1,0:T(1,128)} %broadcast_in_dim.32), calls=%async_computation.5 | async-start | bytes 229376 | tf_op jit(solution)/shard_map/all_to_all | solution.py:72
  199.5 4.3 %collective-permute-start.20 = (bf16[4,32,192]{2,1,0:T(8,128)(2,1)S(1)}, bf16[4,32,192]{2,1,0:T(8,128)(2,1)S(1)}, u32[]{:S(2)}, u32[]{:S(2)}) collective-permute-start(bf16[4,32,192]{2,1,0:T(8,128)(2,1)S(1)} %get-tuple-element.33), channel_id=1, source_target_pairs={{0,16},{16,32},{32,48},{48,64},{64,80},{80,96},{96,112},{112,128},... | collective-permute-start | bytes 147464 | tf_op jit(solution)/shard_map/ppermute | solution.py:23
  206.5 2.3 collective-permute-done.21
  210.5 5.0 %collective-permute-start.22 = (bf16[40,4,192]{2,1,0:T(4,128)(2,1)}, bf16[40,4,192]{2,1,0:T(4,128)(2,1)}, u32[]{:S(2)}, u32[]{:S(2)}) collective-permute-start(bf16[40,4,192]{2,1,0:T(4,128)(2,1)} %get-tuple-element.27), channel_id=1, source_target_pairs={{0,1},{1,2},{2,3},{3,4},{4,5},{5,6},{6,7},{7,8},{8,9},{9,10},{10,1... | collective-permute-start | bytes 184328 | tf_op jit(solution)/shard_map/ppermute | solution.py:23
  215.5 1.9 collective-permute-start.23
  220.1 2.0 fusion.62
  223.9 8.7 %all-to-all-start.6 = ((f32[32,1,1536]{2,1,0:T(1,128)}), f32[32,1,1536]{2,1,0:T(1,128)S(1)}, u32[]{:S(2)}, u32[]{:S(2)}) async-start(f32[32,1,1536]{2,1,0:T(1,128)} %all_to_all.55), calls=%async_computation.6 | async-start | bytes 393216 | tf_op jit(solution)/shard_map/all_to_all | solution.py:78
  236.1 2.5 copy.56
  238.6 4.2 %all-to-all-done.6 = f32[32,1,1536]{2,1,0:T(1,128)S(1)} async-done(((f32[32,1,1536]{2,1,0:T(1,128)}), f32[32,1,1536]{2,1,0:T(1,128)S(1)}, u32[]{:S(2)}, u32[]{:S(2)}) %all-to-all-start.6) | async-done | bytes 196640 | tf_op jit(solution)/shard_map/all_to_all | solution.py:78
  244.6 5.6 %add_add_fusion = (f32[32,32,192]{2,1,0:T(8,128)}, f32[32,32,192]{2,1,0:T(8,128)S(1)}) fusion(f32[32,32,192]{2,1,0:T(8,128)} %bitcast.90, f32[192]{0:T(256)} %copy-done.44, f32[32,32]{1,0:T(8,128)} %get-tuple-element.46, f32[192]{0:T(256)} %copy-done.45, f32[32,32]{1,0:T(8,128)} %get-tuple-element.45, f32[192]{0:T(256)} %copy-done.46, ...), kind=kLoop, calls=%fused_computation.87 | loop fusion | flops 11403264 | bytes 4769792 | tf_op jit(solution)/shard_map/add | solution.py:137
  252.3 5.1 %collective-permute-start.27 = (f32[32,1,192]{2,1,0:T(1,128)S(1)}, f32[32,1,192]{2,1,0:T(1,128)S(1)}, u32[]{:S(2)}, u32[]{:S(2)}) collective-permute-start(f32[32,1,192]{2,1,0:T(1,128)S(1)} %get-tuple-element.14), channel_id=1, source_target_pairs={{0,1},{1,2},{2,3},{3,4},{4,5},{5,6},{6,7},{7,8},{8,9},{9,10},{10,1... | collective-permute-start | bytes 73736 | tf_op jit(solution)/shard_map/ppermute | solution.py:41
  257.4 3.1 %collective-permute-start.25 = (f32[1,32,192]{2,1,0:T(8,128)S(1)}, f32[1,32,192]{2,1,0:T(8,128)S(1)}, u32[]{:S(2)}, u32[]{:S(2)}) collective-permute-start(f32[1,32,192]{2,1,0:T(8,128)S(1)} %get-tuple-element.15), channel_id=1, source_target_pairs={{0,16},{16,32},{32,48},{48,64},{64,80},{80,96},{96,112},{112,128},... | collective-permute-start | bytes 73736 | tf_op jit(solution)/shard_map/ppermute | solution.py:39
  262.7 2.4 collective-permute-done.24
  267.5 8.2 %all-to-all-start.7 = ((f32[16,1,192]{2,1,0:T(1,128)}), f32[16,1,192]{2,1,0:T(1,128)S(1)}, u32[]{:S(2)}, u32[]{:S(2)}) async-start(f32[16,1,192]{2,1,0:T(1,128)} %broadcast_in_dim.33), calls=%async_computation.7 | async-start | bytes 32768 | tf_op jit(solution)/shard_map/all_to_all | solution.py:72
  276.7 6.4 %all-to-all-done.7 = f32[16,1,192]{2,1,0:T(1,128)S(1)} async-done(((f32[16,1,192]{2,1,0:T(1,128)}), f32[16,1,192]{2,1,0:T(1,128)S(1)}, u32[]{:S(2)}, u32[]{:S(2)}) %all-to-all-start.7) | async-done | bytes 12320 | tf_op jit(solution)/shard_map/all_to_all | solution.py:72
  283.3 15.5 %all_to_all.65 = f32[32,1,768]{2,1,0:T(1,128)S(1)} all-to-all(f32[32,1,768]{2,1,0:T(1,128)S(1)} %broadcast_in_dim.69), channel_id=1, replica_groups=mesh['gx'=32,'gy'=16] {'gx'}, dimensions={0} | all-to-all | bytes 196608 | tf_op jit(solution)/shard_map/all_to_all | solution.py:72
  (222 shorter events, 76.9 us)
Async XLA Ops:
  0.6 78.6 %copy-start = (bf16[1,1,1024,1600]{2,3,1,0:T(8,128)(2,1)S(1)}, bf16[1,1,1024,1600]{2,3,1,0:T(8,128)(2,1)}, u32[]{:S(2)}) copy-start(bf16[1,1,1024,1600]{2,3,1,0:T(8,128)(2,1)} %param.10) | copy-start | bytes 9830404
  0.6 26.5 %all-to-all-start = ((f32[32,8,128]{2,1,0:T(8,128)}), f32[32,8,128]{2,1,0:T(8,128)S(1)}, u32[]{:S(2)}, u32[]{:S(2)}) async-start(f32[32,8,128]{2,1,0:T(8,128)} %bitcast.97), calls=%async_computation | async-start | bytes 262144 | tf_op jit(solution)/shard_map/all_to_all | solution.py:101
  15.9 75.1 %collective-permute-start.6 = (f32[1,32]{1,0:T(1,128)}, f32[1,32]{1,0:T(1,128)}, u32[]{:S(2)}, u32[]{:S(2)}) collective-permute-start(f32[1,32]{1,0:T(1,128)} %get-tuple-element.53), channel_id=1, source_target_pairs={{0,16},{16,32},{32,48},{48,64},{64,80},{80,96},{96,112},{112,128},... | collective-permute-start | bytes 392 | tf_op jit(solution)/shard_map/ppermute | solution.py:39
  19.5 76.6 %collective-permute-start.4 = (f32[1,32]{1,0:T(1,128)}, f32[1,32]{1,0:T(1,128)}, u32[]{:S(2)}, u32[]{:S(2)}) collective-permute-start(f32[1,32]{1,0:T(1,128)} %get-tuple-element.54), channel_id=1, source_target_pairs={{16,0},{32,16},{48,32},{64,48},{80,64},{96,80},{112,96},{128,112},... | collective-permute-start | bytes 392 | tf_op jit(solution)/shard_map/ppermute | solution.py:40
  22.3 77.0 %collective-permute-start.8 = (f32[32,1]{1,0:T(8,128)}, f32[32,1]{1,0:T(8,128)}, u32[]{:S(2)}, u32[]{:S(2)}) collective-permute-start(f32[32,1]{1,0:T(8,128)} %get-tuple-element.51), channel_id=1, source_target_pairs={{1,0},{2,1},{3,2},{4,3},{5,4},{6,5},{7,6},{8,7},{9,8},{10,9},{11,1... | collective-permute-start | bytes 392 | tf_op jit(solution)/shard_map/ppermute | solution.py:42
  27.2 59.5 %copy-start.9 = (f32[32,32]{1,0:T(8,128)}, f32[32,32]{1,0:T(8,128)S(1)}, u32[]{:S(2)}) copy-start(f32[32,32]{1,0:T(8,128)S(1)} %get-tuple-element.40) | copy-start | bytes 12292
  30.9 26.0 %all-to-all-start.1 = ((f32[16,1,1728]{2,1,0:T(1,128)}), f32[16,1,1728]{2,1,0:T(1,128)S(1)}, u32[]{:S(2)}, u32[]{:S(2)}) async-start(f32[16,1,1728]{2,1,0:T(1,128)} %broadcast_in_dim.26), calls=%async_computation.1 | async-start | bytes 229376 | tf_op jit(solution)/shard_map/all_to_all | solution.py:72
  39.0 6.9 %collective-permute-start = (bf16[4,32,192]{2,1,0:T(8,128)(2,1)S(1)}, bf16[4,32,192]{2,1,0:T(8,128)(2,1)S(1)}, u32[]{:S(2)}, u32[]{:S(2)}) collective-permute-start(bf16[4,32,192]{2,1,0:T(8,128)(2,1)S(1)} %get-tuple-element.37), channel_id=1, source_target_pairs={{0,16},{16,32},{32,48},{48,64},{64,80},{80,96},{96,112},{112,128},... | collective-permute-start | bytes 147464 | tf_op jit(solution)/shard_map/ppermute | solution.py:23
  43.3 5.0 %collective-permute-start.1 = (bf16[4,32,192]{2,1,0:T(8,128)(2,1)S(1)}, bf16[4,32,192]{2,1,0:T(8,128)(2,1)S(1)}, u32[]{:S(2)}, u32[]{:S(2)}) collective-permute-start(bf16[4,32,192]{2,1,0:T(8,128)(2,1)S(1)} %get-tuple-element.38), channel_id=1, source_target_pairs={{16,0},{32,16},{48,32},{64,48},{80,64},{96,80},{112,96},{128,112},... | collective-permute-start | bytes 147464 | tf_op jit(solution)/shard_map/ppermute | solution.py:25
  50.0 23.7 %collective-permute-start.2 = (bf16[40,4,192]{2,1,0:T(4,128)(2,1)}, bf16[40,4,192]{2,1,0:T(4,128)(2,1)}, u32[]{:S(2)}, u32[]{:S(2)}) collective-permute-start(bf16[40,4,192]{2,1,0:T(4,128)(2,1)} %get-tuple-element.31), channel_id=1, source_target_pairs={{0,1},{1,2},{2,3},{3,4},{4,5},{5,6},{6,7},{7,8},{8,9},{9,10},{10,1... | collective-permute-start | bytes 184328 | tf_op jit(solution)/shard_map/ppermute | solution.py:23
  55.0 22.7 %collective-permute-start.3 = (bf16[40,4,192]{2,1,0:T(4,128)(2,1)}, bf16[40,4,192]{2,1,0:T(4,128)(2,1)}, u32[]{:S(2)}, u32[]{:S(2)}) collective-permute-start(bf16[40,4,192]{2,1,0:T(4,128)(2,1)} %get-tuple-element.32), channel_id=1, source_target_pairs={{1,0},{2,1},{3,2},{4,3},{5,4},{6,5},{7,6},{8,7},{9,8},{10,9},{11,1... | collective-permute-start | bytes 184328 | tf_op jit(solution)/shard_map/ppermute | solution.py:25
  63.4 20.5 %all-to-all-start.2 = ((f32[32,1,1536]{2,1,0:T(1,128)}), f32[32,1,1536]{2,1,0:T(1,128)}, u32[]{:S(2)}, u32[]{:S(2)}) async-start(f32[32,1,1536]{2,1,0:T(1,128)} %all_to_all.53), calls=%async_computation.2 | async-start | bytes 393216 | tf_op jit(solution)/shard_map/all_to_all | solution.py:78
  73.8 26.7 %collective-permute-start.10 = (f32[32,1]{1,0:T(8,128)}, f32[32,1]{1,0:T(8,128)}, u32[]{:S(2)}, u32[]{:S(2)}) collective-permute-start(f32[32,1]{1,0:T(8,128)} %get-tuple-element.52), channel_id=1, source_target_pairs={{0,1},{1,2},{2,3},{3,4},{4,5},{5,6},{6,7},{7,8},{8,9},{9,10},{10,1... | collective-permute-start | bytes 392 | tf_op jit(solution)/shard_map/ppermute | solution.py:41
  86.5 20.8 %copy-start.43 = (f32[192]{0:T(256)}, f32[192]{0:T(256)S(1)}, u32[]{:S(2)}) copy-start(f32[192]{0:T(256)S(1)} %get-tuple-element.71) | copy-start | bytes 2308
  86.6 20.8 %copy-start.44 = (f32[192]{0:T(256)}, f32[192]{0:T(256)S(1)}, u32[]{:S(2)}) copy-start(f32[192]{0:T(256)S(1)} %get-tuple-element.72) | copy-start | bytes 2308
  86.6 20.8 %copy-start.45 = (f32[192]{0:T(256)}, f32[192]{0:T(256)S(1)}, u32[]{:S(2)}) copy-start(f32[192]{0:T(256)S(1)} %get-tuple-element.73) | copy-start | bytes 2308
  86.6 20.8 %copy-start.46 = (f32[192]{0:T(256)}, f32[192]{0:T(256)S(1)}, u32[]{:S(2)}) copy-start(f32[192]{0:T(256)S(1)} %get-tuple-element.74) | copy-start | bytes 2308
  86.6 20.8 %copy-start.47 = (f32[192]{0:T(256)}, f32[192]{0:T(256)S(1)}, u32[]{:S(2)}) copy-start(f32[192]{0:T(256)S(1)} %get-tuple-element.75) | copy-start | bytes 2308
  86.6 20.8 %copy-start.48 = (f32[192]{0:T(256)}, f32[192]{0:T(256)S(1)}, u32[]{:S(2)}) copy-start(f32[192]{0:T(256)S(1)} %get-tuple-element.76) | copy-start | bytes 2308
  86.6 20.8 %copy-start.49 = (f32[192]{0:T(256)}, f32[192]{0:T(256)S(1)}, u32[]{:S(2)}) copy-start(f32[192]{0:T(256)S(1)} %get-tuple-element.77) | copy-start | bytes 2308
  86.6 20.8 %copy-start.50 = (f32[192]{0:T(256)}, f32[192]{0:T(256)S(1)}, u32[]{:S(2)}) copy-start(f32[192]{0:T(256)S(1)} %get-tuple-element.78) | copy-start | bytes 2308
  89.1 12.4 %collective-permute-start.9 = (f32[32,1,192]{2,1,0:T(1,128)S(1)}, f32[32,1,192]{2,1,0:T(1,128)S(1)}, u32[]{:S(2)}, u32[]{:S(2)}) collective-permute-start(f32[32,1,192]{2,1,0:T(1,128)S(1)} %get-tuple-element.21), channel_id=1, source_target_pairs={{1,0},{2,1},{3,2},{4,3},{5,4},{6,5},{7,6},{8,7},{9,8},{10,9},{11,1... | collective-permute-start | bytes 73736 | tf_op jit(solution)/shard_map/ppermute | solution.py:42
  91.0 10.4 %collective-permute-start.11 = (f32[32,1,192]{2,1,0:T(1,128)S(1)}, f32[32,1,192]{2,1,0:T(1,128)S(1)}, u32[]{:S(2)}, u32[]{:S(2)}) collective-permute-start(f32[32,1,192]{2,1,0:T(1,128)S(1)} %get-tuple-element.22), channel_id=1, source_target_pairs={{0,1},{1,2},{2,3},{3,4},{4,5},{5,6},{6,7},{7,8},{8,9},{9,10},{10,1... | collective-permute-start | bytes 73736 | tf_op jit(solution)/shard_map/ppermute | solution.py:41
  96.1 5.3 %collective-permute-start.7 = (f32[1,32,192]{2,1,0:T(8,128)S(1)}, f32[1,32,192]{2,1,0:T(8,128)S(1)}, u32[]{:S(2)}, u32[]{:S(2)}) collective-permute-start(f32[1,32,192]{2,1,0:T(8,128)S(1)} %get-tuple-element.23), channel_id=1, source_target_pairs={{0,16},{16,32},{32,48},{48,64},{64,80},{80,96},{96,112},{112,128},... | collective-permute-start | bytes 73736 | tf_op jit(solution)/shard_map/ppermute | solution.py:39
  99.2 4.7 %collective-permute-start.5 = (f32[1,32,192]{2,1,0:T(8,128)S(1)}, f32[1,32,192]{2,1,0:T(8,128)S(1)}, u32[]{:S(2)}, u32[]{:S(2)}) collective-permute-start(f32[1,32,192]{2,1,0:T(8,128)S(1)} %get-tuple-element.24), channel_id=1, source_target_pairs={{16,0},{32,16},{48,32},{64,48},{80,64},{96,80},{112,96},{128,112},... | collective-permute-start | bytes 73736 | tf_op jit(solution)/shard_map/ppermute | solution.py:40
  112.7 25.8 %all-to-all-start.3 = ((f32[16,1,1728]{2,1,0:T(1,128)}), f32[16,1,1728]{2,1,0:T(1,128)}, u32[]{:S(2)}, u32[]{:S(2)}) async-start(f32[16,1,1728]{2,1,0:T(1,128)} %broadcast_in_dim.29), calls=%async_computation.3 | async-start | bytes 229376 | tf_op jit(solution)/shard_map/all_to_all | solution.py:72
  121.8 4.2 %collective-permute-start.12 = (bf16[4,32,192]{2,1,0:T(8,128)(2,1)S(1)}, bf16[4,32,192]{2,1,0:T(8,128)(2,1)S(1)}, u32[]{:S(2)}, u32[]{:S(2)}) collective-permute-start(bf16[4,32,192]{2,1,0:T(8,128)(2,1)S(1)} %get-tuple-element.35), channel_id=1, source_target_pairs={{0,16},{16,32},{32,48},{48,64},{64,80},{80,96},{96,112},{112,128},... | collective-permute-start | bytes 147464 | tf_op jit(solution)/shard_map/ppermute | solution.py:23
  124.7 5.8 %collective-permute-start.13 = (bf16[4,32,192]{2,1,0:T(8,128)(2,1)S(1)}, bf16[4,32,192]{2,1,0:T(8,128)(2,1)S(1)}, u32[]{:S(2)}, u32[]{:S(2)}) collective-permute-start(bf16[4,32,192]{2,1,0:T(8,128)(2,1)S(1)} %get-tuple-element.36), channel_id=1, source_target_pairs={{16,0},{32,16},{48,32},{64,48},{80,64},{96,80},{112,96},{128,112},... | collective-permute-start | bytes 147464 | tf_op jit(solution)/shard_map/ppermute | solution.py:25
  132.3 23.0 %collective-permute-start.14 = (bf16[40,4,192]{2,1,0:T(4,128)(2,1)}, bf16[40,4,192]{2,1,0:T(4,128)(2,1)}, u32[]{:S(2)}, u32[]{:S(2)}) collective-permute-start(bf16[40,4,192]{2,1,0:T(4,128)(2,1)} %get-tuple-element.29), channel_id=1, source_target_pairs={{0,1},{1,2},{2,3},{3,4},{4,5},{5,6},{6,7},{7,8},{8,9},{9,10},{10,1... | collective-permute-start | bytes 184328 | tf_op jit(solution)/shard_map/ppermute | solution.py:23
  136.6 18.7 %collective-permute-start.15 = (bf16[40,4,192]{2,1,0:T(4,128)(2,1)}, bf16[40,4,192]{2,1,0:T(4,128)(2,1)}, u32[]{:S(2)}, u32[]{:S(2)}) collective-permute-start(bf16[40,4,192]{2,1,0:T(4,128)(2,1)} %get-tuple-element.30), channel_id=1, source_target_pairs={{1,0},{2,1},{3,2},{4,3},{5,4},{6,5},{7,6},{8,7},{9,8},{10,9},{11,1... | collective-permute-start | bytes 184328 | tf_op jit(solution)/shard_map/ppermute | solution.py:25
  145.8 19.7 %all-to-all-start.4 = ((f32[32,1,1536]{2,1,0:T(1,128)}), f32[32,1,1536]{2,1,0:T(1,128)}, u32[]{:S(2)}, u32[]{:S(2)}) async-start(f32[32,1,1536]{2,1,0:T(1,128)} %all_to_all.54), calls=%async_computation.4 | async-start | bytes 393216 | tf_op jit(solution)/shard_map/all_to_all | solution.py:78
  171.9 11.4 %collective-permute-start.17 = (f32[1,32,192]{2,1,0:T(8,128)S(1)}, f32[1,32,192]{2,1,0:T(8,128)S(1)}, u32[]{:S(2)}, u32[]{:S(2)}) collective-permute-start(f32[1,32,192]{2,1,0:T(8,128)S(1)} %get-tuple-element.19), channel_id=1, source_target_pairs={{0,16},{16,32},{32,48},{48,64},{64,80},{80,96},{96,112},{112,128},... | collective-permute-start | bytes 73736 | tf_op jit(solution)/shard_map/ppermute | solution.py:39
  175.0 8.3 %collective-permute-start.16 = (f32[1,32,192]{2,1,0:T(8,128)S(1)}, f32[1,32,192]{2,1,0:T(8,128)S(1)}, u32[]{:S(2)}, u32[]{:S(2)}) collective-permute-start(f32[1,32,192]{2,1,0:T(8,128)S(1)} %get-tuple-element.20), channel_id=1, source_target_pairs={{16,0},{32,16},{48,32},{64,48},{80,64},{96,80},{112,96},{128,112},... | collective-permute-start | bytes 73736 | tf_op jit(solution)/shard_map/ppermute | solution.py:40
  176.3 7.1 %collective-permute-start.18 = (f32[32,1,192]{2,1,0:T(1,128)S(1)}, f32[32,1,192]{2,1,0:T(1,128)S(1)}, u32[]{:S(2)}, u32[]{:S(2)}) collective-permute-start(f32[32,1,192]{2,1,0:T(1,128)S(1)} %get-tuple-element.17), channel_id=1, source_target_pairs={{1,0},{2,1},{3,2},{4,3},{5,4},{6,5},{7,6},{8,7},{9,8},{10,9},{11,1... | collective-permute-start | bytes 73736 | tf_op jit(solution)/shard_map/ppermute | solution.py:42
  178.2 6.1 %collective-permute-start.19 = (f32[32,1,192]{2,1,0:T(1,128)S(1)}, f32[32,1,192]{2,1,0:T(1,128)S(1)}, u32[]{:S(2)}, u32[]{:S(2)}) collective-permute-start(f32[32,1,192]{2,1,0:T(1,128)S(1)} %get-tuple-element.18), channel_id=1, source_target_pairs={{0,1},{1,2},{2,3},{3,4},{4,5},{5,6},{6,7},{7,8},{8,9},{9,10},{10,1... | collective-permute-start | bytes 73736 | tf_op jit(solution)/shard_map/ppermute | solution.py:41
  188.8 28.7 %all-to-all-start.5 = ((f32[16,1,1728]{2,1,0:T(1,128)}), f32[16,1,1728]{2,1,0:T(1,128)S(1)}, u32[]{:S(2)}, u32[]{:S(2)}) async-start(f32[16,1,1728]{2,1,0:T(1,128)} %broadcast_in_dim.32), calls=%async_computation.5 | async-start | bytes 229376 | tf_op jit(solution)/shard_map/all_to_all | solution.py:72
  199.5 7.0 %collective-permute-start.20 = (bf16[4,32,192]{2,1,0:T(8,128)(2,1)S(1)}, bf16[4,32,192]{2,1,0:T(8,128)(2,1)S(1)}, u32[]{:S(2)}, u32[]{:S(2)}) collective-permute-start(bf16[4,32,192]{2,1,0:T(8,128)(2,1)S(1)} %get-tuple-element.33), channel_id=1, source_target_pairs={{0,16},{16,32},{32,48},{48,64},{64,80},{80,96},{96,112},{112,128},... | collective-permute-start | bytes 147464 | tf_op jit(solution)/shard_map/ppermute | solution.py:23
  203.8 5.0 %collective-permute-start.21 = (bf16[4,32,192]{2,1,0:T(8,128)(2,1)S(1)}, bf16[4,32,192]{2,1,0:T(8,128)(2,1)S(1)}, u32[]{:S(2)}, u32[]{:S(2)}) collective-permute-start(bf16[4,32,192]{2,1,0:T(8,128)(2,1)S(1)} %get-tuple-element.34), channel_id=1, source_target_pairs={{16,0},{32,16},{48,32},{64,48},{80,64},{96,80},{112,96},{128,112},... | collective-permute-start | bytes 147464 | tf_op jit(solution)/shard_map/ppermute | solution.py:25
  210.5 22.2 %collective-permute-start.22 = (bf16[40,4,192]{2,1,0:T(4,128)(2,1)}, bf16[40,4,192]{2,1,0:T(4,128)(2,1)}, u32[]{:S(2)}, u32[]{:S(2)}) collective-permute-start(bf16[40,4,192]{2,1,0:T(4,128)(2,1)} %get-tuple-element.27), channel_id=1, source_target_pairs={{0,1},{1,2},{2,3},{3,4},{4,5},{5,6},{6,7},{7,8},{8,9},{9,10},{10,1... | collective-permute-start | bytes 184328 | tf_op jit(solution)/shard_map/ppermute | solution.py:23
  215.5 17.2 %collective-permute-start.23 = (bf16[40,4,192]{2,1,0:T(4,128)(2,1)}, bf16[40,4,192]{2,1,0:T(4,128)(2,1)}, u32[]{:S(2)}, u32[]{:S(2)}) collective-permute-start(bf16[40,4,192]{2,1,0:T(4,128)(2,1)} %get-tuple-element.28), channel_id=1, source_target_pairs={{1,0},{2,1},{3,2},{4,3},{5,4},{6,5},{7,6},{8,7},{9,8},{10,9},{11,1... | collective-permute-start | bytes 184328 | tf_op jit(solution)/shard_map/ppermute | solution.py:25
  223.9 18.9 %all-to-all-start.6 = ((f32[32,1,1536]{2,1,0:T(1,128)}), f32[32,1,1536]{2,1,0:T(1,128)S(1)}, u32[]{:S(2)}, u32[]{:S(2)}) async-start(f32[32,1,1536]{2,1,0:T(1,128)} %all_to_all.55), calls=%async_computation.6 | async-start | bytes 393216 | tf_op jit(solution)/shard_map/all_to_all | solution.py:78
  244.6 20.6 %copy-start.5 = (f32[32,32,192]{2,1,0:T(8,128)S(1)}, f32[32,32,192]{2,1,0:T(8,128)}, u32[]{:S(2)}) copy-start(f32[32,32,192]{2,1,0:T(8,128)} %copy-done.4) | copy-start | bytes 2359300
  250.3 32.9 %copy-start.59 = (f32[192]{0:T(256)S(1)}, f32[192]{0:T(256)}, u32[]{:S(2)}) copy-start(f32[192]{0:T(256)} %slice_reduce_fusion.2) | copy-start | bytes 2308
  250.3 12.4 %collective-permute-start.26 = (f32[32,1,192]{2,1,0:T(1,128)S(1)}, f32[32,1,192]{2,1,0:T(1,128)S(1)}, u32[]{:S(2)}, u32[]{:S(2)}) collective-permute-start(f32[32,1,192]{2,1,0:T(1,128)S(1)} %get-tuple-element.13), channel_id=1, source_target_pairs={{1,0},{2,1},{3,2},{4,3},{5,4},{6,5},{7,6},{8,7},{9,8},{10,9},{11,1... | collective-permute-start | bytes 73736 | tf_op jit(solution)/shard_map/ppermute | solution.py:42
  252.3 10.4 %collective-permute-start.27 = (f32[32,1,192]{2,1,0:T(1,128)S(1)}, f32[32,1,192]{2,1,0:T(1,128)S(1)}, u32[]{:S(2)}, u32[]{:S(2)}) collective-permute-start(f32[32,1,192]{2,1,0:T(1,128)S(1)} %get-tuple-element.14), channel_id=1, source_target_pairs={{0,1},{1,2},{2,3},{3,4},{4,5},{5,6},{6,7},{7,8},{8,9},{9,10},{10,1... | collective-permute-start | bytes 73736 | tf_op jit(solution)/shard_map/ppermute | solution.py:41
  257.4 5.4 %collective-permute-start.25 = (f32[1,32,192]{2,1,0:T(8,128)S(1)}, f32[1,32,192]{2,1,0:T(8,128)S(1)}, u32[]{:S(2)}, u32[]{:S(2)}) collective-permute-start(f32[1,32,192]{2,1,0:T(8,128)S(1)} %get-tuple-element.15), channel_id=1, source_target_pairs={{0,16},{16,32},{32,48},{48,64},{64,80},{80,96},{96,112},{112,128},... | collective-permute-start | bytes 73736 | tf_op jit(solution)/shard_map/ppermute | solution.py:39
  260.5 4.7 %collective-permute-start.24 = (f32[1,32,192]{2,1,0:T(8,128)S(1)}, f32[1,32,192]{2,1,0:T(8,128)S(1)}, u32[]{:S(2)}, u32[]{:S(2)}) collective-permute-start(f32[1,32,192]{2,1,0:T(8,128)S(1)} %get-tuple-element.16), channel_id=1, source_target_pairs={{16,0},{32,16},{48,32},{64,48},{80,64},{96,80},{112,96},{128,112},... | collective-permute-start | bytes 73736 | tf_op jit(solution)/shard_map/ppermute | solution.py:40
  267.5 15.6 %all-to-all-start.7 = ((f32[16,1,192]{2,1,0:T(1,128)}), f32[16,1,192]{2,1,0:T(1,128)S(1)}, u32[]{:S(2)}, u32[]{:S(2)}) async-start(f32[16,1,192]{2,1,0:T(1,128)} %broadcast_in_dim.33), calls=%async_computation.7 | async-start | bytes 32768 | tf_op jit(solution)/shard_map/all_to_all | solution.py:72
  (48 other events, 456.4 us)

commit v10 on v9

--- a/solution.py
+++ b/solution.py
@@ -112,10 +112,8 @@
         flat_core = current.reshape(patch * patch, fields)
         restricted = jnp.dot(flat_basis, flat_core, precision=highest)
         squares = jnp.sum(flat_core * flat_core, axis=0)
-        carried = jnp.concatenate([restricted, squares[None]], axis=0)
-        gathered = gathered_by_exchange(carried, "gy")
-        row_total = jnp.sum(gathered[:, modes], axis=0)
-        row_coarse = gathered[:, :modes].reshape(cols_y * modes, fields)
+        gathered = gathered_by_exchange(restricted, "gy")
+        row_coarse = gathered.reshape(cols_y * modes, fields)
         partial = jnp.dot(coarse_block, row_coarse, precision=highest).reshape(
             rows_x, modes, fields
         )
@@ -123,7 +121,7 @@
         prolonged = basis[0][:, :, None] * coarse_part[0]
         for mode in range(1, modes):
             prolonged = prolonged + basis[mode][:, :, None] * coarse_part[mode]
-        return (local_part + prolonged, row_total)
+        return (local_part + prolonged, squares)
 
     centre = 0.5 * (upper_bound + lower_bound)
     half_width = 0.5 * (upper_bound - lower_bound)
@@ -146,8 +144,9 @@
         else:
             flat_state = state.reshape(patch * patch, fields)
             last = jnp.sum(flat_state * flat_state, axis=0)
-            history.append(jnp.sum(gathered_by_exchange(last, "gy"), axis=0))
+            history.append(last)
     rows = jnp.stack([initial] + history)
+    rows = jnp.sum(gathered_by_exchange(rows, "gy"), axis=0)
     totals = jnp.sum(gathered_by_exchange(rows, "gx"), axis=0)
     return (solution, jnp.sqrt(totals[1:] / cells), jnp.sqrt(totals[0] / cells))
 

time: 303 us -> 301 us (level)
  blocking collectives: 15.5 us -> 30.9 us
  starting transfers between devices: 158 us -> 149 us
  other arithmetic: 45.5 us -> 41.7 us
  waiting for transfers between devices: 30.2 us -> 27 us
    all_to_all x1 -> x2, blocking collectives: 15.5 us -> 30.9 us  [gathered_by_exchange(): lax.all_to_all(copies, axis, 0, 0, tiled=True)]
    all_to_all x4 -> x3, starting transfers between devices: 33.5 us -> 25.3 us  [gathered_by_exchange(): lax.all_to_all(copies, axis, 0, 0, tiled=True)]
    all_to_all x4 -> x3, waiting for transfers between devices: 6.41 us -> 0.01 us  [gathered_by_exchange(): lax.all_to_all(copies, axis, 0, 0, tiled=True)]
    reshape x3 -> x0, local copies, waits for them, and re-layouts: 5.13 us -> none  [gathered_by_exchange(): lax.all_to_all(copies, axis, 0, 0, tiled=True)]
    reduce_sum x5 -> x1, other arithmetic: 5.1 us -> 0.05 us  [on_device(): rows = jnp.sum(gathered_by_exchange(rows, 'gy'), axis=0)]
    another operation x0 -> x3, local copies, waits for them, and re-layouts: none -> 3.59 us  [precondition(): row_coarse = gathered.reshape(cols_y * modes, fields)]
  transfers between devices with their start and end apart: 36 -> 35, of which waited for: 10 -> 9; matrix products, arithmetic and copies ran while one was open for 19% -> 17% of each run, Pallas kernels for 0% -> 0%
where the time goes in v10:
time: 301 us; the launch traced here: 299 us
  starting transfers between devices  149 us (50%)
  other arithmetic  41.7 us (14%)
  local copies, waits for them, and re-layouts  33.6 us (11%)
  blocking collectives  30.9 us (10%)
  waiting for transfers between devices  27 us (9%)
  matrix products  14 us (5%)
    all_to_all x2, blocking collectives, gathered_by_exchange(): lax.all_to_all(copies, axis, 0, 0, tiled=True)  30.9 us
    all_to_all x3, starting transfers between devices, summed_by_exchange(): received = lax.all_to_all(flat, axis, 0, 0, tiled=True)  28.4 us
    ppermute x6, starting transfers between devices, extended(): lax.ppermute(tail, axis, [(i, (i + 1) % count) for i in range(ends)])  25.6 us
    all_to_all x3, starting transfers between devices, gathered_by_exchange(): lax.all_to_all(copies, axis, 0, 0, tiled=True)  25.3 us
    ppermute x4, starting transfers between devices, with_edges(): west = lax.ppermute(cells[:, -1:], 'gy', right)  19.2 us
    all_to_all x1, starting transfers between devices, on_device(): pieces = lax.all_to_all(pieces, 'gx', 0, 0, tiled=True)  14 us
    ppermute x4, starting transfers between devices, with_edges(): north = lax.ppermute(cells[-1:], 'gx', down)  12.9 us
    ppermute x6, waiting for transfers between devices, extended(): lax.ppermute(head, axis, [((i + 1) % count, i) for i in range(ends)])  11.3 us
  transfers between devices with their start and end apart: 35, of which 9 were waited for; matrix products, arithmetic and copies ran while one was open for 17% of the time, Pallas kernels for 0%

profile of v10, /device:TPU:1, one launch (start us, length us, event | category | flops | bytes accessed | tf_op | source)
XLA Modules:
  0.0 298.6 jit_solution(15442564015795888950)
XLA Ops:
  0.6 14.0 %all-to-all-start = ((f32[32,8,128]{2,1,0:T(8,128)}), f32[32,8,128]{2,1,0:T(8,128)S(1)}, u32[]{:S(2)}, u32[]{:S(2)}) async-start(f32[32,8,128]{2,1,0:T(8,128)} %bitcast.88), calls=%async_computation | async-start | bytes 262144 | tf_op jit(solution)/shard_map/all_to_all | solution.py:101
  15.9 3.7 %collective-permute-start.6 = (f32[1,32]{1,0:T(1,128)}, f32[1,32]{1,0:T(1,128)}, u32[]{:S(2)}, u32[]{:S(2)}) collective-permute-start(f32[1,32]{1,0:T(1,128)} %get-tuple-element.55), channel_id=1, source_target_pairs={{0,16},{16,32},{32,48},{48,64},{64,80},{80,96},{96,112},{112,128},... | collective-permute-start | bytes 392 | tf_op jit(solution)/shard_map/ppermute | solution.py:39
  22.4 3.4 %collective-permute-start.8 = (f32[32,1]{1,0:T(8,128)}, f32[32,1]{1,0:T(8,128)}, u32[]{:S(2)}, u32[]{:S(2)}) collective-permute-start(f32[32,1]{1,0:T(8,128)} %get-tuple-element.53), channel_id=1, source_target_pairs={{1,0},{2,1},{3,2},{4,3},{5,4},{6,5},{7,6},{8,7},{9,8},{10,9},{11,1... | collective-permute-start | bytes 392 | tf_op jit(solution)/shard_map/ppermute | solution.py:42
  27.3 2.0 convolution_bitcast_fusion.2
  31.6 7.2 %all-to-all-start.1 = ((f32[16,1,1536]{2,1,0:T(1,128)}), f32[16,1,1536]{2,1,0:T(1,128)S(1)}, u32[]{:S(2)}, u32[]{:S(2)}) async-start(f32[16,1,1536]{2,1,0:T(1,128)} %broadcast_in_dim.19), calls=%async_computation.1 | async-start | bytes 196608 | tf_op jit(solution)/shard_map/all_to_all | solution.py:72
  39.7 4.3 %collective-permute-start = (bf16[4,32,192]{2,1,0:T(8,128)(2,1)S(1)}, bf16[4,32,192]{2,1,0:T(8,128)(2,1)S(1)}, u32[]{:S(2)}, u32[]{:S(2)}) collective-permute-start(bf16[4,32,192]{2,1,0:T(8,128)(2,1)S(1)} %get-tuple-element.39), channel_id=1, source_target_pairs={{0,16},{16,32},{32,48},{48,64},{64,80},{80,96},{96,112},{112,128},... | collective-permute-start | bytes 147464 | tf_op jit(solution)/shard_map/ppermute | solution.py:23
  45.9 3.1 %collective-permute-done.1 = bf16[4,32,192]{2,1,0:T(8,128)(2,1)S(1)} collective-permute-done((bf16[4,32,192]{2,1,0:T(8,128)(2,1)S(1)}, bf16[4,32,192]{2,1,0:T(8,128)(2,1)S(1)}, u32[]{:S(2)}, u32[]{:S(2)}) %collective-permute-start.1) | collective-permute-done | bytes 49184 | tf_op jit(solution)/shard_map/ppermute | solution.py:25
  50.7 5.0 %collective-permute-start.2 = (bf16[40,4,192]{2,1,0:T(4,128)(2,1)}, bf16[40,4,192]{2,1,0:T(4,128)(2,1)}, u32[]{:S(2)}, u32[]{:S(2)}) collective-permute-start(bf16[40,4,192]{2,1,0:T(4,128)(2,1)} %get-tuple-element.33), channel_id=1, source_target_pairs={{0,1},{1,2},{2,3},{3,4},{4,5},{5,6},{6,7},{7,8},{8,9},{9,10},{10,1... | collective-permute-start | bytes 184328 | tf_op jit(solution)/shard_map/ppermute | solution.py:23
  55.7 1.9 collective-permute-start.3
  62.4 10.2 %all-to-all-start.2 = ((f32[32,1,1536]{2,1,0:T(1,128)}), f32[32,1,1536]{2,1,0:T(1,128)}, u32[]{:S(2)}, u32[]{:S(2)}) async-start(f32[32,1,1536]{2,1,0:T(1,128)} %all_to_all.53), calls=%async_computation.2 | async-start | bytes 393216 | tf_op jit(solution)/shard_map/all_to_all | solution.py:78
  72.6 3.9 %collective-permute-start.10 = (f32[32,1]{1,0:T(8,128)}, f32[32,1]{1,0:T(8,128)}, u32[]{:S(2)}, u32[]{:S(2)}) collective-permute-start(f32[32,1]{1,0:T(8,128)} %get-tuple-element.54), channel_id=1, source_target_pairs={{0,1},{1,2},{2,3},{3,4},{4,5},{5,6},{6,7},{7,8},{8,9},{9,10},{10,1... | collective-permute-start | bytes 392 | tf_op jit(solution)/shard_map/ppermute | solution.py:41
  80.0 2.5 copy.48
  85.6 2.3 broadcast_multiply_fusion
  87.9 1.9 collective-permute-start.9
  89.9 5.1 %collective-permute-start.11 = (f32[32,1,192]{2,1,0:T(1,128)S(1)}, f32[32,1,192]{2,1,0:T(1,128)S(1)}, u32[]{:S(2)}, u32[]{:S(2)}) collective-permute-start(f32[32,1,192]{2,1,0:T(1,128)S(1)} %get-tuple-element.26), channel_id=1, source_target_pairs={{0,1},{1,2},{2,3},{3,4},{4,5},{5,6},{6,7},{7,8},{8,9},{9,10},{10,1... | collective-permute-start | bytes 73736 | tf_op jit(solution)/shard_map/ppermute | solution.py:41
  95.0 3.1 %collective-permute-start.7 = (f32[1,32,192]{2,1,0:T(8,128)S(1)}, f32[1,32,192]{2,1,0:T(8,128)S(1)}, u32[]{:S(2)}, u32[]{:S(2)}) collective-permute-start(f32[1,32,192]{2,1,0:T(8,128)S(1)} %get-tuple-element.27), channel_id=1, source_target_pairs={{0,16},{16,32},{32,48},{48,64},{64,80},{80,96},{96,112},{112,128},... | collective-permute-start | bytes 73736 | tf_op jit(solution)/shard_map/ppermute | solution.py:39
  100.4 2.4 collective-permute-done.5
  102.8 4.0 %multiply_reduce_fusion.1 = (f32[192]{0:T(256)}, f32[32,32,192]{2,1,0:T(8,128)S(1)}) fusion(f32[32,32,192]{2,1,0:T(8,128)S(1)} %copy-done.5, f32[32,32,192]{2,1,0:T(8,128)S(1)} %broadcast_multiply_fusion, f32[1,32,192]{2,1,0:T(8,128)S(1)} %collective-permute-done.5, f32[1,32,192]{2,1,0:T(8,128)S(1)} %collective-permute-done.7, ...), kind=kLoop, calls=%fused_computation.86 | loop fusion | flops 9043776 | bytes 3304192 | tf_op jit(solution)/shard_map/reduce_sum | solution.py:114
  111.8 8.2 %all-to-all-start.3 = ((f32[16,1,1536]{2,1,0:T(1,128)}), f32[16,1,1536]{2,1,0:T(1,128)}, u32[]{:S(2)}, u32[]{:S(2)}) async-start(f32[16,1,1536]{2,1,0:T(1,128)} %broadcast_in_dim.21), calls=%async_computation.3 | async-start | bytes 196608 | tf_op jit(solution)/shard_map/all_to_all | solution.py:72
  121.0 2.9 collective-permute-start.12
  125.2 4.5 %collective-permute-done.13 = bf16[4,32,192]{2,1,0:T(8,128)(2,1)S(1)} collective-permute-done((bf16[4,32,192]{2,1,0:T(8,128)(2,1)S(1)}, bf16[4,32,192]{2,1,0:T(8,128)(2,1)S(1)}, u32[]{:S(2)}, u32[]{:S(2)}) %collective-permute-start.13) | collective-permute-done | bytes 49184 | tf_op jit(solution)/shard_map/ppermute | solution.py:25
  131.4 4.3 %collective-permute-start.14 = (bf16[40,4,192]{2,1,0:T(4,128)(2,1)}, bf16[40,4,192]{2,1,0:T(4,128)(2,1)}, u32[]{:S(2)}, u32[]{:S(2)}) collective-permute-start(bf16[40,4,192]{2,1,0:T(4,128)(2,1)} %get-tuple-element.31), channel_id=1, source_target_pairs={{0,1},{1,2},{2,3},{3,4},{4,5},{5,6},{6,7},{7,8},{8,9},{9,10},{10,1... | collective-permute-start | bytes 184328 | tf_op jit(solution)/shard_map/ppermute | solution.py:23
  135.7 1.9 collective-permute-start.15
  141.0 2.0 fusion.64
  143.0 1.9 all_to_all.54
  144.9 9.5 %all-to-all-start.4 = ((f32[32,1,1536]{2,1,0:T(1,128)}), f32[32,1,1536]{2,1,0:T(1,128)}, u32[]{:S(2)}, u32[]{:S(2)}) async-start(f32[32,1,1536]{2,1,0:T(1,128)} %all_to_all.54), calls=%async_computation.4 | async-start | bytes 393216 | tf_op jit(solution)/shard_map/all_to_all | solution.py:78
  157.7 2.4 copy.52
  160.1 4.5 %all-to-all-done.4 = f32[32,1,1536]{2,1,0:T(1,128)} async-done(((f32[32,1,1536]{2,1,0:T(1,128)}), f32[32,1,1536]{2,1,0:T(1,128)}, u32[]{:S(2)}, u32[]{:S(2)}) %all-to-all-start.4) | async-done | bytes 196640 | tf_op jit(solution)/shard_map/all_to_all | solution.py:78
  167.3 3.5 %multiply_add_fusion.1 = f32[32,32,192]{2,1,0:T(8,128)S(1)} fusion(f32[32,32,192]{2,1,0:T(8,128)} %bitcast.82, f32[192]{0:T(256)S(1)} %get-tuple-element.66, f32[192]{0:T(256)S(1)} %get-tuple-element.67, f32[192]{0:T(256)S(1)} %get-tuple-element.68, f32[192]{0:T(256)S(1)} %get-tuple-element.69, f32[192]{0:T(256)S(1)} %get-tuple-element.70, ...), kind=kLoop, calls=%fused_computation.90 | loop fusion | flops 6881280 | bytes 2404352 | tf_op jit(solution)/shard_map/add | solution.py:142
  171.0 3.0 %collective-permute-start.17 = (f32[1,32,192]{2,1,0:T(8,128)S(1)}, f32[1,32,192]{2,1,0:T(8,128)S(1)}, u32[]{:S(2)}, u32[]{:S(2)}) collective-permute-start(f32[1,32,192]{2,1,0:T(8,128)S(1)} %get-tuple-element.23), channel_id=1, source_target_pairs={{0,16},{16,32},{32,48},{48,64},{64,80},{80,96},{96,112},{112,128},... | collective-permute-start | bytes 73736 | tf_op jit(solution)/shard_map/ppermute | solution.py:39
  175.3 1.9 collective-permute-start.18
  177.3 5.1 %collective-permute-start.19 = (f32[32,1,192]{2,1,0:T(1,128)S(1)}, f32[32,1,192]{2,1,0:T(1,128)S(1)}, u32[]{:S(2)}, u32[]{:S(2)}) collective-permute-start(f32[32,1,192]{2,1,0:T(1,128)S(1)} %get-tuple-element.22), channel_id=1, source_target_pairs={{0,1},{1,2},{2,3},{3,4},{4,5},{5,6},{6,7},{7,8},{8,9},{9,10},{10,1... | collective-permute-start | bytes 73736 | tf_op jit(solution)/shard_map/ppermute | solution.py:41
  183.4 2.4 fusion.82
  189.5 9.8 %all-to-all-start.5 = ((f32[16,1,1536]{2,1,0:T(1,128)}), f32[16,1,1536]{2,1,0:T(1,128)S(1)}, u32[]{:S(2)}, u32[]{:S(2)}) async-start(f32[16,1,1536]{2,1,0:T(1,128)} %broadcast_in_dim.23), calls=%async_computation.5 | async-start | bytes 196608 | tf_op jit(solution)/shard_map/all_to_all | solution.py:72
  200.2 4.3 %collective-permute-start.20 = (bf16[4,32,192]{2,1,0:T(8,128)(2,1)S(1)}, bf16[4,32,192]{2,1,0:T(8,128)(2,1)S(1)}, u32[]{:S(2)}, u32[]{:S(2)}) collective-permute-start(bf16[4,32,192]{2,1,0:T(8,128)(2,1)S(1)} %get-tuple-element.35), channel_id=1, source_target_pairs={{0,16},{16,32},{32,48},{48,64},{64,80},{80,96},{96,112},{112,128},... | collective-permute-start | bytes 147464 | tf_op jit(solution)/shard_map/ppermute | solution.py:23
  205.8 3.7 %collective-permute-done.21 = bf16[4,32,192]{2,1,0:T(8,128)(2,1)S(1)} collective-permute-done((bf16[4,32,192]{2,1,0:T(8,128)(2,1)S(1)}, bf16[4,32,192]{2,1,0:T(8,128)(2,1)S(1)}, u32[]{:S(2)}, u32[]{:S(2)}) %collective-permute-start.21) | collective-permute-done | bytes 49184 | tf_op jit(solution)/shard_map/ppermute | solution.py:25
  211.3 5.0 %collective-permute-start.22 = (bf16[40,4,192]{2,1,0:T(4,128)(2,1)}, bf16[40,4,192]{2,1,0:T(4,128)(2,1)}, u32[]{:S(2)}, u32[]{:S(2)}) collective-permute-start(bf16[40,4,192]{2,1,0:T(4,128)(2,1)} %get-tuple-element.29), channel_id=1, source_target_pairs={{0,1},{1,2},{2,3},{3,4},{4,5},{5,6},{6,7},{7,8},{8,9},{9,10},{10,1... | collective-permute-start | bytes 184328 | tf_op jit(solution)/shard_map/ppermute | solution.py:23
  216.2 1.9 collective-permute-start.23
  223.0 8.7 %all-to-all-start.6 = ((f32[32,1,1536]{2,1,0:T(1,128)}), f32[32,1,1536]{2,1,0:T(1,128)S(1)}, u32[]{:S(2)}, u32[]{:S(2)}) async-start(f32[32,1,1536]{2,1,0:T(1,128)} %all_to_all.55), calls=%async_computation.6 | async-start | bytes 393216 | tf_op jit(solution)/shard_map/all_to_all | solution.py:78
  235.1 2.5 copy.56
  237.6 4.3 %all-to-all-done.6 = f32[32,1,1536]{2,1,0:T(1,128)S(1)} async-done(((f32[32,1,1536]{2,1,0:T(1,128)}), f32[32,1,1536]{2,1,0:T(1,128)S(1)}, u32[]{:S(2)}, u32[]{:S(2)}) %all-to-all-start.6) | async-done | bytes 196640 | tf_op jit(solution)/shard_map/all_to_all | solution.py:78
  243.6 5.6 %add_add_fusion = (f32[32,32,192]{2,1,0:T(8,128)}, f32[32,32,192]{2,1,0:T(8,128)S(1)}) fusion(f32[32,32,192]{2,1,0:T(8,128)} %bitcast.81, f32[192]{0:T(256)} %copy-done.44, f32[32,32]{1,0:T(8,128)} %get-tuple-element.48, f32[192]{0:T(256)} %copy-done.45, f32[32,32]{1,0:T(8,128)} %get-tuple-element.47, f32[192]{0:T(256)} %copy-done.46, ...), kind=kLoop, calls=%fused_computation.89 | loop fusion | flops 11403264 | bytes 4769792 | tf_op jit(solution)/shard_map/add | solution.py:135
  249.4 1.9 collective-permute-start.26
  251.3 5.1 %collective-permute-start.27 = (f32[32,1,192]{2,1,0:T(1,128)S(1)}, f32[32,1,192]{2,1,0:T(1,128)S(1)}, u32[]{:S(2)}, u32[]{:S(2)}) collective-permute-start(f32[32,1,192]{2,1,0:T(1,128)S(1)} %get-tuple-element.18), channel_id=1, source_target_pairs={{0,1},{1,2},{2,3},{3,4},{4,5},{5,6},{6,7},{7,8},{8,9},{9,10},{10,1... | collective-permute-start | bytes 73736 | tf_op jit(solution)/shard_map/ppermute | solution.py:41
  256.4 3.1 %collective-permute-start.25 = (f32[1,32,192]{2,1,0:T(8,128)S(1)}, f32[1,32,192]{2,1,0:T(8,128)S(1)}, u32[]{:S(2)}, u32[]{:S(2)}) collective-permute-start(f32[1,32,192]{2,1,0:T(8,128)S(1)} %get-tuple-element.19), channel_id=1, source_target_pairs={{0,16},{16,32},{32,48},{48,64},{64,80},{80,96},{96,112},{112,128},... | collective-permute-start | bytes 73736 | tf_op jit(solution)/shard_map/ppermute | solution.py:39
  260.8 3.3 %collective-permute-done.24 = f32[1,32,192]{2,1,0:T(8,128)S(1)} collective-permute-done((f32[1,32,192]{2,1,0:T(8,128)S(1)}, f32[1,32,192]{2,1,0:T(8,128)S(1)}, u32[]{:S(2)}, u32[]{:S(2)}) %collective-permute-start.24) | collective-permute-done | bytes 24608 | tf_op jit(solution)/shard_map/ppermute | solution.py:40
  266.2 15.5 %all_to_all.65 = f32[16,1,768]{2,1,0:T(1,128)S(1)} all-to-all(f32[16,1,768]{2,1,0:T(1,128)S(1)} %broadcast_in_dim.25), channel_id=1, replica_groups=mesh['gx'=32,'gy'=16] {'gy'}, dimensions={0} | all-to-all | bytes 98304 | tf_op jit(solution)/shard_map/all_to_all | solution.py:72
  281.8 15.4 %all_to_all.66 = f32[32,1,768]{2,1,0:T(1,128)S(1)} all-to-all(f32[32,1,768]{2,1,0:T(1,128)S(1)} %broadcast_in_dim.26), channel_id=1, replica_groups=mesh['gx'=32,'gy'=16] {'gx'}, dimensions={0} | all-to-all | bytes 196608 | tf_op jit(solution)/shard_map/all_to_all | solution.py:72
  (216 shorter events, 68.6 us)
Async XLA Ops:
  0.6 77.5 %copy-start = (bf16[1,1,1024,1600]{2,3,1,0:T(8,128)(2,1)S(1)}, bf16[1,1,1024,1600]{2,3,1,0:T(8,128)(2,1)}, u32[]{:S(2)}) copy-start(bf16[1,1,1024,1600]{2,3,1,0:T(8,128)(2,1)} %param.10) | copy-start | bytes 9830404
  0.6 26.7 %all-to-all-start = ((f32[32,8,128]{2,1,0:T(8,128)}), f32[32,8,128]{2,1,0:T(8,128)S(1)}, u32[]{:S(2)}, u32[]{:S(2)}) async-start(f32[32,8,128]{2,1,0:T(8,128)} %bitcast.88), calls=%async_computation | async-start | bytes 262144 | tf_op jit(solution)/shard_map/all_to_all | solution.py:101
  15.9 74.0 %collective-permute-start.6 = (f32[1,32]{1,0:T(1,128)}, f32[1,32]{1,0:T(1,128)}, u32[]{:S(2)}, u32[]{:S(2)}) collective-permute-start(f32[1,32]{1,0:T(1,128)} %get-tuple-element.55), channel_id=1, source_target_pairs={{0,16},{16,32},{32,48},{48,64},{64,80},{80,96},{96,112},{112,128},... | collective-permute-start | bytes 392 | tf_op jit(solution)/shard_map/ppermute | solution.py:39
  19.6 75.4 %collective-permute-start.4 = (f32[1,32]{1,0:T(1,128)}, f32[1,32]{1,0:T(1,128)}, u32[]{:S(2)}, u32[]{:S(2)}) collective-permute-start(f32[1,32]{1,0:T(1,128)} %get-tuple-element.56), channel_id=1, source_target_pairs={{16,0},{32,16},{48,32},{64,48},{80,64},{96,80},{112,96},{128,112},... | collective-permute-start | bytes 392 | tf_op jit(solution)/shard_map/ppermute | solution.py:40
  22.4 75.7 %collective-permute-start.8 = (f32[32,1]{1,0:T(8,128)}, f32[32,1]{1,0:T(8,128)}, u32[]{:S(2)}, u32[]{:S(2)}) collective-permute-start(f32[32,1]{1,0:T(8,128)} %get-tuple-element.53), channel_id=1, source_target_pairs={{1,0},{2,1},{3,2},{4,3},{5,4},{6,5},{7,6},{8,7},{9,8},{10,9},{11,1... | collective-permute-start | bytes 392 | tf_op jit(solution)/shard_map/ppermute | solution.py:42
  31.6 26.1 %all-to-all-start.1 = ((f32[16,1,1536]{2,1,0:T(1,128)}), f32[16,1,1536]{2,1,0:T(1,128)S(1)}, u32[]{:S(2)}, u32[]{:S(2)}) async-start(f32[16,1,1536]{2,1,0:T(1,128)} %broadcast_in_dim.19), calls=%async_computation.1 | async-start | bytes 196608 | tf_op jit(solution)/shard_map/all_to_all | solution.py:72
  39.7 6.2 %collective-permute-start = (bf16[4,32,192]{2,1,0:T(8,128)(2,1)S(1)}, bf16[4,32,192]{2,1,0:T(8,128)(2,1)S(1)}, u32[]{:S(2)}, u32[]{:S(2)}) collective-permute-start(bf16[4,32,192]{2,1,0:T(8,128)(2,1)S(1)} %get-tuple-element.39), channel_id=1, source_target_pairs={{0,16},{16,32},{32,48},{48,64},{64,80},{80,96},{96,112},{112,128},... | collective-permute-start | bytes 147464 | tf_op jit(solution)/shard_map/ppermute | solution.py:23
  43.9 5.0 %collective-permute-start.1 = (bf16[4,32,192]{2,1,0:T(8,128)(2,1)S(1)}, bf16[4,32,192]{2,1,0:T(8,128)(2,1)S(1)}, u32[]{:S(2)}, u32[]{:S(2)}) collective-permute-start(bf16[4,32,192]{2,1,0:T(8,128)(2,1)S(1)} %get-tuple-element.40), channel_id=1, source_target_pairs={{16,0},{32,16},{48,32},{64,48},{80,64},{96,80},{112,96},{128,112},... | collective-permute-start | bytes 147464 | tf_op jit(solution)/shard_map/ppermute | solution.py:25
  50.7 21.9 %collective-permute-start.2 = (bf16[40,4,192]{2,1,0:T(4,128)(2,1)}, bf16[40,4,192]{2,1,0:T(4,128)(2,1)}, u32[]{:S(2)}, u32[]{:S(2)}) collective-permute-start(bf16[40,4,192]{2,1,0:T(4,128)(2,1)} %get-tuple-element.33), channel_id=1, source_target_pairs={{0,1},{1,2},{2,3},{3,4},{4,5},{5,6},{6,7},{7,8},{8,9},{9,10},{10,1... | collective-permute-start | bytes 184328 | tf_op jit(solution)/shard_map/ppermute | solution.py:23
  55.7 20.9 %collective-permute-start.3 = (bf16[40,4,192]{2,1,0:T(4,128)(2,1)}, bf16[40,4,192]{2,1,0:T(4,128)(2,1)}, u32[]{:S(2)}, u32[]{:S(2)}) collective-permute-start(bf16[40,4,192]{2,1,0:T(4,128)(2,1)} %get-tuple-element.34), channel_id=1, source_target_pairs={{1,0},{2,1},{3,2},{4,3},{5,4},{6,5},{7,6},{8,7},{9,8},{10,9},{11,1... | collective-permute-start | bytes 184328 | tf_op jit(solution)/shard_map/ppermute | solution.py:25
  62.4 20.4 %all-to-all-start.2 = ((f32[32,1,1536]{2,1,0:T(1,128)}), f32[32,1,1536]{2,1,0:T(1,128)}, u32[]{:S(2)}, u32[]{:S(2)}) async-start(f32[32,1,1536]{2,1,0:T(1,128)} %all_to_all.53), calls=%async_computation.2 | async-start | bytes 393216 | tf_op jit(solution)/shard_map/all_to_all | solution.py:78
  72.6 26.8 %collective-permute-start.10 = (f32[32,1]{1,0:T(8,128)}, f32[32,1]{1,0:T(8,128)}, u32[]{:S(2)}, u32[]{:S(2)}) collective-permute-start(f32[32,1]{1,0:T(8,128)} %get-tuple-element.54), channel_id=1, source_target_pairs={{0,1},{1,2},{2,3},{3,4},{4,5},{5,6},{6,7},{7,8},{8,9},{9,10},{10,1... | collective-permute-start | bytes 392 | tf_op jit(solution)/shard_map/ppermute | solution.py:41
  85.4 21.4 %copy-start.43 = (f32[192]{0:T(256)}, f32[192]{0:T(256)S(1)}, u32[]{:S(2)}) copy-start(f32[192]{0:T(256)S(1)} %get-tuple-element.73) | copy-start | bytes 2308
  85.4 21.4 %copy-start.44 = (f32[192]{0:T(256)}, f32[192]{0:T(256)S(1)}, u32[]{:S(2)}) copy-start(f32[192]{0:T(256)S(1)} %get-tuple-element.74) | copy-start | bytes 2308
  85.4 21.4 %copy-start.45 = (f32[192]{0:T(256)}, f32[192]{0:T(256)S(1)}, u32[]{:S(2)}) copy-start(f32[192]{0:T(256)S(1)} %get-tuple-element.75) | copy-start | bytes 2308
  85.4 21.4 %copy-start.46 = (f32[192]{0:T(256)}, f32[192]{0:T(256)S(1)}, u32[]{:S(2)}) copy-start(f32[192]{0:T(256)S(1)} %get-tuple-element.76) | copy-start | bytes 2308
  85.4 21.4 %copy-start.47 = (f32[192]{0:T(256)}, f32[192]{0:T(256)S(1)}, u32[]{:S(2)}) copy-start(f32[192]{0:T(256)S(1)} %get-tuple-element.77) | copy-start | bytes 2308
  85.5 21.4 %copy-start.48 = (f32[192]{0:T(256)}, f32[192]{0:T(256)S(1)}, u32[]{:S(2)}) copy-start(f32[192]{0:T(256)S(1)} %get-tuple-element.78) | copy-start | bytes 2308
  85.5 21.4 %copy-start.49 = (f32[192]{0:T(256)}, f32[192]{0:T(256)S(1)}, u32[]{:S(2)}) copy-start(f32[192]{0:T(256)S(1)} %get-tuple-element.79) | copy-start | bytes 2308
  85.5 21.4 %copy-start.50 = (f32[192]{0:T(256)}, f32[192]{0:T(256)S(1)}, u32[]{:S(2)}) copy-start(f32[192]{0:T(256)S(1)} %get-tuple-element.80) | copy-start | bytes 2308
  87.9 12.4 %collective-permute-start.9 = (f32[32,1,192]{2,1,0:T(1,128)S(1)}, f32[32,1,192]{2,1,0:T(1,128)S(1)}, u32[]{:S(2)}, u32[]{:S(2)}) collective-permute-start(f32[32,1,192]{2,1,0:T(1,128)S(1)} %get-tuple-element.25), channel_id=1, source_target_pairs={{1,0},{2,1},{3,2},{4,3},{5,4},{6,5},{7,6},{8,7},{9,8},{10,9},{11,1... | collective-permute-start | bytes 73736 | tf_op jit(solution)/shard_map/ppermute | solution.py:42
  89.9 10.5 %collective-permute-start.11 = (f32[32,1,192]{2,1,0:T(1,128)S(1)}, f32[32,1,192]{2,1,0:T(1,128)S(1)}, u32[]{:S(2)}, u32[]{:S(2)}) collective-permute-start(f32[32,1,192]{2,1,0:T(1,128)S(1)} %get-tuple-element.26), channel_id=1, source_target_pairs={{0,1},{1,2},{2,3},{3,4},{4,5},{5,6},{6,7},{7,8},{8,9},{9,10},{10,1... | collective-permute-start | bytes 73736 | tf_op jit(solution)/shard_map/ppermute | solution.py:41
  95.0 5.4 %collective-permute-start.7 = (f32[1,32,192]{2,1,0:T(8,128)S(1)}, f32[1,32,192]{2,1,0:T(8,128)S(1)}, u32[]{:S(2)}, u32[]{:S(2)}) collective-permute-start(f32[1,32,192]{2,1,0:T(8,128)S(1)} %get-tuple-element.27), channel_id=1, source_target_pairs={{0,16},{16,32},{32,48},{48,64},{64,80},{80,96},{96,112},{112,128},... | collective-permute-start | bytes 73736 | tf_op jit(solution)/shard_map/ppermute | solution.py:39
  98.1 4.7 %collective-permute-start.5 = (f32[1,32,192]{2,1,0:T(8,128)S(1)}, f32[1,32,192]{2,1,0:T(8,128)S(1)}, u32[]{:S(2)}, u32[]{:S(2)}) collective-permute-start(f32[1,32,192]{2,1,0:T(8,128)S(1)} %get-tuple-element.28), channel_id=1, source_target_pairs={{16,0},{32,16},{48,32},{64,48},{80,64},{96,80},{112,96},{128,112},... | collective-permute-start | bytes 73736 | tf_op jit(solution)/shard_map/ppermute | solution.py:40
  111.8 25.8 %all-to-all-start.3 = ((f32[16,1,1536]{2,1,0:T(1,128)}), f32[16,1,1536]{2,1,0:T(1,128)}, u32[]{:S(2)}, u32[]{:S(2)}) async-start(f32[16,1,1536]{2,1,0:T(1,128)} %broadcast_in_dim.21), calls=%async_computation.3 | async-start | bytes 196608 | tf_op jit(solution)/shard_map/all_to_all | solution.py:72
  121.0 4.2 %collective-permute-start.12 = (bf16[4,32,192]{2,1,0:T(8,128)(2,1)S(1)}, bf16[4,32,192]{2,1,0:T(8,128)(2,1)S(1)}, u32[]{:S(2)}, u32[]{:S(2)}) collective-permute-start(bf16[4,32,192]{2,1,0:T(8,128)(2,1)S(1)} %get-tuple-element.37), channel_id=1, source_target_pairs={{0,16},{16,32},{32,48},{48,64},{64,80},{80,96},{96,112},{112,128},... | collective-permute-start | bytes 147464 | tf_op jit(solution)/shard_map/ppermute | solution.py:23
  123.8 5.8 %collective-permute-start.13 = (bf16[4,32,192]{2,1,0:T(8,128)(2,1)S(1)}, bf16[4,32,192]{2,1,0:T(8,128)(2,1)S(1)}, u32[]{:S(2)}, u32[]{:S(2)}) collective-permute-start(bf16[4,32,192]{2,1,0:T(8,128)(2,1)S(1)} %get-tuple-element.38), channel_id=1, source_target_pairs={{16,0},{32,16},{48,32},{64,48},{80,64},{96,80},{112,96},{128,112},... | collective-permute-start | bytes 147464 | tf_op jit(solution)/shard_map/ppermute | solution.py:25
  131.4 23.0 %collective-permute-start.14 = (bf16[40,4,192]{2,1,0:T(4,128)(2,1)}, bf16[40,4,192]{2,1,0:T(4,128)(2,1)}, u32[]{:S(2)}, u32[]{:S(2)}) collective-permute-start(bf16[40,4,192]{2,1,0:T(4,128)(2,1)} %get-tuple-element.31), channel_id=1, source_target_pairs={{0,1},{1,2},{2,3},{3,4},{4,5},{5,6},{6,7},{7,8},{8,9},{9,10},{10,1... | collective-permute-start | bytes 184328 | tf_op jit(solution)/shard_map/ppermute | solution.py:23
  135.7 18.7 %collective-permute-start.15 = (bf16[40,4,192]{2,1,0:T(4,128)(2,1)}, bf16[40,4,192]{2,1,0:T(4,128)(2,1)}, u32[]{:S(2)}, u32[]{:S(2)}) collective-permute-start(bf16[40,4,192]{2,1,0:T(4,128)(2,1)} %get-tuple-element.32), channel_id=1, source_target_pairs={{1,0},{2,1},{3,2},{4,3},{5,4},{6,5},{7,6},{8,7},{9,8},{10,9},{11,1... | collective-permute-start | bytes 184328 | tf_op jit(solution)/shard_map/ppermute | solution.py:25
  144.9 19.7 %all-to-all-start.4 = ((f32[32,1,1536]{2,1,0:T(1,128)}), f32[32,1,1536]{2,1,0:T(1,128)}, u32[]{:S(2)}, u32[]{:S(2)}) async-start(f32[32,1,1536]{2,1,0:T(1,128)} %all_to_all.54), calls=%async_computation.4 | async-start | bytes 393216 | tf_op jit(solution)/shard_map/all_to_all | solution.py:78
  171.0 11.4 %collective-permute-start.17 = (f32[1,32,192]{2,1,0:T(8,128)S(1)}, f32[1,32,192]{2,1,0:T(8,128)S(1)}, u32[]{:S(2)}, u32[]{:S(2)}) collective-permute-start(f32[1,32,192]{2,1,0:T(8,128)S(1)} %get-tuple-element.23), channel_id=1, source_target_pairs={{0,16},{16,32},{32,48},{48,64},{64,80},{80,96},{96,112},{112,128},... | collective-permute-start | bytes 73736 | tf_op jit(solution)/shard_map/ppermute | solution.py:39
  174.0 8.3 %collective-permute-start.16 = (f32[1,32,192]{2,1,0:T(8,128)S(1)}, f32[1,32,192]{2,1,0:T(8,128)S(1)}, u32[]{:S(2)}, u32[]{:S(2)}) collective-permute-start(f32[1,32,192]{2,1,0:T(8,128)S(1)} %get-tuple-element.24), channel_id=1, source_target_pairs={{16,0},{32,16},{48,32},{64,48},{80,64},{96,80},{112,96},{128,112},... | collective-permute-start | bytes 73736 | tf_op jit(solution)/shard_map/ppermute | solution.py:40
  175.3 7.1 %collective-permute-start.18 = (f32[32,1,192]{2,1,0:T(1,128)S(1)}, f32[32,1,192]{2,1,0:T(1,128)S(1)}, u32[]{:S(2)}, u32[]{:S(2)}) collective-permute-start(f32[32,1,192]{2,1,0:T(1,128)S(1)} %get-tuple-element.21), channel_id=1, source_target_pairs={{1,0},{2,1},{3,2},{4,3},{5,4},{6,5},{7,6},{8,7},{9,8},{10,9},{11,1... | collective-permute-start | bytes 73736 | tf_op jit(solution)/shard_map/ppermute | solution.py:42
  177.3 6.1 %collective-permute-start.19 = (f32[32,1,192]{2,1,0:T(1,128)S(1)}, f32[32,1,192]{2,1,0:T(1,128)S(1)}, u32[]{:S(2)}, u32[]{:S(2)}) collective-permute-start(f32[32,1,192]{2,1,0:T(1,128)S(1)} %get-tuple-element.22), channel_id=1, source_target_pairs={{0,1},{1,2},{2,3},{3,4},{4,5},{5,6},{6,7},{7,8},{8,9},{9,10},{10,1... | collective-permute-start | bytes 73736 | tf_op jit(solution)/shard_map/ppermute | solution.py:41
  189.5 28.7 %all-to-all-start.5 = ((f32[16,1,1536]{2,1,0:T(1,128)}), f32[16,1,1536]{2,1,0:T(1,128)S(1)}, u32[]{:S(2)}, u32[]{:S(2)}) async-start(f32[16,1,1536]{2,1,0:T(1,128)} %broadcast_in_dim.23), calls=%async_computation.5 | async-start | bytes 196608 | tf_op jit(solution)/shard_map/all_to_all | solution.py:72
  200.2 5.6 %collective-permute-start.20 = (bf16[4,32,192]{2,1,0:T(8,128)(2,1)S(1)}, bf16[4,32,192]{2,1,0:T(8,128)(2,1)S(1)}, u32[]{:S(2)}, u32[]{:S(2)}) collective-permute-start(bf16[4,32,192]{2,1,0:T(8,128)(2,1)S(1)} %get-tuple-element.35), channel_id=1, source_target_pairs={{0,16},{16,32},{32,48},{48,64},{64,80},{80,96},{96,112},{112,128},... | collective-permute-start | bytes 147464 | tf_op jit(solution)/shard_map/ppermute | solution.py:23
  204.5 5.0 %collective-permute-start.21 = (bf16[4,32,192]{2,1,0:T(8,128)(2,1)S(1)}, bf16[4,32,192]{2,1,0:T(8,128)(2,1)S(1)}, u32[]{:S(2)}, u32[]{:S(2)}) collective-permute-start(bf16[4,32,192]{2,1,0:T(8,128)(2,1)S(1)} %get-tuple-element.36), channel_id=1, source_target_pairs={{16,0},{32,16},{48,32},{64,48},{80,64},{96,80},{112,96},{128,112},... | collective-permute-start | bytes 147464 | tf_op jit(solution)/shard_map/ppermute | solution.py:25
  211.3 20.4 %collective-permute-start.22 = (bf16[40,4,192]{2,1,0:T(4,128)(2,1)}, bf16[40,4,192]{2,1,0:T(4,128)(2,1)}, u32[]{:S(2)}, u32[]{:S(2)}) collective-permute-start(bf16[40,4,192]{2,1,0:T(4,128)(2,1)} %get-tuple-element.29), channel_id=1, source_target_pairs={{0,1},{1,2},{2,3},{3,4},{4,5},{5,6},{6,7},{7,8},{8,9},{9,10},{10,1... | collective-permute-start | bytes 184328 | tf_op jit(solution)/shard_map/ppermute | solution.py:23
  216.2 15.5 %collective-permute-start.23 = (bf16[40,4,192]{2,1,0:T(4,128)(2,1)}, bf16[40,4,192]{2,1,0:T(4,128)(2,1)}, u32[]{:S(2)}, u32[]{:S(2)}) collective-permute-start(bf16[40,4,192]{2,1,0:T(4,128)(2,1)} %get-tuple-element.30), channel_id=1, source_target_pairs={{1,0},{2,1},{3,2},{4,3},{5,4},{6,5},{7,6},{8,7},{9,8},{10,9},{11,1... | collective-permute-start | bytes 184328 | tf_op jit(solution)/shard_map/ppermute | solution.py:25
  223.0 18.9 %all-to-all-start.6 = ((f32[32,1,1536]{2,1,0:T(1,128)}), f32[32,1,1536]{2,1,0:T(1,128)S(1)}, u32[]{:S(2)}, u32[]{:S(2)}) async-start(f32[32,1,1536]{2,1,0:T(1,128)} %all_to_all.55), calls=%async_computation.6 | async-start | bytes 393216 | tf_op jit(solution)/shard_map/all_to_all | solution.py:78
  243.6 20.6 %copy-start.7 = (f32[32,32,192]{2,1,0:T(8,128)S(1)}, f32[32,32,192]{2,1,0:T(8,128)}, u32[]{:S(2)}) copy-start(f32[32,32,192]{2,1,0:T(8,128)} %copy-done.6) | copy-start | bytes 2359300
  243.6 20.6 %copy-start.22 = (f32[32,32]{1,0:T(8,128)S(1)}, f32[32,32]{1,0:T(8,128)}, u32[]{:S(2)}) copy-start(f32[32,32]{1,0:T(8,128)} %copy-done.20) | copy-start | bytes 12292
  243.6 20.6 %copy-start.25 = (f32[32,32]{1,0:T(8,128)S(1)}, f32[32,32]{1,0:T(8,128)}, u32[]{:S(2)}) copy-start(f32[32,32]{1,0:T(8,128)} %copy-done.23) | copy-start | bytes 12292
  243.6 20.6 %copy-start.28 = (f32[32,32]{1,0:T(8,128)S(1)}, f32[32,32]{1,0:T(8,128)}, u32[]{:S(2)}) copy-start(f32[32,32]{1,0:T(8,128)} %copy-done.26) | copy-start | bytes 12292
  249.4 11.4 %collective-permute-start.26 = (f32[32,1,192]{2,1,0:T(1,128)S(1)}, f32[32,1,192]{2,1,0:T(1,128)S(1)}, u32[]{:S(2)}, u32[]{:S(2)}) collective-permute-start(f32[32,1,192]{2,1,0:T(1,128)S(1)} %get-tuple-element.17), channel_id=1, source_target_pairs={{1,0},{2,1},{3,2},{4,3},{5,4},{6,5},{7,6},{8,7},{9,8},{10,9},{11,1... | collective-permute-start | bytes 73736 | tf_op jit(solution)/shard_map/ppermute | solution.py:42
  251.3 9.5 %collective-permute-start.27 = (f32[32,1,192]{2,1,0:T(1,128)S(1)}, f32[32,1,192]{2,1,0:T(1,128)S(1)}, u32[]{:S(2)}, u32[]{:S(2)}) collective-permute-start(f32[32,1,192]{2,1,0:T(1,128)S(1)} %get-tuple-element.18), channel_id=1, source_target_pairs={{0,1},{1,2},{2,3},{3,4},{4,5},{5,6},{6,7},{7,8},{8,9},{9,10},{10,1... | collective-permute-start | bytes 73736 | tf_op jit(solution)/shard_map/ppermute | solution.py:41
  256.4 4.4 %collective-permute-start.25 = (f32[1,32,192]{2,1,0:T(8,128)S(1)}, f32[1,32,192]{2,1,0:T(8,128)S(1)}, u32[]{:S(2)}, u32[]{:S(2)}) collective-permute-start(f32[1,32,192]{2,1,0:T(8,128)S(1)} %get-tuple-element.19), channel_id=1, source_target_pairs={{0,16},{16,32},{32,48},{48,64},{64,80},{80,96},{96,112},{112,128},... | collective-permute-start | bytes 73736 | tf_op jit(solution)/shard_map/ppermute | solution.py:39
  259.5 4.7 %collective-permute-start.24 = (f32[1,32,192]{2,1,0:T(8,128)S(1)}, f32[1,32,192]{2,1,0:T(8,128)S(1)}, u32[]{:S(2)}, u32[]{:S(2)}) collective-permute-start(f32[1,32,192]{2,1,0:T(8,128)S(1)} %get-tuple-element.20), channel_id=1, source_target_pairs={{16,0},{32,16},{48,32},{64,48},{80,64},{96,80},{112,96},{128,112},... | collective-permute-start | bytes 73736 | tf_op jit(solution)/shard_map/ppermute | solution.py:40
  (48 other events, 437.6 us)

commit v11 on v10

--- a/solution.py
+++ b/solution.py
@@ -103,7 +103,7 @@
     coarse_block = pieces.reshape(rows_x * modes, cols_y * modes)
 
     def rounded_window(current):
-        return extended(current.astype(jnp.bfloat16), (("gx", 0), ("gy", 1)), margin)
+        return extended(current.astype(jnp.bfloat16), (("gy", 1), ("gx", 0)), margin)
 
     def precondition(current):
         window = rounded_window(current).reshape(extent * extent, fields)

time: 301 us -> 298 us (0.990)
    ppermute x4, starting transfers between devices: 19.2 us -> 15.1 us  [with_edges(): west = lax.ppermute(cells[:, -1:], 'gy', right)]
where the time goes in v11:
time: 298 us; the launch traced here: 295 us
  starting transfers between devices  146 us (49%)
  other arithmetic  41.4 us (14%)
  local copies, waits for them, and re-layouts  34 us (11%)
  blocking collectives  30.3 us (10%)
  waiting for transfers between devices  27.7 us (9%)
  matrix products  14 us (5%)
    all_to_all x3, starting transfers between devices, summed_by_exchange(): received = lax.all_to_all(flat, axis, 0, 0, tiled=True)  30.7 us
    all_to_all x2, blocking collectives, gathered_by_exchange(): lax.all_to_all(copies, axis, 0, 0, tiled=True)  30.3 us
    all_to_all x3, starting transfers between devices, gathered_by_exchange(): lax.all_to_all(copies, axis, 0, 0, tiled=True)  24.1 us
    ppermute x6, starting transfers between devices, extended(): lax.ppermute(tail, axis, [(i, (i + 1) % count) for i in range(ends)])  23.3 us
    ppermute x4, starting transfers between devices, with_edges(): north = lax.ppermute(cells[-1:], 'gx', down)  15.1 us
    ppermute x4, starting transfers between devices, with_edges(): west = lax.ppermute(cells[:, -1:], 'gy', right)  15.1 us
    all_to_all x1, starting transfers between devices, on_device(): pieces = lax.all_to_all(pieces, 'gx', 0, 0, tiled=True)  14 us
    all_to_all x3, waiting for transfers between devices, summed_by_exchange(): received = lax.all_to_all(flat, axis, 0, 0, tiled=True)  10.7 us
  transfers between devices with their start and end apart: 35, of which 9 were waited for; matrix products, arithmetic and copies ran while one was open for 17% of the time, Pallas kernels for 0%

profile of v11, /device:TPU:1, one launch (start us, length us, event | category | flops | bytes accessed | tf_op | source)
XLA Modules:
  0.0 295.4 jit_solution(10791660290263131728)
XLA Ops:
  0.6 14.0 %all-to-all-start = ((f32[32,8,128]{2,1,0:T(8,128)}), f32[32,8,128]{2,1,0:T(8,128)S(1)}, u32[]{:S(2)}, u32[]{:S(2)}) async-start(f32[32,8,128]{2,1,0:T(8,128)} %bitcast.88), calls=%async_computation | async-start | bytes 262144 | tf_op jit(solution)/shard_map/all_to_all | solution.py:101
  15.9 3.7 %collective-permute-start.6 = (f32[1,32]{1,0:T(1,128)}, f32[1,32]{1,0:T(1,128)}, u32[]{:S(2)}, u32[]{:S(2)}) collective-permute-start(f32[1,32]{1,0:T(1,128)} %get-tuple-element.55), channel_id=1, source_target_pairs={{0,16},{16,32},{32,48},{48,64},{64,80},{80,96},{96,112},{112,128},... | collective-permute-start | bytes 392 | tf_op jit(solution)/shard_map/ppermute | solution.py:39
  22.4 3.4 %collective-permute-start.8 = (f32[32,1]{1,0:T(8,128)}, f32[32,1]{1,0:T(8,128)}, u32[]{:S(2)}, u32[]{:S(2)}) collective-permute-start(f32[32,1]{1,0:T(8,128)} %get-tuple-element.53), channel_id=1, source_target_pairs={{1,0},{2,1},{3,2},{4,3},{5,4},{6,5},{7,6},{8,7},{9,8},{10,9},{11,1... | collective-permute-start | bytes 392 | tf_op jit(solution)/shard_map/ppermute | solution.py:42
  27.3 2.0 convolution_bitcast_fusion.2
  31.6 7.2 %all-to-all-start.1 = ((f32[16,1,1536]{2,1,0:T(1,128)}), f32[16,1,1536]{2,1,0:T(1,128)S(1)}, u32[]{:S(2)}, u32[]{:S(2)}) async-start(f32[16,1,1536]{2,1,0:T(1,128)} %broadcast_in_dim.19), calls=%async_computation.1 | async-start | bytes 196608 | tf_op jit(solution)/shard_map/all_to_all | solution.py:72
  39.8 3.5 %collective-permute-start = (bf16[32,4,192]{2,1,0:T(4,128)(2,1)S(1)}, bf16[32,4,192]{2,1,0:T(4,128)(2,1)S(1)}, u32[]{:S(2)}, u32[]{:S(2)}) collective-permute-start(bf16[32,4,192]{2,1,0:T(4,128)(2,1)S(1)} %get-tuple-element.39), channel_id=1, source_target_pairs={{0,1},{1,2},{2,3},{3,4},{4,5},{5,6},{6,7},{7,8},{8,9},{9,10},{10,1... | collective-permute-start | bytes 147464 | tf_op jit(solution)/shard_map/ppermute | solution.py:23
  43.4 1.9 collective-permute-start.1
  45.9 3.0 %collective-permute-done.1 = bf16[32,4,192]{2,1,0:T(4,128)(2,1)S(1)} collective-permute-done((bf16[32,4,192]{2,1,0:T(4,128)(2,1)S(1)}, bf16[32,4,192]{2,1,0:T(4,128)(2,1)S(1)}, u32[]{:S(2)}, u32[]{:S(2)}) %collective-permute-start.1) | collective-permute-done | bytes 49184 | tf_op jit(solution)/shard_map/ppermute | solution.py:25
  50.6 4.9 %collective-permute-start.2 = (bf16[4,40,192]{2,1,0:T(8,128)(2,1)}, bf16[4,40,192]{2,1,0:T(8,128)(2,1)}, u32[]{:S(2)}, u32[]{:S(2)}) collective-permute-start(bf16[4,40,192]{2,1,0:T(8,128)(2,1)} %get-tuple-element.33), channel_id=1, source_target_pairs={{0,16},{16,32},{32,48},{48,64},{64,80},{80,96},{96,112},{112,128},... | collective-permute-start | bytes 184328 | tf_op jit(solution)/shard_map/ppermute | solution.py:23
  61.5 11.5 %all-to-all-start.2 = ((f32[32,1,1536]{2,1,0:T(1,128)}), f32[32,1,1536]{2,1,0:T(1,128)}, u32[]{:S(2)}, u32[]{:S(2)}) async-start(f32[32,1,1536]{2,1,0:T(1,128)} %all_to_all.53), calls=%async_computation.2 | async-start | bytes 393216 | tf_op jit(solution)/shard_map/all_to_all | solution.py:78
  73.0 2.7 collective-permute-start.10
  79.1 2.5 copy.48
  86.3 2.3 broadcast_multiply_fusion
  88.7 1.9 collective-permute-start.9
  90.6 3.6 %collective-permute-start.11 = (f32[32,1,192]{2,1,0:T(1,128)S(1)}, f32[32,1,192]{2,1,0:T(1,128)S(1)}, u32[]{:S(2)}, u32[]{:S(2)}) collective-permute-start(f32[32,1,192]{2,1,0:T(1,128)S(1)} %get-tuple-element.26), channel_id=1, source_target_pairs={{0,1},{1,2},{2,3},{3,4},{4,5},{5,6},{6,7},{7,8},{8,9},{9,10},{10,1... | collective-permute-start | bytes 73736 | tf_op jit(solution)/shard_map/ppermute | solution.py:41
  94.3 4.2 %collective-permute-start.7 = (f32[1,32,192]{2,1,0:T(8,128)S(1)}, f32[1,32,192]{2,1,0:T(8,128)S(1)}, u32[]{:S(2)}, u32[]{:S(2)}) collective-permute-start(f32[1,32,192]{2,1,0:T(8,128)S(1)} %get-tuple-element.27), channel_id=1, source_target_pairs={{0,16},{16,32},{32,48},{48,64},{64,80},{80,96},{96,112},{112,128},... | collective-permute-start | bytes 73736 | tf_op jit(solution)/shard_map/ppermute | solution.py:39
  100.7 2.4 collective-permute-done.5
  103.1 4.0 %multiply_reduce_fusion.1 = (f32[192]{0:T(256)}, f32[32,32,192]{2,1,0:T(8,128)S(1)}) fusion(f32[32,32,192]{2,1,0:T(8,128)S(1)} %copy-done.5, f32[32,32,192]{2,1,0:T(8,128)S(1)} %broadcast_multiply_fusion, f32[1,32,192]{2,1,0:T(8,128)S(1)} %collective-permute-done.5, f32[1,32,192]{2,1,0:T(8,128)S(1)} %collective-permute-done.7, ...), kind=kLoop, calls=%fused_computation.86 | loop fusion | flops 9043776 | bytes 3304192 | tf_op jit(solution)/shard_map/reduce_sum | solution.py:114
  112.2 7.4 %all-to-all-start.3 = ((f32[16,1,1536]{2,1,0:T(1,128)}), f32[16,1,1536]{2,1,0:T(1,128)}, u32[]{:S(2)}, u32[]{:S(2)}) async-start(f32[16,1,1536]{2,1,0:T(1,128)} %broadcast_in_dim.21), calls=%async_computation.3 | async-start | bytes 196608 | tf_op jit(solution)/shard_map/all_to_all | solution.py:72
  120.6 3.5 %collective-permute-start.12 = (bf16[32,4,192]{2,1,0:T(4,128)(2,1)S(1)}, bf16[32,4,192]{2,1,0:T(4,128)(2,1)S(1)}, u32[]{:S(2)}, u32[]{:S(2)}) collective-permute-start(bf16[32,4,192]{2,1,0:T(4,128)(2,1)S(1)} %get-tuple-element.37), channel_id=1, source_target_pairs={{0,1},{1,2},{2,3},{3,4},{4,5},{5,6},{6,7},{7,8},{8,9},{9,10},{10,1... | collective-permute-start | bytes 147464 | tf_op jit(solution)/shard_map/ppermute | solution.py:23
  124.1 1.9 collective-permute-start.13
  126.1 3.6 %collective-permute-done.13 = bf16[32,4,192]{2,1,0:T(4,128)(2,1)S(1)} collective-permute-done((bf16[32,4,192]{2,1,0:T(4,128)(2,1)S(1)}, bf16[32,4,192]{2,1,0:T(4,128)(2,1)S(1)}, u32[]{:S(2)}, u32[]{:S(2)}) %collective-permute-start.13) | collective-permute-done | bytes 49184 | tf_op jit(solution)/shard_map/ppermute | solution.py:25
  131.3 3.1 %collective-permute-start.14 = (bf16[4,40,192]{2,1,0:T(8,128)(2,1)}, bf16[4,40,192]{2,1,0:T(8,128)(2,1)}, u32[]{:S(2)}, u32[]{:S(2)}) collective-permute-start(bf16[4,40,192]{2,1,0:T(8,128)(2,1)} %get-tuple-element.31), channel_id=1, source_target_pairs={{0,16},{16,32},{32,48},{48,64},{64,80},{80,96},{96,112},{112,128},... | collective-permute-start | bytes 184328 | tf_op jit(solution)/shard_map/ppermute | solution.py:23
  139.2 2.0 fusion.64
  143.0 11.0 %all-to-all-start.4 = ((f32[32,1,1536]{2,1,0:T(1,128)}), f32[32,1,1536]{2,1,0:T(1,128)}, u32[]{:S(2)}, u32[]{:S(2)}) async-start(f32[32,1,1536]{2,1,0:T(1,128)} %all_to_all.54), calls=%async_computation.4 | async-start | bytes 393216 | tf_op jit(solution)/shard_map/all_to_all | solution.py:78
  157.5 2.4 copy.52
  159.9 4.2 %all-to-all-done.4 = f32[32,1,1536]{2,1,0:T(1,128)} async-done(((f32[32,1,1536]{2,1,0:T(1,128)}), f32[32,1,1536]{2,1,0:T(1,128)}, u32[]{:S(2)}, u32[]{:S(2)}) %all-to-all-start.4) | async-done | bytes 196640 | tf_op jit(solution)/shard_map/all_to_all | solution.py:78
  166.8 3.5 %multiply_add_fusion.1 = f32[32,32,192]{2,1,0:T(8,128)S(1)} fusion(f32[32,32,192]{2,1,0:T(8,128)} %bitcast.82, f32[192]{0:T(256)S(1)} %get-tuple-element.66, f32[192]{0:T(256)S(1)} %get-tuple-element.67, f32[192]{0:T(256)S(1)} %get-tuple-element.68, f32[192]{0:T(256)S(1)} %get-tuple-element.69, f32[192]{0:T(256)S(1)} %get-tuple-element.70, ...), kind=kLoop, calls=%fused_computation.90 | loop fusion | flops 6881280 | bytes 2404352 | tf_op jit(solution)/shard_map/add | solution.py:142
  170.4 3.1 %collective-permute-start.17 = (f32[1,32,192]{2,1,0:T(8,128)S(1)}, f32[1,32,192]{2,1,0:T(8,128)S(1)}, u32[]{:S(2)}, u32[]{:S(2)}) collective-permute-start(f32[1,32,192]{2,1,0:T(8,128)S(1)} %get-tuple-element.23), channel_id=1, source_target_pairs={{0,16},{16,32},{32,48},{48,64},{64,80},{80,96},{96,112},{112,128},... | collective-permute-start | bytes 73736 | tf_op jit(solution)/shard_map/ppermute | solution.py:39
  174.8 1.9 collective-permute-start.18
  176.8 5.1 %collective-permute-start.19 = (f32[32,1,192]{2,1,0:T(1,128)S(1)}, f32[32,1,192]{2,1,0:T(1,128)S(1)}, u32[]{:S(2)}, u32[]{:S(2)}) collective-permute-start(f32[32,1,192]{2,1,0:T(1,128)S(1)} %get-tuple-element.22), channel_id=1, source_target_pairs={{0,1},{1,2},{2,3},{3,4},{4,5},{5,6},{6,7},{7,8},{8,9},{9,10},{10,1... | collective-permute-start | bytes 73736 | tf_op jit(solution)/shard_map/ppermute | solution.py:41
  182.9 2.4 fusion.82
  189.0 9.5 %all-to-all-start.5 = ((f32[16,1,1536]{2,1,0:T(1,128)}), f32[16,1,1536]{2,1,0:T(1,128)S(1)}, u32[]{:S(2)}, u32[]{:S(2)}) async-start(f32[16,1,1536]{2,1,0:T(1,128)} %broadcast_in_dim.23), calls=%async_computation.5 | async-start | bytes 196608 | tf_op jit(solution)/shard_map/all_to_all | solution.py:72
  199.5 3.5 %collective-permute-start.20 = (bf16[32,4,192]{2,1,0:T(4,128)(2,1)S(1)}, bf16[32,4,192]{2,1,0:T(4,128)(2,1)S(1)}, u32[]{:S(2)}, u32[]{:S(2)}) collective-permute-start(bf16[32,4,192]{2,1,0:T(4,128)(2,1)S(1)} %get-tuple-element.35), channel_id=1, source_target_pairs={{0,1},{1,2},{2,3},{3,4},{4,5},{5,6},{6,7},{7,8},{8,9},{9,10},{10,1... | collective-permute-start | bytes 147464 | tf_op jit(solution)/shard_map/ppermute | solution.py:23
  203.1 1.9 collective-permute-start.21
  205.0 3.6 %collective-permute-done.21 = bf16[32,4,192]{2,1,0:T(4,128)(2,1)S(1)} collective-permute-done((bf16[32,4,192]{2,1,0:T(4,128)(2,1)S(1)}, bf16[32,4,192]{2,1,0:T(4,128)(2,1)S(1)}, u32[]{:S(2)}, u32[]{:S(2)}) %collective-permute-start.21) | collective-permute-done | bytes 49184 | tf_op jit(solution)/shard_map/ppermute | solution.py:25
  210.3 4.6 %collective-permute-start.22 = (bf16[4,40,192]{2,1,0:T(8,128)(2,1)}, bf16[4,40,192]{2,1,0:T(8,128)(2,1)}, u32[]{:S(2)}, u32[]{:S(2)}) collective-permute-start(bf16[4,40,192]{2,1,0:T(8,128)(2,1)} %get-tuple-element.29), channel_id=1, source_target_pairs={{0,16},{16,32},{32,48},{48,64},{64,80},{80,96},{96,112},{112,128},... | collective-permute-start | bytes 184328 | tf_op jit(solution)/shard_map/ppermute | solution.py:23
  219.1 1.9 all_to_all.55
  221.0 8.2 %all-to-all-start.6 = ((f32[32,1,1536]{2,1,0:T(1,128)}), f32[32,1,1536]{2,1,0:T(1,128)S(1)}, u32[]{:S(2)}, u32[]{:S(2)}) async-start(f32[32,1,1536]{2,1,0:T(1,128)} %all_to_all.55), calls=%async_computation.6 | async-start | bytes 393216 | tf_op jit(solution)/shard_map/all_to_all | solution.py:78
  232.5 2.5 copy.56
  235.0 4.6 %all-to-all-done.6 = f32[32,1,1536]{2,1,0:T(1,128)S(1)} async-done(((f32[32,1,1536]{2,1,0:T(1,128)}), f32[32,1,1536]{2,1,0:T(1,128)S(1)}, u32[]{:S(2)}, u32[]{:S(2)}) %all-to-all-start.6) | async-done | bytes 196640 | tf_op jit(solution)/shard_map/all_to_all | solution.py:78
  241.4 5.6 %add_add_fusion = (f32[32,32,192]{2,1,0:T(8,128)}, f32[32,32,192]{2,1,0:T(8,128)S(1)}) fusion(f32[32,32,192]{2,1,0:T(8,128)} %bitcast.81, f32[192]{0:T(256)} %copy-done.44, f32[32,32]{1,0:T(8,128)} %get-tuple-element.48, f32[192]{0:T(256)} %copy-done.45, f32[32,32]{1,0:T(8,128)} %get-tuple-element.47, f32[192]{0:T(256)} %copy-done.46, ...), kind=kLoop, calls=%fused_computation.89 | loop fusion | flops 11403264 | bytes 4769792 | tf_op jit(solution)/shard_map/add | solution.py:135
  247.2 1.9 collective-permute-start.26
  249.1 3.6 %collective-permute-start.27 = (f32[32,1,192]{2,1,0:T(1,128)S(1)}, f32[32,1,192]{2,1,0:T(1,128)S(1)}, u32[]{:S(2)}, u32[]{:S(2)}) collective-permute-start(f32[32,1,192]{2,1,0:T(1,128)S(1)} %get-tuple-element.18), channel_id=1, source_target_pairs={{0,1},{1,2},{2,3},{3,4},{4,5},{5,6},{6,7},{7,8},{8,9},{9,10},{10,1... | collective-permute-start | bytes 73736 | tf_op jit(solution)/shard_map/ppermute | solution.py:41
  252.7 4.2 %collective-permute-start.25 = (f32[1,32,192]{2,1,0:T(8,128)S(1)}, f32[1,32,192]{2,1,0:T(8,128)S(1)}, u32[]{:S(2)}, u32[]{:S(2)}) collective-permute-start(f32[1,32,192]{2,1,0:T(8,128)S(1)} %get-tuple-element.19), channel_id=1, source_target_pairs={{0,16},{16,32},{32,48},{48,64},{64,80},{80,96},{96,112},{112,128},... | collective-permute-start | bytes 73736 | tf_op jit(solution)/shard_map/ppermute | solution.py:39
  258.3 3.3 %collective-permute-done.24 = f32[1,32,192]{2,1,0:T(8,128)S(1)} collective-permute-done((f32[1,32,192]{2,1,0:T(8,128)S(1)}, f32[1,32,192]{2,1,0:T(8,128)S(1)}, u32[]{:S(2)}, u32[]{:S(2)}) %collective-permute-start.24) | collective-permute-done | bytes 24608 | tf_op jit(solution)/shard_map/ppermute | solution.py:40
  263.6 14.6 %all_to_all.65 = f32[16,1,768]{2,1,0:T(1,128)S(1)} all-to-all(f32[16,1,768]{2,1,0:T(1,128)S(1)} %broadcast_in_dim.25), channel_id=1, replica_groups=mesh['gx'=32,'gy'=16] {'gy'}, dimensions={0} | all-to-all | bytes 98304 | tf_op jit(solution)/shard_map/all_to_all | solution.py:72
  278.3 15.7 %all_to_all.66 = f32[32,1,768]{2,1,0:T(1,128)S(1)} all-to-all(f32[32,1,768]{2,1,0:T(1,128)S(1)} %broadcast_in_dim.26), channel_id=1, replica_groups=mesh['gx'=32,'gy'=16] {'gx'}, dimensions={0} | all-to-all | bytes 196608 | tf_op jit(solution)/shard_map/all_to_all | solution.py:72
  (216 shorter events, 70.2 us)
Async XLA Ops:
  0.6 76.7 %copy-start = (bf16[1,1,1024,1600]{2,3,1,0:T(8,128)(2,1)S(1)}, bf16[1,1,1024,1600]{2,3,1,0:T(8,128)(2,1)}, u32[]{:S(2)}) copy-start(bf16[1,1,1024,1600]{2,3,1,0:T(8,128)(2,1)} %param.10) | copy-start | bytes 9830404
  0.6 26.7 %all-to-all-start = ((f32[32,8,128]{2,1,0:T(8,128)}), f32[32,8,128]{2,1,0:T(8,128)S(1)}, u32[]{:S(2)}, u32[]{:S(2)}) async-start(f32[32,8,128]{2,1,0:T(8,128)} %bitcast.88), calls=%async_computation | async-start | bytes 262144 | tf_op jit(solution)/shard_map/all_to_all | solution.py:101
  15.9 74.7 %collective-permute-start.6 = (f32[1,32]{1,0:T(1,128)}, f32[1,32]{1,0:T(1,128)}, u32[]{:S(2)}, u32[]{:S(2)}) collective-permute-start(f32[1,32]{1,0:T(1,128)} %get-tuple-element.55), channel_id=1, source_target_pairs={{0,16},{16,32},{32,48},{48,64},{64,80},{80,96},{96,112},{112,128},... | collective-permute-start | bytes 392 | tf_op jit(solution)/shard_map/ppermute | solution.py:39
  19.6 74.6 %collective-permute-start.4 = (f32[1,32]{1,0:T(1,128)}, f32[1,32]{1,0:T(1,128)}, u32[]{:S(2)}, u32[]{:S(2)}) collective-permute-start(f32[1,32]{1,0:T(1,128)} %get-tuple-element.56), channel_id=1, source_target_pairs={{16,0},{32,16},{48,32},{64,48},{80,64},{96,80},{112,96},{128,112},... | collective-permute-start | bytes 392 | tf_op jit(solution)/shard_map/ppermute | solution.py:40
  22.4 76.1 %collective-permute-start.8 = (f32[32,1]{1,0:T(8,128)}, f32[32,1]{1,0:T(8,128)}, u32[]{:S(2)}, u32[]{:S(2)}) collective-permute-start(f32[32,1]{1,0:T(8,128)} %get-tuple-element.53), channel_id=1, source_target_pairs={{1,0},{2,1},{3,2},{4,3},{5,4},{6,5},{7,6},{8,7},{9,8},{10,9},{11,1... | collective-permute-start | bytes 392 | tf_op jit(solution)/shard_map/ppermute | solution.py:42
  31.6 25.2 %all-to-all-start.1 = ((f32[16,1,1536]{2,1,0:T(1,128)}), f32[16,1,1536]{2,1,0:T(1,128)S(1)}, u32[]{:S(2)}, u32[]{:S(2)}) async-start(f32[16,1,1536]{2,1,0:T(1,128)} %broadcast_in_dim.19), calls=%async_computation.1 | async-start | bytes 196608 | tf_op jit(solution)/shard_map/all_to_all | solution.py:72
  39.8 6.1 %collective-permute-start = (bf16[32,4,192]{2,1,0:T(4,128)(2,1)S(1)}, bf16[32,4,192]{2,1,0:T(4,128)(2,1)S(1)}, u32[]{:S(2)}, u32[]{:S(2)}) collective-permute-start(bf16[32,4,192]{2,1,0:T(4,128)(2,1)S(1)} %get-tuple-element.39), channel_id=1, source_target_pairs={{0,1},{1,2},{2,3},{3,4},{4,5},{5,6},{6,7},{7,8},{8,9},{9,10},{10,1... | collective-permute-start | bytes 147464 | tf_op jit(solution)/shard_map/ppermute | solution.py:23
  43.4 5.6 %collective-permute-start.1 = (bf16[32,4,192]{2,1,0:T(4,128)(2,1)S(1)}, bf16[32,4,192]{2,1,0:T(4,128)(2,1)S(1)}, u32[]{:S(2)}, u32[]{:S(2)}) collective-permute-start(bf16[32,4,192]{2,1,0:T(4,128)(2,1)S(1)} %get-tuple-element.40), channel_id=1, source_target_pairs={{1,0},{2,1},{3,2},{4,3},{5,4},{6,5},{7,6},{8,7},{9,8},{10,9},{11,1... | collective-permute-start | bytes 147464 | tf_op jit(solution)/shard_map/ppermute | solution.py:25
  50.6 22.4 %collective-permute-start.2 = (bf16[4,40,192]{2,1,0:T(8,128)(2,1)}, bf16[4,40,192]{2,1,0:T(8,128)(2,1)}, u32[]{:S(2)}, u32[]{:S(2)}) collective-permute-start(bf16[4,40,192]{2,1,0:T(8,128)(2,1)} %get-tuple-element.33), channel_id=1, source_target_pairs={{0,16},{16,32},{32,48},{48,64},{64,80},{80,96},{96,112},{112,128},... | collective-permute-start | bytes 184328 | tf_op jit(solution)/shard_map/ppermute | solution.py:23
  55.5 20.3 %collective-permute-start.3 = (bf16[4,40,192]{2,1,0:T(8,128)(2,1)}, bf16[4,40,192]{2,1,0:T(8,128)(2,1)}, u32[]{:S(2)}, u32[]{:S(2)}) collective-permute-start(bf16[4,40,192]{2,1,0:T(8,128)(2,1)} %get-tuple-element.34), channel_id=1, source_target_pairs={{16,0},{32,16},{48,32},{64,48},{80,64},{96,80},{112,96},{128,112},... | collective-permute-start | bytes 184328 | tf_op jit(solution)/shard_map/ppermute | solution.py:25
  61.5 22.0 %all-to-all-start.2 = ((f32[32,1,1536]{2,1,0:T(1,128)}), f32[32,1,1536]{2,1,0:T(1,128)}, u32[]{:S(2)}, u32[]{:S(2)}) async-start(f32[32,1,1536]{2,1,0:T(1,128)} %all_to_all.53), calls=%async_computation.2 | async-start | bytes 393216 | tf_op jit(solution)/shard_map/all_to_all | solution.py:78
  73.0 26.7 %collective-permute-start.10 = (f32[32,1]{1,0:T(8,128)}, f32[32,1]{1,0:T(8,128)}, u32[]{:S(2)}, u32[]{:S(2)}) collective-permute-start(f32[32,1]{1,0:T(8,128)} %get-tuple-element.54), channel_id=1, source_target_pairs={{0,1},{1,2},{2,3},{3,4},{4,5},{5,6},{6,7},{7,8},{8,9},{9,10},{10,1... | collective-permute-start | bytes 392 | tf_op jit(solution)/shard_map/ppermute | solution.py:41
  86.1 21.0 %copy-start.43 = (f32[192]{0:T(256)}, f32[192]{0:T(256)S(1)}, u32[]{:S(2)}) copy-start(f32[192]{0:T(256)S(1)} %get-tuple-element.73) | copy-start | bytes 2308
  86.1 21.0 %copy-start.44 = (f32[192]{0:T(256)}, f32[192]{0:T(256)S(1)}, u32[]{:S(2)}) copy-start(f32[192]{0:T(256)S(1)} %get-tuple-element.74) | copy-start | bytes 2308
  86.1 21.0 %copy-start.45 = (f32[192]{0:T(256)}, f32[192]{0:T(256)S(1)}, u32[]{:S(2)}) copy-start(f32[192]{0:T(256)S(1)} %get-tuple-element.75) | copy-start | bytes 2308
  86.1 21.0 %copy-start.46 = (f32[192]{0:T(256)}, f32[192]{0:T(256)S(1)}, u32[]{:S(2)}) copy-start(f32[192]{0:T(256)S(1)} %get-tuple-element.76) | copy-start | bytes 2308
  86.2 21.0 %copy-start.47 = (f32[192]{0:T(256)}, f32[192]{0:T(256)S(1)}, u32[]{:S(2)}) copy-start(f32[192]{0:T(256)S(1)} %get-tuple-element.77) | copy-start | bytes 2308
  86.2 21.0 %copy-start.48 = (f32[192]{0:T(256)}, f32[192]{0:T(256)S(1)}, u32[]{:S(2)}) copy-start(f32[192]{0:T(256)S(1)} %get-tuple-element.78) | copy-start | bytes 2308
  86.2 21.0 %copy-start.49 = (f32[192]{0:T(256)}, f32[192]{0:T(256)S(1)}, u32[]{:S(2)}) copy-start(f32[192]{0:T(256)S(1)} %get-tuple-element.79) | copy-start | bytes 2308
  86.2 21.0 %copy-start.50 = (f32[192]{0:T(256)}, f32[192]{0:T(256)S(1)}, u32[]{:S(2)}) copy-start(f32[192]{0:T(256)S(1)} %get-tuple-element.80) | copy-start | bytes 2308
  88.7 12.0 %collective-permute-start.9 = (f32[32,1,192]{2,1,0:T(1,128)S(1)}, f32[32,1,192]{2,1,0:T(1,128)S(1)}, u32[]{:S(2)}, u32[]{:S(2)}) collective-permute-start(f32[32,1,192]{2,1,0:T(1,128)S(1)} %get-tuple-element.25), channel_id=1, source_target_pairs={{1,0},{2,1},{3,2},{4,3},{5,4},{6,5},{7,6},{8,7},{9,8},{10,9},{11,1... | collective-permute-start | bytes 73736 | tf_op jit(solution)/shard_map/ppermute | solution.py:42
  90.6 10.1 %collective-permute-start.11 = (f32[32,1,192]{2,1,0:T(1,128)S(1)}, f32[32,1,192]{2,1,0:T(1,128)S(1)}, u32[]{:S(2)}, u32[]{:S(2)}) collective-permute-start(f32[32,1,192]{2,1,0:T(1,128)S(1)} %get-tuple-element.26), channel_id=1, source_target_pairs={{0,1},{1,2},{2,3},{3,4},{4,5},{5,6},{6,7},{7,8},{8,9},{9,10},{10,1... | collective-permute-start | bytes 73736 | tf_op jit(solution)/shard_map/ppermute | solution.py:41
  94.3 6.5 %collective-permute-start.7 = (f32[1,32,192]{2,1,0:T(8,128)S(1)}, f32[1,32,192]{2,1,0:T(8,128)S(1)}, u32[]{:S(2)}, u32[]{:S(2)}) collective-permute-start(f32[1,32,192]{2,1,0:T(8,128)S(1)} %get-tuple-element.27), channel_id=1, source_target_pairs={{0,16},{16,32},{32,48},{48,64},{64,80},{80,96},{96,112},{112,128},... | collective-permute-start | bytes 73736 | tf_op jit(solution)/shard_map/ppermute | solution.py:39
  98.4 4.7 %collective-permute-start.5 = (f32[1,32,192]{2,1,0:T(8,128)S(1)}, f32[1,32,192]{2,1,0:T(8,128)S(1)}, u32[]{:S(2)}, u32[]{:S(2)}) collective-permute-start(f32[1,32,192]{2,1,0:T(8,128)S(1)} %get-tuple-element.28), channel_id=1, source_target_pairs={{16,0},{32,16},{48,32},{64,48},{80,64},{96,80},{112,96},{128,112},... | collective-permute-start | bytes 73736 | tf_op jit(solution)/shard_map/ppermute | solution.py:40
  112.2 23.6 %all-to-all-start.3 = ((f32[16,1,1536]{2,1,0:T(1,128)}), f32[16,1,1536]{2,1,0:T(1,128)}, u32[]{:S(2)}, u32[]{:S(2)}) async-start(f32[16,1,1536]{2,1,0:T(1,128)} %broadcast_in_dim.21), calls=%async_computation.3 | async-start | bytes 196608 | tf_op jit(solution)/shard_map/all_to_all | solution.py:72
  120.6 5.5 %collective-permute-start.12 = (bf16[32,4,192]{2,1,0:T(4,128)(2,1)S(1)}, bf16[32,4,192]{2,1,0:T(4,128)(2,1)S(1)}, u32[]{:S(2)}, u32[]{:S(2)}) collective-permute-start(bf16[32,4,192]{2,1,0:T(4,128)(2,1)S(1)} %get-tuple-element.37), channel_id=1, source_target_pairs={{0,1},{1,2},{2,3},{3,4},{4,5},{5,6},{6,7},{7,8},{8,9},{9,10},{10,1... | collective-permute-start | bytes 147464 | tf_op jit(solution)/shard_map/ppermute | solution.py:23
  124.1 5.6 %collective-permute-start.13 = (bf16[32,4,192]{2,1,0:T(4,128)(2,1)S(1)}, bf16[32,4,192]{2,1,0:T(4,128)(2,1)S(1)}, u32[]{:S(2)}, u32[]{:S(2)}) collective-permute-start(bf16[32,4,192]{2,1,0:T(4,128)(2,1)S(1)} %get-tuple-element.38), channel_id=1, source_target_pairs={{1,0},{2,1},{3,2},{4,3},{5,4},{6,5},{7,6},{8,7},{9,8},{10,9},{11,1... | collective-permute-start | bytes 147464 | tf_op jit(solution)/shard_map/ppermute | solution.py:25
  131.3 22.7 %collective-permute-start.14 = (bf16[4,40,192]{2,1,0:T(8,128)(2,1)}, bf16[4,40,192]{2,1,0:T(8,128)(2,1)}, u32[]{:S(2)}, u32[]{:S(2)}) collective-permute-start(bf16[4,40,192]{2,1,0:T(8,128)(2,1)} %get-tuple-element.31), channel_id=1, source_target_pairs={{0,16},{16,32},{32,48},{48,64},{64,80},{80,96},{96,112},{112,128},... | collective-permute-start | bytes 184328 | tf_op jit(solution)/shard_map/ppermute | solution.py:23
  134.5 19.6 %collective-permute-start.15 = (bf16[4,40,192]{2,1,0:T(8,128)(2,1)}, bf16[4,40,192]{2,1,0:T(8,128)(2,1)}, u32[]{:S(2)}, u32[]{:S(2)}) collective-permute-start(bf16[4,40,192]{2,1,0:T(8,128)(2,1)} %get-tuple-element.32), channel_id=1, source_target_pairs={{16,0},{32,16},{48,32},{64,48},{80,64},{96,80},{112,96},{128,112},... | collective-permute-start | bytes 184328 | tf_op jit(solution)/shard_map/ppermute | solution.py:25
  143.0 21.0 %all-to-all-start.4 = ((f32[32,1,1536]{2,1,0:T(1,128)}), f32[32,1,1536]{2,1,0:T(1,128)}, u32[]{:S(2)}, u32[]{:S(2)}) async-start(f32[32,1,1536]{2,1,0:T(1,128)} %all_to_all.54), calls=%async_computation.4 | async-start | bytes 393216 | tf_op jit(solution)/shard_map/all_to_all | solution.py:78
  170.4 11.4 %collective-permute-start.17 = (f32[1,32,192]{2,1,0:T(8,128)S(1)}, f32[1,32,192]{2,1,0:T(8,128)S(1)}, u32[]{:S(2)}, u32[]{:S(2)}) collective-permute-start(f32[1,32,192]{2,1,0:T(8,128)S(1)} %get-tuple-element.23), channel_id=1, source_target_pairs={{0,16},{16,32},{32,48},{48,64},{64,80},{80,96},{96,112},{112,128},... | collective-permute-start | bytes 73736 | tf_op jit(solution)/shard_map/ppermute | solution.py:39
  173.5 8.3 %collective-permute-start.16 = (f32[1,32,192]{2,1,0:T(8,128)S(1)}, f32[1,32,192]{2,1,0:T(8,128)S(1)}, u32[]{:S(2)}, u32[]{:S(2)}) collective-permute-start(f32[1,32,192]{2,1,0:T(8,128)S(1)} %get-tuple-element.24), channel_id=1, source_target_pairs={{16,0},{32,16},{48,32},{64,48},{80,64},{96,80},{112,96},{128,112},... | collective-permute-start | bytes 73736 | tf_op jit(solution)/shard_map/ppermute | solution.py:40
  174.8 7.1 %collective-permute-start.18 = (f32[32,1,192]{2,1,0:T(1,128)S(1)}, f32[32,1,192]{2,1,0:T(1,128)S(1)}, u32[]{:S(2)}, u32[]{:S(2)}) collective-permute-start(f32[32,1,192]{2,1,0:T(1,128)S(1)} %get-tuple-element.21), channel_id=1, source_target_pairs={{1,0},{2,1},{3,2},{4,3},{5,4},{6,5},{7,6},{8,7},{9,8},{10,9},{11,1... | collective-permute-start | bytes 73736 | tf_op jit(solution)/shard_map/ppermute | solution.py:42
  176.8 6.1 %collective-permute-start.19 = (f32[32,1,192]{2,1,0:T(1,128)S(1)}, f32[32,1,192]{2,1,0:T(1,128)S(1)}, u32[]{:S(2)}, u32[]{:S(2)}) collective-permute-start(f32[32,1,192]{2,1,0:T(1,128)S(1)} %get-tuple-element.22), channel_id=1, source_target_pairs={{0,1},{1,2},{2,3},{3,4},{4,5},{5,6},{6,7},{7,8},{8,9},{9,10},{10,1... | collective-permute-start | bytes 73736 | tf_op jit(solution)/shard_map/ppermute | solution.py:41
  189.0 27.2 %all-to-all-start.5 = ((f32[16,1,1536]{2,1,0:T(1,128)}), f32[16,1,1536]{2,1,0:T(1,128)S(1)}, u32[]{:S(2)}, u32[]{:S(2)}) async-start(f32[16,1,1536]{2,1,0:T(1,128)} %broadcast_in_dim.23), calls=%async_computation.5 | async-start | bytes 196608 | tf_op jit(solution)/shard_map/all_to_all | solution.py:72
  199.5 5.5 %collective-permute-start.20 = (bf16[32,4,192]{2,1,0:T(4,128)(2,1)S(1)}, bf16[32,4,192]{2,1,0:T(4,128)(2,1)S(1)}, u32[]{:S(2)}, u32[]{:S(2)}) collective-permute-start(bf16[32,4,192]{2,1,0:T(4,128)(2,1)S(1)} %get-tuple-element.35), channel_id=1, source_target_pairs={{0,1},{1,2},{2,3},{3,4},{4,5},{5,6},{6,7},{7,8},{8,9},{9,10},{10,1... | collective-permute-start | bytes 147464 | tf_op jit(solution)/shard_map/ppermute | solution.py:23
  203.1 5.6 %collective-permute-start.21 = (bf16[32,4,192]{2,1,0:T(4,128)(2,1)S(1)}, bf16[32,4,192]{2,1,0:T(4,128)(2,1)S(1)}, u32[]{:S(2)}, u32[]{:S(2)}) collective-permute-start(bf16[32,4,192]{2,1,0:T(4,128)(2,1)S(1)} %get-tuple-element.36), channel_id=1, source_target_pairs={{1,0},{2,1},{3,2},{4,3},{5,4},{6,5},{7,6},{8,7},{9,8},{10,9},{11,1... | collective-permute-start | bytes 147464 | tf_op jit(solution)/shard_map/ppermute | solution.py:25
  210.3 18.9 %collective-permute-start.22 = (bf16[4,40,192]{2,1,0:T(8,128)(2,1)}, bf16[4,40,192]{2,1,0:T(8,128)(2,1)}, u32[]{:S(2)}, u32[]{:S(2)}) collective-permute-start(bf16[4,40,192]{2,1,0:T(8,128)(2,1)} %get-tuple-element.29), channel_id=1, source_target_pairs={{0,16},{16,32},{32,48},{48,64},{64,80},{80,96},{96,112},{112,128},... | collective-permute-start | bytes 184328 | tf_op jit(solution)/shard_map/ppermute | solution.py:23
  214.9 14.3 %collective-permute-start.23 = (bf16[4,40,192]{2,1,0:T(8,128)(2,1)}, bf16[4,40,192]{2,1,0:T(8,128)(2,1)}, u32[]{:S(2)}, u32[]{:S(2)}) collective-permute-start(bf16[4,40,192]{2,1,0:T(8,128)(2,1)} %get-tuple-element.30), channel_id=1, source_target_pairs={{16,0},{32,16},{48,32},{64,48},{80,64},{96,80},{112,96},{128,112},... | collective-permute-start | bytes 184328 | tf_op jit(solution)/shard_map/ppermute | solution.py:25
  221.0 18.7 %all-to-all-start.6 = ((f32[32,1,1536]{2,1,0:T(1,128)}), f32[32,1,1536]{2,1,0:T(1,128)S(1)}, u32[]{:S(2)}, u32[]{:S(2)}) async-start(f32[32,1,1536]{2,1,0:T(1,128)} %all_to_all.55), calls=%async_computation.6 | async-start | bytes 393216 | tf_op jit(solution)/shard_map/all_to_all | solution.py:78
  241.4 20.2 %copy-start.7 = (f32[32,32,192]{2,1,0:T(8,128)S(1)}, f32[32,32,192]{2,1,0:T(8,128)}, u32[]{:S(2)}) copy-start(f32[32,32,192]{2,1,0:T(8,128)} %copy-done.6) | copy-start | bytes 2359300
  241.4 20.2 %copy-start.22 = (f32[32,32]{1,0:T(8,128)S(1)}, f32[32,32]{1,0:T(8,128)}, u32[]{:S(2)}) copy-start(f32[32,32]{1,0:T(8,128)} %copy-done.20) | copy-start | bytes 12292
  241.4 20.2 %copy-start.25 = (f32[32,32]{1,0:T(8,128)S(1)}, f32[32,32]{1,0:T(8,128)}, u32[]{:S(2)}) copy-start(f32[32,32]{1,0:T(8,128)} %copy-done.23) | copy-start | bytes 12292
  241.4 20.2 %copy-start.28 = (f32[32,32]{1,0:T(8,128)S(1)}, f32[32,32]{1,0:T(8,128)}, u32[]{:S(2)}) copy-start(f32[32,32]{1,0:T(8,128)} %copy-done.26) | copy-start | bytes 12292
  247.2 11.1 %collective-permute-start.26 = (f32[32,1,192]{2,1,0:T(1,128)S(1)}, f32[32,1,192]{2,1,0:T(1,128)S(1)}, u32[]{:S(2)}, u32[]{:S(2)}) collective-permute-start(f32[32,1,192]{2,1,0:T(1,128)S(1)} %get-tuple-element.17), channel_id=1, source_target_pairs={{1,0},{2,1},{3,2},{4,3},{5,4},{6,5},{7,6},{8,7},{9,8},{10,9},{11,1... | collective-permute-start | bytes 73736 | tf_op jit(solution)/shard_map/ppermute | solution.py:42
  249.1 9.1 %collective-permute-start.27 = (f32[32,1,192]{2,1,0:T(1,128)S(1)}, f32[32,1,192]{2,1,0:T(1,128)S(1)}, u32[]{:S(2)}, u32[]{:S(2)}) collective-permute-start(f32[32,1,192]{2,1,0:T(1,128)S(1)} %get-tuple-element.18), channel_id=1, source_target_pairs={{0,1},{1,2},{2,3},{3,4},{4,5},{5,6},{6,7},{7,8},{8,9},{9,10},{10,1... | collective-permute-start | bytes 73736 | tf_op jit(solution)/shard_map/ppermute | solution.py:41
  252.7 5.5 %collective-permute-start.25 = (f32[1,32,192]{2,1,0:T(8,128)S(1)}, f32[1,32,192]{2,1,0:T(8,128)S(1)}, u32[]{:S(2)}, u32[]{:S(2)}) collective-permute-start(f32[1,32,192]{2,1,0:T(8,128)S(1)} %get-tuple-element.19), channel_id=1, source_target_pairs={{0,16},{16,32},{32,48},{48,64},{64,80},{80,96},{96,112},{112,128},... | collective-permute-start | bytes 73736 | tf_op jit(solution)/shard_map/ppermute | solution.py:39
  256.9 4.7 %collective-permute-start.24 = (f32[1,32,192]{2,1,0:T(8,128)S(1)}, f32[1,32,192]{2,1,0:T(8,128)S(1)}, u32[]{:S(2)}, u32[]{:S(2)}) collective-permute-start(f32[1,32,192]{2,1,0:T(8,128)S(1)} %get-tuple-element.20), channel_id=1, source_target_pairs={{16,0},{32,16},{48,32},{64,48},{80,64},{96,80},{112,96},{128,112},... | collective-permute-start | bytes 73736 | tf_op jit(solution)/shard_map/ppermute | solution.py:40
  (48 other events, 446.7 us)
